TPU v7x, 256 devices: a whole 4x4x8 slice. The times are simulated.
256 devices in a mesh: geo: 8 (over x, core), curve: 32 (over y, z).
Axes of the slice: x: 4, y: 4, z: 8, core: 2. Of those that a mesh axis runs over, the one named last changes fastest.
Arguments:
- tokens: bfloat16 [262144, 512], P(('geo', 'curve')), parts along dimension 0, may hold values from -80 to 80
- w_query: bfloat16 [512, 512], replicated, may hold values from -0.25 to 0.25
- w_keyval: bfloat16 [512, 1024], replicated, may hold values from -0.25 to 0.25
- w_out: bfloat16 [512, 512], replicated, may hold values from -0.25 to 0.25
- block_list: int32 [2048, 12], P(('geo', 'curve')), parts along dimension 0, may hold values from 0 to 255, as said below
- block_count: int32 [2048], P(('geo', 'curve')), parts along dimension 0, may hold values from 2 to 12, as said below
- bnd_ids: int32 [4096], P('geo'), parts along dimension 0, may hold values from 0 to 32767, as said below
Outputs:
- mixed: bfloat16 [262144, 512], P(('geo', 'curve')), parts along dimension 0
There are 8 independent parts, one for each index of `geo`. A program takes and returns all parts, laid end to end along the dimension named above; an argument that names none is the same for every part. Nothing has to cross between parts.
Inputs may be any that keep to these rules, and one draw needn't show every extreme that they name: `block_list`: entry 0 of row b is b itself; the other entries of a row are distinct blocks other than b whose owners lie at most two devices of curve away from b's owner (device index = block // 8); entries at or past block_count[b] are not used. `block_count`: it equals 12 on the first block of every device. `bnd_ids`: Distinct; listed in increasing order of owner id // 1024; exactly eight owners hold 128, 128, 96, 64, 48, 24, 16 and 8 of them, the other devices none.
All inputs are finite; a program needn't handle non-finite values.
Results may differ from a plain program's by a relative error of at most 0.012.
The roundings to bfloat16 on the way count: a program that leaves them out, or rounds other values in their place, can miss the bound.
Values may be sent and summed in bfloat16 or wider, within the bound.
No kernel may reach another device: no remote copies, remote signals or barrier semaphores. Data moves between devices by JAX's collectives and lax.ppermute only.
A program may use at most 128 MiB of HBM per device.

v0:
```python
import jax
import jax.numpy as jnp
from jax import lax
from jax.sharding import PartitionSpec as P

HEADS = 8
BLOCK = 128
NB = 12
BCAP = 128


def from_behind(value, axis, steps):
    count = lax.axis_size(axis)
    first, last = (max(0, -steps), min(count, count - steps))
    return lax.ppermute(value, axis, [(source, source + steps) for source in range(first, last)])


def head_major(rows, w_keyval, width):
    head_dim = width // HEADS
    weight = w_keyval.reshape(width, 2 * HEADS, head_dim)
    return jnp.einsum("td,dhe->hte", rows, weight, preferred_element_type=jnp.float32).astype(
        jnp.bfloat16
    )


def on_device(tokens, w_query, w_keyval, w_out, block_list, block_count, bnd_ids):
    tok_dev, width = tokens.shape
    head_dim = width // HEADS
    nblocks = tok_dev // BLOCK
    npairs = nblocks // 2
    nbound = bnd_ids.shape[0]
    scale = 1.0 / head_dim**0.5
    member = lax.axis_index("curve")
    query_w = w_query.reshape(width, HEADS, head_dim)
    queries = jnp.einsum(
        "gbtd,dhe->ghbte",
        tokens.reshape(npairs, 2, BLOCK, width),
        query_w,
        preferred_element_type=jnp.float32,
    ).astype(jnp.bfloat16)
    keyvals = head_major(tokens, w_keyval, width)
    pieces = []
    for offset in (-2, -1, 0, 1, 2):
        if offset == 0:
            pieces.append(keyvals)
        else:
            pieces.append(from_behind(keyvals, "curve", -offset))
    nearby = jnp.concatenate(pieces, axis=1).reshape(2 * HEADS, 5 * nblocks, BLOCK, head_dim)
    owner = bnd_ids // tok_dev
    my_start = jnp.sum((owner < member).astype(jnp.int32))
    padded_ids = jnp.concatenate([bnd_ids, jnp.zeros((BCAP,), jnp.int32)])
    my_ids = lax.dynamic_slice_in_dim(padded_ids, my_start, BCAP)
    local_pos = jnp.clip(my_ids - member * tok_dev, 0, tok_dev - 1)
    slot_range = jnp.arange(nbound, dtype=jnp.int32)
    owner_start = jnp.sum((owner[None, :] < owner[:, None]).astype(jnp.int32), axis=1)
    source = owner * BCAP + slot_range - owner_start
    rows = jnp.take(tokens, local_pos, axis=0)
    gathered = lax.all_gather(rows, "curve", axis=0, tiled=True)
    bnd_kv = head_major(jnp.take(gathered, source, axis=0), w_keyval, width)
    bkeys = bnd_kv[:HEADS]
    bvals = bnd_kv[HEADS:]
    first_block = (member - 2) * nblocks
    lists = (block_list - first_block).reshape(npairs, 2, NB)
    counts = block_count.reshape(npairs, 2)

    def attend(item):
        query, relative, count = item
        picked = jnp.take(nearby, relative.reshape(2 * NB), axis=1)
        picked = picked.reshape(2 * HEADS, 2, NB * BLOCK, head_dim)
        keys = picked[:HEADS]
        vals = picked[HEADS:]
        live = (jnp.arange(NB * BLOCK, dtype=jnp.int32) // BLOCK)[None, :] < count[:, None]
        near_scores = (
            jnp.einsum("hgqd,hgkd->hgqk", query, keys, preferred_element_type=jnp.float32) * scale
        )
        near_scores = jnp.where(live[None, :, None, :], near_scores, -1e30)
        far_scores = (
            jnp.einsum("hgqd,hkd->hgqk", query, bkeys, preferred_element_type=jnp.float32) * scale
        )
        top = jnp.maximum(
            jnp.max(near_scores, axis=-1, keepdims=True),
            jnp.max(far_scores, axis=-1, keepdims=True),
        )
        near_exp = jnp.exp(near_scores - top)
        far_exp = jnp.exp(far_scores - top)
        total = jnp.sum(near_exp, axis=-1, keepdims=True) + jnp.sum(far_exp, axis=-1, keepdims=True)
        near_w = (near_exp / total).astype(jnp.bfloat16)
        far_w = (far_exp / total).astype(jnp.bfloat16)
        ctx = jnp.einsum("hgqk,hgkd->hgqd", near_w, vals, preferred_element_type=jnp.float32)
        ctx = ctx + jnp.einsum("hgqk,hkd->hgqd", far_w, bvals, preferred_element_type=jnp.float32)
        return ctx.astype(jnp.bfloat16)

    context = lax.map(attend, (queries, lists, counts))
    out_w = w_out.reshape(HEADS, head_dim, width)
    mixed = jnp.einsum("phgqd,hde->pgqe", context, out_w, preferred_element_type=jnp.float32)
    return mixed.reshape(tok_dev, width).astype(jnp.bfloat16)


def solution(mesh):
    in_specs = (
        P(("geo", "curve"), None),
        P(),
        P(),
        P(),
        P(("geo", "curve"), None),
        P(("geo", "curve")),
        P("geo"),
    )
    out_specs = P(("geo", "curve"), None)
    return jax.shard_map(
        on_device, mesh=mesh, in_specs=in_specs, out_specs=out_specs, check_vma=False
    )
```

profile of v0, /device:TPU:18, one launch (start us, length us, event | category | flops | bytes accessed | tf_op | source)
XLA Modules:
  0.0 544.3 jit_solution(2532507902798652519)
XLA Ops:
  34.2 65.3 %collective-permute-done = bf16[16,1024,64]{1,2,0:T(8,128)(2,1)} collective-permute-done((bf16[16,1024,64]{1,2,0:T(8,128)(2,1)}, bf16[16,1024,64]{1,2,0:T(8,128)(2,1)}, u32[]{:S(2)}, u32[]{:S(2)}) %collective-permute-start) | collective-permute-done | bytes 2097184 | tf_op jit(solution)/shard_map/ppermute | solution.py:15
  102.8 81.8 %collective-permute-done.1 = bf16[16,1024,64]{1,2,0:T(8,128)(2,1)} collective-permute-done((bf16[16,1024,64]{1,2,0:T(8,128)(2,1)}, bf16[16,1024,64]{1,2,0:T(8,128)(2,1)}, u32[]{:S(2)}, u32[]{:S(2)}) %collective-permute-start.1) | collective-permute-done | bytes 2097184 | tf_op jit(solution)/shard_map/ppermute | solution.py:15
  197.7 19.3 %copy.36 = bf16[16,5120,64]{2,1,0:T(8,128)(2,1)} copy(bf16[16,5120,64]{1,2,0:T(8,128)(2,1)} %constant_dynamic-update-slice_fusion) | data formatting | bytes 20971520 | tf_op jit(solution)/shard_map/while | solution.py:93
  223.6 307.9 %while.12 = (s32[]{:T(128)}, bf16[4,8,2,128,64]{3,4,2,1,0:T(8,128)(2,1)}, s32[4,2]{1,0:T(4,128)S(1)}, bf16[4,8,2,128,64]{3,4,2,0,1:T(8,128)(2,1)S(1)}, s32[4,2,1...) while((s32[]{:T(128)}, ...), condition=%wide.region_7.8_spmd, body=%wide.region_2.0_spmd.sunk | while | flops 1124348160 | bytes 206471984 | solution.py:93
  223.7 13.0 %gather_fusion = bf16[24,16,128,64]{3,2,1,0:T(8,128)(2,1)} fusion(bf16[16,40,128,64]{3,2,1,0:T(8,128)(2,1)} %get-tuple-element.246, s32[1024]{0:T(1024)S(1)} %pad_clamp_fusion.4), kind=kCustom, calls=%fused_computation.clone.1 | custom fusion | bytes 12583008 | tf_op jit(solution)/shard_map/while/body/eval_jaxpr/jit(_take)/gather | solution.py:68
  248.4 7.0 %copy.52 = bf16[8,24,128,64]{2,1,3,0:T(8,128)(2,1)} copy(bf16[8,24,128,64]{3,2,0,1:T(8,128)(2,1)} %get-tuple-element.217) | data formatting | bytes 6291456 | tf_op jit(solution)/shard_map/while/body/eval_jaxpr/slice | solution.py:70
  255.4 6.9 %slice.48 = bf16[8,2,1536,64]{2,1,3,0:T(2,128)(2,1)} reshape(bf16[8,24,128,64]{2,1,3,0:T(8,128)(2,1)} %copy.52) | data formatting | bytes 6291456 | tf_op jit(solution)/shard_map/while/body/eval_jaxpr/slice | solution.py:70
  273.7 6.9 %copy.53 = bf16[8,24,128,64]{2,1,3,0:T(8,128)(2,1)} copy(bf16[8,24,128,64]{3,2,0,1:T(8,128)(2,1)} %get-tuple-element.222) | data formatting | bytes 6291456 | tf_op jit(solution)/shard_map/while/body/eval_jaxpr/slice | solution.py:71
  287.6 9.8 %fusion.65 = f32[8,2,128,64]{2,3,1,0:T(8,128)} fusion(f32[8,2,128,1536]{3,2,1,0:T(8,128)} %copy-done.2, f32[8,2,128]{2,1,0:T(2,128)S(1)} %add.116, f32[8,2,128]{2,1,0:T(2,128)S(1)} %max.22, pred[2,1536]{1,0:T(4,128)(4,1)S(1)} %broadcast_compare_fusion.2, bf16[8,2,1536,64]{2,1,3,0:T(2,128)(2,1)} %slice.49), kind=kOutput, calls=%fused_computation.9.clone.1 | convolution fusion | flops 418381824 | bytes 16272384 | tf_op jit(solution)/shard_map/while/body/eval_jaxpr/hgqk,hgkd->hgqd/dot_general | solution.py:89
  300.6 13.0 %gather_fusion = bf16[24,16,128,64]{3,2,1,0:T(8,128)(2,1)} fusion(bf16[16,40,128,64]{3,2,1,0:T(8,128)(2,1)} %get-tuple-element.246, s32[1024]{0:T(1024)S(1)} %pad_clamp_fusion.4), kind=kCustom, calls=%fused_computation.clone.1 | custom fusion | bytes 12583008 | tf_op jit(solution)/shard_map/while/body/eval_jaxpr/jit(_take)/gather | solution.py:68
  325.4 7.0 %copy.52 = bf16[8,24,128,64]{2,1,3,0:T(8,128)(2,1)} copy(bf16[8,24,128,64]{3,2,0,1:T(8,128)(2,1)} %get-tuple-element.217) | data formatting | bytes 6291456 | tf_op jit(solution)/shard_map/while/body/eval_jaxpr/slice | solution.py:70
  332.3 6.9 %slice.48 = bf16[8,2,1536,64]{2,1,3,0:T(2,128)(2,1)} reshape(bf16[8,24,128,64]{2,1,3,0:T(8,128)(2,1)} %copy.52) | data formatting | bytes 6291456 | tf_op jit(solution)/shard_map/while/body/eval_jaxpr/slice | solution.py:70
  350.7 6.9 %copy.53 = bf16[8,24,128,64]{2,1,3,0:T(8,128)(2,1)} copy(bf16[8,24,128,64]{3,2,0,1:T(8,128)(2,1)} %get-tuple-element.222) | data formatting | bytes 6291456 | tf_op jit(solution)/shard_map/while/body/eval_jaxpr/slice | solution.py:71
  364.5 9.8 %fusion.65 = f32[8,2,128,64]{2,3,1,0:T(8,128)} fusion(f32[8,2,128,1536]{3,2,1,0:T(8,128)} %copy-done.2, f32[8,2,128]{2,1,0:T(2,128)S(1)} %add.116, f32[8,2,128]{2,1,0:T(2,128)S(1)} %max.22, pred[2,1536]{1,0:T(4,128)(4,1)S(1)} %broadcast_compare_fusion.2, bf16[8,2,1536,64]{2,1,3,0:T(2,128)(2,1)} %slice.49), kind=kOutput, calls=%fused_computation.9.clone.1 | convolution fusion | flops 418381824 | bytes 16272384 | tf_op jit(solution)/shard_map/while/body/eval_jaxpr/hgqk,hgkd->hgqd/dot_general | solution.py:89
  377.6 13.0 %gather_fusion = bf16[24,16,128,64]{3,2,1,0:T(8,128)(2,1)} fusion(bf16[16,40,128,64]{3,2,1,0:T(8,128)(2,1)} %get-tuple-element.246, s32[1024]{0:T(1024)S(1)} %pad_clamp_fusion.4), kind=kCustom, calls=%fused_computation.clone.1 | custom fusion | bytes 12583008 | tf_op jit(solution)/shard_map/while/body/eval_jaxpr/jit(_take)/gather | solution.py:68
  402.3 7.0 %copy.52 = bf16[8,24,128,64]{2,1,3,0:T(8,128)(2,1)} copy(bf16[8,24,128,64]{3,2,0,1:T(8,128)(2,1)} %get-tuple-element.217) | data formatting | bytes 6291456 | tf_op jit(solution)/shard_map/while/body/eval_jaxpr/slice | solution.py:70
  409.3 6.9 %slice.48 = bf16[8,2,1536,64]{2,1,3,0:T(2,128)(2,1)} reshape(bf16[8,24,128,64]{2,1,3,0:T(8,128)(2,1)} %copy.52) | data formatting | bytes 6291456 | tf_op jit(solution)/shard_map/while/body/eval_jaxpr/slice | solution.py:70
  427.6 6.9 %copy.53 = bf16[8,24,128,64]{2,1,3,0:T(8,128)(2,1)} copy(bf16[8,24,128,64]{3,2,0,1:T(8,128)(2,1)} %get-tuple-element.222) | data formatting | bytes 6291456 | tf_op jit(solution)/shard_map/while/body/eval_jaxpr/slice | solution.py:71
  441.5 9.8 %fusion.65 = f32[8,2,128,64]{2,3,1,0:T(8,128)} fusion(f32[8,2,128,1536]{3,2,1,0:T(8,128)} %copy-done.2, f32[8,2,128]{2,1,0:T(2,128)S(1)} %add.116, f32[8,2,128]{2,1,0:T(2,128)S(1)} %max.22, pred[2,1536]{1,0:T(4,128)(4,1)S(1)} %broadcast_compare_fusion.2, bf16[8,2,1536,64]{2,1,3,0:T(2,128)(2,1)} %slice.49), kind=kOutput, calls=%fused_computation.9.clone.1 | convolution fusion | flops 418381824 | bytes 16272384 | tf_op jit(solution)/shard_map/while/body/eval_jaxpr/hgqk,hgkd->hgqd/dot_general | solution.py:89
  454.6 13.0 %gather_fusion = bf16[24,16,128,64]{3,2,1,0:T(8,128)(2,1)} fusion(bf16[16,40,128,64]{3,2,1,0:T(8,128)(2,1)} %get-tuple-element.246, s32[1024]{0:T(1024)S(1)} %pad_clamp_fusion.4), kind=kCustom, calls=%fused_computation.clone.1 | custom fusion | bytes 12583008 | tf_op jit(solution)/shard_map/while/body/eval_jaxpr/jit(_take)/gather | solution.py:68
  479.3 7.0 %copy.52 = bf16[8,24,128,64]{2,1,3,0:T(8,128)(2,1)} copy(bf16[8,24,128,64]{3,2,0,1:T(8,128)(2,1)} %get-tuple-element.217) | data formatting | bytes 6291456 | tf_op jit(solution)/shard_map/while/body/eval_jaxpr/slice | solution.py:70
  486.3 6.9 %slice.48 = bf16[8,2,1536,64]{2,1,3,0:T(2,128)(2,1)} reshape(bf16[8,24,128,64]{2,1,3,0:T(8,128)(2,1)} %copy.52) | data formatting | bytes 6291456 | tf_op jit(solution)/shard_map/while/body/eval_jaxpr/slice | solution.py:70
  504.6 6.9 %copy.53 = bf16[8,24,128,64]{2,1,3,0:T(8,128)(2,1)} copy(bf16[8,24,128,64]{3,2,0,1:T(8,128)(2,1)} %get-tuple-element.222) | data formatting | bytes 6291456 | tf_op jit(solution)/shard_map/while/body/eval_jaxpr/slice | solution.py:71
  518.5 9.8 %fusion.65 = f32[8,2,128,64]{2,3,1,0:T(8,128)} fusion(f32[8,2,128,1536]{3,2,1,0:T(8,128)} %copy-done.2, f32[8,2,128]{2,1,0:T(2,128)S(1)} %add.116, f32[8,2,128]{2,1,0:T(2,128)S(1)} %max.22, pred[2,1536]{1,0:T(4,128)(4,1)S(1)} %broadcast_compare_fusion.2, bf16[8,2,1536,64]{2,1,3,0:T(2,128)(2,1)} %slice.49), kind=kOutput, calls=%fused_computation.9.clone.1 | convolution fusion | flops 418381824 | bytes 16272384 | tf_op jit(solution)/shard_map/while/body/eval_jaxpr/hgqk,hgkd->hgqd/dot_general | solution.py:89
  (148 shorter events, 187.8 us)
Async XLA Ops:
  6.5 4.2 copy-start
  6.5 26.3 %copy-start.6 = (bf16[512,512]{1,0:T(8,128)(2,1)S(1)}, bf16[512,512]{1,0:T(8,128)(2,1)}, u32[]{:S(2)}) copy-start(bf16[512,512]{1,0:T(8,128)(2,1)} %param.10) | copy-start | bytes 1572868
  6.5 26.6 %copy-start.8 = (s32[8]{0:T(128)S(1)}, s32[8]{0:T(128)}, u32[]{:S(2)}) copy-start(s32[8]{0:T(128)} %param.14) | copy-start | bytes 100
  6.5 26.9 %copy-start.7 = (s32[8,12]{1,0:T(8,128)S(1)}, s32[8,12]{1,0:T(8,128)}, u32[]{:S(2)}) copy-start(s32[8,12]{1,0:T(8,128)} %param.13) | copy-start | bytes 1156
  6.5 210.4 %all-gather.2.cloned.1.call-start = ((), (), s32[]{:S(2)}) async-start(), calls=%async_computation | async-start | bytes 4325376 | tf_op jit(solution)/shard_map/all_gather | solution.py:58
  16.5 83.0 %collective-permute-start = (bf16[16,1024,64]{1,2,0:T(8,128)(2,1)}, bf16[16,1024,64]{1,2,0:T(8,128)(2,1)}, u32[]{:S(2)}, u32[]{:S(2)}) collective-permute-start(bf16[16,1024,64]{1,2,0:T(8,128)(2,1)} %convert_bitcast_fusion), channel_id=1, source_target_pairs={{0,2},{1,3},{2,4},{3,5},{4,6},{5,7},{6,8},{7,9},{8,10},{9,11},{10,... | collective-permute-start | bytes 6291464 | tf_op jit(solution)/shard_map/ppermute | solution.py:15
  21.7 162.9 %collective-permute-start.1 = (bf16[16,1024,64]{1,2,0:T(8,128)(2,1)}, bf16[16,1024,64]{1,2,0:T(8,128)(2,1)}, u32[]{:S(2)}, u32[]{:S(2)}) collective-permute-start(bf16[16,1024,64]{1,2,0:T(8,128)(2,1)} %convert_bitcast_fusion), channel_id=1, source_target_pairs={{0,1},{1,2},{2,3},{3,4},{4,5},{5,6},{6,7},{7,8},{8,9},{9,10},{10,1... | collective-permute-start | bytes 6291464 | tf_op jit(solution)/shard_map/ppermute | solution.py:15
  25.5 165.6 %collective-permute-start.2 = (bf16[16,1024,64]{1,2,0:T(8,128)(2,1)}, bf16[16,1024,64]{1,2,0:T(8,128)(2,1)}, u32[]{:S(2)}, u32[]{:S(2)}) collective-permute-start(bf16[16,1024,64]{1,2,0:T(8,128)(2,1)} %convert_bitcast_fusion), channel_id=1, source_target_pairs={{1,0},{2,1},{3,2},{4,3},{5,4},{6,5},{7,6},{8,7},{9,8},{10,9},{11,1... | collective-permute-start | bytes 6291464 | tf_op jit(solution)/shard_map/ppermute | solution.py:15
  29.7 164.7 %collective-permute-start.3 = (bf16[16,1024,64]{1,2,0:T(8,128)(2,1)}, bf16[16,1024,64]{1,2,0:T(8,128)(2,1)}, u32[]{:S(2)}, u32[]{:S(2)}) collective-permute-start(bf16[16,1024,64]{1,2,0:T(8,128)(2,1)} %convert_bitcast_fusion), channel_id=1, source_target_pairs={{2,0},{3,1},{4,2},{5,3},{6,4},{7,5},{8,6},{9,7},{10,8},{11,9},{12,... | collective-permute-start | bytes 6291464 | tf_op jit(solution)/shard_map/ppermute | solution.py:15
  197.7 24.0 %copy-start.5 = (bf16[512,1024]{1,0:T(8,128)(2,1)S(1)}, bf16[512,1024]{1,0:T(8,128)(2,1)}, u32[]{:S(2)}) copy-start(bf16[512,1024]{1,0:T(8,128)(2,1)} %param.11) | copy-start | bytes 3145732
  266.4 7.3 %copy-start.2 = (f32[8,2,128,1536]{3,2,1,0:T(8,128)}, f32[8,2,128,1536]{3,2,1,0:T(8,128)S(1)}, u32[]{:S(2)}) copy-start(f32[8,2,128,1536]{3,2,1,0:T(8,128)S(1)} %get-tuple-element.218) | copy-start | bytes 37748740 | tf_op jit(solution)/shard_map/while
  267.3 2.4 copy-start.3
  287.6 9.8 %copy-start.4 = (f32[8,2,128,512]{3,2,1,0:T(8,128)S(1)}, f32[8,2,128,512]{3,2,1,0:T(8,128)}, u32[]{:S(2)}) copy-start(f32[8,2,128,512]{3,2,1,0:T(8,128)} %copy-done.3) | copy-start | bytes 12582916 | tf_op jit(solution)/shard_map/while
  343.4 7.3 %copy-start.2 = (f32[8,2,128,1536]{3,2,1,0:T(8,128)}, f32[8,2,128,1536]{3,2,1,0:T(8,128)S(1)}, u32[]{:S(2)}) copy-start(f32[8,2,128,1536]{3,2,1,0:T(8,128)S(1)} %get-tuple-element.218) | copy-start | bytes 37748740 | tf_op jit(solution)/shard_map/while
  344.2 2.4 copy-start.3
  364.5 9.8 %copy-start.4 = (f32[8,2,128,512]{3,2,1,0:T(8,128)S(1)}, f32[8,2,128,512]{3,2,1,0:T(8,128)}, u32[]{:S(2)}) copy-start(f32[8,2,128,512]{3,2,1,0:T(8,128)} %copy-done.3) | copy-start | bytes 12582916 | tf_op jit(solution)/shard_map/while
  420.3 7.3 %copy-start.2 = (f32[8,2,128,1536]{3,2,1,0:T(8,128)}, f32[8,2,128,1536]{3,2,1,0:T(8,128)S(1)}, u32[]{:S(2)}) copy-start(f32[8,2,128,1536]{3,2,1,0:T(8,128)S(1)} %get-tuple-element.218) | copy-start | bytes 37748740 | tf_op jit(solution)/shard_map/while
  421.2 2.4 copy-start.3
  441.5 9.8 %copy-start.4 = (f32[8,2,128,512]{3,2,1,0:T(8,128)S(1)}, f32[8,2,128,512]{3,2,1,0:T(8,128)}, u32[]{:S(2)}) copy-start(f32[8,2,128,512]{3,2,1,0:T(8,128)} %copy-done.3) | copy-start | bytes 12582916 | tf_op jit(solution)/shard_map/while
  497.3 7.3 %copy-start.2 = (f32[8,2,128,1536]{3,2,1,0:T(8,128)}, f32[8,2,128,1536]{3,2,1,0:T(8,128)S(1)}, u32[]{:S(2)}) copy-start(f32[8,2,128,1536]{3,2,1,0:T(8,128)S(1)} %get-tuple-element.218) | copy-start | bytes 37748740 | tf_op jit(solution)/shard_map/while
  498.2 2.4 copy-start.3
  518.5 9.8 %copy-start.4 = (f32[8,2,128,512]{3,2,1,0:T(8,128)S(1)}, f32[8,2,128,512]{3,2,1,0:T(8,128)}, u32[]{:S(2)}) copy-start(f32[8,2,128,512]{3,2,1,0:T(8,128)} %copy-done.3) | copy-start | bytes 12582916 | tf_op jit(solution)/shard_map/while
  534.5 3.0 copy-start.1
Sparse Core Ops, SparseCore 0:
  12.5 179.4 all-gather.1
where the time goes:
time: 548 us; the launch traced here: 544 us
  local copies, waits for them, and re-layouts  241 us (44%)
  waiting for transfers between devices  147 us (27%)
  matrix products  78.4 us (14%)
  other arithmetic  45.9 us (8%)
  starting transfers between devices  16.3 us (3%)
  between operations  15.5 us (3%)
    ppermute x4, waiting for transfers between devices, from_behind(): lax.ppermute(value, axis, [(source, source + steps) for source in range(f...  147 us
    slice x12, local copies, waits for them, and re-layouts, attend(): vals = picked[HEADS:]  76 us
    slice x8, local copies, waits for them, and re-layouts, attend(): keys = picked[:HEADS]  55.6 us
    gather x4, local copies, waits for them, and re-layouts, attend(): picked = jnp.take(nearby, relative.reshape(2 * NB), axis=1)  51.9 us
    dot_general x4, matrix products, attend(): jnp.einsum('hgqk,hgkd->hgqd', near_w, vals, preferred_element_type=jnp.fl...  39.1 us
    select_n x8, other arithmetic, attend(): picked = jnp.take(nearby, relative.reshape(2 * NB), axis=1)  26.1 us
    while x1, local copies, waits for them, and re-layouts, on_device(): context = lax.map(attend, (queries, lists, counts))  19.3 us
    ppermute x4, starting transfers between devices, from_behind(): lax.ppermute(value, axis, [(source, source + steps) for source in range(f...  16.3 us
  transfers between devices with their start and end apart: 5, of which 2 were waited for; matrix products, arithmetic and copies ran while one was open for 8% of the time, Pallas kernels for 0%

commit v1 on v0

--- a/solution.py
+++ b/solution.py
@@ -38,25 +38,20 @@
         query_w,
         preferred_element_type=jnp.float32,
     ).astype(jnp.bfloat16)
-    keyvals = head_major(tokens, w_keyval, width)
     pieces = []
     for offset in (-2, -1, 0, 1, 2):
         if offset == 0:
-            pieces.append(keyvals)
+            pieces.append(tokens)
         else:
-            pieces.append(from_behind(keyvals, "curve", -offset))
-    nearby = jnp.concatenate(pieces, axis=1).reshape(2 * HEADS, 5 * nblocks, BLOCK, head_dim)
+            pieces.append(from_behind(tokens, "curve", -offset))
+    nearby = head_major(jnp.concatenate(pieces, axis=0), w_keyval, width)
+    nearby = nearby.reshape(2 * HEADS, 5 * nblocks, BLOCK, head_dim)
     owner = bnd_ids // tok_dev
-    my_start = jnp.sum((owner < member).astype(jnp.int32))
-    padded_ids = jnp.concatenate([bnd_ids, jnp.zeros((BCAP,), jnp.int32)])
-    my_ids = lax.dynamic_slice_in_dim(padded_ids, my_start, BCAP)
-    local_pos = jnp.clip(my_ids - member * tok_dev, 0, tok_dev - 1)
-    slot_range = jnp.arange(nbound, dtype=jnp.int32)
-    owner_start = jnp.sum((owner[None, :] < owner[:, None]).astype(jnp.int32), axis=1)
-    source = owner * BCAP + slot_range - owner_start
-    rows = jnp.take(tokens, local_pos, axis=0)
-    gathered = lax.all_gather(rows, "curve", axis=0, tiled=True)
-    bnd_kv = head_major(jnp.take(gathered, source, axis=0), w_keyval, width)
+    local_pos = jnp.clip(bnd_ids - member * tok_dev, 0, tok_dev - 1)
+    mine = owner == member
+    rows = jnp.where(mine[:, None], jnp.take(tokens, local_pos, axis=0), jnp.zeros((), tokens.dtype))
+    gathered = lax.psum(rows, "curve")
+    bnd_kv = head_major(gathered, w_keyval, width)
     bkeys = bnd_kv[:HEADS]
     bvals = bnd_kv[HEADS:]
     first_block = (member - 2) * nblocks

time: 548 us -> 576 us (1.051)
  waiting for transfers between devices: 147 us -> 175 us
  local copies, waits for them, and re-layouts: 241 us -> 231 us
  matrix products: 78.4 us -> 85.1 us
    psum x0 -> x1, waiting for transfers between devices: none -> 175 us  [on_device(): gathered = lax.psum(rows, 'curve')]
    ppermute x4, waiting for transfers between devices: 147 us -> 0.01 us  [from_behind(): lax.ppermute(value, axis, [(source, source + steps) for source in range(f...]
    unnamed x1 -> x2, matrix products: 0.84 us -> 9.71 us
    unnamed x18 -> x21, local copies, waits for them, and re-layouts: 14.8 us -> 8.15 us
  transfers between devices with their start and end apart: 5 -> 5, of which waited for: 2 -> 1; matrix products, arithmetic and copies ran while one was open for 8% -> 2% of each run, Pallas kernels for 0% -> 0%
where the time goes in v1:
time: 576 us; the launch traced here: 571 us
  local copies, waits for them, and re-layouts  231 us (40%)
  waiting for transfers between devices  175 us (30%)
  matrix products  85.1 us (15%)
  other arithmetic  49.7 us (9%)
  starting transfers between devices  16.4 us (3%)
  between operations  13.5 us (2%)
    psum x1, waiting for transfers between devices, on_device(): gathered = lax.psum(rows, 'curve')  175 us
    slice x12, local copies, waits for them, and re-layouts, attend(): vals = picked[HEADS:]  75.9 us
    slice x8, local copies, waits for them, and re-layouts, attend(): keys = picked[:HEADS]  55.6 us
    gather x4, local copies, waits for them, and re-layouts, attend(): picked = jnp.take(nearby, relative.reshape(2 * NB), axis=1)  51.9 us
    dot_general x4, matrix products, attend(): jnp.einsum('hgqk,hgkd->hgqd', near_w, vals, preferred_element_type=jnp.fl...  39.1 us
    select_n x8, other arithmetic, attend(): picked = jnp.take(nearby, relative.reshape(2 * NB), axis=1)  26.1 us
    while x1, local copies, waits for them, and re-layouts, on_device(): context = lax.map(attend, (queries, lists, counts))  19.3 us
    ppermute x4, starting transfers between devices, from_behind(): lax.ppermute(value, axis, [(source, source + steps) for source in range(f...  16.3 us
  transfers between devices with their start and end apart: 5, of which 1 were waited for; matrix products, arithmetic and copies ran while one was open for 2% of the time, Pallas kernels for 0%

profile of v1, /device:TPU:18, one launch (start us, length us, event | category | flops | bytes accessed | tf_op | source)
XLA Modules:
  0.0 571.0 jit_solution(18298492105993924633)
XLA Ops:
  30.2 175.3 %all-reduce.2.cloned.1.call-done = bf16[512,512]{1,0:T(8,128)(2,1)} async-done(((bf16[512,512]{1,0:T(8,128)(2,1)}), bf16[512,512]{1,0:T(8,128)(2,1)}) %all-reduce.2.cloned.1.call-update) | async-done | bytes 524304 | tf_op jit(solution)/shard_map/psum | solution.py:53
  218.5 7.9 %fusion.36 = f32[5120,1024]{0,1:S(1)} fusion(bf16[5120,512]{1,0:T(8,128)(2,1)} %constant_dynamic-update-slice_fusion, bf16[512,1024]{1,0:T(8,128)(2,1)S(1)} %copy-done), kind=kOutput, calls=%fused_computation.75 | convolution fusion | flops 5368709120 | bytes 27262976
  231.6 19.3 %copy.28 = bf16[16,5120,64]{2,1,0:T(8,128)(2,1)} copy(bf16[16,5120,64]{1,2,0:T(8,128)(2,1)} %convert_bitcast_fusion) | data formatting | bytes 20971520 | tf_op jit(solution)/shard_map/while | solution.py:88
  250.9 307.2 %while.12 = (s32[]{:T(128)}, bf16[4,8,2,128,64]{3,4,2,1,0:T(8,128)(2,1)}, s32[4,2]{1,0:T(4,128)S(1)}, bf16[4,8,2,128,64]{3,4,2,0,1:T(8,128)(2,1)S(1)}, s32[4,2,1...) while((s32[]{:T(128)}, ...), condition=%wide.region_6.7_spmd, body=%wide.region_1.6_spmd.sunk | while | flops 1124348160 | bytes 206471984 | solution.py:88
  251.0 13.0 %gather_fusion = bf16[24,16,128,64]{3,2,1,0:T(8,128)(2,1)} fusion(bf16[16,40,128,64]{3,2,1,0:T(8,128)(2,1)} %get-tuple-element.235, s32[1024]{0:T(1024)S(1)} %pad_clamp_fusion.3), kind=kCustom, calls=%fused_computation.clone.1 | custom fusion | bytes 12583008 | tf_op jit(solution)/shard_map/while/body/eval_jaxpr/jit(_take)/gather | solution.py:63
  275.7 6.9 %copy.45 = bf16[8,24,128,64]{2,1,3,0:T(8,128)(2,1)} copy(bf16[8,24,128,64]{3,2,0,1:T(8,128)(2,1)} %get-tuple-element.206) | data formatting | bytes 6291456 | tf_op jit(solution)/shard_map/while/body/eval_jaxpr/slice | solution.py:65
  282.7 6.9 %slice.46 = bf16[8,2,1536,64]{2,1,3,0:T(2,128)(2,1)} reshape(bf16[8,24,128,64]{2,1,3,0:T(8,128)(2,1)} %copy.45) | data formatting | bytes 6291456 | tf_op jit(solution)/shard_map/while/body/eval_jaxpr/slice | solution.py:65
  301.0 6.9 %copy.46 = bf16[8,24,128,64]{2,1,3,0:T(8,128)(2,1)} copy(bf16[8,24,128,64]{3,2,0,1:T(8,128)(2,1)} %get-tuple-element.211) | data formatting | bytes 6291456 | tf_op jit(solution)/shard_map/while/body/eval_jaxpr/slice | solution.py:66
  314.9 9.8 %fusion.63 = f32[8,2,128,64]{2,3,1,0:T(8,128)} fusion(f32[8,2,128,1536]{3,2,1,0:T(8,128)} %copy-done.2, f32[8,2,128]{2,1,0:T(2,128)S(1)} %add.87, f32[8,2,128]{2,1,0:T(2,128)S(1)} %max.16, pred[2,1536]{1,0:T(4,128)(4,1)S(1)} %broadcast_compare_fusion.2, bf16[8,2,1536,64]{2,1,3,0:T(2,128)(2,1)} %slice.47), kind=kOutput, calls=%fused_computation.8.clone.1 | convolution fusion | flops 418381824 | bytes 16272384 | tf_op jit(solution)/shard_map/while/body/eval_jaxpr/hgqk,hgkd->hgqd/dot_general | solution.py:84
  327.8 13.0 %gather_fusion = bf16[24,16,128,64]{3,2,1,0:T(8,128)(2,1)} fusion(bf16[16,40,128,64]{3,2,1,0:T(8,128)(2,1)} %get-tuple-element.235, s32[1024]{0:T(1024)S(1)} %pad_clamp_fusion.3), kind=kCustom, calls=%fused_computation.clone.1 | custom fusion | bytes 12583008 | tf_op jit(solution)/shard_map/while/body/eval_jaxpr/jit(_take)/gather | solution.py:63
  352.6 6.9 %copy.45 = bf16[8,24,128,64]{2,1,3,0:T(8,128)(2,1)} copy(bf16[8,24,128,64]{3,2,0,1:T(8,128)(2,1)} %get-tuple-element.206) | data formatting | bytes 6291456 | tf_op jit(solution)/shard_map/while/body/eval_jaxpr/slice | solution.py:65
  359.5 6.9 %slice.46 = bf16[8,2,1536,64]{2,1,3,0:T(2,128)(2,1)} reshape(bf16[8,24,128,64]{2,1,3,0:T(8,128)(2,1)} %copy.45) | data formatting | bytes 6291456 | tf_op jit(solution)/shard_map/while/body/eval_jaxpr/slice | solution.py:65
  377.8 6.9 %copy.46 = bf16[8,24,128,64]{2,1,3,0:T(8,128)(2,1)} copy(bf16[8,24,128,64]{3,2,0,1:T(8,128)(2,1)} %get-tuple-element.211) | data formatting | bytes 6291456 | tf_op jit(solution)/shard_map/while/body/eval_jaxpr/slice | solution.py:66
  391.7 9.8 %fusion.63 = f32[8,2,128,64]{2,3,1,0:T(8,128)} fusion(f32[8,2,128,1536]{3,2,1,0:T(8,128)} %copy-done.2, f32[8,2,128]{2,1,0:T(2,128)S(1)} %add.87, f32[8,2,128]{2,1,0:T(2,128)S(1)} %max.16, pred[2,1536]{1,0:T(4,128)(4,1)S(1)} %broadcast_compare_fusion.2, bf16[8,2,1536,64]{2,1,3,0:T(2,128)(2,1)} %slice.47), kind=kOutput, calls=%fused_computation.8.clone.1 | convolution fusion | flops 418381824 | bytes 16272384 | tf_op jit(solution)/shard_map/while/body/eval_jaxpr/hgqk,hgkd->hgqd/dot_general | solution.py:84
  404.6 13.0 %gather_fusion = bf16[24,16,128,64]{3,2,1,0:T(8,128)(2,1)} fusion(bf16[16,40,128,64]{3,2,1,0:T(8,128)(2,1)} %get-tuple-element.235, s32[1024]{0:T(1024)S(1)} %pad_clamp_fusion.3), kind=kCustom, calls=%fused_computation.clone.1 | custom fusion | bytes 12583008 | tf_op jit(solution)/shard_map/while/body/eval_jaxpr/jit(_take)/gather | solution.py:63
  429.3 6.9 %copy.45 = bf16[8,24,128,64]{2,1,3,0:T(8,128)(2,1)} copy(bf16[8,24,128,64]{3,2,0,1:T(8,128)(2,1)} %get-tuple-element.206) | data formatting | bytes 6291456 | tf_op jit(solution)/shard_map/while/body/eval_jaxpr/slice | solution.py:65
  436.3 6.9 %slice.46 = bf16[8,2,1536,64]{2,1,3,0:T(2,128)(2,1)} reshape(bf16[8,24,128,64]{2,1,3,0:T(8,128)(2,1)} %copy.45) | data formatting | bytes 6291456 | tf_op jit(solution)/shard_map/while/body/eval_jaxpr/slice | solution.py:65
  454.6 6.9 %copy.46 = bf16[8,24,128,64]{2,1,3,0:T(8,128)(2,1)} copy(bf16[8,24,128,64]{3,2,0,1:T(8,128)(2,1)} %get-tuple-element.211) | data formatting | bytes 6291456 | tf_op jit(solution)/shard_map/while/body/eval_jaxpr/slice | solution.py:66
  468.5 9.8 %fusion.63 = f32[8,2,128,64]{2,3,1,0:T(8,128)} fusion(f32[8,2,128,1536]{3,2,1,0:T(8,128)} %copy-done.2, f32[8,2,128]{2,1,0:T(2,128)S(1)} %add.87, f32[8,2,128]{2,1,0:T(2,128)S(1)} %max.16, pred[2,1536]{1,0:T(4,128)(4,1)S(1)} %broadcast_compare_fusion.2, bf16[8,2,1536,64]{2,1,3,0:T(2,128)(2,1)} %slice.47), kind=kOutput, calls=%fused_computation.8.clone.1 | convolution fusion | flops 418381824 | bytes 16272384 | tf_op jit(solution)/shard_map/while/body/eval_jaxpr/hgqk,hgkd->hgqd/dot_general | solution.py:84
  481.4 13.0 %gather_fusion = bf16[24,16,128,64]{3,2,1,0:T(8,128)(2,1)} fusion(bf16[16,40,128,64]{3,2,1,0:T(8,128)(2,1)} %get-tuple-element.235, s32[1024]{0:T(1024)S(1)} %pad_clamp_fusion.3), kind=kCustom, calls=%fused_computation.clone.1 | custom fusion | bytes 12583008 | tf_op jit(solution)/shard_map/while/body/eval_jaxpr/jit(_take)/gather | solution.py:63
  506.1 6.9 %copy.45 = bf16[8,24,128,64]{2,1,3,0:T(8,128)(2,1)} copy(bf16[8,24,128,64]{3,2,0,1:T(8,128)(2,1)} %get-tuple-element.206) | data formatting | bytes 6291456 | tf_op jit(solution)/shard_map/while/body/eval_jaxpr/slice | solution.py:65
  513.1 6.9 %slice.46 = bf16[8,2,1536,64]{2,1,3,0:T(2,128)(2,1)} reshape(bf16[8,24,128,64]{2,1,3,0:T(8,128)(2,1)} %copy.45) | data formatting | bytes 6291456 | tf_op jit(solution)/shard_map/while/body/eval_jaxpr/slice | solution.py:65
  531.4 6.9 %copy.46 = bf16[8,24,128,64]{2,1,3,0:T(8,128)(2,1)} copy(bf16[8,24,128,64]{3,2,0,1:T(8,128)(2,1)} %get-tuple-element.211) | data formatting | bytes 6291456 | tf_op jit(solution)/shard_map/while/body/eval_jaxpr/slice | solution.py:66
  545.3 9.8 %fusion.63 = f32[8,2,128,64]{2,3,1,0:T(8,128)} fusion(f32[8,2,128,1536]{3,2,1,0:T(8,128)} %copy-done.2, f32[8,2,128]{2,1,0:T(2,128)S(1)} %add.87, f32[8,2,128]{2,1,0:T(2,128)S(1)} %max.16, pred[2,1536]{1,0:T(4,128)(4,1)S(1)} %broadcast_compare_fusion.2, bf16[8,2,1536,64]{2,1,3,0:T(2,128)(2,1)} %slice.47), kind=kOutput, calls=%fused_computation.8.clone.1 | convolution fusion | flops 418381824 | bytes 16272384 | tf_op jit(solution)/shard_map/while/body/eval_jaxpr/hgqk,hgkd->hgqd/dot_general | solution.py:84
  (147 shorter events, 180.5 us)
Async XLA Ops:
  6.5 199.0 %copy-start = (bf16[512,1024]{1,0:T(8,128)(2,1)S(1)}, bf16[512,1024]{1,0:T(8,128)(2,1)}, u32[]{:S(2)}) copy-start(bf16[512,1024]{1,0:T(8,128)(2,1)} %param.11) | copy-start | bytes 3145732
  6.5 5.3 copy-start.5
  6.5 21.6 %copy-start.7 = (bf16[512,512]{1,0:T(8,128)(2,1)S(1)}, bf16[512,512]{1,0:T(8,128)(2,1)}, u32[]{:S(2)}) copy-start(bf16[512,512]{1,0:T(8,128)(2,1)} %param.10) | copy-start | bytes 1572868
  6.5 23.6 %copy-start.9 = (s32[8,12]{1,0:T(8,128)S(1)}, s32[8,12]{1,0:T(8,128)}, u32[]{:S(2)}) copy-start(s32[8,12]{1,0:T(8,128)} %param.13) | copy-start | bytes 1156
  6.5 23.6 %copy-start.10 = (s32[8]{0:T(128)S(1)}, s32[8]{0:T(128)}, u32[]{:S(2)}) copy-start(s32[8]{0:T(128)} %param.14) | copy-start | bytes 100
  6.5 199.0 %all-reduce.2.cloned.1.call-start = ((), (), s32[]{:S(2)}) async-start(), calls=%async_computation | async-start | bytes 1048576 | tf_op jit(solution)/shard_map/psum | solution.py:53
  11.8 196.5 %collective-permute-start = (bf16[1024,512]{1,0:T(8,128)(2,1)S(1)}, bf16[1024,512]{1,0:T(8,128)(2,1)}, u32[]{:S(2)}, u32[]{:S(2)}) collective-permute-start(bf16[1024,512]{1,0:T(8,128)(2,1)S(1)} %copy-done.5), channel_id=1, source_target_pairs={{0,2},{1,3},{2,4},{3,5},{4,6},{5,7},{6,8},{7,9},{8,10},{9,11},{10,... | collective-permute-start | bytes 3145736 | tf_op jit(solution)/shard_map/ppermute | solution.py:15
  17.0 193.6 %collective-permute-start.1 = (bf16[1024,512]{1,0:T(8,128)(2,1)S(1)}, bf16[1024,512]{1,0:T(8,128)(2,1)}, u32[]{:S(2)}, u32[]{:S(2)}) collective-permute-start(bf16[1024,512]{1,0:T(8,128)(2,1)S(1)} %copy-done.5), channel_id=1, source_target_pairs={{0,1},{1,2},{2,3},{3,4},{4,5},{5,6},{6,7},{7,8},{8,9},{9,10},{10,1... | collective-permute-start | bytes 3145736 | tf_op jit(solution)/shard_map/ppermute | solution.py:15
  20.9 193.1 %collective-permute-start.2 = (bf16[1024,512]{1,0:T(8,128)(2,1)S(1)}, bf16[1024,512]{1,0:T(8,128)(2,1)}, u32[]{:S(2)}, u32[]{:S(2)}) collective-permute-start(bf16[1024,512]{1,0:T(8,128)(2,1)S(1)} %copy-done.5), channel_id=1, source_target_pairs={{1,0},{2,1},{3,2},{4,3},{5,4},{6,5},{7,6},{8,7},{9,8},{10,9},{11,1... | collective-permute-start | bytes 3145736 | tf_op jit(solution)/shard_map/ppermute | solution.py:15
  25.0 191.3 %collective-permute-start.3 = (bf16[1024,512]{1,0:T(8,128)(2,1)S(1)}, bf16[1024,512]{1,0:T(8,128)(2,1)}, u32[]{:S(2)}, u32[]{:S(2)}) collective-permute-start(bf16[1024,512]{1,0:T(8,128)(2,1)S(1)} %copy-done.5), channel_id=1, source_target_pairs={{2,0},{3,1},{4,2},{5,3},{6,4},{7,5},{8,6},{9,7},{10,8},{11,9},{12,... | collective-permute-start | bytes 3145736 | tf_op jit(solution)/shard_map/ppermute | solution.py:15
  231.6 19.3 %copy-start.6 = (bf16[4,8,2,128,64]{3,4,2,0,1:T(8,128)(2,1)S(1)}, bf16[4,8,2,128,64]{3,4,2,0,1:T(8,128)(2,1)}, u32[]{:S(2)}) copy-start(bf16[4,8,2,128,64]{3,4,2,0,1:T(8,128)(2,1)} %fusion.29) | copy-start | bytes 3145732
  231.6 19.3 %copy-start.8 = (bf16[8,512,64]{1,2,0:T(8,128)(2,1)S(1)}, bf16[8,512,64]{1,2,0:T(8,128)(2,1)}, u32[]{:S(2)}) copy-start(bf16[8,512,64]{1,2,0:T(8,128)(2,1)} %get-tuple-element.219) | copy-start | bytes 1572868
  293.7 7.3 %copy-start.2 = (f32[8,2,128,1536]{3,2,1,0:T(8,128)}, f32[8,2,128,1536]{3,2,1,0:T(8,128)S(1)}, u32[]{:S(2)}) copy-start(f32[8,2,128,1536]{3,2,1,0:T(8,128)S(1)} %get-tuple-element.207) | copy-start | bytes 37748740 | tf_op jit(solution)/shard_map/while
  294.6 2.4 copy-start.3
  314.9 9.8 %copy-start.4 = (f32[8,2,128,512]{3,2,1,0:T(8,128)S(1)}, f32[8,2,128,512]{3,2,1,0:T(8,128)}, u32[]{:S(2)}) copy-start(f32[8,2,128,512]{3,2,1,0:T(8,128)} %copy-done.3) | copy-start | bytes 12582916 | tf_op jit(solution)/shard_map/while
  370.6 7.3 %copy-start.2 = (f32[8,2,128,1536]{3,2,1,0:T(8,128)}, f32[8,2,128,1536]{3,2,1,0:T(8,128)S(1)}, u32[]{:S(2)}) copy-start(f32[8,2,128,1536]{3,2,1,0:T(8,128)S(1)} %get-tuple-element.207) | copy-start | bytes 37748740 | tf_op jit(solution)/shard_map/while
  371.4 2.4 copy-start.3
  391.7 9.8 %copy-start.4 = (f32[8,2,128,512]{3,2,1,0:T(8,128)S(1)}, f32[8,2,128,512]{3,2,1,0:T(8,128)}, u32[]{:S(2)}) copy-start(f32[8,2,128,512]{3,2,1,0:T(8,128)} %copy-done.3) | copy-start | bytes 12582916 | tf_op jit(solution)/shard_map/while
  447.3 7.3 %copy-start.2 = (f32[8,2,128,1536]{3,2,1,0:T(8,128)}, f32[8,2,128,1536]{3,2,1,0:T(8,128)S(1)}, u32[]{:S(2)}) copy-start(f32[8,2,128,1536]{3,2,1,0:T(8,128)S(1)} %get-tuple-element.207) | copy-start | bytes 37748740 | tf_op jit(solution)/shard_map/while
  448.2 2.4 copy-start.3
  468.5 9.8 %copy-start.4 = (f32[8,2,128,512]{3,2,1,0:T(8,128)S(1)}, f32[8,2,128,512]{3,2,1,0:T(8,128)}, u32[]{:S(2)}) copy-start(f32[8,2,128,512]{3,2,1,0:T(8,128)} %copy-done.3) | copy-start | bytes 12582916 | tf_op jit(solution)/shard_map/while
  524.1 7.3 %copy-start.2 = (f32[8,2,128,1536]{3,2,1,0:T(8,128)}, f32[8,2,128,1536]{3,2,1,0:T(8,128)S(1)}, u32[]{:S(2)}) copy-start(f32[8,2,128,1536]{3,2,1,0:T(8,128)S(1)} %get-tuple-element.207) | copy-start | bytes 37748740 | tf_op jit(solution)/shard_map/while
  545.3 9.8 %copy-start.4 = (f32[8,2,128,512]{3,2,1,0:T(8,128)S(1)}, f32[8,2,128,512]{3,2,1,0:T(8,128)}, u32[]{:S(2)}) copy-start(f32[8,2,128,512]{3,2,1,0:T(8,128)} %copy-done.3) | copy-start | bytes 12582916 | tf_op jit(solution)/shard_map/while
  561.2 3.0 copy-start.1
  (1 other events, 2.4 us)
Sparse Core Ops, SparseCore 0:
  11.9 193.5 all-reduce.1

commit v2 on v1

--- a/solution.py
+++ b/solution.py
@@ -13,6 +13,18 @@
     count = lax.axis_size(axis)
     first, last = (max(0, -steps), min(count, count - steps))
     return lax.ppermute(value, axis, [(source, source + steps) for source in range(first, last)])
+
+
+def share_rows(rows, owner, member):
+    count = lax.axis_size("curve")
+    span = 1
+    while span < count:
+        pairs = [(source, source ^ span) for source in range(count) if source ^ span < count]
+        other = lax.ppermute(rows, "curve", pairs)
+        theirs = (owner // span) == ((member // span) ^ 1)
+        rows = jnp.where(theirs[:, None], other, rows)
+        span *= 2
+    return rows
 
 
 def head_major(rows, w_keyval, width):
@@ -50,7 +62,7 @@
     local_pos = jnp.clip(bnd_ids - member * tok_dev, 0, tok_dev - 1)
     mine = owner == member
     rows = jnp.where(mine[:, None], jnp.take(tokens, local_pos, axis=0), jnp.zeros((), tokens.dtype))
-    gathered = lax.psum(rows, "curve")
+    gathered = share_rows(rows, owner, member)
     bnd_kv = head_major(gathered, w_keyval, width)
     bkeys = bnd_kv[:HEADS]
     bvals = bnd_kv[HEADS:]

time: 576 us -> 522 us (0.906)
  waiting for transfers between devices: 175 us -> 116 us
  between operations: 13.5 us -> 0.24 us
  starting transfers between devices: 16.4 us -> 29 us
    psum x1 -> x0, waiting for transfers between devices: 175 us -> none  [on_device(): gathered = lax.psum(rows, 'curve')]
    ppermute x0 -> x5, waiting for transfers between devices: none -> 68.4 us  [share_rows(): other = lax.ppermute(rows, 'curve', pairs)]
    ppermute x4, waiting for transfers between devices: 0.01 us -> 47.4 us  [from_behind(): lax.ppermute(value, axis, [(source, source + steps) for source in range(f...]
    ppermute x0 -> x5, starting transfers between devices: none -> 12 us  [share_rows(): other = lax.ppermute(rows, 'curve', pairs)]
  transfers between devices with their start and end apart: 5 -> 9, of which waited for: 1 -> 4; matrix products, arithmetic and copies ran while one was open for 2% -> 9% of each run, Pallas kernels for 0% -> 0%
where the time goes in v2:
time: 522 us; the launch traced here: 516 us
  local copies, waits for them, and re-layouts  231 us (44%)
  waiting for transfers between devices  116 us (22%)
  matrix products  87.1 us (17%)
  other arithmetic  52.7 us (10%)
  starting transfers between devices  29 us (6%)
    slice x12, local copies, waits for them, and re-layouts, attend(): vals = picked[HEADS:]  76.1 us
    ppermute x5, waiting for transfers between devices, share_rows(): other = lax.ppermute(rows, 'curve', pairs)  68.4 us
    slice x8, local copies, waits for them, and re-layouts, attend(): keys = picked[:HEADS]  55.5 us
    gather x4, local copies, waits for them, and re-layouts, attend(): picked = jnp.take(nearby, relative.reshape(2 * NB), axis=1)  51.9 us
    ppermute x4, waiting for transfers between devices, from_behind(): lax.ppermute(value, axis, [(source, source + steps) for source in range(f...  47.4 us
    dot_general x4, matrix products, attend(): jnp.einsum('hgqk,hgkd->hgqd', near_w, vals, preferred_element_type=jnp.fl...  39.2 us
    select_n x8, other arithmetic, attend(): picked = jnp.take(nearby, relative.reshape(2 * NB), axis=1)  26.1 us
    while x1, local copies, waits for them, and re-layouts, on_device(): context = lax.map(attend, (queries, lists, counts))  19.3 us
  transfers between devices with their start and end apart: 9, of which 4 were waited for; matrix products, arithmetic and copies ran while one was open for 9% of the time, Pallas kernels for 0%

profile of v2, /device:TPU:18, one launch (start us, length us, event | category | flops | bytes accessed | tf_op | source)
XLA Modules:
  0.0 515.8 jit_solution(6657637745804410589)
XLA Ops:
  13.7 27.6 %collective-permute-done.4 = bf16[512,512]{1,0:T(8,128)(2,1)S(1)} collective-permute-done((bf16[512,512]{1,0:T(8,128)(2,1)S(1)}, bf16[512,512]{1,0:T(8,128)(2,1)S(1)}, u32[]{:S(2)}, u32[]{:S(2)}) %collective-permute-start.4) | collective-permute-done | bytes 524320 | tf_op jit(solution)/shard_map/ppermute | solution.py:23
  59.6 36.8 %collective-permute-done.5 = bf16[512,512]{1,0:T(8,128)(2,1)S(1)} collective-permute-done((bf16[512,512]{1,0:T(8,128)(2,1)S(1)}, bf16[512,512]{1,0:T(8,128)(2,1)S(1)}, u32[]{:S(2)}, u32[]{:S(2)}) %collective-permute-start.5) | collective-permute-done | bytes 524320 | tf_op jit(solution)/shard_map/ppermute | solution.py:23
  108.8 47.4 %collective-permute-done.3 = bf16[1024,512]{1,0:T(8,128)(2,1)} collective-permute-done((bf16[1024,512]{1,0:T(8,128)(2,1)S(1)}, bf16[1024,512]{1,0:T(8,128)(2,1)}, u32[]{:S(2)}, u32[]{:S(2)}) %collective-permute-start.3) | collective-permute-done | bytes 1048608 | tf_op jit(solution)/shard_map/ppermute | solution.py:15
  159.8 7.9 %fusion.46 = f32[5120,1024]{0,1:S(1)} fusion(bf16[5120,512]{1,0:T(8,128)(2,1)} %copy-done.8, bf16[512,1024]{1,0:T(8,128)(2,1)S(1)} %copy-done), kind=kOutput, calls=%fused_computation.106 | convolution fusion | flops 5368709120 | bytes 27262976
  179.4 19.3 %copy.28 = bf16[16,5120,64]{2,1,0:T(8,128)(2,1)} copy(bf16[16,5120,64]{1,2,0:T(8,128)(2,1)} %convert_bitcast_fusion) | data formatting | bytes 20971520 | tf_op jit(solution)/shard_map/while | solution.py:100
  201.8 307.9 %while.12 = (s32[]{:T(128)}, bf16[4,8,2,128,64]{3,4,2,1,0:T(8,128)(2,1)}, s32[4,2]{1,0:T(4,128)S(1)}, bf16[4,8,2,128,64]{3,4,2,0,1:T(8,128)(2,1)S(1)}, s32[4,2,1...) while((s32[]{:T(128)}, ...), condition=%wide.region_5.6_spmd, body=%wide.region_0.5_spmd.sunk | while | flops 1124348160 | bytes 206471984 | solution.py:100
  201.9 13.0 %gather_fusion = bf16[24,16,128,64]{3,2,1,0:T(8,128)(2,1)} fusion(bf16[16,40,128,64]{3,2,1,0:T(8,128)(2,1)} %get-tuple-element.243, s32[1024]{0:T(1024)S(1)} %pad_clamp_fusion.3), kind=kCustom, calls=%fused_computation.clone.1 | custom fusion | bytes 12583008 | tf_op jit(solution)/shard_map/while/body/eval_jaxpr/jit(_take)/gather | solution.py:75
  233.6 7.0 %slice.46 = bf16[8,2,1536,64]{2,1,3,0:T(2,128)(2,1)} reshape(bf16[8,24,128,64]{2,1,3,0:T(8,128)(2,1)} %copy.45) | data formatting | bytes 6291456 | tf_op jit(solution)/shard_map/while/body/eval_jaxpr/slice | solution.py:77
  252.0 6.9 %copy.46 = bf16[8,24,128,64]{2,1,3,0:T(8,128)(2,1)} copy(bf16[8,24,128,64]{3,2,0,1:T(8,128)(2,1)} %get-tuple-element.219) | data formatting | bytes 6291456 | tf_op jit(solution)/shard_map/while/body/eval_jaxpr/slice | solution.py:78
  258.9 6.9 %slice.47 = bf16[8,2,1536,64]{2,1,3,0:T(2,128)(2,1)} reshape(bf16[8,24,128,64]{2,1,3,0:T(8,128)(2,1)} %copy.46) | data formatting | bytes 6291456 | tf_op jit(solution)/shard_map/while/body/eval_jaxpr/slice | solution.py:78
  265.8 9.8 %fusion.71 = f32[8,2,128,64]{2,3,1,0:T(8,128)} fusion(f32[8,2,128,1536]{3,2,1,0:T(8,128)} %copy-done.2, f32[8,2,128]{2,1,0:T(2,128)S(1)} %add.95, f32[8,2,128]{2,1,0:T(2,128)S(1)} %max.16, pred[2,1536]{1,0:T(4,128)(4,1)S(1)} %broadcast_compare_fusion.5, bf16[8,2,1536,64]{2,1,3,0:T(2,128)(2,1)} %slice.47), kind=kOutput, calls=%fused_computation.8.clone.1 | convolution fusion | flops 418381824 | bytes 16272384 | tf_op jit(solution)/shard_map/while/body/eval_jaxpr/hgqk,hgkd->hgqd/dot_general | solution.py:96
  278.9 12.9 %gather_fusion = bf16[24,16,128,64]{3,2,1,0:T(8,128)(2,1)} fusion(bf16[16,40,128,64]{3,2,1,0:T(8,128)(2,1)} %get-tuple-element.243, s32[1024]{0:T(1024)S(1)} %pad_clamp_fusion.3), kind=kCustom, calls=%fused_computation.clone.1 | custom fusion | bytes 12583008 | tf_op jit(solution)/shard_map/while/body/eval_jaxpr/jit(_take)/gather | solution.py:75
  310.6 7.0 %slice.46 = bf16[8,2,1536,64]{2,1,3,0:T(2,128)(2,1)} reshape(bf16[8,24,128,64]{2,1,3,0:T(8,128)(2,1)} %copy.45) | data formatting | bytes 6291456 | tf_op jit(solution)/shard_map/while/body/eval_jaxpr/slice | solution.py:77
  335.9 6.9 %slice.47 = bf16[8,2,1536,64]{2,1,3,0:T(2,128)(2,1)} reshape(bf16[8,24,128,64]{2,1,3,0:T(8,128)(2,1)} %copy.46) | data formatting | bytes 6291456 | tf_op jit(solution)/shard_map/while/body/eval_jaxpr/slice | solution.py:78
  342.8 9.8 %fusion.71 = f32[8,2,128,64]{2,3,1,0:T(8,128)} fusion(f32[8,2,128,1536]{3,2,1,0:T(8,128)} %copy-done.2, f32[8,2,128]{2,1,0:T(2,128)S(1)} %add.95, f32[8,2,128]{2,1,0:T(2,128)S(1)} %max.16, pred[2,1536]{1,0:T(4,128)(4,1)S(1)} %broadcast_compare_fusion.5, bf16[8,2,1536,64]{2,1,3,0:T(2,128)(2,1)} %slice.47), kind=kOutput, calls=%fused_computation.8.clone.1 | convolution fusion | flops 418381824 | bytes 16272384 | tf_op jit(solution)/shard_map/while/body/eval_jaxpr/hgqk,hgkd->hgqd/dot_general | solution.py:96
  355.9 13.0 %gather_fusion = bf16[24,16,128,64]{3,2,1,0:T(8,128)(2,1)} fusion(bf16[16,40,128,64]{3,2,1,0:T(8,128)(2,1)} %get-tuple-element.243, s32[1024]{0:T(1024)S(1)} %pad_clamp_fusion.3), kind=kCustom, calls=%fused_computation.clone.1 | custom fusion | bytes 12583008 | tf_op jit(solution)/shard_map/while/body/eval_jaxpr/jit(_take)/gather | solution.py:75
  387.6 7.0 %slice.46 = bf16[8,2,1536,64]{2,1,3,0:T(2,128)(2,1)} reshape(bf16[8,24,128,64]{2,1,3,0:T(8,128)(2,1)} %copy.45) | data formatting | bytes 6291456 | tf_op jit(solution)/shard_map/while/body/eval_jaxpr/slice | solution.py:77
  412.8 6.9 %slice.47 = bf16[8,2,1536,64]{2,1,3,0:T(2,128)(2,1)} reshape(bf16[8,24,128,64]{2,1,3,0:T(8,128)(2,1)} %copy.46) | data formatting | bytes 6291456 | tf_op jit(solution)/shard_map/while/body/eval_jaxpr/slice | solution.py:78
  419.8 9.8 %fusion.71 = f32[8,2,128,64]{2,3,1,0:T(8,128)} fusion(f32[8,2,128,1536]{3,2,1,0:T(8,128)} %copy-done.2, f32[8,2,128]{2,1,0:T(2,128)S(1)} %add.95, f32[8,2,128]{2,1,0:T(2,128)S(1)} %max.16, pred[2,1536]{1,0:T(4,128)(4,1)S(1)} %broadcast_compare_fusion.5, bf16[8,2,1536,64]{2,1,3,0:T(2,128)(2,1)} %slice.47), kind=kOutput, calls=%fused_computation.8.clone.1 | convolution fusion | flops 418381824 | bytes 16272384 | tf_op jit(solution)/shard_map/while/body/eval_jaxpr/hgqk,hgkd->hgqd/dot_general | solution.py:96
  432.9 13.0 %gather_fusion = bf16[24,16,128,64]{3,2,1,0:T(8,128)(2,1)} fusion(bf16[16,40,128,64]{3,2,1,0:T(8,128)(2,1)} %get-tuple-element.243, s32[1024]{0:T(1024)S(1)} %pad_clamp_fusion.3), kind=kCustom, calls=%fused_computation.clone.1 | custom fusion | bytes 12583008 | tf_op jit(solution)/shard_map/while/body/eval_jaxpr/jit(_take)/gather | solution.py:75
  464.5 7.0 %slice.46 = bf16[8,2,1536,64]{2,1,3,0:T(2,128)(2,1)} reshape(bf16[8,24,128,64]{2,1,3,0:T(8,128)(2,1)} %copy.45) | data formatting | bytes 6291456 | tf_op jit(solution)/shard_map/while/body/eval_jaxpr/slice | solution.py:77
  482.9 6.9 %copy.46 = bf16[8,24,128,64]{2,1,3,0:T(8,128)(2,1)} copy(bf16[8,24,128,64]{3,2,0,1:T(8,128)(2,1)} %get-tuple-element.219) | data formatting | bytes 6291456 | tf_op jit(solution)/shard_map/while/body/eval_jaxpr/slice | solution.py:78
  489.8 6.9 %slice.47 = bf16[8,2,1536,64]{2,1,3,0:T(2,128)(2,1)} reshape(bf16[8,24,128,64]{2,1,3,0:T(8,128)(2,1)} %copy.46) | data formatting | bytes 6291456 | tf_op jit(solution)/shard_map/while/body/eval_jaxpr/slice | solution.py:78
  496.8 9.8 %fusion.71 = f32[8,2,128,64]{2,3,1,0:T(8,128)} fusion(f32[8,2,128,1536]{3,2,1,0:T(8,128)} %copy-done.2, f32[8,2,128]{2,1,0:T(2,128)S(1)} %add.95, f32[8,2,128]{2,1,0:T(2,128)S(1)} %max.16, pred[2,1536]{1,0:T(4,128)(4,1)S(1)} %broadcast_compare_fusion.5, bf16[8,2,1536,64]{2,1,3,0:T(2,128)(2,1)} %slice.47), kind=kOutput, calls=%fused_computation.8.clone.1 | convolution fusion | flops 418381824 | bytes 16272384 | tf_op jit(solution)/shard_map/while/body/eval_jaxpr/hgqk,hgkd->hgqd/dot_general | solution.py:96
  (159 shorter events, 215.9 us)
Async XLA Ops:
  0.0 159.8 %copy-start = (bf16[512,1024]{1,0:T(8,128)(2,1)S(1)}, bf16[512,1024]{1,0:T(8,128)(2,1)}, u32[]{:S(2)}) copy-start(bf16[512,1024]{1,0:T(8,128)(2,1)} %param.11) | copy-start | bytes 3145732
  0.0 6.5 %copy-start.5 = (bf16[1024,512]{1,0:T(8,128)(2,1)S(1)}, bf16[1024,512]{1,0:T(8,128)(2,1)}, u32[]{:S(2)}) copy-start(bf16[1024,512]{1,0:T(8,128)(2,1)} %param.9) | copy-start | bytes 3145732
  0.9 58.7 %copy-start.10 = (s32[8]{0:T(128)S(1)}, s32[8]{0:T(128)}, u32[]{:S(2)}) copy-start(s32[8]{0:T(128)} %param.14) | copy-start | bytes 100
  0.9 58.7 %copy-start.9 = (s32[8,12]{1,0:T(8,128)S(1)}, s32[8,12]{1,0:T(8,128)}, u32[]{:S(2)}) copy-start(s32[8,12]{1,0:T(8,128)} %param.13) | copy-start | bytes 1156
  4.5 36.8 %collective-permute-start.4 = (bf16[512,512]{1,0:T(8,128)(2,1)S(1)}, bf16[512,512]{1,0:T(8,128)(2,1)S(1)}, u32[]{:S(2)}, u32[]{:S(2)}) collective-permute-start(bf16[512,512]{1,0:T(8,128)(2,1)S(1)} %select_select_fusion), channel_id=1, source_target_pairs={{0,1},{1,0},{2,3},{3,2},{4,5},{5,4},{6,7},{7,6},{8,9},{9,8},{10,11... | collective-permute-start | bytes 1572872 | tf_op jit(solution)/shard_map/ppermute | solution.py:23
  6.5 98.3 %collective-permute-start = (bf16[1024,512]{1,0:T(8,128)(2,1)S(1)}, bf16[1024,512]{1,0:T(8,128)(2,1)}, u32[]{:S(2)}, u32[]{:S(2)}) collective-permute-start(bf16[1024,512]{1,0:T(8,128)(2,1)S(1)} %copy-done.5), channel_id=1, source_target_pairs={{0,2},{1,3},{2,4},{3,5},{4,6},{5,7},{6,8},{7,9},{8,10},{9,11},{10,... | collective-permute-start | bytes 3145736 | tf_op jit(solution)/shard_map/ppermute | solution.py:15
  11.7 94.4 %collective-permute-start.1 = (bf16[1024,512]{1,0:T(8,128)(2,1)S(1)}, bf16[1024,512]{1,0:T(8,128)(2,1)}, u32[]{:S(2)}, u32[]{:S(2)}) collective-permute-start(bf16[1024,512]{1,0:T(8,128)(2,1)S(1)} %copy-done.5), channel_id=1, source_target_pairs={{0,1},{1,2},{2,3},{3,4},{4,5},{5,6},{6,7},{7,8},{8,9},{9,10},{10,1... | collective-permute-start | bytes 3145736 | tf_op jit(solution)/shard_map/ppermute | solution.py:15
  41.6 54.8 %collective-permute-start.5 = (bf16[512,512]{1,0:T(8,128)(2,1)S(1)}, bf16[512,512]{1,0:T(8,128)(2,1)S(1)}, u32[]{:S(2)}, u32[]{:S(2)}) collective-permute-start(bf16[512,512]{1,0:T(8,128)(2,1)S(1)} %broadcast_select_fusion), channel_id=1, source_target_pairs={{0,2},{1,3},{2,0},{3,1},{4,6},{5,7},{6,4},{7,5},{8,10},{9,11},{10,... | collective-permute-start | bytes 1572872 | tf_op jit(solution)/shard_map/ppermute | solution.py:23
  45.0 62.5 %collective-permute-start.2 = (bf16[1024,512]{1,0:T(8,128)(2,1)S(1)}, bf16[1024,512]{1,0:T(8,128)(2,1)}, u32[]{:S(2)}, u32[]{:S(2)}) collective-permute-start(bf16[1024,512]{1,0:T(8,128)(2,1)S(1)} %copy-done.5), channel_id=1, source_target_pairs={{1,0},{2,1},{3,2},{4,3},{5,4},{6,5},{7,6},{8,7},{9,8},{10,9},{11,1... | collective-permute-start | bytes 3145736 | tf_op jit(solution)/shard_map/ppermute | solution.py:15
  51.4 104.8 %collective-permute-start.3 = (bf16[1024,512]{1,0:T(8,128)(2,1)S(1)}, bf16[1024,512]{1,0:T(8,128)(2,1)}, u32[]{:S(2)}, u32[]{:S(2)}) collective-permute-start(bf16[1024,512]{1,0:T(8,128)(2,1)S(1)} %copy-done.5), channel_id=1, source_target_pairs={{2,0},{3,1},{4,2},{5,3},{6,4},{7,5},{8,6},{9,7},{10,8},{11,9},{12,... | collective-permute-start | bytes 3145736 | tf_op jit(solution)/shard_map/ppermute | solution.py:15
  98.4 59.1 %collective-permute-start.6 = (bf16[512,512]{1,0:T(8,128)(2,1)S(1)}, bf16[512,512]{1,0:T(8,128)(2,1)S(1)}, u32[]{:S(2)}, u32[]{:S(2)}) collective-permute-start(bf16[512,512]{1,0:T(8,128)(2,1)S(1)} %broadcast_select_fusion.1), channel_id=1, source_target_pairs={{0,4},{1,5},{2,6},{3,7},{4,0},{5,1},{6,2},{7,3},{8,12},{9,13},{10,... | collective-permute-start | bytes 1572872 | tf_op jit(solution)/shard_map/ppermute | solution.py:23
  159.8 12.0 %collective-permute-start.7 = (bf16[512,512]{1,0:T(8,128)(2,1)S(1)}, bf16[512,512]{1,0:T(8,128)(2,1)}, u32[]{:S(2)}, u32[]{:S(2)}) collective-permute-start(bf16[512,512]{1,0:T(8,128)(2,1)S(1)} %broadcast_select_fusion.2), channel_id=1, source_target_pairs={{0,8},{1,9},{2,10},{3,11},{4,12},{5,13},{6,14},{7,15},{8,0},{9,1},... | collective-permute-start | bytes 1572872 | tf_op jit(solution)/shard_map/ppermute | solution.py:23
  173.8 24.9 %collective-permute-start.8 = (bf16[512,512]{1,0:T(8,128)(2,1)}, bf16[512,512]{1,0:T(8,128)(2,1)}, u32[]{:S(2)}, u32[]{:S(2)}) collective-permute-start(bf16[512,512]{1,0:T(8,128)(2,1)} %broadcast_select_fusion.3), channel_id=1, source_target_pairs={{0,16},{1,17},{2,18},{3,19},{4,20},{5,21},{6,22},{7,23},{8,24},{9,... | collective-permute-start | bytes 1572872 | tf_op jit(solution)/shard_map/ppermute | solution.py:23
  198.7 3.2 copy-start.6
  244.7 7.3 %copy-start.2 = (f32[8,2,128,1536]{3,2,1,0:T(8,128)}, f32[8,2,128,1536]{3,2,1,0:T(8,128)S(1)}, u32[]{:S(2)}) copy-start(f32[8,2,128,1536]{3,2,1,0:T(8,128)S(1)} %get-tuple-element.215) | copy-start | bytes 37748740 | tf_op jit(solution)/shard_map/while
  245.5 2.4 copy-start.3
  265.8 9.8 %copy-start.4 = (f32[8,2,128,512]{3,2,1,0:T(8,128)S(1)}, f32[8,2,128,512]{3,2,1,0:T(8,128)}, u32[]{:S(2)}) copy-start(f32[8,2,128,512]{3,2,1,0:T(8,128)} %copy-done.3) | copy-start | bytes 12582916 | tf_op jit(solution)/shard_map/while
  321.6 7.3 %copy-start.2 = (f32[8,2,128,1536]{3,2,1,0:T(8,128)}, f32[8,2,128,1536]{3,2,1,0:T(8,128)S(1)}, u32[]{:S(2)}) copy-start(f32[8,2,128,1536]{3,2,1,0:T(8,128)S(1)} %get-tuple-element.215) | copy-start | bytes 37748740 | tf_op jit(solution)/shard_map/while
  342.8 9.8 %copy-start.4 = (f32[8,2,128,512]{3,2,1,0:T(8,128)S(1)}, f32[8,2,128,512]{3,2,1,0:T(8,128)}, u32[]{:S(2)}) copy-start(f32[8,2,128,512]{3,2,1,0:T(8,128)} %copy-done.3) | copy-start | bytes 12582916 | tf_op jit(solution)/shard_map/while
  398.6 7.3 %copy-start.2 = (f32[8,2,128,1536]{3,2,1,0:T(8,128)}, f32[8,2,128,1536]{3,2,1,0:T(8,128)S(1)}, u32[]{:S(2)}) copy-start(f32[8,2,128,1536]{3,2,1,0:T(8,128)S(1)} %get-tuple-element.215) | copy-start | bytes 37748740 | tf_op jit(solution)/shard_map/while
  419.8 9.8 %copy-start.4 = (f32[8,2,128,512]{3,2,1,0:T(8,128)S(1)}, f32[8,2,128,512]{3,2,1,0:T(8,128)}, u32[]{:S(2)}) copy-start(f32[8,2,128,512]{3,2,1,0:T(8,128)} %copy-done.3) | copy-start | bytes 12582916 | tf_op jit(solution)/shard_map/while
  475.6 7.3 %copy-start.2 = (f32[8,2,128,1536]{3,2,1,0:T(8,128)}, f32[8,2,128,1536]{3,2,1,0:T(8,128)S(1)}, u32[]{:S(2)}) copy-start(f32[8,2,128,1536]{3,2,1,0:T(8,128)S(1)} %get-tuple-element.215) | copy-start | bytes 37748740 | tf_op jit(solution)/shard_map/while
  496.8 9.8 %copy-start.4 = (f32[8,2,128,512]{3,2,1,0:T(8,128)S(1)}, f32[8,2,128,512]{3,2,1,0:T(8,128)}, u32[]{:S(2)}) copy-start(f32[8,2,128,512]{3,2,1,0:T(8,128)} %copy-done.3) | copy-start | bytes 12582916 | tf_op jit(solution)/shard_map/while
  512.8 3.0 copy-start.1
  (5 other events, 10.3 us)

commit v3 on v2

v3 whole, which is shorter than its diff:
```python
import jax
import jax.numpy as jnp
from jax import lax
from jax.experimental import pallas as pl
from jax.experimental.pallas import tpu as pltpu
from jax.sharding import PartitionSpec as P

HEADS = 8
BLOCK = 128
NB = 12
BCAP = 128


def from_behind(value, axis, steps):
    count = lax.axis_size(axis)
    first, last = (max(0, -steps), min(count, count - steps))
    return lax.ppermute(value, axis, [(source, source + steps) for source in range(first, last)])


def share_rows(rows, owner, member):
    count = lax.axis_size("curve")
    span = 1
    while span < count:
        pairs = [(source, source ^ span) for source in range(count) if source ^ span < count]
        other = lax.ppermute(rows, "curve", pairs)
        theirs = (owner // span) == ((member // span) ^ 1)
        rows = jnp.where(theirs[:, None], other, rows)
        span *= 2
    return rows


def attention_kernel(rel_ref, cnt_ref, q_ref, kt_ref, vt_ref, bkt_ref, bvt_ref, o_ref):
    b = pl.program_id(0)
    count = cnt_ref[b]
    picks = [rel_ref[b * NB + i] for i in range(NB)]
    width = NB * BLOCK + bkt_ref.shape[2]
    lane = lax.broadcasted_iota(jnp.int32, (1, width), 1)
    live = (lane // BLOCK < count) | (lane >= NB * BLOCK)
    scale = 1.0 / q_ref.shape[3] ** 0.5
    for h in range(HEADS):
        query = q_ref[0, h]
        keys = jnp.concatenate([kt_ref[p, h] for p in picks] + [bkt_ref[h]], axis=1)
        scores = jnp.dot(query, keys, preferred_element_type=jnp.float32) * scale
        scores = jnp.where(live, scores, -1e30)
        top = jnp.max(scores, axis=1, keepdims=True)
        expo = jnp.exp(scores - top)
        total = jnp.sum(expo, axis=1, keepdims=True)
        weights = (expo / total).astype(jnp.bfloat16)
        values = jnp.concatenate([vt_ref[p, h] for p in picks] + [bvt_ref[h]], axis=1)
        ctx = lax.dot_general(
            values, weights, (((1,), (1,)), ((), ())), preferred_element_type=jnp.float32
        )
        o_ref[0, h] = ctx.astype(jnp.bfloat16)


def attention(rel, counts, q, kt, vt, bkt, bvt):
    nq = q.shape[0]
    nkb = kt.shape[0]
    head_dim = q.shape[3]
    nbound = bkt.shape[2]
    grid_spec = pltpu.PrefetchScalarGridSpec(
        num_scalar_prefetch=2,
        grid=(nq,),
        in_specs=[
            pl.BlockSpec((1, HEADS, BLOCK, head_dim), lambda b, r, c: (b, 0, 0, 0)),
            pl.BlockSpec((nkb, HEADS, head_dim, BLOCK), lambda b, r, c: (0, 0, 0, 0)),
            pl.BlockSpec((nkb, HEADS, head_dim, BLOCK), lambda b, r, c: (0, 0, 0, 0)),
            pl.BlockSpec((HEADS, head_dim, nbound), lambda b, r, c: (0, 0, 0)),
            pl.BlockSpec((HEADS, head_dim, nbound), lambda b, r, c: (0, 0, 0)),
        ],
        out_specs=pl.BlockSpec((1, HEADS, head_dim, BLOCK), lambda b, r, c: (b, 0, 0, 0)),
    )
    return pl.pallas_call(
        attention_kernel,
        grid_spec=grid_spec,
        out_shape=jax.ShapeDtypeStruct((nq, HEADS, head_dim, BLOCK), jnp.bfloat16),
    )(rel, counts, q, kt, vt, bkt, bvt)


def key_tiles(keyvals, width, head_dim):
    rows = keyvals.shape[0]
    keys = keyvals[:, :width].reshape(rows // BLOCK, BLOCK, HEADS, head_dim)
    vals = keyvals[:, width:].reshape(rows // BLOCK, BLOCK, HEADS, head_dim)
    return keys.transpose(0, 2, 3, 1), vals.transpose(0, 2, 3, 1)


def on_device(tokens, w_query, w_keyval, w_out, block_list, block_count, bnd_ids):
    tok_dev, width = tokens.shape
    head_dim = width // HEADS
    nblocks = tok_dev // BLOCK
    member = lax.axis_index("curve")
    queries = jnp.dot(tokens, w_query, preferred_element_type=jnp.float32).astype(jnp.bfloat16)
    queries = queries.reshape(nblocks, BLOCK, HEADS, head_dim).transpose(0, 2, 1, 3)
    pieces = []
    for offset in (-2, -1, 0, 1, 2):
        if offset == 0:
            pieces.append(tokens)
        else:
            pieces.append(from_behind(tokens, "curve", -offset))
    nearby = jnp.dot(
        jnp.concatenate(pieces, axis=0), w_keyval, preferred_element_type=jnp.float32
    ).astype(jnp.bfloat16)
    kt, vt = key_tiles(nearby, width, head_dim)
    owner = bnd_ids // tok_dev
    local_pos = jnp.clip(bnd_ids - member * tok_dev, 0, tok_dev - 1)
    mine = owner == member
    rows = jnp.where(mine[:, None], jnp.take(tokens, local_pos, axis=0), jnp.zeros((), tokens.dtype))
    gathered = share_rows(rows, owner, member)
    bnd_kv = jnp.dot(gathered, w_keyval, preferred_element_type=jnp.float32).astype(jnp.bfloat16)
    bkt, bvt = key_tiles(bnd_kv, width, head_dim)
    bkt = bkt.transpose(1, 2, 0, 3).reshape(HEADS, head_dim, -1)
    bvt = bvt.transpose(1, 2, 0, 3).reshape(HEADS, head_dim, -1)
    first_block = (member - 2) * nblocks
    rel = jnp.clip(block_list - first_block, 0, 5 * nblocks - 1).reshape(-1).astype(jnp.int32)
    context = attention(rel, block_count.astype(jnp.int32), queries, kt, vt, bkt, bvt)
    out_w = w_out.reshape(HEADS, head_dim, width)
    mixed = jnp.einsum("bhdt,hde->bte", context, out_w, preferred_element_type=jnp.float32)
    return mixed.reshape(tok_dev, width).astype(jnp.bfloat16)


def solution(mesh):
    in_specs = (
        P(("geo", "curve"), None),
        P(),
        P(),
        P(),
        P(("geo", "curve"), None),
        P(("geo", "curve")),
        P("geo"),
    )
    out_specs = P(("geo", "curve"), None)
    return jax.shard_map(
        on_device, mesh=mesh, in_specs=in_specs, out_specs=out_specs, check_vma=False
    )
```

time: 522 us -> 282 us (0.54)
  local copies, waits for them, and re-layouts: 231 us -> 80.3 us
  matrix products: 87.1 us -> 14.5 us
  other arithmetic: 52.7 us -> 1.76 us
  Pallas kernels: 0 us -> 39.4 us
    slice x21 -> x4, local copies, waits for them, and re-layouts: 133 us -> 9.17 us  [the longest x3 8.96 us: key_tiles(): vals = keyvals[:, width:].reshape(rows // BLOCK, BLOCK, HEADS, head_dim)]
    dot_general x18 -> x4, matrix products: 77 us -> 14.5 us  [the longest x1 8.18 us: on_device(): jnp.dot(jnp.concatenate(pieces, axis=0), w_keyval, preferred_element_type...]
    reshape x9 -> x11, local copies, waits for them, and re-layouts: 0.74 us -> 60.1 us  [the longest x3 25.1 us: key_tiles(): vals = keyvals[:, width:].reshape(rows // BLOCK, BLOCK, HEADS, head_dim)]
    gather x4 -> x0, local copies, waits for them, and re-layouts: 51.9 us -> none  [attend(): picked = jnp.take(nearby, relative.reshape(2 * NB), axis=1)]
    pallas_call x0 -> x1, Pallas kernels: none -> 39.4 us  [attention(): pl.pallas_call(attention_kernel, grid_spec=grid_spec, out_shape=jax.Shape...]
    while x25 -> x0, local copies, waits for them, and re-layouts: 28.9 us -> none  [the longest x1 19.3 us: on_device(): context = lax.map(attend, (queries, lists, counts))]
    select_n x12 -> x0, other arithmetic: 26.1 us -> none  [the longest x8 26.1 us: attend(): picked = jnp.take(nearby, relative.reshape(2 * NB), axis=1)]
    reduce_sum x8 -> x0, other arithmetic: 16 us -> none  [the longest x4 11.1 us: attend(): jnp.sum(near_exp, axis=-1, keepdims=True)]
  transfers between devices with their start and end apart: 9 -> 9, of which waited for: 4 -> 4; matrix products, arithmetic and copies ran while one was open for 9% -> 30% of each run, Pallas kernels for 0% -> 0%
where the time goes in v3:
time: 282 us; the launch traced here: 277 us
  waiting for transfers between devices  111 us (39%)
  local copies, waits for them, and re-layouts  80.3 us (28%)
  Pallas kernels  39.4 us (14%)
  starting transfers between devices  29.7 us (11%)
  matrix products  14.5 us (5%)
    ppermute x5, waiting for transfers between devices, share_rows(): other = lax.ppermute(rows, 'curve', pairs)  62.1 us
    ppermute x4, waiting for transfers between devices, from_behind(): lax.ppermute(value, axis, [(source, source + steps) for source in range(f...  48.8 us
    pallas_call x1, Pallas kernels, attention(): pl.pallas_call(attention_kernel, grid_spec=grid_spec, out_shape=jax.Shape...  39.4 us
    reshape x3, local copies, waits for them, and re-layouts, key_tiles(): vals = keyvals[:, width:].reshape(rows // BLOCK, BLOCK, HEADS, head_dim)  25.1 us
    reshape x3, local copies, waits for them, and re-layouts, key_tiles(): keys = keyvals[:, :width].reshape(rows // BLOCK, BLOCK, HEADS, head_dim)  25 us
    ppermute x4, starting transfers between devices, from_behind(): lax.ppermute(value, axis, [(source, source + steps) for source in range(f...  17 us
    ppermute x5, starting transfers between devices, share_rows(): other = lax.ppermute(rows, 'curve', pairs)  12.8 us
    slice x3, local copies, waits for them, and re-layouts, key_tiles(): vals = keyvals[:, width:].reshape(rows // BLOCK, BLOCK, HEADS, head_dim)  8.96 us
  transfers between devices with their start and end apart: 9, of which 4 were waited for; matrix products, arithmetic and copies ran while one was open for 30% of the time, Pallas kernels for 0%

profile of v3, /device:TPU:18, one launch (start us, length us, event | category | flops | bytes accessed | tf_op | source)
XLA Modules:
  0.0 277.0 jit_solution(860653183763824558)
XLA Ops:
  0.9 3.3 %gather_fusion = bf16[512,512]{1,0:T(8,128)(2,1)S(1)} fusion(bf16[1024,512]{1,0:T(8,128)(2,1)} %param.7, s32[1024]{0:T(1024)S(1)} %pad_clamp_fusion), kind=kCustom, calls=%fused_computation | custom fusion | bytes 1050624 | tf_op jit(solution)/shard_map/jit(_take)/gather | solution.py:107
  4.5 2.0 collective-permute-start.4
  6.5 5.2 %collective-permute-start = (bf16[1024,512]{1,0:T(8,128)(2,1)S(1)}, bf16[1024,512]{1,0:T(8,128)(2,1)}, u32[]{:S(2)}, u32[]{:S(2)}) collective-permute-start(bf16[1024,512]{1,0:T(8,128)(2,1)S(1)} %copy-done.1), channel_id=1, source_target_pairs={{0,2},{1,3},{2,4},{3,5},{4,6},{5,7},{6,8},{7,9},{8,10},{9,11},{10,... | collective-permute-start | bytes 3145736 | tf_op jit(solution)/shard_map/ppermute | solution.py:17
  11.7 2.0 collective-permute-start.1
  13.7 27.6 %collective-permute-done.4 = bf16[512,512]{1,0:T(8,128)(2,1)S(1)} collective-permute-done((bf16[512,512]{1,0:T(8,128)(2,1)S(1)}, bf16[512,512]{1,0:T(8,128)(2,1)S(1)}, u32[]{:S(2)}, u32[]{:S(2)}) %collective-permute-start.4) | collective-permute-done | bytes 524320 | tf_op jit(solution)/shard_map/ppermute | solution.py:25
  41.6 3.4 %collective-permute-start.5 = (bf16[512,512]{1,0:T(8,128)(2,1)S(1)}, bf16[512,512]{1,0:T(8,128)(2,1)S(1)}, u32[]{:S(2)}, u32[]{:S(2)}) collective-permute-start(bf16[512,512]{1,0:T(8,128)(2,1)S(1)} %broadcast_select_fusion), channel_id=1, source_target_pairs={{0,2},{1,3},{2,0},{3,1},{4,6},{5,7},{6,4},{7,5},{8,10},{9,11},{10,... | collective-permute-start | bytes 1572872 | tf_op jit(solution)/shard_map/ppermute | solution.py:25
  44.9 6.4 %collective-permute-start.2 = (bf16[1024,512]{1,0:T(8,128)(2,1)S(1)}, bf16[1024,512]{1,0:T(8,128)(2,1)}, u32[]{:S(2)}, u32[]{:S(2)}) collective-permute-start(bf16[1024,512]{1,0:T(8,128)(2,1)S(1)} %copy-done.1), channel_id=1, source_target_pairs={{1,0},{2,1},{3,2},{4,3},{5,4},{6,5},{7,6},{8,7},{9,8},{10,9},{11,1... | collective-permute-start | bytes 3145736 | tf_op jit(solution)/shard_map/ppermute | solution.py:17
  51.3 3.4 %collective-permute-start.3 = (bf16[1024,512]{1,0:T(8,128)(2,1)S(1)}, bf16[1024,512]{1,0:T(8,128)(2,1)}, u32[]{:S(2)}, u32[]{:S(2)}) collective-permute-start(bf16[1024,512]{1,0:T(8,128)(2,1)S(1)} %copy-done.1), channel_id=1, source_target_pairs={{2,0},{3,1},{4,2},{5,3},{6,4},{7,5},{8,6},{9,7},{10,8},{11,9},{12,... | collective-permute-start | bytes 3145736 | tf_op jit(solution)/shard_map/ppermute | solution.py:17
  55.4 2.7 convolution_convert_fusion.2
  58.1 3.9 %reshape.59 = bf16[8,128,8,64]{3,2,1,0:T(8,128)(2,1)} reshape(bf16[1024,512]{1,0:T(8,128)(2,1)} %convolution_convert_fusion.2) | data formatting | bytes 2097152 | tf_op jit(solution)/shard_map/reshape | solution.py:93
  62.0 3.5 %copy.32 = bf16[8,128,8,64]{3,1,2,0:T(8,128)(2,1)} copy(bf16[8,128,8,64]{3,2,1,0:T(8,128)(2,1)} %reshape.59) | data formatting | bytes 2097152 | tf_op jit(solution)/shard_map/reshape | solution.py:93
  65.5 30.9 %collective-permute-done.5 = bf16[512,512]{1,0:T(8,128)(2,1)S(1)} collective-permute-done((bf16[512,512]{1,0:T(8,128)(2,1)S(1)}, bf16[512,512]{1,0:T(8,128)(2,1)S(1)}, u32[]{:S(2)}, u32[]{:S(2)}) %collective-permute-start.5) | collective-permute-done | bytes 524320 | tf_op jit(solution)/shard_map/ppermute | solution.py:25
  96.6 6.7 %collective-permute-start.6 = (bf16[512,512]{1,0:T(8,128)(2,1)S(1)}, bf16[512,512]{1,0:T(8,128)(2,1)S(1)}, u32[]{:S(2)}, u32[]{:S(2)}) collective-permute-start(bf16[512,512]{1,0:T(8,128)(2,1)S(1)} %broadcast_select_fusion.1), channel_id=1, source_target_pairs={{0,4},{1,5},{2,6},{3,7},{4,0},{5,1},{6,2},{7,3},{8,12},{9,13},{10,... | collective-permute-start | bytes 1572872 | tf_op jit(solution)/shard_map/ppermute | solution.py:25
  107.3 48.8 %collective-permute-done.3 = bf16[1024,512]{1,0:T(8,128)(2,1)} collective-permute-done((bf16[1024,512]{1,0:T(8,128)(2,1)S(1)}, bf16[1024,512]{1,0:T(8,128)(2,1)}, u32[]{:S(2)}, u32[]{:S(2)}) %collective-permute-start.3) | collective-permute-done | bytes 1048608 | tf_op jit(solution)/shard_map/ppermute | solution.py:17
  157.7 8.2 %convolution_convert_fusion = bf16[5120,1024]{1,0:T(8,128)(2,1)} fusion(bf16[5120,512]{1,0:T(8,128)(2,1)S(1)} %constant_dynamic-update-slice_fusion, bf16[512,1024]{1,0:T(8,128)(2,1)S(1)} %copy-done), kind=kOutput, calls=%fused_computation.1 | convolution fusion | flops 5373952000 | bytes 16777216 | tf_op jit(solution)/shard_map/dot_general | solution.py:100
  165.9 3.7 %collective-permute-done.7 = bf16[512,512]{1,0:T(8,128)(2,1)S(1)} collective-permute-done((bf16[512,512]{1,0:T(8,128)(2,1)S(1)}, bf16[512,512]{1,0:T(8,128)(2,1)S(1)}, u32[]{:S(2)}, u32[]{:S(2)}) %collective-permute-start.7) | collective-permute-done | bytes 524320 | tf_op jit(solution)/shard_map/ppermute | solution.py:25
  170.3 8.7 %fusion.13 = (bf16[5120,512]{1,0:T(8,128)(2,1)}, bf16[5120,512]{1,0:T(8,128)(2,1)}) fusion(bf16[5120,1024]{1,0:T(8,128)(2,1)} %convolution_convert_fusion), kind=kLoop, calls=%fused_computation.55 | loop fusion | bytes 20971520 | tf_op jit(solution)/shard_map/slice | solution.py:83
  178.9 13.9 %reshape.60 = bf16[40,128,8,64]{3,2,1,0:T(8,128)(2,1)} reshape(bf16[5120,512]{1,0:T(8,128)(2,1)} %get-tuple-element.10) | data formatting | bytes 10485760 | tf_op jit(solution)/shard_map/reshape | solution.py:82
  192.8 11.0 %copy.13 = bf16[40,128,8,64]{1,3,2,0:T(8,128)(2,1)} copy(bf16[40,128,8,64]{3,2,1,0:T(8,128)(2,1)} %reshape.60) | data formatting | bytes 10485760 | tf_op jit(solution)/shard_map/reshape | solution.py:82
  203.9 13.9 %reshape.61 = bf16[40,128,8,64]{3,2,1,0:T(8,128)(2,1)} reshape(bf16[5120,512]{1,0:T(8,128)(2,1)} %get-tuple-element.9) | data formatting | bytes 10485760 | tf_op jit(solution)/shard_map/reshape | solution.py:83
  217.8 11.0 %copy.15 = bf16[40,128,8,64]{1,3,2,0:T(8,128)(2,1)} copy(bf16[40,128,8,64]{3,2,1,0:T(8,128)(2,1)} %reshape.61) | data formatting | bytes 10485760 | tf_op jit(solution)/shard_map/reshape | solution.py:83
  232.3 39.4 %shard_map.73 = bf16[8,8,64,128]{3,2,1,0:T(8,128)(2,1)} custom-call(s32[96]{0:T(128)} %reshape.40.rel_ref, s32[8]{0:T(128)} %cnt_ref.1, bf16[8,8,128,64]{3,2,1,0:T(8,128)(2,1)} %bitcast.27, bf16[40,8,64,128]{3,2,1,0:T(8,128)(2,1)} %bitcast.25, bf16[40,8,64,128]{3,2,1,0:T(8,128)(2,1)} %bitcast.26, bf16[8,64,512]{2,1,0:T(8,128)(2,1)} %reshape.45.bkt_ref, ...), custom_call_target="tpu_custom_call" | custom-call | tf_op jit(solution)/shard_map/pallas_call | solution.py:73
  271.8 1.9 copy.18
  274.2 2.9 %bitcast_convert_fusion = bf16[1024,512]{1,0:T(8,128)(2,1)} fusion(bf16[1024,64,8]{0,2,1:T(8,128)(2,1)S(1)} %reshape.63, bf16[8,64,512]{2,1,0:T(8,128)(2,1)} %bitcast.31), kind=kOutput, calls=%fused_computation.2 | convolution fusion | flops 537395200 | bytes 2621440 | tf_op jit(solution)/shard_map/bhdt,hde->bte/dot_general | solution.py:117
  (37 shorter events, 12.4 us)
Async XLA Ops:
  0.0 157.7 %copy-start = (bf16[512,1024]{1,0:T(8,128)(2,1)S(1)}, bf16[512,1024]{1,0:T(8,128)(2,1)}, u32[]{:S(2)}) copy-start(bf16[512,1024]{1,0:T(8,128)(2,1)} %param.9) | copy-start | bytes 3145732
  0.0 6.5 %copy-start.1 = (bf16[1024,512]{1,0:T(8,128)(2,1)S(1)}, bf16[1024,512]{1,0:T(8,128)(2,1)}, u32[]{:S(2)}) copy-start(bf16[1024,512]{1,0:T(8,128)(2,1)} %param.7) | copy-start | bytes 3145732
  0.0 54.7 %copy-start.2 = (s32[8,12]{1,0:T(8,128)S(1)}, s32[8,12]{1,0:T(8,128)}, u32[]{:S(2)}) copy-start(s32[8,12]{1,0:T(8,128)} %param.11) | copy-start | bytes 1156
  4.5 36.8 %collective-permute-start.4 = (bf16[512,512]{1,0:T(8,128)(2,1)S(1)}, bf16[512,512]{1,0:T(8,128)(2,1)S(1)}, u32[]{:S(2)}, u32[]{:S(2)}) collective-permute-start(bf16[512,512]{1,0:T(8,128)(2,1)S(1)} %select_select_fusion), channel_id=1, source_target_pairs={{0,1},{1,0},{2,3},{3,2},{4,5},{5,4},{6,7},{7,6},{8,9},{9,8},{10,11... | collective-permute-start | bytes 1572872 | tf_op jit(solution)/shard_map/ppermute | solution.py:25
  6.5 96.8 %collective-permute-start = (bf16[1024,512]{1,0:T(8,128)(2,1)S(1)}, bf16[1024,512]{1,0:T(8,128)(2,1)}, u32[]{:S(2)}, u32[]{:S(2)}) collective-permute-start(bf16[1024,512]{1,0:T(8,128)(2,1)S(1)} %copy-done.1), channel_id=1, source_target_pairs={{0,2},{1,3},{2,4},{3,5},{4,6},{5,7},{6,8},{7,9},{8,10},{9,11},{10,... | collective-permute-start | bytes 3145736 | tf_op jit(solution)/shard_map/ppermute | solution.py:17
  11.7 92.9 %collective-permute-start.1 = (bf16[1024,512]{1,0:T(8,128)(2,1)S(1)}, bf16[1024,512]{1,0:T(8,128)(2,1)}, u32[]{:S(2)}, u32[]{:S(2)}) collective-permute-start(bf16[1024,512]{1,0:T(8,128)(2,1)S(1)} %copy-done.1), channel_id=1, source_target_pairs={{0,1},{1,2},{2,3},{3,4},{4,5},{5,6},{6,7},{7,8},{8,9},{9,10},{10,1... | collective-permute-start | bytes 3145736 | tf_op jit(solution)/shard_map/ppermute | solution.py:17
  41.6 54.8 %collective-permute-start.5 = (bf16[512,512]{1,0:T(8,128)(2,1)S(1)}, bf16[512,512]{1,0:T(8,128)(2,1)S(1)}, u32[]{:S(2)}, u32[]{:S(2)}) collective-permute-start(bf16[512,512]{1,0:T(8,128)(2,1)S(1)} %broadcast_select_fusion), channel_id=1, source_target_pairs={{0,2},{1,3},{2,0},{3,1},{4,6},{5,7},{6,4},{7,5},{8,10},{9,11},{10,... | collective-permute-start | bytes 1572872 | tf_op jit(solution)/shard_map/ppermute | solution.py:25
  44.9 61.0 %collective-permute-start.2 = (bf16[1024,512]{1,0:T(8,128)(2,1)S(1)}, bf16[1024,512]{1,0:T(8,128)(2,1)}, u32[]{:S(2)}, u32[]{:S(2)}) collective-permute-start(bf16[1024,512]{1,0:T(8,128)(2,1)S(1)} %copy-done.1), channel_id=1, source_target_pairs={{1,0},{2,1},{3,2},{4,3},{5,4},{6,5},{7,6},{8,7},{9,8},{10,9},{11,1... | collective-permute-start | bytes 3145736 | tf_op jit(solution)/shard_map/ppermute | solution.py:17
  51.3 104.8 %collective-permute-start.3 = (bf16[1024,512]{1,0:T(8,128)(2,1)S(1)}, bf16[1024,512]{1,0:T(8,128)(2,1)}, u32[]{:S(2)}, u32[]{:S(2)}) collective-permute-start(bf16[1024,512]{1,0:T(8,128)(2,1)S(1)} %copy-done.1), channel_id=1, source_target_pairs={{2,0},{3,1},{4,2},{5,3},{6,4},{7,5},{8,6},{9,7},{10,8},{11,9},{12,... | collective-permute-start | bytes 3145736 | tf_op jit(solution)/shard_map/ppermute | solution.py:17
  96.6 60.8 %collective-permute-start.6 = (bf16[512,512]{1,0:T(8,128)(2,1)S(1)}, bf16[512,512]{1,0:T(8,128)(2,1)S(1)}, u32[]{:S(2)}, u32[]{:S(2)}) collective-permute-start(bf16[512,512]{1,0:T(8,128)(2,1)S(1)} %broadcast_select_fusion.1), channel_id=1, source_target_pairs={{0,4},{1,5},{2,6},{3,7},{4,0},{5,1},{6,2},{7,3},{8,12},{9,13},{10,... | collective-permute-start | bytes 1572872 | tf_op jit(solution)/shard_map/ppermute | solution.py:25
  157.6 11.9 %collective-permute-start.7 = (bf16[512,512]{1,0:T(8,128)(2,1)S(1)}, bf16[512,512]{1,0:T(8,128)(2,1)S(1)}, u32[]{:S(2)}, u32[]{:S(2)}) collective-permute-start(bf16[512,512]{1,0:T(8,128)(2,1)S(1)} %broadcast_select_fusion.2), channel_id=1, source_target_pairs={{0,8},{1,9},{2,10},{3,11},{4,12},{5,13},{6,14},{7,15},{8,0},{9,1},... | collective-permute-start | bytes 1572872 | tf_op jit(solution)/shard_map/ppermute | solution.py:25
  169.7 59.1 %collective-permute-start.8 = (bf16[512,512]{1,0:T(8,128)(2,1)S(1)}, bf16[512,512]{1,0:T(8,128)(2,1)S(1)}, u32[]{:S(2)}, u32[]{:S(2)}) collective-permute-start(bf16[512,512]{1,0:T(8,128)(2,1)S(1)} %broadcast_select_fusion.3), channel_id=1, source_target_pairs={{0,16},{1,17},{2,18},{3,19},{4,20},{5,21},{6,22},{7,23},{8,24},{9,... | collective-permute-start | bytes 1572872 | tf_op jit(solution)/shard_map/ppermute | solution.py:25

commit v4 on v3

--- a/solution.py
+++ b/solution.py
@@ -29,7 +29,7 @@
     return rows
 
 
-def attention_kernel(rel_ref, cnt_ref, q_ref, kt_ref, vt_ref, bkt_ref, bvt_ref, o_ref):
+def attention_kernel(rel_ref, cnt_ref, q_ref, kvt_ref, bkt_ref, bvt_ref, o_ref):
     b = pl.program_id(0)
     count = cnt_ref[b]
     picks = [rel_ref[b * NB + i] for i in range(NB)]
@@ -39,23 +39,23 @@
     scale = 1.0 / q_ref.shape[3] ** 0.5
     for h in range(HEADS):
         query = q_ref[0, h]
-        keys = jnp.concatenate([kt_ref[p, h] for p in picks] + [bkt_ref[h]], axis=1)
+        keys = jnp.concatenate([kvt_ref[p, h] for p in picks] + [bkt_ref[h]], axis=1)
         scores = jnp.dot(query, keys, preferred_element_type=jnp.float32) * scale
         scores = jnp.where(live, scores, -1e30)
         top = jnp.max(scores, axis=1, keepdims=True)
         expo = jnp.exp(scores - top)
         total = jnp.sum(expo, axis=1, keepdims=True)
         weights = (expo / total).astype(jnp.bfloat16)
-        values = jnp.concatenate([vt_ref[p, h] for p in picks] + [bvt_ref[h]], axis=1)
+        values = jnp.concatenate([kvt_ref[p, HEADS + h] for p in picks] + [bvt_ref[h]], axis=1)
         ctx = lax.dot_general(
             values, weights, (((1,), (1,)), ((), ())), preferred_element_type=jnp.float32
         )
         o_ref[0, h] = ctx.astype(jnp.bfloat16)
 
 
-def attention(rel, counts, q, kt, vt, bkt, bvt):
+def attention(rel, counts, q, kvt, bkt, bvt):
     nq = q.shape[0]
-    nkb = kt.shape[0]
+    nkb = kvt.shape[0]
     head_dim = q.shape[3]
     nbound = bkt.shape[2]
     grid_spec = pltpu.PrefetchScalarGridSpec(
@@ -63,8 +63,7 @@
         grid=(nq,),
         in_specs=[
             pl.BlockSpec((1, HEADS, BLOCK, head_dim), lambda b, r, c: (b, 0, 0, 0)),
-            pl.BlockSpec((nkb, HEADS, head_dim, BLOCK), lambda b, r, c: (0, 0, 0, 0)),
-            pl.BlockSpec((nkb, HEADS, head_dim, BLOCK), lambda b, r, c: (0, 0, 0, 0)),
+            pl.BlockSpec((nkb, 2 * HEADS, head_dim, BLOCK), lambda b, r, c: (0, 0, 0, 0)),
             pl.BlockSpec((HEADS, head_dim, nbound), lambda b, r, c: (0, 0, 0)),
             pl.BlockSpec((HEADS, head_dim, nbound), lambda b, r, c: (0, 0, 0)),
         ],
@@ -74,7 +73,7 @@
         attention_kernel,
         grid_spec=grid_spec,
         out_shape=jax.ShapeDtypeStruct((nq, HEADS, head_dim, BLOCK), jnp.bfloat16),
-    )(rel, counts, q, kt, vt, bkt, bvt)
+    )(rel, counts, q, kvt, bkt, bvt)
 
 
 def key_tiles(keyvals, width, head_dim):
@@ -97,10 +96,12 @@
             pieces.append(tokens)
         else:
             pieces.append(from_behind(tokens, "curve", -offset))
-    nearby = jnp.dot(
-        jnp.concatenate(pieces, axis=0), w_keyval, preferred_element_type=jnp.float32
+    nearby = jnp.concatenate(pieces, axis=0).reshape(5 * nblocks, BLOCK, width)
+    kv_w = w_keyval.reshape(width, 2 * HEADS, head_dim).transpose(1, 2, 0)
+    kvt = jnp.einsum(
+        "hdc,btc->hbdt", kv_w, nearby, preferred_element_type=jnp.float32
     ).astype(jnp.bfloat16)
-    kt, vt = key_tiles(nearby, width, head_dim)
+    kvt = kvt.transpose(1, 0, 2, 3)
     owner = bnd_ids // tok_dev
     local_pos = jnp.clip(bnd_ids - member * tok_dev, 0, tok_dev - 1)
     mine = owner == member
@@ -112,7 +113,7 @@
     bvt = bvt.transpose(1, 2, 0, 3).reshape(HEADS, head_dim, -1)
     first_block = (member - 2) * nblocks
     rel = jnp.clip(block_list - first_block, 0, 5 * nblocks - 1).reshape(-1).astype(jnp.int32)
-    context = attention(rel, block_count.astype(jnp.int32), queries, kt, vt, bkt, bvt)
+    context = attention(rel, block_count.astype(jnp.int32), queries, kvt, bkt, bvt)
     out_w = w_out.reshape(HEADS, head_dim, width)
     mixed = jnp.einsum("bhdt,hde->bte", context, out_w, preferred_element_type=jnp.float32)
     return mixed.reshape(tok_dev, width).astype(jnp.bfloat16)

time: 282 us -> 202 us (0.72)
  the two profiles are of different devices: /device:TPU:18 before, /device:TPU:78 now
where the time goes in v4:
time: 202 us
  waiting for transfers between devices  99.1 us (49%)
  Pallas kernels  39.7 us (20%)
  starting transfers between devices  25.5 us (13%)
  local copies, waits for them, and re-layouts  22.2 us (11%)
  matrix products  12.1 us (6%)
  other arithmetic  2.82 us (1%)
    ppermute x5, waiting for transfers between devices, share_rows(): other = lax.ppermute(rows, 'curve', pairs)  73.6 us
    pallas_call x1, Pallas kernels, attention(): pl.pallas_call(attention_kernel, grid_spec=grid_spec, out_shape=jax.Shape...  39.7 us
    ppermute x4, waiting for transfers between devices, from_behind(): lax.ppermute(value, axis, [(source, source + steps) for source in range(f...  25.5 us
    ppermute x4, starting transfers between devices, from_behind(): lax.ppermute(value, axis, [(source, source + steps) for source in range(f...  15.9 us
    ppermute x5, starting transfers between devices, share_rows(): other = lax.ppermute(rows, 'curve', pairs)  9.65 us
    dot_general x1, matrix products, on_device(): jnp.einsum('hdc,btc->hbdt', kv_w, nearby, preferred_element_type=jnp.floa...  7.82 us
    unnamed x15, local copies, waits for them, and re-layouts  6.24 us
    reshape x2, local copies, waits for them, and re-layouts, on_device(): queries.reshape(nblocks, BLOCK, HEADS, head_dim).transpose(0, 2, 1, 3)  5.6 us
  transfers between devices with their start and end apart: 9, of which 7 were waited for; matrix products, arithmetic and copies ran while one was open for 12% of the time, Pallas kernels for 0%

profile of v4, /device:TPU:78, one launch (start us, length us, event | category | flops | bytes accessed | tf_op | source)
XLA Modules:
  0.0 201.7 jit_solution(15995980847676668288)
XLA Ops:
  0.9 3.3 %gather_fusion = bf16[512,512]{1,0:T(8,128)(2,1)S(1)} fusion(bf16[1024,512]{1,0:T(8,128)(2,1)} %param.7, s32[1024]{0:T(1024)S(1)} %pad_clamp_fusion), kind=kCustom, calls=%fused_computation | custom fusion | bytes 1050624 | tf_op jit(solution)/shard_map/jit(_take)/gather | solution.py:108
  4.5 2.0 collective-permute-start.4
  6.5 11.9 %collective-permute-done.4 = bf16[512,512]{1,0:T(8,128)(2,1)S(1)} collective-permute-done((bf16[512,512]{1,0:T(8,128)(2,1)S(1)}, bf16[512,512]{1,0:T(8,128)(2,1)S(1)}, u32[]{:S(2)}, u32[]{:S(2)}) %collective-permute-start.4) | collective-permute-done | bytes 524320 | tf_op jit(solution)/shard_map/ppermute | solution.py:25
  18.8 7.7 %collective-permute-start = (bf16[1024,512]{1,0:T(8,128)(2,1)S(1)}, bf16[1024,512]{1,0:T(8,128)(2,1)}, u32[]{:S(2)}, u32[]{:S(2)}) collective-permute-start(bf16[1024,512]{1,0:T(8,128)(2,1)S(1)} %copy-done.1), channel_id=1, source_target_pairs={{0,2},{1,3},{2,4},{3,5},{4,6},{5,7},{6,8},{7,9},{8,10},{9,11},{10,... | collective-permute-start | bytes 3145736 | tf_op jit(solution)/shard_map/ppermute | solution.py:17
  26.5 2.9 %collective-permute-start.1 = (bf16[1024,512]{1,0:T(8,128)(2,1)S(1)}, bf16[1024,512]{1,0:T(8,128)(2,1)}, u32[]{:S(2)}, u32[]{:S(2)}) collective-permute-start(bf16[1024,512]{1,0:T(8,128)(2,1)S(1)} %copy-done.1), channel_id=1, source_target_pairs={{0,1},{1,2},{2,3},{3,4},{4,5},{5,6},{6,7},{7,8},{8,9},{9,10},{10,1... | collective-permute-start | bytes 3145736 | tf_op jit(solution)/shard_map/ppermute | solution.py:17
  29.4 2.9 %collective-permute-start.2 = (bf16[1024,512]{1,0:T(8,128)(2,1)S(1)}, bf16[1024,512]{1,0:T(8,128)(2,1)}, u32[]{:S(2)}, u32[]{:S(2)}) collective-permute-start(bf16[1024,512]{1,0:T(8,128)(2,1)S(1)} %copy-done.1), channel_id=1, source_target_pairs={{1,0},{2,1},{3,2},{4,3},{5,4},{6,5},{7,6},{8,7},{9,8},{10,9},{11,1... | collective-permute-start | bytes 3145736 | tf_op jit(solution)/shard_map/ppermute | solution.py:17
  32.3 2.4 %collective-permute-start.3 = (bf16[1024,512]{1,0:T(8,128)(2,1)S(1)}, bf16[1024,512]{1,0:T(8,128)(2,1)}, u32[]{:S(2)}, u32[]{:S(2)}) collective-permute-start(bf16[1024,512]{1,0:T(8,128)(2,1)S(1)} %copy-done.1), channel_id=1, source_target_pairs={{2,0},{3,1},{4,2},{5,3},{6,4},{7,5},{8,6},{9,7},{10,8},{11,9},{12,... | collective-permute-start | bytes 3145736 | tf_op jit(solution)/shard_map/ppermute | solution.py:17
  34.7 7.3 %collective-permute-done.5 = bf16[512,512]{1,0:T(8,128)(2,1)S(1)} collective-permute-done((bf16[512,512]{1,0:T(8,128)(2,1)S(1)}, bf16[512,512]{1,0:T(8,128)(2,1)S(1)}, u32[]{:S(2)}, u32[]{:S(2)}) %collective-permute-start.5) | collective-permute-done | bytes 524320 | tf_op jit(solution)/shard_map/ppermute | solution.py:25
  42.1 5.7 %collective-permute-start.6 = (bf16[512,512]{1,0:T(8,128)(2,1)S(1)}, bf16[512,512]{1,0:T(8,128)(2,1)}, u32[]{:S(2)}, u32[]{:S(2)}) collective-permute-start(bf16[512,512]{1,0:T(8,128)(2,1)S(1)} %broadcast_select_fusion.1), channel_id=1, source_target_pairs={{0,4},{1,5},{2,6},{3,7},{4,0},{5,1},{6,2},{7,3},{8,12},{9,13},{10,... | collective-permute-start | bytes 1572872 | tf_op jit(solution)/shard_map/ppermute | solution.py:25
  48.5 2.3 %copy.13 = bf16[512,1024]{0,1:T(8,128)(2,1)} copy(bf16[512,1024]{1,0:T(8,128)(2,1)} %param.9) | data formatting | bytes 2097152 | tf_op args[2]
  50.7 1.7 convolution_convert_fusion.1
  52.5 2.1 %reshape.61 = bf16[8,128,8,64]{3,2,1,0:T(8,128)(2,1)} reshape(bf16[1024,512]{1,0:T(8,128)(2,1)S(1)} %convolution_convert_fusion.1) | data formatting | bytes 2097152 | tf_op jit(solution)/shard_map/reshape | solution.py:92
  54.6 3.5 %copy.27 = bf16[8,128,8,64]{3,1,2,0:T(8,128)(2,1)} copy(bf16[8,128,8,64]{3,2,1,0:T(8,128)(2,1)} %reshape.61) | data formatting | bytes 2097152 | tf_op jit(solution)/shard_map/reshape | solution.py:92
  58.1 21.7 %collective-permute-done = bf16[1024,512]{1,0:T(8,128)(2,1)} collective-permute-done((bf16[1024,512]{1,0:T(8,128)(2,1)S(1)}, bf16[1024,512]{1,0:T(8,128)(2,1)}, u32[]{:S(2)}, u32[]{:S(2)}) %collective-permute-start) | collective-permute-done | bytes 1048608 | tf_op jit(solution)/shard_map/ppermute | solution.py:17
  81.1 47.3 %collective-permute-done.6 = bf16[512,512]{1,0:T(8,128)(2,1)} collective-permute-done((bf16[512,512]{1,0:T(8,128)(2,1)S(1)}, bf16[512,512]{1,0:T(8,128)(2,1)}, u32[]{:S(2)}, u32[]{:S(2)}) %collective-permute-start.6) | collective-permute-done | bytes 524320 | tf_op jit(solution)/shard_map/ppermute | solution.py:25
  130.2 3.7 %collective-permute-done.1 = bf16[1024,512]{1,0:T(8,128)(2,1)} collective-permute-done((bf16[1024,512]{1,0:T(8,128)(2,1)S(1)}, bf16[1024,512]{1,0:T(8,128)(2,1)}, u32[]{:S(2)}, u32[]{:S(2)}) %collective-permute-start.1) | collective-permute-done | bytes 1048608 | tf_op jit(solution)/shard_map/ppermute | solution.py:17
  135.3 1.3 constant_dynamic-update-slice_fusion.1
  136.6 1.3 constant_dynamic-update-slice_fusion
  137.9 3.6 %collective-permute-done.7 = bf16[512,512]{1,0:T(8,128)(2,1)S(1)} collective-permute-done((bf16[512,512]{1,0:T(8,128)(2,1)S(1)}, bf16[512,512]{1,0:T(8,128)(2,1)S(1)}, u32[]{:S(2)}, u32[]{:S(2)}) %collective-permute-start.7) | collective-permute-done | bytes 524320 | tf_op jit(solution)/shard_map/ppermute | solution.py:25
  142.9 7.8 %convert_bitcast_fusion.kvt_ref = bf16[40,16,64,128]{3,2,1,0:T(8,128)(2,1)} fusion(bf16[40,128,512,1]{2,1,3,0:T(8,128)(2,1)S(1)} %bitcast.41, bf16[16,64,512,1]{2,1,0,3:T(8,128)(2,1)S(1)} %bitcast.40), kind=kOutput, calls=%fused_computation.1 | convolution fusion | flops 5373952000 | bytes 16777216 | tf_op jit(solution)/shard_map/hdc,btc->hbdt/dot_general | solution.py:101
  150.7 3.5 %collective-permute-done.8 = bf16[512,512]{1,0:T(8,128)(2,1)S(1)} collective-permute-done((bf16[512,512]{1,0:T(8,128)(2,1)S(1)}, bf16[512,512]{1,0:T(8,128)(2,1)S(1)}, u32[]{:S(2)}, u32[]{:S(2)}) %collective-permute-start.8) | collective-permute-done | bytes 524320 | tf_op jit(solution)/shard_map/ppermute | solution.py:25
  157.8 39.7 %shard_map.73 = bf16[8,8,64,128]{3,2,1,0:T(8,128)(2,1)} custom-call(s32[96]{0:T(128)} %reshape.40.rel_ref, s32[8]{0:T(128)} %cnt_ref.1, bf16[8,8,128,64]{3,2,1,0:T(8,128)(2,1)} %bitcast.36, bf16[40,16,64,128]{3,2,1,0:T(8,128)(2,1)} %convert_bitcast_fusion.kvt_ref, bf16[8,64,512]{2,1,0:T(8,128)(2,1)} %reshape.45.bkt_ref, bf16[8,64,512]{2,1,0:T(8,128)(2,1)} %reshape.47.bvt_ref), custom_call_target="tpu_custom_call" | custom-call | tf_op jit(solution)/shard_map/pallas_call | solution.py:72
  197.5 1.9 copy.16
  199.9 1.8 bitcast_convert_fusion
  (37 shorter events, 12.0 us)
Async XLA Ops:
  0.0 199.9 %copy-start = (bf16[512,512]{1,0:T(8,128)(2,1)S(1)}, bf16[512,512]{1,0:T(8,128)(2,1)}, u32[]{:S(2)}) copy-start(bf16[512,512]{1,0:T(8,128)(2,1)} %param.10) | copy-start | bytes 1572868
  0.0 18.8 %copy-start.1 = (bf16[1024,512]{1,0:T(8,128)(2,1)S(1)}, bf16[1024,512]{1,0:T(8,128)(2,1)}, u32[]{:S(2)}) copy-start(bf16[1024,512]{1,0:T(8,128)(2,1)} %param.7) | copy-start | bytes 3145732
  0.0 47.9 %copy-start.4 = (s32[8,12]{1,0:T(8,128)S(1)}, s32[8,12]{1,0:T(8,128)}, u32[]{:S(2)}) copy-start(s32[8,12]{1,0:T(8,128)} %param.11) | copy-start | bytes 1156
  4.5 13.9 %collective-permute-start.4 = (bf16[512,512]{1,0:T(8,128)(2,1)S(1)}, bf16[512,512]{1,0:T(8,128)(2,1)S(1)}, u32[]{:S(2)}, u32[]{:S(2)}) collective-permute-start(bf16[512,512]{1,0:T(8,128)(2,1)S(1)} %select_select_fusion), channel_id=1, source_target_pairs={{0,1},{1,0},{2,3},{3,2},{4,5},{5,4},{6,7},{7,6},{8,9},{9,8},{10,11... | collective-permute-start | bytes 1572872 | tf_op jit(solution)/shard_map/ppermute | solution.py:25
  18.7 23.3 %collective-permute-start.5 = (bf16[512,512]{1,0:T(8,128)(2,1)S(1)}, bf16[512,512]{1,0:T(8,128)(2,1)S(1)}, u32[]{:S(2)}, u32[]{:S(2)}) collective-permute-start(bf16[512,512]{1,0:T(8,128)(2,1)S(1)} %broadcast_select_fusion), channel_id=1, source_target_pairs={{0,2},{1,3},{2,0},{3,1},{4,6},{5,7},{6,4},{7,5},{8,10},{9,11},{10,... | collective-permute-start | bytes 1572872 | tf_op jit(solution)/shard_map/ppermute | solution.py:25
  18.8 61.0 %collective-permute-start = (bf16[1024,512]{1,0:T(8,128)(2,1)S(1)}, bf16[1024,512]{1,0:T(8,128)(2,1)}, u32[]{:S(2)}, u32[]{:S(2)}) collective-permute-start(bf16[1024,512]{1,0:T(8,128)(2,1)S(1)} %copy-done.1), channel_id=1, source_target_pairs={{0,2},{1,3},{2,4},{3,5},{4,6},{5,7},{6,8},{7,9},{8,10},{9,11},{10,... | collective-permute-start | bytes 3145736 | tf_op jit(solution)/shard_map/ppermute | solution.py:17
  26.5 107.5 %collective-permute-start.1 = (bf16[1024,512]{1,0:T(8,128)(2,1)S(1)}, bf16[1024,512]{1,0:T(8,128)(2,1)}, u32[]{:S(2)}, u32[]{:S(2)}) collective-permute-start(bf16[1024,512]{1,0:T(8,128)(2,1)S(1)} %copy-done.1), channel_id=1, source_target_pairs={{0,1},{1,2},{2,3},{3,4},{4,5},{5,6},{6,7},{7,8},{8,9},{9,10},{10,1... | collective-permute-start | bytes 3145736 | tf_op jit(solution)/shard_map/ppermute | solution.py:17
  29.4 105.9 %collective-permute-start.2 = (bf16[1024,512]{1,0:T(8,128)(2,1)S(1)}, bf16[1024,512]{1,0:T(8,128)(2,1)}, u32[]{:S(2)}, u32[]{:S(2)}) collective-permute-start(bf16[1024,512]{1,0:T(8,128)(2,1)S(1)} %copy-done.1), channel_id=1, source_target_pairs={{1,0},{2,1},{3,2},{4,3},{5,4},{6,5},{7,6},{8,7},{9,8},{10,9},{11,1... | collective-permute-start | bytes 3145736 | tf_op jit(solution)/shard_map/ppermute | solution.py:17
  32.3 104.3 %collective-permute-start.3 = (bf16[1024,512]{1,0:T(8,128)(2,1)S(1)}, bf16[1024,512]{1,0:T(8,128)(2,1)}, u32[]{:S(2)}, u32[]{:S(2)}) collective-permute-start(bf16[1024,512]{1,0:T(8,128)(2,1)S(1)} %copy-done.1), channel_id=1, source_target_pairs={{2,0},{3,1},{4,2},{5,3},{6,4},{7,5},{8,6},{9,7},{10,8},{11,9},{12,... | collective-permute-start | bytes 3145736 | tf_op jit(solution)/shard_map/ppermute | solution.py:17
  42.1 86.3 %collective-permute-start.6 = (bf16[512,512]{1,0:T(8,128)(2,1)S(1)}, bf16[512,512]{1,0:T(8,128)(2,1)}, u32[]{:S(2)}, u32[]{:S(2)}) collective-permute-start(bf16[512,512]{1,0:T(8,128)(2,1)S(1)} %broadcast_select_fusion.1), channel_id=1, source_target_pairs={{0,4},{1,5},{2,6},{3,7},{4,0},{5,1},{6,2},{7,3},{8,12},{9,13},{10,... | collective-permute-start | bytes 1572872 | tf_op jit(solution)/shard_map/ppermute | solution.py:25
  129.7 13.2 %copy-start.3 = (bf16[512,1024]{0,1:T(8,128)(2,1)S(1)}, bf16[512,1024]{0,1:T(8,128)(2,1)}, u32[]{:S(2)}) copy-start(bf16[512,1024]{0,1:T(8,128)(2,1)} %copy.13) | copy-start | bytes 3145732
  129.7 11.8 %collective-permute-start.7 = (bf16[512,512]{1,0:T(8,128)(2,1)S(1)}, bf16[512,512]{1,0:T(8,128)(2,1)S(1)}, u32[]{:S(2)}, u32[]{:S(2)}) collective-permute-start(bf16[512,512]{1,0:T(8,128)(2,1)S(1)} %broadcast_select_fusion.2), channel_id=1, source_target_pairs={{0,8},{1,9},{2,10},{3,11},{4,12},{5,13},{6,14},{7,15},{8,0},{9,1},... | collective-permute-start | bytes 1572872 | tf_op jit(solution)/shard_map/ppermute | solution.py:25
  141.6 12.6 %collective-permute-start.8 = (bf16[512,512]{1,0:T(8,128)(2,1)S(1)}, bf16[512,512]{1,0:T(8,128)(2,1)S(1)}, u32[]{:S(2)}, u32[]{:S(2)}) collective-permute-start(bf16[512,512]{1,0:T(8,128)(2,1)S(1)} %broadcast_select_fusion.3), channel_id=1, source_target_pairs={{0,16},{1,17},{2,18},{3,19},{4,20},{5,21},{6,22},{7,23},{8,24},{9,... | collective-permute-start | bytes 1572872 | tf_op jit(solution)/shard_map/ppermute | solution.py:25
  142.9 11.3 %copy-start.2 = (bf16[512,1024]{1,0:T(8,128)(2,1)S(1)}, bf16[512,1024]{1,0:T(8,128)(2,1)}, u32[]{:S(2)}) copy-start(bf16[512,1024]{1,0:T(8,128)(2,1)} %param.9) | copy-start | bytes 3145732

commit v5 on v4

--- a/solution.py
+++ b/solution.py
@@ -9,6 +9,7 @@
 BLOCK = 128
 NB = 12
 BCAP = 128
+ROW = 8
 
 
 def from_behind(value, axis, steps):
@@ -17,9 +18,8 @@
     return lax.ppermute(value, axis, [(source, source + steps) for source in range(first, last)])
 
 
-def share_rows(rows, owner, member):
+def share_rows(rows, owner, member, span):
     count = lax.axis_size("curve")
-    span = 1
     while span < count:
         pairs = [(source, source ^ span) for source in range(count) if source ^ span < count]
         other = lax.ppermute(rows, "curve", pairs)
@@ -27,6 +27,33 @@
         rows = jnp.where(theirs[:, None], other, rows)
         span *= 2
     return rows
+
+
+def boundary_rows(tokens, bnd_ids, member):
+    tok_dev = tokens.shape[0]
+    count = lax.axis_size("curve")
+    group = ROW if count % ROW == 0 else 1
+    owner = bnd_ids // tok_dev
+    my_start = jnp.sum((owner < member).astype(jnp.int32))
+    padded_ids = jnp.concatenate([bnd_ids, jnp.zeros((BCAP,), jnp.int32)])
+    my_ids = lax.dynamic_slice_in_dim(padded_ids, my_start, BCAP)
+    compact = jnp.take(tokens, jnp.clip(my_ids - member * tok_dev, 0, tok_dev - 1), axis=0)
+    pieces = [compact]
+    for step in range(1, group):
+        pairs = [
+            (source, (source // group) * group + (source % group + step) % group)
+            for source in range(count)
+        ]
+        pieces.append(lax.ppermute(compact, "curve", pairs))
+    near = jnp.concatenate(pieces, axis=0)
+    owner_start = jnp.sum((owner[None, :] < owner[:, None]).astype(jnp.int32), axis=1)
+    slot = jnp.arange(bnd_ids.shape[0], dtype=jnp.int32)
+    within = jnp.clip(slot - owner_start, 0, BCAP - 1)
+    step_of = (member % group - owner % group) % group
+    rows = jnp.take(near, step_of * BCAP + within, axis=0)
+    ours = (owner // group) == (member // group)
+    rows = jnp.where(ours[:, None], rows, jnp.zeros((), rows.dtype))
+    return share_rows(rows, owner, member, group)
 
 
 def attention_kernel(rel_ref, cnt_ref, q_ref, kvt_ref, bkt_ref, bvt_ref, o_ref):
@@ -102,11 +129,7 @@
         "hdc,btc->hbdt", kv_w, nearby, preferred_element_type=jnp.float32
     ).astype(jnp.bfloat16)
     kvt = kvt.transpose(1, 0, 2, 3)
-    owner = bnd_ids // tok_dev
-    local_pos = jnp.clip(bnd_ids - member * tok_dev, 0, tok_dev - 1)
-    mine = owner == member
-    rows = jnp.where(mine[:, None], jnp.take(tokens, local_pos, axis=0), jnp.zeros((), tokens.dtype))
-    gathered = share_rows(rows, owner, member)
+    gathered = boundary_rows(tokens, bnd_ids, member)
     bnd_kv = jnp.dot(gathered, w_keyval, preferred_element_type=jnp.float32).astype(jnp.bfloat16)
     bkt, bvt = key_tiles(bnd_kv, width, head_dim)
     bkt = bkt.transpose(1, 2, 0, 3).reshape(HEADS, head_dim, -1)

time: 202 us -> 177 us (0.88)
  the two profiles are of different devices: /device:TPU:78 before, /device:TPU:18 now
where the time goes in v5:
time: 177 us; the launch traced here: 176 us
  waiting for transfers between devices  52.8 us (30%)
  starting transfers between devices  40.5 us (23%)
  Pallas kernels  39.4 us (22%)
  local copies, waits for them, and re-layouts  22.6 us (13%)
  matrix products  13.5 us (8%)
  other arithmetic  4.95 us (3%)
  between operations  2.29 us (1%)
    ppermute x4, waiting for transfers between devices, from_behind(): lax.ppermute(value, axis, [(source, source + steps) for source in range(f...  42.7 us
    pallas_call x1, Pallas kernels, attention(): pl.pallas_call(attention_kernel, grid_spec=grid_spec, out_shape=jax.Shape...  39.4 us
    ppermute x7, starting transfers between devices, boundary_rows(): pieces.append(lax.ppermute(compact, 'curve', pairs))  20.3 us
    ppermute x4, starting transfers between devices, from_behind(): lax.ppermute(value, axis, [(source, source + steps) for source in range(f...  15.1 us
    dot_general x1, matrix products, on_device(): jnp.einsum('hdc,btc->hbdt', kv_w, nearby, preferred_element_type=jnp.floa...  7.84 us
    unnamed x21, local copies, waits for them, and re-layouts  6.59 us
    ppermute x7, waiting for transfers between devices, boundary_rows(): pieces.append(lax.ppermute(compact, 'curve', pairs))  6.45 us
    ppermute x2, starting transfers between devices, share_rows(): other = lax.ppermute(rows, 'curve', pairs)  5.12 us
  transfers between devices with their start and end apart: 13, of which 7 were waited for; matrix products, arithmetic and copies ran while one was open for 16% of the time, Pallas kernels for 0%

profile of v5, /device:TPU:18, one launch (start us, length us, event | category | flops | bytes accessed | tf_op | source)
XLA Modules:
  0.0 176.0 jit_solution(6304494008657634184)
XLA Ops:
  4.2 2.2 %gather_fusion = bf16[128,512]{1,0:T(8,128)(2,1)S(1)} fusion(bf16[1024,512]{1,0:T(8,128)(2,1)} %param.7, s32[1024]{0:T(1024)S(1)} %pad_clamp_fusion.1), kind=kCustom, calls=%fused_computation | custom fusion | bytes 262656 | tf_op jit(solution)/shard_map/jit(_take)/gather | solution.py:40
  6.5 2.0 %collective-permute-start.4 = (bf16[128,512]{1,0:T(8,128)(2,1)S(1)}, bf16[128,512]{1,0:T(8,128)(2,1)S(1)}, u32[]{:S(2)}, u32[]{:S(2)}) collective-permute-start(bf16[128,512]{1,0:T(8,128)(2,1)S(1)} %get-tuple-element.12), channel_id=1, source_target_pairs={{0,1},{1,2},{2,3},{3,4},{4,5},{5,6},{6,7},{7,0},{8,9},{9,10},{10,1... | collective-permute-start | bytes 393224 | tf_op jit(solution)/shard_map/ppermute | solution.py:47
  8.5 3.3 %collective-permute-start.5 = (bf16[128,512]{1,0:T(8,128)(2,1)S(1)}, bf16[128,512]{1,0:T(8,128)(2,1)S(1)}, u32[]{:S(2)}, u32[]{:S(2)}) collective-permute-start(bf16[128,512]{1,0:T(8,128)(2,1)S(1)} %get-tuple-element.12), channel_id=1, source_target_pairs={{0,2},{1,3},{2,4},{3,5},{4,6},{5,7},{6,0},{7,1},{8,10},{9,11},{10,... | collective-permute-start | bytes 393224 | tf_op jit(solution)/shard_map/ppermute | solution.py:47
  11.8 4.0 %collective-permute-start.6 = (bf16[128,512]{1,0:T(8,128)(2,1)S(1)}, bf16[128,512]{1,0:T(8,128)(2,1)S(1)}, u32[]{:S(2)}, u32[]{:S(2)}) collective-permute-start(bf16[128,512]{1,0:T(8,128)(2,1)S(1)} %get-tuple-element.12), channel_id=1, source_target_pairs={{0,3},{1,4},{2,5},{3,6},{4,7},{5,0},{6,1},{7,2},{8,11},{9,12},{10,... | collective-permute-start | bytes 393224 | tf_op jit(solution)/shard_map/ppermute | solution.py:47
  16.4 4.9 %collective-permute-start.8 = (bf16[128,512]{1,0:T(8,128)(2,1)S(1)}, bf16[128,512]{1,0:T(8,128)(2,1)S(1)}, u32[]{:S(2)}, u32[]{:S(2)}) collective-permute-start(bf16[128,512]{1,0:T(8,128)(2,1)S(1)} %get-tuple-element.12), channel_id=1, source_target_pairs={{0,5},{1,6},{2,7},{3,0},{4,1},{5,2},{6,3},{7,4},{8,13},{9,14},{10,... | collective-permute-start | bytes 393224 | tf_op jit(solution)/shard_map/ppermute | solution.py:47
  21.7 2.7 %collective-permute-start.9 = (bf16[128,512]{1,0:T(8,128)(2,1)S(1)}, bf16[128,512]{1,0:T(8,128)(2,1)S(1)}, u32[]{:S(2)}, u32[]{:S(2)}) collective-permute-start(bf16[128,512]{1,0:T(8,128)(2,1)S(1)} %get-tuple-element.12), channel_id=1, source_target_pairs={{0,6},{1,7},{2,0},{3,1},{4,2},{5,3},{6,4},{7,5},{8,14},{9,15},{10,... | collective-permute-start | bytes 393224 | tf_op jit(solution)/shard_map/ppermute | solution.py:47
  25.4 2.8 %collective-permute-start.10 = (bf16[128,512]{1,0:T(8,128)(2,1)S(1)}, bf16[128,512]{1,0:T(8,128)(2,1)S(1)}, u32[]{:S(2)}, u32[]{:S(2)}) collective-permute-start(bf16[128,512]{1,0:T(8,128)(2,1)S(1)} %get-tuple-element.12), channel_id=1, source_target_pairs={{0,7},{1,0},{2,1},{3,2},{4,3},{5,4},{6,5},{7,6},{8,15},{9,8},{10,9... | collective-permute-start | bytes 393224 | tf_op jit(solution)/shard_map/ppermute | solution.py:47
  28.2 5.4 %collective-permute-done.6 = bf16[128,512]{1,0:T(8,128)(2,1)S(1)} collective-permute-done((bf16[128,512]{1,0:T(8,128)(2,1)S(1)}, bf16[128,512]{1,0:T(8,128)(2,1)S(1)}, u32[]{:S(2)}, u32[]{:S(2)}) %collective-permute-start.6) | collective-permute-done | bytes 131104 | tf_op jit(solution)/shard_map/ppermute | solution.py:47
  33.6 1.9 %collective-permute-start = (bf16[1024,512]{1,0:T(8,128)(2,1)}, bf16[1024,512]{1,0:T(8,128)(2,1)}, u32[]{:S(2)}, u32[]{:S(2)}) collective-permute-start(bf16[1024,512]{1,0:T(8,128)(2,1)} %param.7), channel_id=1, source_target_pairs={{0,2},{1,3},{2,4},{3,5},{4,6},{5,7},{6,8},{7,9},{8,10},{9,11},{10,... | collective-permute-start | bytes 3145736 | tf_op jit(solution)/shard_map/ppermute | solution.py:18
  35.6 5.2 %collective-permute-start.1 = (bf16[1024,512]{1,0:T(8,128)(2,1)}, bf16[1024,512]{1,0:T(8,128)(2,1)}, u32[]{:S(2)}, u32[]{:S(2)}) collective-permute-start(bf16[1024,512]{1,0:T(8,128)(2,1)} %param.7), channel_id=1, source_target_pairs={{0,1},{1,2},{2,3},{3,4},{4,5},{5,6},{6,7},{7,8},{8,9},{9,10},{10,1... | collective-permute-start | bytes 3145736 | tf_op jit(solution)/shard_map/ppermute | solution.py:18
  40.9 2.0 %gather_fusion.1 = bf16[512,512]{1,0:T(8,128)(2,1)S(1)} fusion(bf16[1024,512]{1,0:T(8,128)(2,1)S(1)} %constant_dynamic-update-slice_fusion.5, s32[1024]{0:T(1024)S(1)} %pad_clamp_fusion), kind=kCustom, calls=%fused_computation.1 | custom fusion | bytes 1050624 | tf_op jit(solution)/shard_map/jit(_take)/gather | solution.py:53
  45.2 4.6 %collective-permute-start.2 = (bf16[1024,512]{1,0:T(8,128)(2,1)}, bf16[1024,512]{1,0:T(8,128)(2,1)}, u32[]{:S(2)}, u32[]{:S(2)}) collective-permute-start(bf16[1024,512]{1,0:T(8,128)(2,1)} %param.7), channel_id=1, source_target_pairs={{1,0},{2,1},{3,2},{4,3},{5,4},{6,5},{7,6},{8,7},{9,8},{10,9},{11,1... | collective-permute-start | bytes 3145736 | tf_op jit(solution)/shard_map/ppermute | solution.py:18
  49.8 3.4 %collective-permute-start.3 = (bf16[1024,512]{1,0:T(8,128)(2,1)}, bf16[1024,512]{1,0:T(8,128)(2,1)}, u32[]{:S(2)}, u32[]{:S(2)}) collective-permute-start(bf16[1024,512]{1,0:T(8,128)(2,1)} %param.7), channel_id=1, source_target_pairs={{2,0},{3,1},{4,2},{5,3},{6,4},{7,5},{8,6},{9,7},{10,8},{11,9},{12,... | collective-permute-start | bytes 3145736 | tf_op jit(solution)/shard_map/ppermute | solution.py:18
  55.2 3.0 %convolution_convert_fusion.1 = bf16[1024,512]{1,0:T(8,128)(2,1)} fusion(bf16[1024,512]{1,0:T(8,128)(2,1)} %param.7, bf16[512,512]{1,0:T(8,128)(2,1)} %param.8), kind=kOutput, calls=%fused_computation.6 | convolution fusion | flops 537395200 | bytes 2621440 | tf_op jit(solution)/shard_map/dot_general | solution.py:118
  58.2 2.8 %reshape.74 = bf16[8,128,8,64]{3,2,1,0:T(8,128)(2,1)S(1)} reshape(bf16[1024,512]{1,0:T(8,128)(2,1)} %convolution_convert_fusion.1) | data formatting | bytes 2097152 | tf_op jit(solution)/shard_map/reshape | solution.py:119
  61.0 1.9 %copy.31 = bf16[8,128,8,64]{3,1,2,0:T(8,128)(2,1)} copy(bf16[8,128,8,64]{3,2,1,0:T(8,128)(2,1)S(1)} %reshape.74) | data formatting | bytes 2097152 | tf_op jit(solution)/shard_map/reshape | solution.py:119
  62.9 3.6 %collective-permute-done.11 = bf16[512,512]{1,0:T(8,128)(2,1)} collective-permute-done((bf16[512,512]{1,0:T(8,128)(2,1)}, bf16[512,512]{1,0:T(8,128)(2,1)}, u32[]{:S(2)}, u32[]{:S(2)}) %collective-permute-start.11) | collective-permute-done | bytes 524320 | tf_op jit(solution)/shard_map/ppermute | solution.py:25
  67.9 3.8 %collective-permute-start.12 = (bf16[512,512]{1,0:T(8,128)(2,1)S(1)}, bf16[512,512]{1,0:T(8,128)(2,1)S(1)}, u32[]{:S(2)}, u32[]{:S(2)}) collective-permute-start(bf16[512,512]{1,0:T(8,128)(2,1)S(1)} %broadcast_select_fusion), channel_id=1, source_target_pairs={{0,16},{1,17},{2,18},{3,19},{4,20},{5,21},{6,22},{7,23},{8,24},{9,... | collective-permute-start | bytes 1572872 | tf_op jit(solution)/shard_map/ppermute | solution.py:25
  71.7 13.1 %collective-permute-done = bf16[1024,512]{1,0:T(8,128)(2,1)} collective-permute-done((bf16[1024,512]{1,0:T(8,128)(2,1)}, bf16[1024,512]{1,0:T(8,128)(2,1)}, u32[]{:S(2)}, u32[]{:S(2)}) %collective-permute-start) | collective-permute-done | bytes 1048608 | tf_op jit(solution)/shard_map/ppermute | solution.py:18
  86.1 22.1 %collective-permute-done.1 = bf16[1024,512]{1,0:T(8,128)(2,1)} collective-permute-done((bf16[1024,512]{1,0:T(8,128)(2,1)}, bf16[1024,512]{1,0:T(8,128)(2,1)}, u32[]{:S(2)}, u32[]{:S(2)}) %collective-permute-start.1) | collective-permute-done | bytes 1048608 | tf_op jit(solution)/shard_map/ppermute | solution.py:18
  112.1 7.5 %collective-permute-done.3 = bf16[1024,512]{1,0:T(8,128)(2,1)} collective-permute-done((bf16[1024,512]{1,0:T(8,128)(2,1)}, bf16[1024,512]{1,0:T(8,128)(2,1)}, u32[]{:S(2)}, u32[]{:S(2)}) %collective-permute-start.3) | collective-permute-done | bytes 1048608 | tf_op jit(solution)/shard_map/ppermute | solution.py:18
  121.0 7.8 %convert_bitcast_fusion.kvt_ref = bf16[40,16,64,128]{3,2,1,0:T(8,128)(2,1)} fusion(bf16[40,128,512,1]{2,1,3,0:T(8,128)(2,1)S(1)} %bitcast.41, bf16[16,64,512,1]{2,1,0,3:T(8,128)(2,1)S(1)} %bitcast.40), kind=kOutput, calls=%fused_computation.2 | convolution fusion | flops 5373952000 | bytes 16777216 | tf_op jit(solution)/shard_map/hdc,btc->hbdt/dot_general | solution.py:128
  132.4 39.4 %shard_map.73 = bf16[8,8,64,128]{3,2,1,0:T(8,128)(2,1)} custom-call(s32[96]{0:T(128)} %reshape.44.rel_ref, s32[8]{0:T(128)} %cnt_ref.1, bf16[8,8,128,64]{3,2,1,0:T(8,128)(2,1)} %bitcast.36, bf16[40,16,64,128]{3,2,1,0:T(8,128)(2,1)} %convert_bitcast_fusion.kvt_ref, bf16[8,64,512]{2,1,0:T(8,128)(2,1)} %reshape.49.bkt_ref, bf16[8,64,512]{2,1,0:T(8,128)(2,1)} %reshape.51.bvt_ref), custom_call_target="tpu_custom_call" | custom-call | tf_op jit(solution)/shard_map/pallas_call | solution.py:99
  171.8 1.9 %copy.23 = bf16[8,128,64,8]{1,0,3,2:T(8,128)(2,1)S(1)} copy(bf16[8,128,64,8]{1,2,3,0:T(8,128)(2,1)} %bitcast.37) | data formatting | bytes 2097152 | tf_op jit(solution)/shard_map/bhdt,hde->bte/dot_general | solution.py:141
  (56 shorter events, 22.2 us)
Async XLA Ops:
  0.0 174.2 %copy-start = (bf16[512,512]{1,0:T(8,128)(2,1)S(1)}, bf16[512,512]{1,0:T(8,128)(2,1)}, u32[]{:S(2)}) copy-start(bf16[512,512]{1,0:T(8,128)(2,1)} %param.10) | copy-start | bytes 1572868
  0.0 53.2 %copy-start.4 = (s32[8,12]{1,0:T(8,128)S(1)}, s32[8,12]{1,0:T(8,128)}, u32[]{:S(2)}) copy-start(s32[8,12]{1,0:T(8,128)} %param.11) | copy-start | bytes 1156
  0.0 53.9 %copy-start.1 = (bf16[512,1024]{1,0:T(8,128)(2,1)S(1)}, bf16[512,1024]{1,0:T(8,128)(2,1)}, u32[]{:S(2)}) copy-start(bf16[512,1024]{1,0:T(8,128)(2,1)} %param.9) | copy-start | bytes 3145732
  6.5 15.1 %collective-permute-start.4 = (bf16[128,512]{1,0:T(8,128)(2,1)S(1)}, bf16[128,512]{1,0:T(8,128)(2,1)S(1)}, u32[]{:S(2)}, u32[]{:S(2)}) collective-permute-start(bf16[128,512]{1,0:T(8,128)(2,1)S(1)} %get-tuple-element.12), channel_id=1, source_target_pairs={{0,1},{1,2},{2,3},{3,4},{4,5},{5,6},{6,7},{7,0},{8,9},{9,10},{10,1... | collective-permute-start | bytes 393224 | tf_op jit(solution)/shard_map/ppermute | solution.py:47
  8.5 16.9 %collective-permute-start.5 = (bf16[128,512]{1,0:T(8,128)(2,1)S(1)}, bf16[128,512]{1,0:T(8,128)(2,1)S(1)}, u32[]{:S(2)}, u32[]{:S(2)}) collective-permute-start(bf16[128,512]{1,0:T(8,128)(2,1)S(1)} %get-tuple-element.12), channel_id=1, source_target_pairs={{0,2},{1,3},{2,4},{3,5},{4,6},{5,7},{6,0},{7,1},{8,10},{9,11},{10,... | collective-permute-start | bytes 393224 | tf_op jit(solution)/shard_map/ppermute | solution.py:47
  11.8 21.8 %collective-permute-start.6 = (bf16[128,512]{1,0:T(8,128)(2,1)S(1)}, bf16[128,512]{1,0:T(8,128)(2,1)S(1)}, u32[]{:S(2)}, u32[]{:S(2)}) collective-permute-start(bf16[128,512]{1,0:T(8,128)(2,1)S(1)} %get-tuple-element.12), channel_id=1, source_target_pairs={{0,3},{1,4},{2,5},{3,6},{4,7},{5,0},{6,1},{7,2},{8,11},{9,12},{10,... | collective-permute-start | bytes 393224 | tf_op jit(solution)/shard_map/ppermute | solution.py:47
  15.8 19.7 %collective-permute-start.7 = (bf16[128,512]{1,0:T(8,128)(2,1)S(1)}, bf16[128,512]{1,0:T(8,128)(2,1)S(1)}, u32[]{:S(2)}, u32[]{:S(2)}) collective-permute-start(bf16[128,512]{1,0:T(8,128)(2,1)S(1)} %get-tuple-element.12), channel_id=1, source_target_pairs={{0,4},{1,5},{2,6},{3,7},{4,0},{5,1},{6,2},{7,3},{8,12},{9,13},{10,... | collective-permute-start | bytes 393224 | tf_op jit(solution)/shard_map/ppermute | solution.py:47
  16.4 24.4 %collective-permute-start.8 = (bf16[128,512]{1,0:T(8,128)(2,1)S(1)}, bf16[128,512]{1,0:T(8,128)(2,1)S(1)}, u32[]{:S(2)}, u32[]{:S(2)}) collective-permute-start(bf16[128,512]{1,0:T(8,128)(2,1)S(1)} %get-tuple-element.12), channel_id=1, source_target_pairs={{0,5},{1,6},{2,7},{3,0},{4,1},{5,2},{6,3},{7,4},{8,13},{9,14},{10,... | collective-permute-start | bytes 393224 | tf_op jit(solution)/shard_map/ppermute | solution.py:47
  21.7 19.1 %collective-permute-start.9 = (bf16[128,512]{1,0:T(8,128)(2,1)S(1)}, bf16[128,512]{1,0:T(8,128)(2,1)S(1)}, u32[]{:S(2)}, u32[]{:S(2)}) collective-permute-start(bf16[128,512]{1,0:T(8,128)(2,1)S(1)} %get-tuple-element.12), channel_id=1, source_target_pairs={{0,6},{1,7},{2,0},{3,1},{4,2},{5,3},{6,4},{7,5},{8,14},{9,15},{10,... | collective-permute-start | bytes 393224 | tf_op jit(solution)/shard_map/ppermute | solution.py:47
  25.4 15.5 %collective-permute-start.10 = (bf16[128,512]{1,0:T(8,128)(2,1)S(1)}, bf16[128,512]{1,0:T(8,128)(2,1)S(1)}, u32[]{:S(2)}, u32[]{:S(2)}) collective-permute-start(bf16[128,512]{1,0:T(8,128)(2,1)S(1)} %get-tuple-element.12), channel_id=1, source_target_pairs={{0,7},{1,0},{2,1},{3,2},{4,3},{5,4},{6,5},{7,6},{8,15},{9,8},{10,9... | collective-permute-start | bytes 393224 | tf_op jit(solution)/shard_map/ppermute | solution.py:47
  33.6 51.2 %collective-permute-start = (bf16[1024,512]{1,0:T(8,128)(2,1)}, bf16[1024,512]{1,0:T(8,128)(2,1)}, u32[]{:S(2)}, u32[]{:S(2)}) collective-permute-start(bf16[1024,512]{1,0:T(8,128)(2,1)} %param.7), channel_id=1, source_target_pairs={{0,2},{1,3},{2,4},{3,5},{4,6},{5,7},{6,8},{7,9},{8,10},{9,11},{10,... | collective-permute-start | bytes 3145736 | tf_op jit(solution)/shard_map/ppermute | solution.py:18
  35.6 72.7 %collective-permute-start.1 = (bf16[1024,512]{1,0:T(8,128)(2,1)}, bf16[1024,512]{1,0:T(8,128)(2,1)}, u32[]{:S(2)}, u32[]{:S(2)}) collective-permute-start(bf16[1024,512]{1,0:T(8,128)(2,1)} %param.7), channel_id=1, source_target_pairs={{0,1},{1,2},{2,3},{3,4},{4,5},{5,6},{6,7},{7,8},{8,9},{9,10},{10,1... | collective-permute-start | bytes 3145736 | tf_op jit(solution)/shard_map/ppermute | solution.py:18
  43.9 22.6 %collective-permute-start.11 = (bf16[512,512]{1,0:T(8,128)(2,1)}, bf16[512,512]{1,0:T(8,128)(2,1)}, u32[]{:S(2)}, u32[]{:S(2)}) collective-permute-start(bf16[512,512]{1,0:T(8,128)(2,1)} %select_select_fusion), channel_id=1, source_target_pairs={{0,8},{1,9},{2,10},{3,11},{4,12},{5,13},{6,14},{7,15},{8,0},{9,1},... | collective-permute-start | bytes 1572872 | tf_op jit(solution)/shard_map/ppermute | solution.py:25
  45.2 65.6 %collective-permute-start.2 = (bf16[1024,512]{1,0:T(8,128)(2,1)}, bf16[1024,512]{1,0:T(8,128)(2,1)}, u32[]{:S(2)}, u32[]{:S(2)}) collective-permute-start(bf16[1024,512]{1,0:T(8,128)(2,1)} %param.7), channel_id=1, source_target_pairs={{1,0},{2,1},{3,2},{4,3},{5,4},{6,5},{7,6},{8,7},{9,8},{10,9},{11,1... | collective-permute-start | bytes 3145736 | tf_op jit(solution)/shard_map/ppermute | solution.py:18
  49.8 69.8 %collective-permute-start.3 = (bf16[1024,512]{1,0:T(8,128)(2,1)}, bf16[1024,512]{1,0:T(8,128)(2,1)}, u32[]{:S(2)}, u32[]{:S(2)}) collective-permute-start(bf16[1024,512]{1,0:T(8,128)(2,1)} %param.7), channel_id=1, source_target_pairs={{2,0},{3,1},{4,2},{5,3},{6,4},{7,5},{8,6},{9,7},{10,8},{11,9},{12,... | collective-permute-start | bytes 3145736 | tf_op jit(solution)/shard_map/ppermute | solution.py:18
  67.9 53.1 %copy-start.3 = (bf16[512,1024]{0,1:T(8,128)(2,1)S(1)}, bf16[512,1024]{0,1:T(8,128)(2,1)}, u32[]{:S(2)}) copy-start(bf16[512,1024]{0,1:T(8,128)(2,1)} %copy.20) | copy-start | bytes 3145732
  67.9 60.9 %collective-permute-start.12 = (bf16[512,512]{1,0:T(8,128)(2,1)S(1)}, bf16[512,512]{1,0:T(8,128)(2,1)S(1)}, u32[]{:S(2)}, u32[]{:S(2)}) collective-permute-start(bf16[512,512]{1,0:T(8,128)(2,1)S(1)} %broadcast_select_fusion), channel_id=1, source_target_pairs={{0,16},{1,17},{2,18},{3,19},{4,20},{5,21},{6,22},{7,23},{8,24},{9,... | collective-permute-start | bytes 1572872 | tf_op jit(solution)/shard_map/ppermute | solution.py:25
  121.0 7.9 %copy-start.2 = (bf16[512,1024]{1,0:T(8,128)(2,1)S(1)}, bf16[512,1024]{1,0:T(8,128)(2,1)}, u32[]{:S(2)}) copy-start(bf16[512,1024]{1,0:T(8,128)(2,1)} %param.9) | copy-start | bytes 3145732

commit v6 on v5

--- a/solution.py
+++ b/solution.py
@@ -72,7 +72,7 @@
         top = jnp.max(scores, axis=1, keepdims=True)
         expo = jnp.exp(scores - top)
         total = jnp.sum(expo, axis=1, keepdims=True)
-        weights = (expo / total).astype(jnp.bfloat16)
+        weights = (expo * (1.0 / total)).astype(jnp.bfloat16)
         values = jnp.concatenate([kvt_ref[p, HEADS + h] for p in picks] + [bvt_ref[h]], axis=1)
         ctx = lax.dot_general(
             values, weights, (((1,), (1,)), ((), ())), preferred_element_type=jnp.float32
@@ -123,12 +123,17 @@
             pieces.append(tokens)
         else:
             pieces.append(from_behind(tokens, "curve", -offset))
-    nearby = jnp.concatenate(pieces, axis=0).reshape(5 * nblocks, BLOCK, width)
     kv_w = w_keyval.reshape(width, 2 * HEADS, head_dim).transpose(1, 2, 0)
-    kvt = jnp.einsum(
-        "hdc,btc->hbdt", kv_w, nearby, preferred_element_type=jnp.float32
-    ).astype(jnp.bfloat16)
-    kvt = kvt.transpose(1, 0, 2, 3)
+    kvt = jnp.zeros((5 * nblocks, 2 * HEADS, head_dim, BLOCK), jnp.bfloat16)
+    for index in (2, 0, 1, 3, 4):
+        piece = pieces[index]
+        part = jnp.einsum(
+            "hdc,btc->bhdt",
+            kv_w,
+            piece.reshape(nblocks, BLOCK, width),
+            preferred_element_type=jnp.float32,
+        ).astype(jnp.bfloat16)
+        kvt = kvt.at[index * nblocks : (index + 1) * nblocks].set(part)
     gathered = boundary_rows(tokens, bnd_ids, member)
     bnd_kv = jnp.dot(gathered, w_keyval, preferred_element_type=jnp.float32).astype(jnp.bfloat16)
     bkt, bvt = key_tiles(bnd_kv, width, head_dim)

time: 177 us -> 166 us (0.938)
  waiting for transfers between devices: 52.8 us -> 30.6 us
  matrix products: 13.5 us -> 24.9 us
  local copies, waits for them, and re-layouts: 22.6 us -> 24.6 us
    ppermute x4, waiting for transfers between devices: 42.7 us -> 25.2 us  [from_behind(): lax.ppermute(value, axis, [(source, source + steps) for source in range(f...]
    dot_general x1 -> x5, matrix products: 7.84 us -> 19.4 us  [on_device(): jnp.einsum('hdc,btc->bhdt', kv_w, piece.reshape(nblocks, BLOCK, width), p...]
    scatter x0 -> x1, local copies, waits for them, and re-layouts: none -> 8.32 us  [on_device(): kvt = kvt.at[index * nblocks:(index + 1) * nblocks].set(part)]
    unnamed x21 -> x19, local copies, waits for them, and re-layouts: 6.59 us -> 1.59 us
    ppermute x2, waiting for transfers between devices: 3.63 us -> 0.01 us  [share_rows(): other = lax.ppermute(rows, 'curve', pairs)]
    ppermute x2, starting transfers between devices: 5.12 us -> 3.09 us  [share_rows(): other = lax.ppermute(rows, 'curve', pairs)]
  transfers between devices with their start and end apart: 13 -> 13, of which waited for: 7 -> 3; matrix products, arithmetic and copies ran while one was open for 16% -> 25% of each run, Pallas kernels for 0% -> 0%
where the time goes in v6:
time: 166 us; the launch traced here: 165 us
  Pallas kernels  39.4 us (24%)
  starting transfers between devices  38.8 us (23%)
  waiting for transfers between devices  30.6 us (18%)
  matrix products  24.9 us (15%)
  local copies, waits for them, and re-layouts  24.6 us (15%)
  other arithmetic  4.86 us (3%)
  between operations  2.25 us (1%)
    pallas_call x1, Pallas kernels, attention(): pl.pallas_call(attention_kernel, grid_spec=grid_spec, out_shape=jax.Shape...  39.4 us
    ppermute x4, waiting for transfers between devices, from_behind(): lax.ppermute(value, axis, [(source, source + steps) for source in range(f...  25.2 us
    ppermute x7, starting transfers between devices, boundary_rows(): pieces.append(lax.ppermute(compact, 'curve', pairs))  19.8 us
    dot_general x5, matrix products, on_device(): jnp.einsum('hdc,btc->bhdt', kv_w, piece.reshape(nblocks, BLOCK, width), p...  19.4 us
    ppermute x4, starting transfers between devices, from_behind(): lax.ppermute(value, axis, [(source, source + steps) for source in range(f...  16 us
    scatter x1, local copies, waits for them, and re-layouts, on_device(): kvt = kvt.at[index * nblocks:(index + 1) * nblocks].set(part)  8.32 us
    ppermute x7, waiting for transfers between devices, boundary_rows(): pieces.append(lax.ppermute(compact, 'curve', pairs))  5.4 us
    reshape x2, local copies, waits for them, and re-layouts, on_device(): queries.reshape(nblocks, BLOCK, HEADS, head_dim).transpose(0, 2, 1, 3)  4.69 us
  transfers between devices with their start and end apart: 13, of which 3 were waited for; matrix products, arithmetic and copies ran while one was open for 25% of the time, Pallas kernels for 0%

profile of v6, /device:TPU:18, one launch (start us, length us, event | category | flops | bytes accessed | tf_op | source)
XLA Modules:
  0.0 165.5 jit_solution(579467642934099822)
XLA Ops:
  4.1 2.2 %gather_fusion = bf16[128,512]{1,0:T(8,128)(2,1)S(1)} fusion(bf16[1024,512]{1,0:T(8,128)(2,1)} %param.17, s32[1024]{0:T(1024)S(1)} %pad_clamp_fusion.1), kind=kCustom, calls=%fused_computation | custom fusion | bytes 262656 | tf_op jit(solution)/shard_map/jit(_take)/gather | solution.py:40
  6.5 2.0 %collective-permute-start.4 = (bf16[128,512]{1,0:T(8,128)(2,1)S(1)}, bf16[128,512]{1,0:T(8,128)(2,1)S(1)}, u32[]{:S(2)}, u32[]{:S(2)}) collective-permute-start(bf16[128,512]{1,0:T(8,128)(2,1)S(1)} %get-tuple-element.72), channel_id=1, source_target_pairs={{0,1},{1,2},{2,3},{3,4},{4,5},{5,6},{6,7},{7,0},{8,9},{9,10},{10,1... | collective-permute-start | bytes 393224 | tf_op jit(solution)/shard_map/ppermute | solution.py:47
  8.4 3.3 %collective-permute-start.5 = (bf16[128,512]{1,0:T(8,128)(2,1)S(1)}, bf16[128,512]{1,0:T(8,128)(2,1)S(1)}, u32[]{:S(2)}, u32[]{:S(2)}) collective-permute-start(bf16[128,512]{1,0:T(8,128)(2,1)S(1)} %get-tuple-element.72), channel_id=1, source_target_pairs={{0,2},{1,3},{2,4},{3,5},{4,6},{5,7},{6,0},{7,1},{8,10},{9,11},{10,... | collective-permute-start | bytes 393224 | tf_op jit(solution)/shard_map/ppermute | solution.py:47
  11.7 4.0 %collective-permute-start.6 = (bf16[128,512]{1,0:T(8,128)(2,1)S(1)}, bf16[128,512]{1,0:T(8,128)(2,1)S(1)}, u32[]{:S(2)}, u32[]{:S(2)}) collective-permute-start(bf16[128,512]{1,0:T(8,128)(2,1)S(1)} %get-tuple-element.72), channel_id=1, source_target_pairs={{0,3},{1,4},{2,5},{3,6},{4,7},{5,0},{6,1},{7,2},{8,11},{9,12},{10,... | collective-permute-start | bytes 393224 | tf_op jit(solution)/shard_map/ppermute | solution.py:47
  16.3 4.9 %collective-permute-start.8 = (bf16[128,512]{1,0:T(8,128)(2,1)S(1)}, bf16[128,512]{1,0:T(8,128)(2,1)S(1)}, u32[]{:S(2)}, u32[]{:S(2)}) collective-permute-start(bf16[128,512]{1,0:T(8,128)(2,1)S(1)} %get-tuple-element.72), channel_id=1, source_target_pairs={{0,5},{1,6},{2,7},{3,0},{4,1},{5,2},{6,3},{7,4},{8,13},{9,14},{10,... | collective-permute-start | bytes 393224 | tf_op jit(solution)/shard_map/ppermute | solution.py:47
  23.1 2.7 %collective-permute-start.9 = (bf16[128,512]{1,0:T(8,128)(2,1)S(1)}, bf16[128,512]{1,0:T(8,128)(2,1)S(1)}, u32[]{:S(2)}, u32[]{:S(2)}) collective-permute-start(bf16[128,512]{1,0:T(8,128)(2,1)S(1)} %get-tuple-element.72), channel_id=1, source_target_pairs={{0,6},{1,7},{2,0},{3,1},{4,2},{5,3},{6,4},{7,5},{8,14},{9,15},{10,... | collective-permute-start | bytes 393224 | tf_op jit(solution)/shard_map/ppermute | solution.py:47
  25.9 2.3 %collective-permute-start.10 = (bf16[128,512]{1,0:T(8,128)(2,1)S(1)}, bf16[128,512]{1,0:T(8,128)(2,1)S(1)}, u32[]{:S(2)}, u32[]{:S(2)}) collective-permute-start(bf16[128,512]{1,0:T(8,128)(2,1)S(1)} %get-tuple-element.72), channel_id=1, source_target_pairs={{0,7},{1,0},{2,1},{3,2},{4,3},{5,4},{6,5},{7,6},{8,15},{9,8},{10,9... | collective-permute-start | bytes 393224 | tf_op jit(solution)/shard_map/ppermute | solution.py:47
  28.1 5.4 %collective-permute-done.6 = bf16[128,512]{1,0:T(8,128)(2,1)S(1)} collective-permute-done((bf16[128,512]{1,0:T(8,128)(2,1)S(1)}, bf16[128,512]{1,0:T(8,128)(2,1)S(1)}, u32[]{:S(2)}, u32[]{:S(2)}) %collective-permute-start.6) | collective-permute-done | bytes 131104 | tf_op jit(solution)/shard_map/ppermute | solution.py:47
  33.5 1.9 %collective-permute-start = (bf16[1024,512]{1,0:T(8,128)(2,1)}, bf16[1024,512]{1,0:T(8,128)(2,1)}, u32[]{:S(2)}, u32[]{:S(2)}) collective-permute-start(bf16[1024,512]{1,0:T(8,128)(2,1)} %param.17), channel_id=1, source_target_pairs={{0,2},{1,3},{2,4},{3,5},{4,6},{5,7},{6,8},{7,9},{8,10},{9,11},{10,... | collective-permute-start | bytes 3145736 | tf_op jit(solution)/shard_map/ppermute | solution.py:18
  35.5 5.2 %collective-permute-start.1 = (bf16[1024,512]{1,0:T(8,128)(2,1)}, bf16[1024,512]{1,0:T(8,128)(2,1)}, u32[]{:S(2)}, u32[]{:S(2)}) collective-permute-start(bf16[1024,512]{1,0:T(8,128)(2,1)} %param.17), channel_id=1, source_target_pairs={{0,1},{1,2},{2,3},{3,4},{4,5},{5,6},{6,7},{7,8},{8,9},{9,10},{10,1... | collective-permute-start | bytes 3145736 | tf_op jit(solution)/shard_map/ppermute | solution.py:18
  40.7 5.5 %collective-permute-start.2 = (bf16[1024,512]{1,0:T(8,128)(2,1)}, bf16[1024,512]{1,0:T(8,128)(2,1)}, u32[]{:S(2)}, u32[]{:S(2)}) collective-permute-start(bf16[1024,512]{1,0:T(8,128)(2,1)} %param.17), channel_id=1, source_target_pairs={{1,0},{2,1},{3,2},{4,3},{5,4},{6,5},{7,6},{8,7},{9,8},{10,9},{11,1... | collective-permute-start | bytes 3145736 | tf_op jit(solution)/shard_map/ppermute | solution.py:18
  46.2 3.4 %collective-permute-start.3 = (bf16[1024,512]{1,0:T(8,128)(2,1)}, bf16[1024,512]{1,0:T(8,128)(2,1)}, u32[]{:S(2)}, u32[]{:S(2)}) collective-permute-start(bf16[1024,512]{1,0:T(8,128)(2,1)} %param.17), channel_id=1, source_target_pairs={{2,0},{3,1},{4,2},{5,3},{6,4},{7,5},{8,6},{9,7},{10,8},{11,9},{12,... | collective-permute-start | bytes 3145736 | tf_op jit(solution)/shard_map/ppermute | solution.py:18
  49.7 2.0 %gather_fusion.1 = bf16[512,512]{1,0:T(8,128)(2,1)S(1)} fusion(bf16[1024,512]{1,0:T(8,128)(2,1)S(1)} %constant_dynamic-update-slice_fusion, s32[1024]{0:T(1024)S(1)} %pad_clamp_fusion), kind=kCustom, calls=%fused_computation.1 | custom fusion | bytes 1050624 | tf_op jit(solution)/shard_map/jit(_take)/gather | solution.py:53
  53.9 3.9 %convert_bitcast_fusion = bf16[8,16,64,128]{3,2,1,0:T(8,128)(2,1)} fusion(bf16[8,128,512,1]{2,1,3,0:T(8,128)(2,1)} %bitcast.3, bf16[16,64,512,1]{2,1,0,3:T(8,128)(2,1)S(1)} %bitcast.76), kind=kOutput, calls=%fused_computation.8 | convolution fusion | flops 1074790400 | bytes 4194304 | tf_op jit(solution)/shard_map/hdc,btc->bhdt/dot_general | solution.py:130
  57.8 2.9 %convolution_convert_fusion.1 = bf16[1024,512]{1,0:T(8,128)(2,1)} fusion(bf16[1024,512]{1,0:T(8,128)(2,1)} %param.17, bf16[512,512]{1,0:T(8,128)(2,1)S(1)} %copy-done.5), kind=kOutput, calls=%fused_computation.10 | convolution fusion | flops 537395200 | bytes 2621440 | tf_op jit(solution)/shard_map/dot_general | solution.py:118
  61.4 2.8 %reshape.263 = bf16[8,128,8,64]{3,2,1,0:T(8,128)(2,1)S(1)} reshape(bf16[1024,512]{1,0:T(8,128)(2,1)} %convolution_convert_fusion.1) | data formatting | bytes 2097152 | tf_op jit(solution)/shard_map/reshape | solution.py:119
  66.1 8.3 %scatter.16 = bf16[40,16,64,128]{3,2,1,0:T(8,128)(2,1)} pad(bf16[8,16,64,128]{3,2,1,0:T(8,128)(2,1)} %convert_bitcast_fusion, bf16[]{:T(256)} %constant.248.clone.1), padding=16_16x0_0x0_0x0_0 | pad | bytes 12582914 | tf_op jit(solution)/shard_map/scatter | solution.py:136
  77.5 6.0 %collective-permute-done = bf16[1024,512]{1,0:T(8,128)(2,1)} collective-permute-done((bf16[1024,512]{1,0:T(8,128)(2,1)}, bf16[1024,512]{1,0:T(8,128)(2,1)}, u32[]{:S(2)}, u32[]{:S(2)}) %collective-permute-start) | collective-permute-done | bytes 1048608 | tf_op jit(solution)/shard_map/ppermute | solution.py:18
  83.5 3.8 %bitcast_dynamic-update-slice_fusion.3 = bf16[40,16,64,128]{3,2,1,0:T(8,128)(2,1)} fusion(bf16[40,16,64,128]{3,2,1,0:T(8,128)(2,1)} %scatter.16, bf16[8,128,512,1]{2,1,3,0:T(8,128)(2,1)} %bitcast.10, bf16[16,64,512,1]{2,1,0,3:T(8,128)(2,1)S(1)} %bitcast.77), kind=kOutput, calls=%fused_computation.6 | convolution fusion | flops 1074790400 | bytes 4194304 | tf_op jit(solution)/shard_map/hdc,btc->bhdt/dot_general | solution.py:130
  87.3 19.2 %collective-permute-done.1 = bf16[1024,512]{1,0:T(8,128)(2,1)} collective-permute-done((bf16[1024,512]{1,0:T(8,128)(2,1)}, bf16[1024,512]{1,0:T(8,128)(2,1)}, u32[]{:S(2)}, u32[]{:S(2)}) %collective-permute-start.1) | collective-permute-done | bytes 1048608 | tf_op jit(solution)/shard_map/ppermute | solution.py:18
  106.5 3.8 %bitcast_dynamic-update-slice_fusion.2 = bf16[40,16,64,128]{3,2,1,0:T(8,128)(2,1)} fusion(bf16[40,16,64,128]{3,2,1,0:T(8,128)(2,1)} %bitcast_dynamic-update-slice_fusion.3, bf16[8,128,512,1]{2,1,3,0:T(8,128)(2,1)} %bitcast.16, bf16[16,64,512,1]{2,1,0,3:T(8,128)(2,1)S(1)} %bitcast.78), kind=kOutput, calls=%fused_computation.5 | convolution fusion | flops 1074790400 | bytes 4194304 | tf_op jit(solution)/shard_map/hdc,btc->bhdt/dot_general | solution.py:130
  110.4 3.9 %bitcast_dynamic-update-slice_fusion.1 = bf16[40,16,64,128]{3,2,1,0:T(8,128)(2,1)} fusion(bf16[40,16,64,128]{3,2,1,0:T(8,128)(2,1)} %bitcast_dynamic-update-slice_fusion.2, bf16[8,128,512,1]{2,1,3,0:T(8,128)(2,1)} %bitcast.20, bf16[16,64,512,1]{2,1,0,3:T(8,128)(2,1)S(1)} %bitcast.79), kind=kOutput, calls=%fused_computation.4 | convolution fusion | flops 1074790400 | bytes 4194304 | tf_op jit(solution)/shard_map/hdc,btc->bhdt/dot_general | solution.py:130
  114.2 4.0 %bitcast_dynamic-update-slice_fusion.kvt_ref = bf16[40,16,64,128]{3,2,1,0:T(8,128)(2,1)} fusion(bf16[40,16,64,128]{3,2,1,0:T(8,128)(2,1)} %bitcast_dynamic-update-slice_fusion.1, bf16[8,128,512,1]{2,1,3,0:T(8,128)(2,1)} %bitcast.24, bf16[16,64,512,1]{2,1,0,3:T(8,128)(2,1)S(1)} %bitcast.80), kind=kOutput, calls=%fused_computation.3 | convolution fusion | flops 1074790400 | bytes 4194304 | tf_op jit(solution)/shard_map/hdc,btc->bhdt/dot_general | solution.py:130
  121.8 39.4 %shard_map.73 = bf16[8,8,64,128]{3,2,1,0:T(8,128)(2,1)} custom-call(s32[96]{0:T(128)} %reshape.225.rel_ref, s32[8]{0:T(128)} %cnt_ref.1, bf16[8,8,128,64]{3,2,1,0:T(8,128)(2,1)} %bitcast.72, bf16[40,16,64,128]{3,2,1,0:T(8,128)(2,1)} %bitcast_dynamic-update-slice_fusion.kvt_ref, bf16[8,64,512]{2,1,0:T(8,128)(2,1)} %reshape.234.bkt_ref, ...), custom_call_target="tpu_custom_call" | custom-call | tf_op jit(solution)/shard_map/pallas_call | solution.py:99
  (58 shorter events, 20.4 us)
Async XLA Ops:
  0.0 163.6 %copy-start = (bf16[512,512]{1,0:T(8,128)(2,1)S(1)}, bf16[512,512]{1,0:T(8,128)(2,1)}, u32[]{:S(2)}) copy-start(bf16[512,512]{1,0:T(8,128)(2,1)} %param.20) | copy-start | bytes 1572868
  6.5 16.6 %collective-permute-start.4 = (bf16[128,512]{1,0:T(8,128)(2,1)S(1)}, bf16[128,512]{1,0:T(8,128)(2,1)S(1)}, u32[]{:S(2)}, u32[]{:S(2)}) collective-permute-start(bf16[128,512]{1,0:T(8,128)(2,1)S(1)} %get-tuple-element.72), channel_id=1, source_target_pairs={{0,1},{1,2},{2,3},{3,4},{4,5},{5,6},{6,7},{7,0},{8,9},{9,10},{10,1... | collective-permute-start | bytes 393224 | tf_op jit(solution)/shard_map/ppermute | solution.py:47
  8.4 17.4 %collective-permute-start.5 = (bf16[128,512]{1,0:T(8,128)(2,1)S(1)}, bf16[128,512]{1,0:T(8,128)(2,1)S(1)}, u32[]{:S(2)}, u32[]{:S(2)}) collective-permute-start(bf16[128,512]{1,0:T(8,128)(2,1)S(1)} %get-tuple-element.72), channel_id=1, source_target_pairs={{0,2},{1,3},{2,4},{3,5},{4,6},{5,7},{6,0},{7,1},{8,10},{9,11},{10,... | collective-permute-start | bytes 393224 | tf_op jit(solution)/shard_map/ppermute | solution.py:47
  11.7 21.8 %collective-permute-start.6 = (bf16[128,512]{1,0:T(8,128)(2,1)S(1)}, bf16[128,512]{1,0:T(8,128)(2,1)S(1)}, u32[]{:S(2)}, u32[]{:S(2)}) collective-permute-start(bf16[128,512]{1,0:T(8,128)(2,1)S(1)} %get-tuple-element.72), channel_id=1, source_target_pairs={{0,3},{1,4},{2,5},{3,6},{4,7},{5,0},{6,1},{7,2},{8,11},{9,12},{10,... | collective-permute-start | bytes 393224 | tf_op jit(solution)/shard_map/ppermute | solution.py:47
  15.8 19.7 %collective-permute-start.7 = (bf16[128,512]{1,0:T(8,128)(2,1)S(1)}, bf16[128,512]{1,0:T(8,128)(2,1)S(1)}, u32[]{:S(2)}, u32[]{:S(2)}) collective-permute-start(bf16[128,512]{1,0:T(8,128)(2,1)S(1)} %get-tuple-element.72), channel_id=1, source_target_pairs={{0,4},{1,5},{2,6},{3,7},{4,0},{5,1},{6,2},{7,3},{8,12},{9,13},{10,... | collective-permute-start | bytes 393224 | tf_op jit(solution)/shard_map/ppermute | solution.py:47
  16.3 24.4 %collective-permute-start.8 = (bf16[128,512]{1,0:T(8,128)(2,1)S(1)}, bf16[128,512]{1,0:T(8,128)(2,1)S(1)}, u32[]{:S(2)}, u32[]{:S(2)}) collective-permute-start(bf16[128,512]{1,0:T(8,128)(2,1)S(1)} %get-tuple-element.72), channel_id=1, source_target_pairs={{0,5},{1,6},{2,7},{3,0},{4,1},{5,2},{6,3},{7,4},{8,13},{9,14},{10,... | collective-permute-start | bytes 393224 | tf_op jit(solution)/shard_map/ppermute | solution.py:47
  23.1 34.7 %copy-start.2 = (bf16[512,1024]{0,1:T(8,128)(2,1)}, bf16[512,1024]{0,1:T(8,128)(2,1)S(1)}, u32[]{:S(2)}) copy-start(bf16[512,1024]{0,1:T(8,128)(2,1)S(1)} %copy.20) | copy-start | bytes 3145732
  23.1 23.1 %collective-permute-start.9 = (bf16[128,512]{1,0:T(8,128)(2,1)S(1)}, bf16[128,512]{1,0:T(8,128)(2,1)S(1)}, u32[]{:S(2)}, u32[]{:S(2)}) collective-permute-start(bf16[128,512]{1,0:T(8,128)(2,1)S(1)} %get-tuple-element.72), channel_id=1, source_target_pairs={{0,6},{1,7},{2,0},{3,1},{4,2},{5,3},{6,4},{7,5},{8,14},{9,15},{10,... | collective-permute-start | bytes 393224 | tf_op jit(solution)/shard_map/ppermute | solution.py:47
  25.9 23.8 %collective-permute-start.10 = (bf16[128,512]{1,0:T(8,128)(2,1)S(1)}, bf16[128,512]{1,0:T(8,128)(2,1)S(1)}, u32[]{:S(2)}, u32[]{:S(2)}) collective-permute-start(bf16[128,512]{1,0:T(8,128)(2,1)S(1)} %get-tuple-element.72), channel_id=1, source_target_pairs={{0,7},{1,0},{2,1},{3,2},{4,3},{5,4},{6,5},{7,6},{8,15},{9,8},{10,9... | collective-permute-start | bytes 393224 | tf_op jit(solution)/shard_map/ppermute | solution.py:47
  33.5 50.0 %collective-permute-start = (bf16[1024,512]{1,0:T(8,128)(2,1)}, bf16[1024,512]{1,0:T(8,128)(2,1)}, u32[]{:S(2)}, u32[]{:S(2)}) collective-permute-start(bf16[1024,512]{1,0:T(8,128)(2,1)} %param.17), channel_id=1, source_target_pairs={{0,2},{1,3},{2,4},{3,5},{4,6},{5,7},{6,8},{7,9},{8,10},{9,11},{10,... | collective-permute-start | bytes 3145736 | tf_op jit(solution)/shard_map/ppermute | solution.py:18
  35.5 71.1 %collective-permute-start.1 = (bf16[1024,512]{1,0:T(8,128)(2,1)}, bf16[1024,512]{1,0:T(8,128)(2,1)}, u32[]{:S(2)}, u32[]{:S(2)}) collective-permute-start(bf16[1024,512]{1,0:T(8,128)(2,1)} %param.17), channel_id=1, source_target_pairs={{0,1},{1,2},{2,3},{3,4},{4,5},{5,6},{6,7},{7,8},{8,9},{9,10},{10,1... | collective-permute-start | bytes 3145736 | tf_op jit(solution)/shard_map/ppermute | solution.py:18
  40.7 69.7 %collective-permute-start.2 = (bf16[1024,512]{1,0:T(8,128)(2,1)}, bf16[1024,512]{1,0:T(8,128)(2,1)}, u32[]{:S(2)}, u32[]{:S(2)}) collective-permute-start(bf16[1024,512]{1,0:T(8,128)(2,1)} %param.17), channel_id=1, source_target_pairs={{1,0},{2,1},{3,2},{4,3},{5,4},{6,5},{7,6},{8,7},{9,8},{10,9},{11,1... | collective-permute-start | bytes 3145736 | tf_op jit(solution)/shard_map/ppermute | solution.py:18
  46.2 68.0 %collective-permute-start.3 = (bf16[1024,512]{1,0:T(8,128)(2,1)}, bf16[1024,512]{1,0:T(8,128)(2,1)}, u32[]{:S(2)}, u32[]{:S(2)}) collective-permute-start(bf16[1024,512]{1,0:T(8,128)(2,1)} %param.17), channel_id=1, source_target_pairs={{2,0},{3,1},{4,2},{5,3},{6,4},{7,5},{8,6},{9,7},{10,8},{11,9},{12,... | collective-permute-start | bytes 3145736 | tf_op jit(solution)/shard_map/ppermute | solution.py:18
  51.6 6.2 %copy-start.5 = (bf16[512,512]{1,0:T(8,128)(2,1)S(1)}, bf16[512,512]{1,0:T(8,128)(2,1)}, u32[]{:S(2)}) copy-start(bf16[512,512]{1,0:T(8,128)(2,1)} %param.18) | copy-start | bytes 1572868
  52.6 21.7 %collective-permute-start.11 = (bf16[512,512]{1,0:T(8,128)(2,1)}, bf16[512,512]{1,0:T(8,128)(2,1)}, u32[]{:S(2)}, u32[]{:S(2)}) collective-permute-start(bf16[512,512]{1,0:T(8,128)(2,1)} %select_select_fusion), channel_id=1, source_target_pairs={{0,8},{1,9},{2,10},{3,11},{4,12},{5,13},{6,14},{7,15},{8,0},{9,1},... | collective-permute-start | bytes 1572872 | tf_op jit(solution)/shard_map/ppermute | solution.py:25
  53.9 6.8 %copy-start.4 = (s32[8,12]{1,0:T(8,128)S(1)}, s32[8,12]{1,0:T(8,128)}, u32[]{:S(2)}) copy-start(s32[8,12]{1,0:T(8,128)} %param.21) | copy-start | bytes 1156
  66.1 17.4 %copy-start.3 = (bf16[512,1024]{0,1:T(8,128)(2,1)S(1)}, bf16[512,1024]{0,1:T(8,128)(2,1)}, u32[]{:S(2)}) copy-start(bf16[512,1024]{0,1:T(8,128)(2,1)} %copy-done.2) | copy-start | bytes 3145732
  75.7 42.5 %collective-permute-start.12 = (bf16[512,512]{1,0:T(8,128)(2,1)S(1)}, bf16[512,512]{1,0:T(8,128)(2,1)S(1)}, u32[]{:S(2)}, u32[]{:S(2)}) collective-permute-start(bf16[512,512]{1,0:T(8,128)(2,1)S(1)} %broadcast_select_fusion), channel_id=1, source_target_pairs={{0,16},{1,17},{2,18},{3,19},{4,20},{5,21},{6,22},{7,23},{8,24},{9,... | collective-permute-start | bytes 1572872 | tf_op jit(solution)/shard_map/ppermute | solution.py:25
  114.2 4.0 %copy-start.1 = (bf16[512,1024]{1,0:T(8,128)(2,1)S(1)}, bf16[512,1024]{1,0:T(8,128)(2,1)}, u32[]{:S(2)}) copy-start(bf16[512,1024]{1,0:T(8,128)(2,1)} %param.19) | copy-start | bytes 3145732

commit v7 on v6

--- a/solution.py
+++ b/solution.py
@@ -10,6 +10,8 @@
 NB = 12
 BCAP = 128
 ROW = 8
+CLASSES = (4, 8, NB)
+LOG2E = 1.4426950408889634
 
 
 def from_behind(value, axis, steps):
@@ -56,21 +58,19 @@
     return share_rows(rows, owner, member, group)
 
 
-def attention_kernel(rel_ref, cnt_ref, q_ref, kvt_ref, bkt_ref, bvt_ref, o_ref):
-    b = pl.program_id(0)
-    count = cnt_ref[b]
-    picks = [rel_ref[b * NB + i] for i in range(NB)]
-    width = NB * BLOCK + bkt_ref.shape[2]
+def attend_heads(picks, count, q_ref, kvt_ref, bkt_ref, bvt_ref, o_ref):
+    near = len(picks) * BLOCK
+    width = near + bkt_ref.shape[2]
     lane = lax.broadcasted_iota(jnp.int32, (1, width), 1)
-    live = (lane // BLOCK < count) | (lane >= NB * BLOCK)
-    scale = 1.0 / q_ref.shape[3] ** 0.5
+    live = (lane // BLOCK < count) | (lane >= near)
+    rate = LOG2E / q_ref.shape[3] ** 0.5
     for h in range(HEADS):
         query = q_ref[0, h]
         keys = jnp.concatenate([kvt_ref[p, h] for p in picks] + [bkt_ref[h]], axis=1)
-        scores = jnp.dot(query, keys, preferred_element_type=jnp.float32) * scale
+        scores = jnp.dot(query, keys, preferred_element_type=jnp.float32)
         scores = jnp.where(live, scores, -1e30)
         top = jnp.max(scores, axis=1, keepdims=True)
-        expo = jnp.exp(scores - top)
+        expo = jnp.exp2((scores - top) * rate)
         total = jnp.sum(expo, axis=1, keepdims=True)
         weights = (expo * (1.0 / total)).astype(jnp.bfloat16)
         values = jnp.concatenate([kvt_ref[p, HEADS + h] for p in picks] + [bvt_ref[h]], axis=1)
@@ -78,6 +78,20 @@
             values, weights, (((1,), (1,)), ((), ())), preferred_element_type=jnp.float32
         )
         o_ref[0, h] = ctx.astype(jnp.bfloat16)
+
+
+def attention_kernel(rel_ref, cnt_ref, q_ref, kvt_ref, bkt_ref, bvt_ref, o_ref):
+    b = pl.program_id(0)
+    count = cnt_ref[b]
+    picks = [rel_ref[b * NB + i] for i in range(NB)]
+    low = 0
+    for high in CLASSES:
+
+        @pl.when((count > low) & (count <= high))
+        def _():
+            attend_heads(picks[:high], count, q_ref, kvt_ref, bkt_ref, bvt_ref, o_ref)
+
+        low = high
 
 
 def attention(rel, counts, q, kvt, bkt, bvt):

time: 166 us -> 162 us (0.976)
  the two profiles are of different devices: /device:TPU:18 before, /device:TPU:228 now
where the time goes in v7:
time: 162 us; the launch traced here: 161 us
  starting transfers between devices  43.9 us (27%)
  Pallas kernels  37 us (23%)
  matrix products  24.9 us (15%)
  local copies, waits for them, and re-layouts  24.6 us (15%)
  waiting for transfers between devices  23.4 us (14%)
  other arithmetic  4.86 us (3%)
  between operations  2.25 us (1%)
    pallas_call x1, Pallas kernels, attention(): pl.pallas_call(attention_kernel, grid_spec=grid_spec, out_shape=jax.Shape...  37 us
    dot_general x5, matrix products, on_device(): jnp.einsum('hdc,btc->bhdt', kv_w, piece.reshape(nblocks, BLOCK, width), p...  19.4 us
    ppermute x2, waiting for transfers between devices, share_rows(): other = lax.ppermute(rows, 'curve', pairs)  19.3 us
    ppermute x4, starting transfers between devices, from_behind(): lax.ppermute(value, axis, [(source, source + steps) for source in range(f...  19.2 us
    ppermute x7, starting transfers between devices, boundary_rows(): pieces.append(lax.ppermute(compact, 'curve', pairs))  12.7 us
    ppermute x2, starting transfers between devices, share_rows(): other = lax.ppermute(rows, 'curve', pairs)  12 us
    scatter x1, local copies, waits for them, and re-layouts, on_device(): kvt = kvt.at[index * nblocks:(index + 1) * nblocks].set(part)  8.32 us
    reshape x2, local copies, waits for them, and re-layouts, on_device(): queries.reshape(nblocks, BLOCK, HEADS, head_dim).transpose(0, 2, 1, 3)  4.69 us
  transfers between devices with their start and end apart: 13, of which 3 were waited for; matrix products, arithmetic and copies ran while one was open for 26% of the time, Pallas kernels for 0%

profile of v7, /device:TPU:228, one launch (start us, length us, event | category | flops | bytes accessed | tf_op | source)
XLA Modules:
  0.0 160.9 jit_solution(4653859195141064070)
XLA Ops:
  4.1 2.2 %gather_fusion = bf16[128,512]{1,0:T(8,128)(2,1)S(1)} fusion(bf16[1024,512]{1,0:T(8,128)(2,1)} %param.17, s32[1024]{0:T(1024)S(1)} %pad_clamp_fusion.1), kind=kCustom, calls=%fused_computation | custom fusion | bytes 262656 | tf_op jit(solution)/shard_map/jit(_take)/gather | solution.py:42
  7.2 4.9 %collective-permute-start.6 = (bf16[128,512]{1,0:T(8,128)(2,1)S(1)}, bf16[128,512]{1,0:T(8,128)(2,1)S(1)}, u32[]{:S(2)}, u32[]{:S(2)}) collective-permute-start(bf16[128,512]{1,0:T(8,128)(2,1)S(1)} %get-tuple-element.72), channel_id=1, source_target_pairs={{0,3},{1,4},{2,5},{3,6},{4,7},{5,0},{6,1},{7,2},{8,11},{9,12},{10,... | collective-permute-start | bytes 393224 | tf_op jit(solution)/shard_map/ppermute | solution.py:49
  13.0 3.4 %collective-permute-start.8 = (bf16[128,512]{1,0:T(8,128)(2,1)S(1)}, bf16[128,512]{1,0:T(8,128)(2,1)S(1)}, u32[]{:S(2)}, u32[]{:S(2)}) collective-permute-start(bf16[128,512]{1,0:T(8,128)(2,1)S(1)} %get-tuple-element.72), channel_id=1, source_target_pairs={{0,5},{1,6},{2,7},{3,0},{4,1},{5,2},{6,3},{7,4},{8,13},{9,14},{10,... | collective-permute-start | bytes 393224 | tf_op jit(solution)/shard_map/ppermute | solution.py:49
  18.3 2.7 %collective-permute-start.9 = (bf16[128,512]{1,0:T(8,128)(2,1)S(1)}, bf16[128,512]{1,0:T(8,128)(2,1)S(1)}, u32[]{:S(2)}, u32[]{:S(2)}) collective-permute-start(bf16[128,512]{1,0:T(8,128)(2,1)S(1)} %get-tuple-element.72), channel_id=1, source_target_pairs={{0,6},{1,7},{2,0},{3,1},{4,2},{5,3},{6,4},{7,5},{8,14},{9,15},{10,... | collective-permute-start | bytes 393224 | tf_op jit(solution)/shard_map/ppermute | solution.py:49
  22.3 2.8 %collective-permute-done.6 = bf16[128,512]{1,0:T(8,128)(2,1)S(1)} collective-permute-done((bf16[128,512]{1,0:T(8,128)(2,1)S(1)}, bf16[128,512]{1,0:T(8,128)(2,1)S(1)}, u32[]{:S(2)}, u32[]{:S(2)}) %collective-permute-start.6) | collective-permute-done | bytes 131104 | tf_op jit(solution)/shard_map/ppermute | solution.py:49
  25.1 11.4 %collective-permute-start = (bf16[1024,512]{1,0:T(8,128)(2,1)}, bf16[1024,512]{1,0:T(8,128)(2,1)}, u32[]{:S(2)}, u32[]{:S(2)}) collective-permute-start(bf16[1024,512]{1,0:T(8,128)(2,1)} %param.17), channel_id=1, source_target_pairs={{0,2},{1,3},{2,4},{3,5},{4,6},{5,7},{6,8},{7,9},{8,10},{9,11},{10,... | collective-permute-start | bytes 3145736 | tf_op jit(solution)/shard_map/ppermute | solution.py:20
  36.6 1.9 %collective-permute-start.1 = (bf16[1024,512]{1,0:T(8,128)(2,1)}, bf16[1024,512]{1,0:T(8,128)(2,1)}, u32[]{:S(2)}, u32[]{:S(2)}) collective-permute-start(bf16[1024,512]{1,0:T(8,128)(2,1)} %param.17), channel_id=1, source_target_pairs={{0,1},{1,2},{2,3},{3,4},{4,5},{5,6},{6,7},{7,8},{8,9},{9,10},{10,1... | collective-permute-start | bytes 3145736 | tf_op jit(solution)/shard_map/ppermute | solution.py:20
  38.5 3.9 %collective-permute-start.2 = (bf16[1024,512]{1,0:T(8,128)(2,1)}, bf16[1024,512]{1,0:T(8,128)(2,1)}, u32[]{:S(2)}, u32[]{:S(2)}) collective-permute-start(bf16[1024,512]{1,0:T(8,128)(2,1)} %param.17), channel_id=1, source_target_pairs={{1,0},{2,1},{3,2},{4,3},{5,4},{6,5},{7,6},{8,7},{9,8},{10,9},{11,1... | collective-permute-start | bytes 3145736 | tf_op jit(solution)/shard_map/ppermute | solution.py:20
  42.5 1.9 %collective-permute-start.3 = (bf16[1024,512]{1,0:T(8,128)(2,1)}, bf16[1024,512]{1,0:T(8,128)(2,1)}, u32[]{:S(2)}, u32[]{:S(2)}) collective-permute-start(bf16[1024,512]{1,0:T(8,128)(2,1)} %param.17), channel_id=1, source_target_pairs={{2,0},{3,1},{4,2},{5,3},{6,4},{7,5},{8,6},{9,7},{10,8},{11,9},{12,... | collective-permute-start | bytes 3145736 | tf_op jit(solution)/shard_map/ppermute | solution.py:20
  44.5 2.0 %gather_fusion.1 = bf16[512,512]{1,0:T(8,128)(2,1)S(1)} fusion(bf16[1024,512]{1,0:T(8,128)(2,1)S(1)} %constant_dynamic-update-slice_fusion, s32[1024]{0:T(1024)S(1)} %pad_clamp_fusion), kind=kCustom, calls=%fused_computation.1 | custom fusion | bytes 1050624 | tf_op jit(solution)/shard_map/jit(_take)/gather | solution.py:55
  49.0 3.9 %convert_bitcast_fusion = bf16[8,16,64,128]{3,2,1,0:T(8,128)(2,1)} fusion(bf16[8,128,512,1]{2,1,3,0:T(8,128)(2,1)} %bitcast.3, bf16[16,64,512,1]{2,1,0,3:T(8,128)(2,1)S(1)} %bitcast.76), kind=kOutput, calls=%fused_computation.8 | convolution fusion | flops 1074790400 | bytes 4194304 | tf_op jit(solution)/shard_map/hdc,btc->bhdt/dot_general | solution.py:144
  52.9 2.9 %convolution_convert_fusion.1 = bf16[1024,512]{1,0:T(8,128)(2,1)} fusion(bf16[1024,512]{1,0:T(8,128)(2,1)} %param.17, bf16[512,512]{1,0:T(8,128)(2,1)S(1)} %copy-done.5), kind=kOutput, calls=%fused_computation.10 | convolution fusion | flops 537395200 | bytes 2621440 | tf_op jit(solution)/shard_map/dot_general | solution.py:132
  56.5 2.8 %reshape.263 = bf16[8,128,8,64]{3,2,1,0:T(8,128)(2,1)S(1)} reshape(bf16[1024,512]{1,0:T(8,128)(2,1)} %convolution_convert_fusion.1) | data formatting | bytes 2097152 | tf_op jit(solution)/shard_map/reshape | solution.py:133
  59.3 1.9 %copy.35 = bf16[8,128,8,64]{3,1,2,0:T(8,128)(2,1)} copy(bf16[8,128,8,64]{3,2,1,0:T(8,128)(2,1)S(1)} %reshape.263) | data formatting | bytes 2097152 | tf_op jit(solution)/shard_map/reshape | solution.py:133
  61.2 8.3 %scatter.16 = bf16[40,16,64,128]{3,2,1,0:T(8,128)(2,1)} pad(bf16[8,16,64,128]{3,2,1,0:T(8,128)(2,1)} %convert_bitcast_fusion, bf16[]{:T(256)} %constant.248.clone.1), padding=16_16x0_0x0_0x0_0 | pad | bytes 12582914 | tf_op jit(solution)/shard_map/scatter | solution.py:150
  69.5 19.3 %collective-permute-done.11 = bf16[512,512]{1,0:T(8,128)(2,1)} collective-permute-done((bf16[512,512]{1,0:T(8,128)(2,1)}, bf16[512,512]{1,0:T(8,128)(2,1)}, u32[]{:S(2)}, u32[]{:S(2)}) %collective-permute-start.11) | collective-permute-done | bytes 524320 | tf_op jit(solution)/shard_map/ppermute | solution.py:27
  90.1 10.4 %collective-permute-start.12 = (bf16[512,512]{1,0:T(8,128)(2,1)S(1)}, bf16[512,512]{1,0:T(8,128)(2,1)S(1)}, u32[]{:S(2)}, u32[]{:S(2)}) collective-permute-start(bf16[512,512]{1,0:T(8,128)(2,1)S(1)} %broadcast_select_fusion), channel_id=1, source_target_pairs={{0,16},{1,17},{2,18},{3,19},{4,20},{5,21},{6,22},{7,23},{8,24},{9,... | collective-permute-start | bytes 1572872 | tf_op jit(solution)/shard_map/ppermute | solution.py:27
  100.5 3.8 %bitcast_dynamic-update-slice_fusion.3 = bf16[40,16,64,128]{3,2,1,0:T(8,128)(2,1)} fusion(bf16[40,16,64,128]{3,2,1,0:T(8,128)(2,1)} %scatter.16, bf16[8,128,512,1]{2,1,3,0:T(8,128)(2,1)} %bitcast.10, bf16[16,64,512,1]{2,1,0,3:T(8,128)(2,1)S(1)} %bitcast.77), kind=kOutput, calls=%fused_computation.6 | convolution fusion | flops 1074790400 | bytes 4194304 | tf_op jit(solution)/shard_map/hdc,btc->bhdt/dot_general | solution.py:144
  104.4 3.8 %bitcast_dynamic-update-slice_fusion.2 = bf16[40,16,64,128]{3,2,1,0:T(8,128)(2,1)} fusion(bf16[40,16,64,128]{3,2,1,0:T(8,128)(2,1)} %bitcast_dynamic-update-slice_fusion.3, bf16[8,128,512,1]{2,1,3,0:T(8,128)(2,1)} %bitcast.16, bf16[16,64,512,1]{2,1,0,3:T(8,128)(2,1)S(1)} %bitcast.78), kind=kOutput, calls=%fused_computation.5 | convolution fusion | flops 1074790400 | bytes 4194304 | tf_op jit(solution)/shard_map/hdc,btc->bhdt/dot_general | solution.py:144
  108.2 3.9 %bitcast_dynamic-update-slice_fusion.1 = bf16[40,16,64,128]{3,2,1,0:T(8,128)(2,1)} fusion(bf16[40,16,64,128]{3,2,1,0:T(8,128)(2,1)} %bitcast_dynamic-update-slice_fusion.2, bf16[8,128,512,1]{2,1,3,0:T(8,128)(2,1)} %bitcast.20, bf16[16,64,512,1]{2,1,0,3:T(8,128)(2,1)S(1)} %bitcast.79), kind=kOutput, calls=%fused_computation.4 | convolution fusion | flops 1074790400 | bytes 4194304 | tf_op jit(solution)/shard_map/hdc,btc->bhdt/dot_general | solution.py:144
  112.1 4.0 %bitcast_dynamic-update-slice_fusion.kvt_ref = bf16[40,16,64,128]{3,2,1,0:T(8,128)(2,1)} fusion(bf16[40,16,64,128]{3,2,1,0:T(8,128)(2,1)} %bitcast_dynamic-update-slice_fusion.1, bf16[8,128,512,1]{2,1,3,0:T(8,128)(2,1)} %bitcast.24, bf16[16,64,512,1]{2,1,0,3:T(8,128)(2,1)S(1)} %bitcast.80), kind=kOutput, calls=%fused_computation.3 | convolution fusion | flops 1074790400 | bytes 4194304 | tf_op jit(solution)/shard_map/hdc,btc->bhdt/dot_general | solution.py:144
  119.7 37.0 %shard_map.73 = bf16[8,8,64,128]{3,2,1,0:T(8,128)(2,1)} custom-call(s32[96]{0:T(128)} %reshape.225.rel_ref, s32[8]{0:T(128)} %cnt_ref.1, bf16[8,8,128,64]{3,2,1,0:T(8,128)(2,1)} %bitcast.72, bf16[40,16,64,128]{3,2,1,0:T(8,128)(2,1)} %bitcast_dynamic-update-slice_fusion.kvt_ref, bf16[8,64,512]{2,1,0:T(8,128)(2,1)} %reshape.234.bkt_ref, ...), custom_call_target="tpu_custom_call" | custom-call | tf_op jit(solution)/shard_map/pallas_call | solution.py:113
  156.7 1.9 %copy.23 = bf16[8,128,64,8]{1,0,3,2:T(8,128)(2,1)S(1)} copy(bf16[8,128,64,8]{1,2,3,0:T(8,128)(2,1)} %bitcast.73) | data formatting | bytes 2097152 | tf_op jit(solution)/shard_map/bhdt,hde->bte/dot_general | solution.py:160
  159.1 1.8 %bitcast_convert_fusion = bf16[1024,512]{1,0:T(8,128)(2,1)} fusion(bf16[1024,64,8]{0,2,1:T(8,128)(2,1)S(1)} %dot_general.36, bf16[8,64,512]{2,1,0:T(8,128)(2,1)S(1)} %bitcast.71), kind=kOutput, calls=%fused_computation.2 | convolution fusion | flops 537395200 | bytes 2621440 | tf_op jit(solution)/shard_map/bhdt,hde->bte/dot_general | solution.py:160
  (58 shorter events, 15.6 us)
Async XLA Ops:
  0.0 159.1 %copy-start = (bf16[512,512]{1,0:T(8,128)(2,1)S(1)}, bf16[512,512]{1,0:T(8,128)(2,1)}, u32[]{:S(2)}) copy-start(bf16[512,512]{1,0:T(8,128)(2,1)} %param.20) | copy-start | bytes 1572868
  6.5 11.8 %collective-permute-start.4 = (bf16[128,512]{1,0:T(8,128)(2,1)S(1)}, bf16[128,512]{1,0:T(8,128)(2,1)S(1)}, u32[]{:S(2)}, u32[]{:S(2)}) collective-permute-start(bf16[128,512]{1,0:T(8,128)(2,1)S(1)} %get-tuple-element.72), channel_id=1, source_target_pairs={{0,1},{1,2},{2,3},{3,4},{4,5},{5,6},{6,7},{7,0},{8,9},{9,10},{10,1... | collective-permute-start | bytes 393224 | tf_op jit(solution)/shard_map/ppermute | solution.py:49
  6.5 15.7 %collective-permute-start.5 = (bf16[128,512]{1,0:T(8,128)(2,1)S(1)}, bf16[128,512]{1,0:T(8,128)(2,1)S(1)}, u32[]{:S(2)}, u32[]{:S(2)}) collective-permute-start(bf16[128,512]{1,0:T(8,128)(2,1)S(1)} %get-tuple-element.72), channel_id=1, source_target_pairs={{0,2},{1,3},{2,4},{3,5},{4,6},{5,7},{6,0},{7,1},{8,10},{9,11},{10,... | collective-permute-start | bytes 393224 | tf_op jit(solution)/shard_map/ppermute | solution.py:49
  7.2 17.9 %collective-permute-start.6 = (bf16[128,512]{1,0:T(8,128)(2,1)S(1)}, bf16[128,512]{1,0:T(8,128)(2,1)S(1)}, u32[]{:S(2)}, u32[]{:S(2)}) collective-permute-start(bf16[128,512]{1,0:T(8,128)(2,1)S(1)} %get-tuple-element.72), channel_id=1, source_target_pairs={{0,3},{1,4},{2,5},{3,6},{4,7},{5,0},{6,1},{7,2},{8,11},{9,12},{10,... | collective-permute-start | bytes 393224 | tf_op jit(solution)/shard_map/ppermute | solution.py:49
  12.1 24.4 %collective-permute-start.7 = (bf16[128,512]{1,0:T(8,128)(2,1)S(1)}, bf16[128,512]{1,0:T(8,128)(2,1)S(1)}, u32[]{:S(2)}, u32[]{:S(2)}) collective-permute-start(bf16[128,512]{1,0:T(8,128)(2,1)S(1)} %get-tuple-element.72), channel_id=1, source_target_pairs={{0,4},{1,5},{2,6},{3,7},{4,0},{5,1},{6,2},{7,3},{8,12},{9,13},{10,... | collective-permute-start | bytes 393224 | tf_op jit(solution)/shard_map/ppermute | solution.py:49
  13.0 25.5 %collective-permute-start.8 = (bf16[128,512]{1,0:T(8,128)(2,1)S(1)}, bf16[128,512]{1,0:T(8,128)(2,1)S(1)}, u32[]{:S(2)}, u32[]{:S(2)}) collective-permute-start(bf16[128,512]{1,0:T(8,128)(2,1)S(1)} %get-tuple-element.72), channel_id=1, source_target_pairs={{0,5},{1,6},{2,7},{3,0},{4,1},{5,2},{6,3},{7,4},{8,13},{9,14},{10,... | collective-permute-start | bytes 393224 | tf_op jit(solution)/shard_map/ppermute | solution.py:49
  18.2 34.7 %copy-start.2 = (bf16[512,1024]{0,1:T(8,128)(2,1)}, bf16[512,1024]{0,1:T(8,128)(2,1)S(1)}, u32[]{:S(2)}) copy-start(bf16[512,1024]{0,1:T(8,128)(2,1)S(1)} %copy.20) | copy-start | bytes 3145732
  18.3 24.2 %collective-permute-start.9 = (bf16[128,512]{1,0:T(8,128)(2,1)S(1)}, bf16[128,512]{1,0:T(8,128)(2,1)S(1)}, u32[]{:S(2)}, u32[]{:S(2)}) collective-permute-start(bf16[128,512]{1,0:T(8,128)(2,1)S(1)} %get-tuple-element.72), channel_id=1, source_target_pairs={{0,6},{1,7},{2,0},{3,1},{4,2},{5,3},{6,4},{7,5},{8,14},{9,15},{10,... | collective-permute-start | bytes 393224 | tf_op jit(solution)/shard_map/ppermute | solution.py:49
  22.3 22.2 %collective-permute-start.10 = (bf16[128,512]{1,0:T(8,128)(2,1)S(1)}, bf16[128,512]{1,0:T(8,128)(2,1)S(1)}, u32[]{:S(2)}, u32[]{:S(2)}) collective-permute-start(bf16[128,512]{1,0:T(8,128)(2,1)S(1)} %get-tuple-element.72), channel_id=1, source_target_pairs={{0,7},{1,0},{2,1},{3,2},{4,3},{5,4},{6,5},{7,6},{8,15},{9,8},{10,9... | collective-permute-start | bytes 393224 | tf_op jit(solution)/shard_map/ppermute | solution.py:49
  25.1 75.4 %collective-permute-start = (bf16[1024,512]{1,0:T(8,128)(2,1)}, bf16[1024,512]{1,0:T(8,128)(2,1)}, u32[]{:S(2)}, u32[]{:S(2)}) collective-permute-start(bf16[1024,512]{1,0:T(8,128)(2,1)} %param.17), channel_id=1, source_target_pairs={{0,2},{1,3},{2,4},{3,5},{4,6},{5,7},{6,8},{7,9},{8,10},{9,11},{10,... | collective-permute-start | bytes 3145736 | tf_op jit(solution)/shard_map/ppermute | solution.py:20
  36.6 67.8 %collective-permute-start.1 = (bf16[1024,512]{1,0:T(8,128)(2,1)}, bf16[1024,512]{1,0:T(8,128)(2,1)}, u32[]{:S(2)}, u32[]{:S(2)}) collective-permute-start(bf16[1024,512]{1,0:T(8,128)(2,1)} %param.17), channel_id=1, source_target_pairs={{0,1},{1,2},{2,3},{3,4},{4,5},{5,6},{6,7},{7,8},{8,9},{9,10},{10,1... | collective-permute-start | bytes 3145736 | tf_op jit(solution)/shard_map/ppermute | solution.py:20
  38.5 69.7 %collective-permute-start.2 = (bf16[1024,512]{1,0:T(8,128)(2,1)}, bf16[1024,512]{1,0:T(8,128)(2,1)}, u32[]{:S(2)}, u32[]{:S(2)}) collective-permute-start(bf16[1024,512]{1,0:T(8,128)(2,1)} %param.17), channel_id=1, source_target_pairs={{1,0},{2,1},{3,2},{4,3},{5,4},{6,5},{7,6},{8,7},{9,8},{10,9},{11,1... | collective-permute-start | bytes 3145736 | tf_op jit(solution)/shard_map/ppermute | solution.py:20
  42.5 69.6 %collective-permute-start.3 = (bf16[1024,512]{1,0:T(8,128)(2,1)}, bf16[1024,512]{1,0:T(8,128)(2,1)}, u32[]{:S(2)}, u32[]{:S(2)}) collective-permute-start(bf16[1024,512]{1,0:T(8,128)(2,1)} %param.17), channel_id=1, source_target_pairs={{2,0},{3,1},{4,2},{5,3},{6,4},{7,5},{8,6},{9,7},{10,8},{11,9},{12,... | collective-permute-start | bytes 3145736 | tf_op jit(solution)/shard_map/ppermute | solution.py:20
  46.5 6.5 %copy-start.5 = (bf16[512,512]{1,0:T(8,128)(2,1)S(1)}, bf16[512,512]{1,0:T(8,128)(2,1)}, u32[]{:S(2)}) copy-start(bf16[512,512]{1,0:T(8,128)(2,1)} %param.18) | copy-start | bytes 1572868
  47.5 41.3 %collective-permute-start.11 = (bf16[512,512]{1,0:T(8,128)(2,1)}, bf16[512,512]{1,0:T(8,128)(2,1)}, u32[]{:S(2)}, u32[]{:S(2)}) collective-permute-start(bf16[512,512]{1,0:T(8,128)(2,1)} %select_select_fusion), channel_id=1, source_target_pairs={{0,8},{1,9},{2,10},{3,11},{4,12},{5,13},{6,14},{7,15},{8,0},{9,1},... | collective-permute-start | bytes 1572872 | tf_op jit(solution)/shard_map/ppermute | solution.py:27
  49.0 6.8 %copy-start.4 = (s32[8,12]{1,0:T(8,128)S(1)}, s32[8,12]{1,0:T(8,128)}, u32[]{:S(2)}) copy-start(s32[8,12]{1,0:T(8,128)} %param.21) | copy-start | bytes 1156
  61.2 39.4 %copy-start.3 = (bf16[512,1024]{0,1:T(8,128)(2,1)S(1)}, bf16[512,1024]{0,1:T(8,128)(2,1)}, u32[]{:S(2)}) copy-start(bf16[512,1024]{0,1:T(8,128)(2,1)} %copy-done.2) | copy-start | bytes 3145732
  90.1 26.0 %collective-permute-start.12 = (bf16[512,512]{1,0:T(8,128)(2,1)S(1)}, bf16[512,512]{1,0:T(8,128)(2,1)S(1)}, u32[]{:S(2)}, u32[]{:S(2)}) collective-permute-start(bf16[512,512]{1,0:T(8,128)(2,1)S(1)} %broadcast_select_fusion), channel_id=1, source_target_pairs={{0,16},{1,17},{2,18},{3,19},{4,20},{5,21},{6,22},{7,23},{8,24},{9,... | collective-permute-start | bytes 1572872 | tf_op jit(solution)/shard_map/ppermute | solution.py:27
  112.1 4.0 %copy-start.1 = (bf16[512,1024]{1,0:T(8,128)(2,1)S(1)}, bf16[512,1024]{1,0:T(8,128)(2,1)}, u32[]{:S(2)}) copy-start(bf16[512,1024]{1,0:T(8,128)(2,1)} %param.19) | copy-start | bytes 3145732

commit v8 on v7

--- a/solution.py
+++ b/solution.py
@@ -58,12 +58,13 @@
     return share_rows(rows, owner, member, group)
 
 
-def attend_heads(picks, count, q_ref, kvt_ref, bkt_ref, bvt_ref, o_ref):
+def attend_heads(picks, count, q_ref, kvt_ref, bkt_ref, bvt_ref, w_ref, o_ref):
     near = len(picks) * BLOCK
     width = near + bkt_ref.shape[2]
     lane = lax.broadcasted_iota(jnp.int32, (1, width), 1)
     live = (lane // BLOCK < count) | (lane >= near)
     rate = LOG2E / q_ref.shape[3] ** 0.5
+    contexts = []
     for h in range(HEADS):
         query = q_ref[0, h]
         keys = jnp.concatenate([kvt_ref[p, h] for p in picks] + [bkt_ref[h]], axis=1)
@@ -77,10 +78,15 @@
         ctx = lax.dot_general(
             values, weights, (((1,), (1,)), ((), ())), preferred_element_type=jnp.float32
         )
-        o_ref[0, h] = ctx.astype(jnp.bfloat16)
+        contexts.append(ctx.astype(jnp.bfloat16))
+    context = jnp.concatenate(contexts, axis=0)
+    mixed = lax.dot_general(
+        context, w_ref[...], (((0,), (0,)), ((), ())), preferred_element_type=jnp.float32
+    )
+    o_ref[0] = mixed.astype(jnp.bfloat16)
 
 
-def attention_kernel(rel_ref, cnt_ref, q_ref, kvt_ref, bkt_ref, bvt_ref, o_ref):
+def attention_kernel(rel_ref, cnt_ref, q_ref, kvt_ref, bkt_ref, bvt_ref, w_ref, o_ref):
     b = pl.program_id(0)
     count = cnt_ref[b]
     picks = [rel_ref[b * NB + i] for i in range(NB)]
@@ -89,16 +95,17 @@
 
         @pl.when((count > low) & (count <= high))
         def _():
-            attend_heads(picks[:high], count, q_ref, kvt_ref, bkt_ref, bvt_ref, o_ref)
+            attend_heads(picks[:high], count, q_ref, kvt_ref, bkt_ref, bvt_ref, w_ref, o_ref)
 
         low = high
 
 
-def attention(rel, counts, q, kvt, bkt, bvt):
+def attention(rel, counts, q, kvt, bkt, bvt, w_out):
     nq = q.shape[0]
     nkb = kvt.shape[0]
     head_dim = q.shape[3]
     nbound = bkt.shape[2]
+    width = w_out.shape[0]
     grid_spec = pltpu.PrefetchScalarGridSpec(
         num_scalar_prefetch=2,
         grid=(nq,),
@@ -107,14 +114,15 @@
             pl.BlockSpec((nkb, 2 * HEADS, head_dim, BLOCK), lambda b, r, c: (0, 0, 0, 0)),
             pl.BlockSpec((HEADS, head_dim, nbound), lambda b, r, c: (0, 0, 0)),
             pl.BlockSpec((HEADS, head_dim, nbound), lambda b, r, c: (0, 0, 0)),
+            pl.BlockSpec((width, width), lambda b, r, c: (0, 0)),
         ],
-        out_specs=pl.BlockSpec((1, HEADS, head_dim, BLOCK), lambda b, r, c: (b, 0, 0, 0)),
+        out_specs=pl.BlockSpec((1, BLOCK, width), lambda b, r, c: (b, 0, 0)),
     )
     return pl.pallas_call(
         attention_kernel,
         grid_spec=grid_spec,
-        out_shape=jax.ShapeDtypeStruct((nq, HEADS, head_dim, BLOCK), jnp.bfloat16),
-    )(rel, counts, q, kvt, bkt, bvt)
+        out_shape=jax.ShapeDtypeStruct((nq, BLOCK, width), jnp.bfloat16),
+    )(rel, counts, q, kvt, bkt, bvt, w_out)
 
 
 def key_tiles(keyvals, width, head_dim):
@@ -155,10 +163,8 @@
     bvt = bvt.transpose(1, 2, 0, 3).reshape(HEADS, head_dim, -1)
     first_block = (member - 2) * nblocks
     rel = jnp.clip(block_list - first_block, 0, 5 * nblocks - 1).reshape(-1).astype(jnp.int32)
-    context = attention(rel, block_count.astype(jnp.int32), queries, kvt, bkt, bvt)
-    out_w = w_out.reshape(HEADS, head_dim, width)
-    mixed = jnp.einsum("bhdt,hde->bte", context, out_w, preferred_element_type=jnp.float32)
-    return mixed.reshape(tok_dev, width).astype(jnp.bfloat16)
+    mixed = attention(rel, block_count.astype(jnp.int32), queries, kvt, bkt, bvt, w_out)
+    return mixed.reshape(tok_dev, width)
 
 
 def solution(mesh):

time: 162 us -> 160 us (0.988)
  the two profiles are of different devices: /device:TPU:228 before, /device:TPU:18 now
where the time goes in v8:
time: 160 us; the launch traced here: 159 us
  starting transfers between devices  38.9 us (24%)
  Pallas kernels  37.7 us (24%)
  waiting for transfers between devices  30.6 us (19%)
  matrix products  23.1 us (14%)
  local copies, waits for them, and re-layouts  22.2 us (14%)
  other arithmetic  4.86 us (3%)
  between operations  2.22 us (1%)
    pallas_call x1, Pallas kernels, attention(): pl.pallas_call(attention_kernel, grid_spec=grid_spec, out_shape=jax.Shape...  37.7 us
    ppermute x4, waiting for transfers between devices, from_behind(): lax.ppermute(value, axis, [(source, source + steps) for source in range(f...  25.2 us
    ppermute x7, starting transfers between devices, boundary_rows(): pieces.append(lax.ppermute(compact, 'curve', pairs))  19.8 us
    dot_general x5, matrix products, on_device(): jnp.einsum('hdc,btc->bhdt', kv_w, piece.reshape(nblocks, BLOCK, width), p...  19.4 us
    ppermute x4, starting transfers between devices, from_behind(): lax.ppermute(value, axis, [(source, source + steps) for source in range(f...  16 us
    scatter x1, local copies, waits for them, and re-layouts, on_device(): kvt = kvt.at[index * nblocks:(index + 1) * nblocks].set(part)  8.31 us
    ppermute x7, waiting for transfers between devices, boundary_rows(): pieces.append(lax.ppermute(compact, 'curve', pairs))  5.4 us
    reshape x2, local copies, waits for them, and re-layouts, on_device(): queries.reshape(nblocks, BLOCK, HEADS, head_dim).transpose(0, 2, 1, 3)  4.7 us
  transfers between devices with their start and end apart: 13, of which 3 were waited for; matrix products, arithmetic and copies ran while one was open for 26% of the time, Pallas kernels for 0%

profile of v8, /device:TPU:18, one launch (start us, length us, event | category | flops | bytes accessed | tf_op | source)
XLA Modules:
  0.0 159.5 jit_solution(14555037054419766637)
XLA Ops:
  4.1 2.2 %gather_fusion = bf16[128,512]{1,0:T(8,128)(2,1)S(1)} fusion(bf16[1024,512]{1,0:T(8,128)(2,1)} %param.17, s32[1024]{0:T(1024)S(1)} %pad_clamp_fusion.1), kind=kCustom, calls=%fused_computation | custom fusion | bytes 262656 | tf_op jit(solution)/shard_map/jit(_take)/gather | solution.py:42
  6.5 2.0 %collective-permute-start.4 = (bf16[128,512]{1,0:T(8,128)(2,1)S(1)}, bf16[128,512]{1,0:T(8,128)(2,1)S(1)}, u32[]{:S(2)}, u32[]{:S(2)}) collective-permute-start(bf16[128,512]{1,0:T(8,128)(2,1)S(1)} %get-tuple-element.72), channel_id=1, source_target_pairs={{0,1},{1,2},{2,3},{3,4},{4,5},{5,6},{6,7},{7,0},{8,9},{9,10},{10,1... | collective-permute-start | bytes 393224 | tf_op jit(solution)/shard_map/ppermute | solution.py:49
  8.4 3.3 %collective-permute-start.5 = (bf16[128,512]{1,0:T(8,128)(2,1)S(1)}, bf16[128,512]{1,0:T(8,128)(2,1)S(1)}, u32[]{:S(2)}, u32[]{:S(2)}) collective-permute-start(bf16[128,512]{1,0:T(8,128)(2,1)S(1)} %get-tuple-element.72), channel_id=1, source_target_pairs={{0,2},{1,3},{2,4},{3,5},{4,6},{5,7},{6,0},{7,1},{8,10},{9,11},{10,... | collective-permute-start | bytes 393224 | tf_op jit(solution)/shard_map/ppermute | solution.py:49
  11.7 4.0 %collective-permute-start.6 = (bf16[128,512]{1,0:T(8,128)(2,1)S(1)}, bf16[128,512]{1,0:T(8,128)(2,1)S(1)}, u32[]{:S(2)}, u32[]{:S(2)}) collective-permute-start(bf16[128,512]{1,0:T(8,128)(2,1)S(1)} %get-tuple-element.72), channel_id=1, source_target_pairs={{0,3},{1,4},{2,5},{3,6},{4,7},{5,0},{6,1},{7,2},{8,11},{9,12},{10,... | collective-permute-start | bytes 393224 | tf_op jit(solution)/shard_map/ppermute | solution.py:49
  16.3 4.9 %collective-permute-start.8 = (bf16[128,512]{1,0:T(8,128)(2,1)S(1)}, bf16[128,512]{1,0:T(8,128)(2,1)S(1)}, u32[]{:S(2)}, u32[]{:S(2)}) collective-permute-start(bf16[128,512]{1,0:T(8,128)(2,1)S(1)} %get-tuple-element.72), channel_id=1, source_target_pairs={{0,5},{1,6},{2,7},{3,0},{4,1},{5,2},{6,3},{7,4},{8,13},{9,14},{10,... | collective-permute-start | bytes 393224 | tf_op jit(solution)/shard_map/ppermute | solution.py:49
  23.1 2.7 %collective-permute-start.9 = (bf16[128,512]{1,0:T(8,128)(2,1)S(1)}, bf16[128,512]{1,0:T(8,128)(2,1)S(1)}, u32[]{:S(2)}, u32[]{:S(2)}) collective-permute-start(bf16[128,512]{1,0:T(8,128)(2,1)S(1)} %get-tuple-element.72), channel_id=1, source_target_pairs={{0,6},{1,7},{2,0},{3,1},{4,2},{5,3},{6,4},{7,5},{8,14},{9,15},{10,... | collective-permute-start | bytes 393224 | tf_op jit(solution)/shard_map/ppermute | solution.py:49
  25.9 2.3 %collective-permute-start.10 = (bf16[128,512]{1,0:T(8,128)(2,1)S(1)}, bf16[128,512]{1,0:T(8,128)(2,1)S(1)}, u32[]{:S(2)}, u32[]{:S(2)}) collective-permute-start(bf16[128,512]{1,0:T(8,128)(2,1)S(1)} %get-tuple-element.72), channel_id=1, source_target_pairs={{0,7},{1,0},{2,1},{3,2},{4,3},{5,4},{6,5},{7,6},{8,15},{9,8},{10,9... | collective-permute-start | bytes 393224 | tf_op jit(solution)/shard_map/ppermute | solution.py:49
  28.1 5.4 %collective-permute-done.6 = bf16[128,512]{1,0:T(8,128)(2,1)S(1)} collective-permute-done((bf16[128,512]{1,0:T(8,128)(2,1)S(1)}, bf16[128,512]{1,0:T(8,128)(2,1)S(1)}, u32[]{:S(2)}, u32[]{:S(2)}) %collective-permute-start.6) | collective-permute-done | bytes 131104 | tf_op jit(solution)/shard_map/ppermute | solution.py:49
  33.5 1.9 %collective-permute-start = (bf16[1024,512]{1,0:T(8,128)(2,1)}, bf16[1024,512]{1,0:T(8,128)(2,1)}, u32[]{:S(2)}, u32[]{:S(2)}) collective-permute-start(bf16[1024,512]{1,0:T(8,128)(2,1)} %param.17), channel_id=1, source_target_pairs={{0,2},{1,3},{2,4},{3,5},{4,6},{5,7},{6,8},{7,9},{8,10},{9,11},{10,... | collective-permute-start | bytes 3145736 | tf_op jit(solution)/shard_map/ppermute | solution.py:20
  35.5 5.2 %collective-permute-start.1 = (bf16[1024,512]{1,0:T(8,128)(2,1)}, bf16[1024,512]{1,0:T(8,128)(2,1)}, u32[]{:S(2)}, u32[]{:S(2)}) collective-permute-start(bf16[1024,512]{1,0:T(8,128)(2,1)} %param.17), channel_id=1, source_target_pairs={{0,1},{1,2},{2,3},{3,4},{4,5},{5,6},{6,7},{7,8},{8,9},{9,10},{10,1... | collective-permute-start | bytes 3145736 | tf_op jit(solution)/shard_map/ppermute | solution.py:20
  40.7 5.5 %collective-permute-start.2 = (bf16[1024,512]{1,0:T(8,128)(2,1)}, bf16[1024,512]{1,0:T(8,128)(2,1)}, u32[]{:S(2)}, u32[]{:S(2)}) collective-permute-start(bf16[1024,512]{1,0:T(8,128)(2,1)} %param.17), channel_id=1, source_target_pairs={{1,0},{2,1},{3,2},{4,3},{5,4},{6,5},{7,6},{8,7},{9,8},{10,9},{11,1... | collective-permute-start | bytes 3145736 | tf_op jit(solution)/shard_map/ppermute | solution.py:20
  46.2 3.4 %collective-permute-start.3 = (bf16[1024,512]{1,0:T(8,128)(2,1)}, bf16[1024,512]{1,0:T(8,128)(2,1)}, u32[]{:S(2)}, u32[]{:S(2)}) collective-permute-start(bf16[1024,512]{1,0:T(8,128)(2,1)} %param.17), channel_id=1, source_target_pairs={{2,0},{3,1},{4,2},{5,3},{6,4},{7,5},{8,6},{9,7},{10,8},{11,9},{12,... | collective-permute-start | bytes 3145736 | tf_op jit(solution)/shard_map/ppermute | solution.py:20
  49.7 2.0 %gather_fusion.1 = bf16[512,512]{1,0:T(8,128)(2,1)S(1)} fusion(bf16[1024,512]{1,0:T(8,128)(2,1)S(1)} %constant_dynamic-update-slice_fusion, s32[1024]{0:T(1024)S(1)} %pad_clamp_fusion), kind=kCustom, calls=%fused_computation.1 | custom fusion | bytes 1050624 | tf_op jit(solution)/shard_map/jit(_take)/gather | solution.py:55
  53.9 3.9 %convert_bitcast_fusion = bf16[8,16,64,128]{3,2,1,0:T(8,128)(2,1)} fusion(bf16[8,128,512,1]{2,1,3,0:T(8,128)(2,1)} %bitcast.3, bf16[16,64,512,1]{2,1,0,3:T(8,128)(2,1)S(1)} %bitcast.66), kind=kOutput, calls=%fused_computation.7 | convolution fusion | flops 1074790400 | bytes 4194304 | tf_op jit(solution)/shard_map/hdc,btc->bhdt/dot_general | solution.py:152
  57.8 2.9 %convolution_convert_fusion.1 = bf16[1024,512]{1,0:T(8,128)(2,1)} fusion(bf16[1024,512]{1,0:T(8,128)(2,1)} %param.17, bf16[512,512]{1,0:T(8,128)(2,1)S(1)} %copy-done), kind=kOutput, calls=%fused_computation.9 | convolution fusion | flops 537395200 | bytes 2621440 | tf_op jit(solution)/shard_map/dot_general | solution.py:140
  61.3 2.8 %reshape.260 = bf16[8,128,8,64]{3,2,1,0:T(8,128)(2,1)S(1)} reshape(bf16[1024,512]{1,0:T(8,128)(2,1)} %convolution_convert_fusion.1) | data formatting | bytes 2097152 | tf_op jit(solution)/shard_map/reshape | solution.py:141
  66.0 8.3 %scatter.16 = bf16[40,16,64,128]{3,2,1,0:T(8,128)(2,1)} pad(bf16[8,16,64,128]{3,2,1,0:T(8,128)(2,1)} %convert_bitcast_fusion, bf16[]{:T(256)} %constant.248.clone.1), padding=16_16x0_0x0_0x0_0 | pad | bytes 12582914 | tf_op jit(solution)/shard_map/scatter | solution.py:158
  77.5 6.0 %collective-permute-done = bf16[1024,512]{1,0:T(8,128)(2,1)} collective-permute-done((bf16[1024,512]{1,0:T(8,128)(2,1)}, bf16[1024,512]{1,0:T(8,128)(2,1)}, u32[]{:S(2)}, u32[]{:S(2)}) %collective-permute-start) | collective-permute-done | bytes 1048608 | tf_op jit(solution)/shard_map/ppermute | solution.py:20
  83.5 3.9 %bitcast_dynamic-update-slice_fusion.3 = bf16[40,16,64,128]{3,2,1,0:T(8,128)(2,1)} fusion(bf16[40,16,64,128]{3,2,1,0:T(8,128)(2,1)} %scatter.16, bf16[8,128,512,1]{2,1,3,0:T(8,128)(2,1)} %bitcast.10, bf16[16,64,512,1]{2,1,0,3:T(8,128)(2,1)S(1)} %bitcast.67), kind=kOutput, calls=%fused_computation.5 | convolution fusion | flops 1074790400 | bytes 4194304 | tf_op jit(solution)/shard_map/hdc,btc->bhdt/dot_general | solution.py:152
  87.3 19.2 %collective-permute-done.1 = bf16[1024,512]{1,0:T(8,128)(2,1)} collective-permute-done((bf16[1024,512]{1,0:T(8,128)(2,1)}, bf16[1024,512]{1,0:T(8,128)(2,1)}, u32[]{:S(2)}, u32[]{:S(2)}) %collective-permute-start.1) | collective-permute-done | bytes 1048608 | tf_op jit(solution)/shard_map/ppermute | solution.py:20
  106.5 3.8 %bitcast_dynamic-update-slice_fusion.2 = bf16[40,16,64,128]{3,2,1,0:T(8,128)(2,1)} fusion(bf16[40,16,64,128]{3,2,1,0:T(8,128)(2,1)} %bitcast_dynamic-update-slice_fusion.3, bf16[8,128,512,1]{2,1,3,0:T(8,128)(2,1)} %bitcast.16, bf16[16,64,512,1]{2,1,0,3:T(8,128)(2,1)S(1)} %bitcast.68), kind=kOutput, calls=%fused_computation.4 | convolution fusion | flops 1074790400 | bytes 4194304 | tf_op jit(solution)/shard_map/hdc,btc->bhdt/dot_general | solution.py:152
  110.4 3.9 %bitcast_dynamic-update-slice_fusion.1 = bf16[40,16,64,128]{3,2,1,0:T(8,128)(2,1)} fusion(bf16[40,16,64,128]{3,2,1,0:T(8,128)(2,1)} %bitcast_dynamic-update-slice_fusion.2, bf16[8,128,512,1]{2,1,3,0:T(8,128)(2,1)} %bitcast.20, bf16[16,64,512,1]{2,1,0,3:T(8,128)(2,1)S(1)} %bitcast.69), kind=kOutput, calls=%fused_computation.3 | convolution fusion | flops 1074790400 | bytes 4194304 | tf_op jit(solution)/shard_map/hdc,btc->bhdt/dot_general | solution.py:152
  114.2 4.0 %bitcast_dynamic-update-slice_fusion.kvt_ref = bf16[40,16,64,128]{3,2,1,0:T(8,128)(2,1)} fusion(bf16[40,16,64,128]{3,2,1,0:T(8,128)(2,1)} %bitcast_dynamic-update-slice_fusion.1, bf16[8,128,512,1]{2,1,3,0:T(8,128)(2,1)} %bitcast.24, bf16[16,64,512,1]{2,1,0,3:T(8,128)(2,1)S(1)} %bitcast.70), kind=kOutput, calls=%fused_computation.2 | convolution fusion | flops 1074790400 | bytes 4194304 | tf_op jit(solution)/shard_map/hdc,btc->bhdt/dot_general | solution.py:152
  121.8 37.7 %shard_map.73 = bf16[8,128,512]{2,1,0:T(8,128)(2,1)} custom-call(s32[96]{0:T(128)} %reshape.223.rel_ref, s32[8]{0:T(128)} %cnt_ref.1, bf16[8,8,128,64]{3,2,1,0:T(8,128)(2,1)} %bitcast.63, bf16[40,16,64,128]{3,2,1,0:T(8,128)(2,1)} %bitcast_dynamic-update-slice_fusion.kvt_ref, bf16[8,64,512]{2,1,0:T(8,128)(2,1)} %reshape.232.bkt_ref, ...), custom_call_target="tpu_custom_call" | custom-call | tf_op jit(solution)/shard_map/pallas_call | solution.py:121
  (53 shorter events, 16.2 us)
Async XLA Ops:
  0.0 57.8 %copy-start = (bf16[512,512]{1,0:T(8,128)(2,1)S(1)}, bf16[512,512]{1,0:T(8,128)(2,1)}, u32[]{:S(2)}) copy-start(bf16[512,512]{1,0:T(8,128)(2,1)} %param.18) | copy-start | bytes 1572868
  6.5 16.6 %collective-permute-start.4 = (bf16[128,512]{1,0:T(8,128)(2,1)S(1)}, bf16[128,512]{1,0:T(8,128)(2,1)S(1)}, u32[]{:S(2)}, u32[]{:S(2)}) collective-permute-start(bf16[128,512]{1,0:T(8,128)(2,1)S(1)} %get-tuple-element.72), channel_id=1, source_target_pairs={{0,1},{1,2},{2,3},{3,4},{4,5},{5,6},{6,7},{7,0},{8,9},{9,10},{10,1... | collective-permute-start | bytes 393224 | tf_op jit(solution)/shard_map/ppermute | solution.py:49
  8.4 17.4 %collective-permute-start.5 = (bf16[128,512]{1,0:T(8,128)(2,1)S(1)}, bf16[128,512]{1,0:T(8,128)(2,1)S(1)}, u32[]{:S(2)}, u32[]{:S(2)}) collective-permute-start(bf16[128,512]{1,0:T(8,128)(2,1)S(1)} %get-tuple-element.72), channel_id=1, source_target_pairs={{0,2},{1,3},{2,4},{3,5},{4,6},{5,7},{6,0},{7,1},{8,10},{9,11},{10,... | collective-permute-start | bytes 393224 | tf_op jit(solution)/shard_map/ppermute | solution.py:49
  11.7 21.8 %collective-permute-start.6 = (bf16[128,512]{1,0:T(8,128)(2,1)S(1)}, bf16[128,512]{1,0:T(8,128)(2,1)S(1)}, u32[]{:S(2)}, u32[]{:S(2)}) collective-permute-start(bf16[128,512]{1,0:T(8,128)(2,1)S(1)} %get-tuple-element.72), channel_id=1, source_target_pairs={{0,3},{1,4},{2,5},{3,6},{4,7},{5,0},{6,1},{7,2},{8,11},{9,12},{10,... | collective-permute-start | bytes 393224 | tf_op jit(solution)/shard_map/ppermute | solution.py:49
  15.8 19.7 %collective-permute-start.7 = (bf16[128,512]{1,0:T(8,128)(2,1)S(1)}, bf16[128,512]{1,0:T(8,128)(2,1)S(1)}, u32[]{:S(2)}, u32[]{:S(2)}) collective-permute-start(bf16[128,512]{1,0:T(8,128)(2,1)S(1)} %get-tuple-element.72), channel_id=1, source_target_pairs={{0,4},{1,5},{2,6},{3,7},{4,0},{5,1},{6,2},{7,3},{8,12},{9,13},{10,... | collective-permute-start | bytes 393224 | tf_op jit(solution)/shard_map/ppermute | solution.py:49
  16.3 24.4 %collective-permute-start.8 = (bf16[128,512]{1,0:T(8,128)(2,1)S(1)}, bf16[128,512]{1,0:T(8,128)(2,1)S(1)}, u32[]{:S(2)}, u32[]{:S(2)}) collective-permute-start(bf16[128,512]{1,0:T(8,128)(2,1)S(1)} %get-tuple-element.72), channel_id=1, source_target_pairs={{0,5},{1,6},{2,7},{3,0},{4,1},{5,2},{6,3},{7,4},{8,13},{9,14},{10,... | collective-permute-start | bytes 393224 | tf_op jit(solution)/shard_map/ppermute | solution.py:49
  23.1 34.7 %copy-start.2 = (bf16[512,1024]{0,1:T(8,128)(2,1)}, bf16[512,1024]{0,1:T(8,128)(2,1)S(1)}, u32[]{:S(2)}) copy-start(bf16[512,1024]{0,1:T(8,128)(2,1)S(1)} %copy.18) | copy-start | bytes 3145732
  23.1 23.1 %collective-permute-start.9 = (bf16[128,512]{1,0:T(8,128)(2,1)S(1)}, bf16[128,512]{1,0:T(8,128)(2,1)S(1)}, u32[]{:S(2)}, u32[]{:S(2)}) collective-permute-start(bf16[128,512]{1,0:T(8,128)(2,1)S(1)} %get-tuple-element.72), channel_id=1, source_target_pairs={{0,6},{1,7},{2,0},{3,1},{4,2},{5,3},{6,4},{7,5},{8,14},{9,15},{10,... | collective-permute-start | bytes 393224 | tf_op jit(solution)/shard_map/ppermute | solution.py:49
  25.9 23.8 %collective-permute-start.10 = (bf16[128,512]{1,0:T(8,128)(2,1)S(1)}, bf16[128,512]{1,0:T(8,128)(2,1)S(1)}, u32[]{:S(2)}, u32[]{:S(2)}) collective-permute-start(bf16[128,512]{1,0:T(8,128)(2,1)S(1)} %get-tuple-element.72), channel_id=1, source_target_pairs={{0,7},{1,0},{2,1},{3,2},{4,3},{5,4},{6,5},{7,6},{8,15},{9,8},{10,9... | collective-permute-start | bytes 393224 | tf_op jit(solution)/shard_map/ppermute | solution.py:49
  33.5 50.0 %collective-permute-start = (bf16[1024,512]{1,0:T(8,128)(2,1)}, bf16[1024,512]{1,0:T(8,128)(2,1)}, u32[]{:S(2)}, u32[]{:S(2)}) collective-permute-start(bf16[1024,512]{1,0:T(8,128)(2,1)} %param.17), channel_id=1, source_target_pairs={{0,2},{1,3},{2,4},{3,5},{4,6},{5,7},{6,8},{7,9},{8,10},{9,11},{10,... | collective-permute-start | bytes 3145736 | tf_op jit(solution)/shard_map/ppermute | solution.py:20
  35.5 71.1 %collective-permute-start.1 = (bf16[1024,512]{1,0:T(8,128)(2,1)}, bf16[1024,512]{1,0:T(8,128)(2,1)}, u32[]{:S(2)}, u32[]{:S(2)}) collective-permute-start(bf16[1024,512]{1,0:T(8,128)(2,1)} %param.17), channel_id=1, source_target_pairs={{0,1},{1,2},{2,3},{3,4},{4,5},{5,6},{6,7},{7,8},{8,9},{9,10},{10,1... | collective-permute-start | bytes 3145736 | tf_op jit(solution)/shard_map/ppermute | solution.py:20
  40.7 69.7 %collective-permute-start.2 = (bf16[1024,512]{1,0:T(8,128)(2,1)}, bf16[1024,512]{1,0:T(8,128)(2,1)}, u32[]{:S(2)}, u32[]{:S(2)}) collective-permute-start(bf16[1024,512]{1,0:T(8,128)(2,1)} %param.17), channel_id=1, source_target_pairs={{1,0},{2,1},{3,2},{4,3},{5,4},{6,5},{7,6},{8,7},{9,8},{10,9},{11,1... | collective-permute-start | bytes 3145736 | tf_op jit(solution)/shard_map/ppermute | solution.py:20
  46.2 68.0 %collective-permute-start.3 = (bf16[1024,512]{1,0:T(8,128)(2,1)}, bf16[1024,512]{1,0:T(8,128)(2,1)}, u32[]{:S(2)}, u32[]{:S(2)}) collective-permute-start(bf16[1024,512]{1,0:T(8,128)(2,1)} %param.17), channel_id=1, source_target_pairs={{2,0},{3,1},{4,2},{5,3},{6,4},{7,5},{8,6},{9,7},{10,8},{11,9},{12,... | collective-permute-start | bytes 3145736 | tf_op jit(solution)/shard_map/ppermute | solution.py:20
  52.6 21.7 %collective-permute-start.11 = (bf16[512,512]{1,0:T(8,128)(2,1)}, bf16[512,512]{1,0:T(8,128)(2,1)}, u32[]{:S(2)}, u32[]{:S(2)}) collective-permute-start(bf16[512,512]{1,0:T(8,128)(2,1)} %select_select_fusion), channel_id=1, source_target_pairs={{0,8},{1,9},{2,10},{3,11},{4,12},{5,13},{6,14},{7,15},{8,0},{9,1},... | collective-permute-start | bytes 1572872 | tf_op jit(solution)/shard_map/ppermute | solution.py:27
  53.9 6.8 %copy-start.4 = (s32[8,12]{1,0:T(8,128)S(1)}, s32[8,12]{1,0:T(8,128)}, u32[]{:S(2)}) copy-start(s32[8,12]{1,0:T(8,128)} %param.21) | copy-start | bytes 1156
  66.0 17.5 %copy-start.3 = (bf16[512,1024]{0,1:T(8,128)(2,1)S(1)}, bf16[512,1024]{0,1:T(8,128)(2,1)}, u32[]{:S(2)}) copy-start(bf16[512,1024]{0,1:T(8,128)(2,1)} %copy-done.2) | copy-start | bytes 3145732
  75.7 42.6 %collective-permute-start.12 = (bf16[512,512]{1,0:T(8,128)(2,1)S(1)}, bf16[512,512]{1,0:T(8,128)(2,1)S(1)}, u32[]{:S(2)}, u32[]{:S(2)}) collective-permute-start(bf16[512,512]{1,0:T(8,128)(2,1)S(1)} %broadcast_select_fusion), channel_id=1, source_target_pairs={{0,16},{1,17},{2,18},{3,19},{4,20},{5,21},{6,22},{7,23},{8,24},{9,... | collective-permute-start | bytes 1572872 | tf_op jit(solution)/shard_map/ppermute | solution.py:27
  114.2 4.0 %copy-start.1 = (bf16[512,1024]{1,0:T(8,128)(2,1)S(1)}, bf16[512,1024]{1,0:T(8,128)(2,1)}, u32[]{:S(2)}) copy-start(bf16[512,1024]{1,0:T(8,128)(2,1)} %param.19) | copy-start | bytes 3145732

commit v9 on v8

--- a/solution.py
+++ b/solution.py
@@ -40,14 +40,18 @@
     padded_ids = jnp.concatenate([bnd_ids, jnp.zeros((BCAP,), jnp.int32)])
     my_ids = lax.dynamic_slice_in_dim(padded_ids, my_start, BCAP)
     compact = jnp.take(tokens, jnp.clip(my_ids - member * tok_dev, 0, tok_dev - 1), axis=0)
-    pieces = [compact]
-    for step in range(1, group):
+    ahead = [compact]
+    behind = []
+    for direction, held in ((1, ahead), (-1, behind)):
         pairs = [
-            (source, (source // group) * group + (source % group + step) % group)
+            (source, (source // group) * group + (source % group + direction) % group)
             for source in range(count)
         ]
-        pieces.append(lax.ppermute(compact, "curve", pairs))
-    near = jnp.concatenate(pieces, axis=0)
+        moving = compact
+        for _ in range(group // 2 if direction > 0 else (group - 1) // 2):
+            moving = lax.ppermute(moving, "curve", pairs)
+            held.append(moving)
+    near = jnp.concatenate(ahead + behind[::-1], axis=0)
     owner_start = jnp.sum((owner[None, :] < owner[:, None]).astype(jnp.int32), axis=1)
     slot = jnp.arange(bnd_ids.shape[0], dtype=jnp.int32)
     within = jnp.clip(slot - owner_start, 0, BCAP - 1)

time: 160 us -> 209 us (1.31)
  the two profiles are of different devices: /device:TPU:18 before, /device:TPU:102 now
where the time goes in v9:
time: 209 us
  waiting for transfers between devices  94 us (45%)
  Pallas kernels  35.5 us (17%)
  starting transfers between devices  27.1 us (13%)
  matrix products  23.1 us (11%)
  local copies, waits for them, and re-layouts  22.2 us (11%)
  other arithmetic  4.86 us (2%)
  between operations  2.18 us (1%)
    ppermute x7, waiting for transfers between devices, boundary_rows(): moving = lax.ppermute(moving, 'curve', pairs)  94 us
    pallas_call x1, Pallas kernels, attention(): pl.pallas_call(attention_kernel, grid_spec=grid_spec, out_shape=jax.Shape...  35.5 us
    dot_general x5, matrix products, on_device(): jnp.einsum('hdc,btc->bhdt', kv_w, piece.reshape(nblocks, BLOCK, width), p...  19.4 us
    ppermute x4, starting transfers between devices, from_behind(): lax.ppermute(value, axis, [(source, source + steps) for source in range(f...  12.3 us
    ppermute x7, starting transfers between devices, boundary_rows(): moving = lax.ppermute(moving, 'curve', pairs)  10.1 us
    scatter x1, local copies, waits for them, and re-layouts, on_device(): kvt = kvt.at[index * nblocks:(index + 1) * nblocks].set(part)  8.31 us
    reshape x2, local copies, waits for them, and re-layouts, on_device(): queries.reshape(nblocks, BLOCK, HEADS, head_dim).transpose(0, 2, 1, 3)  4.7 us
    ppermute x2, starting transfers between devices, share_rows(): other = lax.ppermute(rows, 'curve', pairs)  4.66 us
  transfers between devices with their start and end apart: 13, of which 5 were waited for; matrix products, arithmetic and copies ran while one was open for 20% of the time, Pallas kernels for 0%

profile of v9, /device:TPU:102, one launch (start us, length us, event | category | flops | bytes accessed | tf_op | source)
XLA Modules:
  0.0 208.9 jit_solution(49177153289723416)
XLA Ops:
  4.1 2.2 %gather_fusion = bf16[128,512]{1,0:T(8,128)(2,1)S(1)} fusion(bf16[1024,512]{1,0:T(8,128)(2,1)} %param.17, s32[1024]{0:T(1024)S(1)} %pad_clamp_fusion.1), kind=kCustom, calls=%fused_computation | custom fusion | bytes 262656 | tf_op jit(solution)/shard_map/jit(_take)/gather | solution.py:42
  6.5 3.2 %collective-permute-start.4 = (bf16[128,512]{1,0:T(8,128)(2,1)S(1)}, bf16[128,512]{1,0:T(8,128)(2,1)S(1)}, u32[]{:S(2)}, u32[]{:S(2)}) collective-permute-start(bf16[128,512]{1,0:T(8,128)(2,1)S(1)} %get-tuple-element.72), channel_id=1, source_target_pairs={{0,1},{1,2},{2,3},{3,4},{4,5},{5,6},{6,7},{7,0},{8,9},{9,10},{10,1... | collective-permute-start | bytes 393224 | tf_op jit(solution)/shard_map/ppermute | solution.py:52
  9.7 4.4 %collective-permute-start = (bf16[1024,512]{1,0:T(8,128)(2,1)}, bf16[1024,512]{1,0:T(8,128)(2,1)}, u32[]{:S(2)}, u32[]{:S(2)}) collective-permute-start(bf16[1024,512]{1,0:T(8,128)(2,1)} %param.17), channel_id=1, source_target_pairs={{0,2},{1,3},{2,4},{3,5},{4,6},{5,7},{6,8},{7,9},{8,10},{9,11},{10,... | collective-permute-start | bytes 3145736 | tf_op jit(solution)/shard_map/ppermute | solution.py:20
  14.0 2.9 %collective-permute-start.1 = (bf16[1024,512]{1,0:T(8,128)(2,1)}, bf16[1024,512]{1,0:T(8,128)(2,1)}, u32[]{:S(2)}, u32[]{:S(2)}) collective-permute-start(bf16[1024,512]{1,0:T(8,128)(2,1)} %param.17), channel_id=1, source_target_pairs={{0,1},{1,2},{2,3},{3,4},{4,5},{5,6},{6,7},{7,8},{8,9},{9,10},{10,1... | collective-permute-start | bytes 3145736 | tf_op jit(solution)/shard_map/ppermute | solution.py:20
  17.0 3.1 %collective-permute-start.2 = (bf16[1024,512]{1,0:T(8,128)(2,1)}, bf16[1024,512]{1,0:T(8,128)(2,1)}, u32[]{:S(2)}, u32[]{:S(2)}) collective-permute-start(bf16[1024,512]{1,0:T(8,128)(2,1)} %param.17), channel_id=1, source_target_pairs={{1,0},{2,1},{3,2},{4,3},{5,4},{6,5},{7,6},{8,7},{9,8},{10,9},{11,1... | collective-permute-start | bytes 3145736 | tf_op jit(solution)/shard_map/ppermute | solution.py:20
  20.4 2.1 %collective-permute-start.5 = (bf16[128,512]{1,0:T(8,128)(2,1)S(1)}, bf16[128,512]{1,0:T(8,128)(2,1)S(1)}, u32[]{:S(2)}, u32[]{:S(2)}) collective-permute-start(bf16[128,512]{1,0:T(8,128)(2,1)S(1)} %collective-permute-done.4), channel_id=1, source_target_pairs={{0,1},{1,2},{2,3},{3,4},{4,5},{5,6},{6,7},{7,0},{8,9},{9,10},{10,1... | collective-permute-start | bytes 393224 | tf_op jit(solution)/shard_map/ppermute | solution.py:52
  22.5 63.2 %collective-permute-done.5 = bf16[128,512]{1,0:T(8,128)(2,1)S(1)} collective-permute-done((bf16[128,512]{1,0:T(8,128)(2,1)S(1)}, bf16[128,512]{1,0:T(8,128)(2,1)S(1)}, u32[]{:S(2)}, u32[]{:S(2)}) %collective-permute-start.5) | collective-permute-done | bytes 131104 | tf_op jit(solution)/shard_map/ppermute | solution.py:52
  85.8 1.9 collective-permute-start.6
  89.4 1.8 collective-permute-done.6
  91.2 2.7 %collective-permute-start.7 = (bf16[128,512]{1,0:T(8,128)(2,1)S(1)}, bf16[128,512]{1,0:T(8,128)(2,1)S(1)}, u32[]{:S(2)}, u32[]{:S(2)}) collective-permute-start(bf16[128,512]{1,0:T(8,128)(2,1)S(1)} %collective-permute-done.6), channel_id=1, source_target_pairs={{0,1},{1,2},{2,3},{3,4},{4,5},{5,6},{6,7},{7,0},{8,9},{9,10},{10,1... | collective-permute-start | bytes 393224 | tf_op jit(solution)/shard_map/ppermute | solution.py:52
  96.4 1.9 collective-permute-start.3
  98.3 26.4 %collective-permute-done.10 = bf16[128,512]{1,0:T(8,128)(2,1)S(1)} collective-permute-done((bf16[128,512]{1,0:T(8,128)(2,1)S(1)}, bf16[128,512]{1,0:T(8,128)(2,1)S(1)}, u32[]{:S(2)}, u32[]{:S(2)}) %collective-permute-start.10) | collective-permute-done | bytes 131104 | tf_op jit(solution)/shard_map/ppermute | solution.py:52
  124.8 2.0 gather_fusion.1
  127.8 3.9 %convert_bitcast_fusion = bf16[8,16,64,128]{3,2,1,0:T(8,128)(2,1)} fusion(bf16[8,128,512,1]{2,1,3,0:T(8,128)(2,1)} %bitcast.3, bf16[16,64,512,1]{2,1,0,3:T(8,128)(2,1)S(1)} %bitcast.66), kind=kOutput, calls=%fused_computation.7 | convolution fusion | flops 1074790400 | bytes 4194304 | tf_op jit(solution)/shard_map/hdc,btc->bhdt/dot_general | solution.py:156
  131.7 2.9 %convolution_convert_fusion.1 = bf16[1024,512]{1,0:T(8,128)(2,1)} fusion(bf16[1024,512]{1,0:T(8,128)(2,1)} %param.17, bf16[512,512]{1,0:T(8,128)(2,1)S(1)} %copy-done), kind=kOutput, calls=%fused_computation.9 | convolution fusion | flops 537395200 | bytes 2621440 | tf_op jit(solution)/shard_map/dot_general | solution.py:144
  135.2 2.8 %reshape.260 = bf16[8,128,8,64]{3,2,1,0:T(8,128)(2,1)S(1)} reshape(bf16[1024,512]{1,0:T(8,128)(2,1)} %convolution_convert_fusion.1) | data formatting | bytes 2097152 | tf_op jit(solution)/shard_map/reshape | solution.py:145
  138.0 1.9 copy.29
  139.9 8.3 %scatter.16 = bf16[40,16,64,128]{3,2,1,0:T(8,128)(2,1)} pad(bf16[8,16,64,128]{3,2,1,0:T(8,128)(2,1)} %convert_bitcast_fusion, bf16[]{:T(256)} %constant.248.clone.1), padding=16_16x0_0x0_0x0_0 | pad | bytes 12582914 | tf_op jit(solution)/shard_map/scatter | solution.py:162
  149.6 4.7 %collective-permute-start.12 = (bf16[512,512]{1,0:T(8,128)(2,1)S(1)}, bf16[512,512]{1,0:T(8,128)(2,1)S(1)}, u32[]{:S(2)}, u32[]{:S(2)}) collective-permute-start(bf16[512,512]{1,0:T(8,128)(2,1)S(1)} %broadcast_select_fusion), channel_id=1, source_target_pairs={{0,16},{1,17},{2,18},{3,19},{4,20},{5,21},{6,22},{7,23},{8,24},{9,... | collective-permute-start | bytes 1572872 | tf_op jit(solution)/shard_map/ppermute | solution.py:27
  154.2 3.9 %bitcast_dynamic-update-slice_fusion.3 = bf16[40,16,64,128]{3,2,1,0:T(8,128)(2,1)} fusion(bf16[40,16,64,128]{3,2,1,0:T(8,128)(2,1)} %scatter.16, bf16[8,128,512,1]{2,1,3,0:T(8,128)(2,1)} %bitcast.10, bf16[16,64,512,1]{2,1,0,3:T(8,128)(2,1)S(1)} %bitcast.67), kind=kOutput, calls=%fused_computation.5 | convolution fusion | flops 1074790400 | bytes 4194304 | tf_op jit(solution)/shard_map/hdc,btc->bhdt/dot_general | solution.py:156
  158.1 3.8 %bitcast_dynamic-update-slice_fusion.2 = bf16[40,16,64,128]{3,2,1,0:T(8,128)(2,1)} fusion(bf16[40,16,64,128]{3,2,1,0:T(8,128)(2,1)} %bitcast_dynamic-update-slice_fusion.3, bf16[8,128,512,1]{2,1,3,0:T(8,128)(2,1)} %bitcast.16, bf16[16,64,512,1]{2,1,0,3:T(8,128)(2,1)S(1)} %bitcast.68), kind=kOutput, calls=%fused_computation.4 | convolution fusion | flops 1074790400 | bytes 4194304 | tf_op jit(solution)/shard_map/hdc,btc->bhdt/dot_general | solution.py:156
  161.9 3.9 %bitcast_dynamic-update-slice_fusion.1 = bf16[40,16,64,128]{3,2,1,0:T(8,128)(2,1)} fusion(bf16[40,16,64,128]{3,2,1,0:T(8,128)(2,1)} %bitcast_dynamic-update-slice_fusion.2, bf16[8,128,512,1]{2,1,3,0:T(8,128)(2,1)} %bitcast.20, bf16[16,64,512,1]{2,1,0,3:T(8,128)(2,1)S(1)} %bitcast.69), kind=kOutput, calls=%fused_computation.3 | convolution fusion | flops 1074790400 | bytes 4194304 | tf_op jit(solution)/shard_map/hdc,btc->bhdt/dot_general | solution.py:156
  165.8 4.0 %bitcast_dynamic-update-slice_fusion.kvt_ref = bf16[40,16,64,128]{3,2,1,0:T(8,128)(2,1)} fusion(bf16[40,16,64,128]{3,2,1,0:T(8,128)(2,1)} %bitcast_dynamic-update-slice_fusion.1, bf16[8,128,512,1]{2,1,3,0:T(8,128)(2,1)} %bitcast.24, bf16[16,64,512,1]{2,1,0,3:T(8,128)(2,1)S(1)} %bitcast.70), kind=kOutput, calls=%fused_computation.2 | convolution fusion | flops 1074790400 | bytes 4194304 | tf_op jit(solution)/shard_map/hdc,btc->bhdt/dot_general | solution.py:156
  173.3 35.5 %shard_map.73 = bf16[8,128,512]{2,1,0:T(8,128)(2,1)} custom-call(s32[96]{0:T(128)} %reshape.223.rel_ref, s32[8]{0:T(128)} %cnt_ref.1, bf16[8,8,128,64]{3,2,1,0:T(8,128)(2,1)} %bitcast.63, bf16[40,16,64,128]{3,2,1,0:T(8,128)(2,1)} %bitcast_dynamic-update-slice_fusion.kvt_ref, bf16[8,64,512]{2,1,0:T(8,128)(2,1)} %reshape.232.bkt_ref, ...), custom_call_target="tpu_custom_call" | custom-call | tf_op jit(solution)/shard_map/pallas_call | solution.py:125
  (53 shorter events, 13.3 us)
Async XLA Ops:
  0.0 131.7 %copy-start = (bf16[512,512]{1,0:T(8,128)(2,1)S(1)}, bf16[512,512]{1,0:T(8,128)(2,1)}, u32[]{:S(2)}) copy-start(bf16[512,512]{1,0:T(8,128)(2,1)} %param.18) | copy-start | bytes 1572868
  6.5 14.0 %collective-permute-start.4 = (bf16[128,512]{1,0:T(8,128)(2,1)S(1)}, bf16[128,512]{1,0:T(8,128)(2,1)S(1)}, u32[]{:S(2)}, u32[]{:S(2)}) collective-permute-start(bf16[128,512]{1,0:T(8,128)(2,1)S(1)} %get-tuple-element.72), channel_id=1, source_target_pairs={{0,1},{1,2},{2,3},{3,4},{4,5},{5,6},{6,7},{7,0},{8,9},{9,10},{10,1... | collective-permute-start | bytes 393224 | tf_op jit(solution)/shard_map/ppermute | solution.py:52
  9.7 79.6 %collective-permute-start.8 = (bf16[128,512]{1,0:T(8,128)(2,1)S(1)}, bf16[128,512]{1,0:T(8,128)(2,1)S(1)}, u32[]{:S(2)}, u32[]{:S(2)}) collective-permute-start(bf16[128,512]{1,0:T(8,128)(2,1)S(1)} %get-tuple-element.72), channel_id=1, source_target_pairs={{0,7},{1,0},{2,1},{3,2},{4,3},{5,4},{6,5},{7,6},{8,15},{9,8},{10,9... | collective-permute-start | bytes 393224 | tf_op jit(solution)/shard_map/ppermute | solution.py:52
  9.7 144.5 %collective-permute-start = (bf16[1024,512]{1,0:T(8,128)(2,1)}, bf16[1024,512]{1,0:T(8,128)(2,1)}, u32[]{:S(2)}, u32[]{:S(2)}) collective-permute-start(bf16[1024,512]{1,0:T(8,128)(2,1)} %param.17), channel_id=1, source_target_pairs={{0,2},{1,3},{2,4},{3,5},{4,6},{5,7},{6,8},{7,9},{8,10},{9,11},{10,... | collective-permute-start | bytes 3145736 | tf_op jit(solution)/shard_map/ppermute | solution.py:20
  14.0 144.0 %collective-permute-start.1 = (bf16[1024,512]{1,0:T(8,128)(2,1)}, bf16[1024,512]{1,0:T(8,128)(2,1)}, u32[]{:S(2)}, u32[]{:S(2)}) collective-permute-start(bf16[1024,512]{1,0:T(8,128)(2,1)} %param.17), channel_id=1, source_target_pairs={{0,1},{1,2},{2,3},{3,4},{4,5},{5,6},{6,7},{7,8},{8,9},{9,10},{10,1... | collective-permute-start | bytes 3145736 | tf_op jit(solution)/shard_map/ppermute | solution.py:20
  17.0 144.9 %collective-permute-start.2 = (bf16[1024,512]{1,0:T(8,128)(2,1)}, bf16[1024,512]{1,0:T(8,128)(2,1)}, u32[]{:S(2)}, u32[]{:S(2)}) collective-permute-start(bf16[1024,512]{1,0:T(8,128)(2,1)} %param.17), channel_id=1, source_target_pairs={{1,0},{2,1},{3,2},{4,3},{5,4},{6,5},{7,6},{8,7},{9,8},{10,9},{11,1... | collective-permute-start | bytes 3145736 | tf_op jit(solution)/shard_map/ppermute | solution.py:20
  20.4 65.4 %collective-permute-start.5 = (bf16[128,512]{1,0:T(8,128)(2,1)S(1)}, bf16[128,512]{1,0:T(8,128)(2,1)S(1)}, u32[]{:S(2)}, u32[]{:S(2)}) collective-permute-start(bf16[128,512]{1,0:T(8,128)(2,1)S(1)} %collective-permute-done.4), channel_id=1, source_target_pairs={{0,1},{1,2},{2,3},{3,4},{4,5},{5,6},{6,7},{7,0},{8,9},{9,10},{10,1... | collective-permute-start | bytes 393224 | tf_op jit(solution)/shard_map/ppermute | solution.py:52
  85.8 5.4 %collective-permute-start.6 = (bf16[128,512]{1,0:T(8,128)(2,1)S(1)}, bf16[128,512]{1,0:T(8,128)(2,1)S(1)}, u32[]{:S(2)}, u32[]{:S(2)}) collective-permute-start(bf16[128,512]{1,0:T(8,128)(2,1)S(1)} %collective-permute-done.5), channel_id=1, source_target_pairs={{0,1},{1,2},{2,3},{3,4},{4,5},{5,6},{6,7},{7,0},{8,9},{9,10},{10,1... | collective-permute-start | bytes 393224 | tf_op jit(solution)/shard_map/ppermute | solution.py:52
  89.2 42.5 %copy-start.2 = (bf16[512,1024]{0,1:T(8,128)(2,1)}, bf16[512,1024]{0,1:T(8,128)(2,1)S(1)}, u32[]{:S(2)}) copy-start(bf16[512,1024]{0,1:T(8,128)(2,1)S(1)} %copy.18) | copy-start | bytes 3145732
  89.2 6.3 %collective-permute-start.9 = (bf16[128,512]{1,0:T(8,128)(2,1)S(1)}, bf16[128,512]{1,0:T(8,128)(2,1)S(1)}, u32[]{:S(2)}, u32[]{:S(2)}) collective-permute-start(bf16[128,512]{1,0:T(8,128)(2,1)S(1)} %collective-permute-done.8), channel_id=1, source_target_pairs={{0,7},{1,0},{2,1},{3,2},{4,3},{5,4},{6,5},{7,6},{8,15},{9,8},{10,9... | collective-permute-start | bytes 393224 | tf_op jit(solution)/shard_map/ppermute | solution.py:52
  91.2 5.2 %collective-permute-start.7 = (bf16[128,512]{1,0:T(8,128)(2,1)S(1)}, bf16[128,512]{1,0:T(8,128)(2,1)S(1)}, u32[]{:S(2)}, u32[]{:S(2)}) collective-permute-start(bf16[128,512]{1,0:T(8,128)(2,1)S(1)} %collective-permute-done.6), channel_id=1, source_target_pairs={{0,1},{1,2},{2,3},{3,4},{4,5},{5,6},{6,7},{7,0},{8,9},{9,10},{10,1... | collective-permute-start | bytes 393224 | tf_op jit(solution)/shard_map/ppermute | solution.py:52
  95.5 29.3 %collective-permute-start.10 = (bf16[128,512]{1,0:T(8,128)(2,1)S(1)}, bf16[128,512]{1,0:T(8,128)(2,1)S(1)}, u32[]{:S(2)}, u32[]{:S(2)}) collective-permute-start(bf16[128,512]{1,0:T(8,128)(2,1)S(1)} %collective-permute-done.9), channel_id=1, source_target_pairs={{0,7},{1,0},{2,1},{3,2},{4,3},{5,4},{6,5},{7,6},{8,15},{9,8},{10,9... | collective-permute-start | bytes 393224 | tf_op jit(solution)/shard_map/ppermute | solution.py:52
  96.4 69.4 %collective-permute-start.3 = (bf16[1024,512]{1,0:T(8,128)(2,1)}, bf16[1024,512]{1,0:T(8,128)(2,1)}, u32[]{:S(2)}, u32[]{:S(2)}) collective-permute-start(bf16[1024,512]{1,0:T(8,128)(2,1)} %param.17), channel_id=1, source_target_pairs={{2,0},{3,1},{4,2},{5,3},{6,4},{7,5},{8,6},{9,7},{10,8},{11,9},{12,... | collective-permute-start | bytes 3145736 | tf_op jit(solution)/shard_map/ppermute | solution.py:20
  127.8 20.4 %collective-permute-start.11 = (bf16[512,512]{1,0:T(8,128)(2,1)}, bf16[512,512]{1,0:T(8,128)(2,1)}, u32[]{:S(2)}, u32[]{:S(2)}) collective-permute-start(bf16[512,512]{1,0:T(8,128)(2,1)} %select_select_fusion), channel_id=1, source_target_pairs={{0,8},{1,9},{2,10},{3,11},{4,12},{5,13},{6,14},{7,15},{8,0},{9,1},... | collective-permute-start | bytes 1572872 | tf_op jit(solution)/shard_map/ppermute | solution.py:27
  127.8 6.8 %copy-start.4 = (s32[8,12]{1,0:T(8,128)S(1)}, s32[8,12]{1,0:T(8,128)}, u32[]{:S(2)}) copy-start(s32[8,12]{1,0:T(8,128)} %param.21) | copy-start | bytes 1156
  139.9 14.3 %copy-start.3 = (bf16[512,1024]{0,1:T(8,128)(2,1)S(1)}, bf16[512,1024]{0,1:T(8,128)(2,1)}, u32[]{:S(2)}) copy-start(bf16[512,1024]{0,1:T(8,128)(2,1)} %copy-done.2) | copy-start | bytes 3145732
  149.6 20.2 %collective-permute-start.12 = (bf16[512,512]{1,0:T(8,128)(2,1)S(1)}, bf16[512,512]{1,0:T(8,128)(2,1)S(1)}, u32[]{:S(2)}, u32[]{:S(2)}) collective-permute-start(bf16[512,512]{1,0:T(8,128)(2,1)S(1)} %broadcast_select_fusion), channel_id=1, source_target_pairs={{0,16},{1,17},{2,18},{3,19},{4,20},{5,21},{6,22},{7,23},{8,24},{9,... | collective-permute-start | bytes 1572872 | tf_op jit(solution)/shard_map/ppermute | solution.py:27
  165.8 4.0 %copy-start.1 = (bf16[512,1024]{1,0:T(8,128)(2,1)S(1)}, bf16[512,1024]{1,0:T(8,128)(2,1)}, u32[]{:S(2)}) copy-start(bf16[512,1024]{1,0:T(8,128)(2,1)} %param.19) | copy-start | bytes 3145732

commit v10 on v8

--- a/solution.py
+++ b/solution.py
@@ -58,23 +58,23 @@
     return share_rows(rows, owner, member, group)
 
 
-def attend_heads(picks, count, q_ref, kvt_ref, bkt_ref, bvt_ref, w_ref, o_ref):
+def attend_heads(picks, count, q_ref, kvt_ref, bkvt_ref, w_ref, o_ref):
     near = len(picks) * BLOCK
-    width = near + bkt_ref.shape[2]
+    width = near + bkvt_ref.shape[2]
     lane = lax.broadcasted_iota(jnp.int32, (1, width), 1)
     live = (lane // BLOCK < count) | (lane >= near)
     rate = LOG2E / q_ref.shape[3] ** 0.5
     contexts = []
     for h in range(HEADS):
         query = q_ref[0, h]
-        keys = jnp.concatenate([kvt_ref[p, h] for p in picks] + [bkt_ref[h]], axis=1)
+        keys = jnp.concatenate([kvt_ref[p, h] for p in picks] + [bkvt_ref[h]], axis=1)
         scores = jnp.dot(query, keys, preferred_element_type=jnp.float32)
         scores = jnp.where(live, scores, -1e30)
         top = jnp.max(scores, axis=1, keepdims=True)
         expo = jnp.exp2((scores - top) * rate)
         total = jnp.sum(expo, axis=1, keepdims=True)
         weights = (expo * (1.0 / total)).astype(jnp.bfloat16)
-        values = jnp.concatenate([kvt_ref[p, HEADS + h] for p in picks] + [bvt_ref[h]], axis=1)
+        values = jnp.concatenate([kvt_ref[p, HEADS + h] for p in picks] + [bkvt_ref[HEADS + h]], axis=1)
         ctx = lax.dot_general(
             values, weights, (((1,), (1,)), ((), ())), preferred_element_type=jnp.float32
         )
@@ -86,7 +86,7 @@
     o_ref[0] = mixed.astype(jnp.bfloat16)
 
 
-def attention_kernel(rel_ref, cnt_ref, q_ref, kvt_ref, bkt_ref, bvt_ref, w_ref, o_ref):
+def attention_kernel(rel_ref, cnt_ref, q_ref, kvt_ref, bkvt_ref, w_ref, o_ref):
     b = pl.program_id(0)
     count = cnt_ref[b]
     picks = [rel_ref[b * NB + i] for i in range(NB)]
@@ -95,16 +95,16 @@
 
         @pl.when((count > low) & (count <= high))
         def _():
-            attend_heads(picks[:high], count, q_ref, kvt_ref, bkt_ref, bvt_ref, w_ref, o_ref)
+            attend_heads(picks[:high], count, q_ref, kvt_ref, bkvt_ref, w_ref, o_ref)
 
         low = high
 
 
-def attention(rel, counts, q, kvt, bkt, bvt, w_out):
+def attention(rel, counts, q, kvt, bkvt, w_out):
     nq = q.shape[0]
     nkb = kvt.shape[0]
     head_dim = q.shape[3]
-    nbound = bkt.shape[2]
+    nbound = bkvt.shape[2]
     width = w_out.shape[0]
     grid_spec = pltpu.PrefetchScalarGridSpec(
         num_scalar_prefetch=2,
@@ -112,8 +112,7 @@
         in_specs=[
             pl.BlockSpec((1, HEADS, BLOCK, head_dim), lambda b, r, c: (b, 0, 0, 0)),
             pl.BlockSpec((nkb, 2 * HEADS, head_dim, BLOCK), lambda b, r, c: (0, 0, 0, 0)),
-            pl.BlockSpec((HEADS, head_dim, nbound), lambda b, r, c: (0, 0, 0)),
-            pl.BlockSpec((HEADS, head_dim, nbound), lambda b, r, c: (0, 0, 0)),
+            pl.BlockSpec((2 * HEADS, head_dim, nbound), lambda b, r, c: (0, 0, 0)),
             pl.BlockSpec((width, width), lambda b, r, c: (0, 0)),
         ],
         out_specs=pl.BlockSpec((1, BLOCK, width), lambda b, r, c: (b, 0, 0)),
@@ -122,14 +121,7 @@
         attention_kernel,
         grid_spec=grid_spec,
         out_shape=jax.ShapeDtypeStruct((nq, BLOCK, width), jnp.bfloat16),
-    )(rel, counts, q, kvt, bkt, bvt, w_out)
-
-
-def key_tiles(keyvals, width, head_dim):
-    rows = keyvals.shape[0]
-    keys = keyvals[:, :width].reshape(rows // BLOCK, BLOCK, HEADS, head_dim)
-    vals = keyvals[:, width:].reshape(rows // BLOCK, BLOCK, HEADS, head_dim)
-    return keys.transpose(0, 2, 3, 1), vals.transpose(0, 2, 3, 1)
+    )(rel, counts, q, kvt, bkvt, w_out)
 
 
 def on_device(tokens, w_query, w_keyval, w_out, block_list, block_count, bnd_ids):
@@ -157,13 +149,12 @@
         ).astype(jnp.bfloat16)
         kvt = kvt.at[index * nblocks : (index + 1) * nblocks].set(part)
     gathered = boundary_rows(tokens, bnd_ids, member)
-    bnd_kv = jnp.dot(gathered, w_keyval, preferred_element_type=jnp.float32).astype(jnp.bfloat16)
-    bkt, bvt = key_tiles(bnd_kv, width, head_dim)
-    bkt = bkt.transpose(1, 2, 0, 3).reshape(HEADS, head_dim, -1)
-    bvt = bvt.transpose(1, 2, 0, 3).reshape(HEADS, head_dim, -1)
+    bkvt = jnp.einsum(
+        "hdc,nc->hdn", kv_w, gathered, preferred_element_type=jnp.float32
+    ).astype(jnp.bfloat16)
     first_block = (member - 2) * nblocks
     rel = jnp.clip(block_list - first_block, 0, 5 * nblocks - 1).reshape(-1).astype(jnp.int32)
-    mixed = attention(rel, block_count.astype(jnp.int32), queries, kvt, bkt, bvt, w_out)
+    mixed = attention(rel, block_count.astype(jnp.int32), queries, kvt, bkvt, w_out)
     return mixed.reshape(tok_dev, width)
 
 

time: 160 us -> 159 us (level); the launches traced: 159 us -> 156 us
  local copies, waits for them, and re-layouts: 22.2 us -> 19.5 us
  Pallas kernels: 37.7 us -> 35.5 us
    reshape x4 -> x0, local copies, waits for them, and re-layouts: 2.28 us -> none  [the longest x1 1.03 us: on_device(): bkt = bkt.transpose(1, 2, 0, 3).reshape(HEADS, head_dim, -1)]
    pallas_call x1, Pallas kernels: 37.7 us -> 35.5 us  [attention(): pl.pallas_call(attention_kernel, grid_spec=grid_spec, out_shape=jax.Shape...]
  transfers between devices with their start and end apart: 13 -> 13, of which waited for: 3 -> 3; matrix products, arithmetic and copies ran while one was open for 26% -> 27% of each run, Pallas kernels for 0% -> 0%
where the time goes in v10:
time: 159 us; the launch traced here: 156 us
  starting transfers between devices  38.8 us (24%)
  Pallas kernels  35.5 us (22%)
  waiting for transfers between devices  30.6 us (19%)
  matrix products  24.1 us (15%)
  local copies, waits for them, and re-layouts  19.5 us (12%)
  other arithmetic  4.87 us (3%)
  between operations  2.18 us (1%)
    pallas_call x1, Pallas kernels, attention(): pl.pallas_call(attention_kernel, grid_spec=grid_spec, out_shape=jax.Shape...  35.5 us
    ppermute x4, waiting for transfers between devices, from_behind(): lax.ppermute(value, axis, [(source, source + steps) for source in range(f...  25.2 us
    ppermute x7, starting transfers between devices, boundary_rows(): pieces.append(lax.ppermute(compact, 'curve', pairs))  19.8 us
    dot_general x5, matrix products, on_device(): jnp.einsum('hdc,btc->bhdt', kv_w, piece.reshape(nblocks, BLOCK, width), p...  19.3 us
    ppermute x4, starting transfers between devices, from_behind(): lax.ppermute(value, axis, [(source, source + steps) for source in range(f...  16 us
    scatter x1, local copies, waits for them, and re-layouts, on_device(): kvt = kvt.at[index * nblocks:(index + 1) * nblocks].set(part)  8.3 us
    ppermute x7, waiting for transfers between devices, boundary_rows(): pieces.append(lax.ppermute(compact, 'curve', pairs))  5.4 us
    reshape x2, local copies, waits for them, and re-layouts, on_device(): queries.reshape(nblocks, BLOCK, HEADS, head_dim).transpose(0, 2, 1, 3)  4.69 us
  transfers between devices with their start and end apart: 13, of which 3 were waited for; matrix products, arithmetic and copies ran while one was open for 27% of the time, Pallas kernels for 0%

profile of v10, /device:TPU:18, one launch (start us, length us, event | category | flops | bytes accessed | tf_op | source)
XLA Modules:
  0.0 155.6 jit_solution(17386878681185918982)
XLA Ops:
  4.1 2.2 %gather_fusion = bf16[128,512]{1,0:T(8,128)(2,1)S(1)} fusion(bf16[1024,512]{1,0:T(8,128)(2,1)} %param.17, s32[1024]{0:T(1024)S(1)} %pad_clamp_fusion.1), kind=kCustom, calls=%fused_computation | custom fusion | bytes 262656 | tf_op jit(solution)/shard_map/jit(_take)/gather | solution.py:42
  6.5 2.0 %collective-permute-start.4 = (bf16[128,512]{1,0:T(8,128)(2,1)S(1)}, bf16[128,512]{1,0:T(8,128)(2,1)S(1)}, u32[]{:S(2)}, u32[]{:S(2)}) collective-permute-start(bf16[128,512]{1,0:T(8,128)(2,1)S(1)} %get-tuple-element.72), channel_id=1, source_target_pairs={{0,1},{1,2},{2,3},{3,4},{4,5},{5,6},{6,7},{7,0},{8,9},{9,10},{10,1... | collective-permute-start | bytes 393224 | tf_op jit(solution)/shard_map/ppermute | solution.py:49
  8.4 3.3 %collective-permute-start.5 = (bf16[128,512]{1,0:T(8,128)(2,1)S(1)}, bf16[128,512]{1,0:T(8,128)(2,1)S(1)}, u32[]{:S(2)}, u32[]{:S(2)}) collective-permute-start(bf16[128,512]{1,0:T(8,128)(2,1)S(1)} %get-tuple-element.72), channel_id=1, source_target_pairs={{0,2},{1,3},{2,4},{3,5},{4,6},{5,7},{6,0},{7,1},{8,10},{9,11},{10,... | collective-permute-start | bytes 393224 | tf_op jit(solution)/shard_map/ppermute | solution.py:49
  11.7 4.0 %collective-permute-start.6 = (bf16[128,512]{1,0:T(8,128)(2,1)S(1)}, bf16[128,512]{1,0:T(8,128)(2,1)S(1)}, u32[]{:S(2)}, u32[]{:S(2)}) collective-permute-start(bf16[128,512]{1,0:T(8,128)(2,1)S(1)} %get-tuple-element.72), channel_id=1, source_target_pairs={{0,3},{1,4},{2,5},{3,6},{4,7},{5,0},{6,1},{7,2},{8,11},{9,12},{10,... | collective-permute-start | bytes 393224 | tf_op jit(solution)/shard_map/ppermute | solution.py:49
  16.3 4.9 %collective-permute-start.8 = (bf16[128,512]{1,0:T(8,128)(2,1)S(1)}, bf16[128,512]{1,0:T(8,128)(2,1)S(1)}, u32[]{:S(2)}, u32[]{:S(2)}) collective-permute-start(bf16[128,512]{1,0:T(8,128)(2,1)S(1)} %get-tuple-element.72), channel_id=1, source_target_pairs={{0,5},{1,6},{2,7},{3,0},{4,1},{5,2},{6,3},{7,4},{8,13},{9,14},{10,... | collective-permute-start | bytes 393224 | tf_op jit(solution)/shard_map/ppermute | solution.py:49
  23.1 2.7 %collective-permute-start.9 = (bf16[128,512]{1,0:T(8,128)(2,1)S(1)}, bf16[128,512]{1,0:T(8,128)(2,1)S(1)}, u32[]{:S(2)}, u32[]{:S(2)}) collective-permute-start(bf16[128,512]{1,0:T(8,128)(2,1)S(1)} %get-tuple-element.72), channel_id=1, source_target_pairs={{0,6},{1,7},{2,0},{3,1},{4,2},{5,3},{6,4},{7,5},{8,14},{9,15},{10,... | collective-permute-start | bytes 393224 | tf_op jit(solution)/shard_map/ppermute | solution.py:49
  25.9 2.3 %collective-permute-start.10 = (bf16[128,512]{1,0:T(8,128)(2,1)S(1)}, bf16[128,512]{1,0:T(8,128)(2,1)S(1)}, u32[]{:S(2)}, u32[]{:S(2)}) collective-permute-start(bf16[128,512]{1,0:T(8,128)(2,1)S(1)} %get-tuple-element.72), channel_id=1, source_target_pairs={{0,7},{1,0},{2,1},{3,2},{4,3},{5,4},{6,5},{7,6},{8,15},{9,8},{10,9... | collective-permute-start | bytes 393224 | tf_op jit(solution)/shard_map/ppermute | solution.py:49
  28.1 5.4 %collective-permute-done.6 = bf16[128,512]{1,0:T(8,128)(2,1)S(1)} collective-permute-done((bf16[128,512]{1,0:T(8,128)(2,1)S(1)}, bf16[128,512]{1,0:T(8,128)(2,1)S(1)}, u32[]{:S(2)}, u32[]{:S(2)}) %collective-permute-start.6) | collective-permute-done | bytes 131104 | tf_op jit(solution)/shard_map/ppermute | solution.py:49
  35.5 5.2 %collective-permute-start.1 = (bf16[1024,512]{1,0:T(8,128)(2,1)}, bf16[1024,512]{1,0:T(8,128)(2,1)}, u32[]{:S(2)}, u32[]{:S(2)}) collective-permute-start(bf16[1024,512]{1,0:T(8,128)(2,1)} %param.17), channel_id=1, source_target_pairs={{0,1},{1,2},{2,3},{3,4},{4,5},{5,6},{6,7},{7,8},{8,9},{9,10},{10,1... | collective-permute-start | bytes 3145736 | tf_op jit(solution)/shard_map/ppermute | solution.py:20
  40.7 5.5 %collective-permute-start.2 = (bf16[1024,512]{1,0:T(8,128)(2,1)}, bf16[1024,512]{1,0:T(8,128)(2,1)}, u32[]{:S(2)}, u32[]{:S(2)}) collective-permute-start(bf16[1024,512]{1,0:T(8,128)(2,1)} %param.17), channel_id=1, source_target_pairs={{1,0},{2,1},{3,2},{4,3},{5,4},{6,5},{7,6},{8,7},{9,8},{10,9},{11,1... | collective-permute-start | bytes 3145736 | tf_op jit(solution)/shard_map/ppermute | solution.py:20
  46.2 3.4 %collective-permute-start.3 = (bf16[1024,512]{1,0:T(8,128)(2,1)}, bf16[1024,512]{1,0:T(8,128)(2,1)}, u32[]{:S(2)}, u32[]{:S(2)}) collective-permute-start(bf16[1024,512]{1,0:T(8,128)(2,1)} %param.17), channel_id=1, source_target_pairs={{2,0},{3,1},{4,2},{5,3},{6,4},{7,5},{8,6},{9,7},{10,8},{11,9},{12,... | collective-permute-start | bytes 3145736 | tf_op jit(solution)/shard_map/ppermute | solution.py:20
  49.7 2.0 %gather_fusion.1 = bf16[512,512]{1,0:T(8,128)(2,1)S(1)} fusion(bf16[1024,512]{1,0:T(8,128)(2,1)S(1)} %constant_dynamic-update-slice_fusion, s32[1024]{0:T(1024)S(1)} %pad_clamp_fusion), kind=kCustom, calls=%fused_computation.1 | custom fusion | bytes 1050624 | tf_op jit(solution)/shard_map/jit(_take)/gather | solution.py:55
  53.9 3.9 %convert_bitcast_fusion = bf16[8,16,64,128]{3,2,1,0:T(8,128)(2,1)} fusion(bf16[8,128,512,1]{2,1,3,0:T(8,128)(2,1)} %bitcast.3, bf16[16,64,512,1]{2,1,0,3:T(8,128)(2,1)S(1)} %bitcast.63), kind=kOutput, calls=%fused_computation.7 | convolution fusion | flops 1074790400 | bytes 4194304 | tf_op jit(solution)/shard_map/hdc,btc->bhdt/dot_general | solution.py:144
  57.8 2.9 %convolution_convert_fusion.1 = bf16[1024,512]{1,0:T(8,128)(2,1)} fusion(bf16[1024,512]{1,0:T(8,128)(2,1)} %param.17, bf16[512,512]{1,0:T(8,128)(2,1)S(1)} %copy-done), kind=kOutput, calls=%fused_computation.9 | convolution fusion | flops 537395200 | bytes 2621440 | tf_op jit(solution)/shard_map/dot_general | solution.py:132
  61.4 2.8 %reshape.245 = bf16[8,128,8,64]{3,2,1,0:T(8,128)(2,1)S(1)} reshape(bf16[1024,512]{1,0:T(8,128)(2,1)} %convolution_convert_fusion.1) | data formatting | bytes 2097152 | tf_op jit(solution)/shard_map/reshape | solution.py:133
  66.1 8.3 %scatter.16 = bf16[40,16,64,128]{3,2,1,0:T(8,128)(2,1)} pad(bf16[8,16,64,128]{3,2,1,0:T(8,128)(2,1)} %convert_bitcast_fusion, bf16[]{:T(256)} %constant.248.clone.1), padding=16_16x0_0x0_0x0_0 | pad | bytes 12582914 | tf_op jit(solution)/shard_map/scatter | solution.py:150
  77.5 6.0 %collective-permute-done = bf16[1024,512]{1,0:T(8,128)(2,1)} collective-permute-done((bf16[1024,512]{1,0:T(8,128)(2,1)}, bf16[1024,512]{1,0:T(8,128)(2,1)}, u32[]{:S(2)}, u32[]{:S(2)}) %collective-permute-start) | collective-permute-done | bytes 1048608 | tf_op jit(solution)/shard_map/ppermute | solution.py:20
  83.5 3.8 %bitcast_dynamic-update-slice_fusion.3 = bf16[40,16,64,128]{3,2,1,0:T(8,128)(2,1)} fusion(bf16[40,16,64,128]{3,2,1,0:T(8,128)(2,1)} %scatter.16, bf16[8,128,512,1]{2,1,3,0:T(8,128)(2,1)} %bitcast.10, bf16[16,64,512,1]{2,1,0,3:T(8,128)(2,1)S(1)} %bitcast.64), kind=kOutput, calls=%fused_computation.5 | convolution fusion | flops 1074790400 | bytes 4194304 | tf_op jit(solution)/shard_map/hdc,btc->bhdt/dot_general | solution.py:144
  87.3 19.2 %collective-permute-done.1 = bf16[1024,512]{1,0:T(8,128)(2,1)} collective-permute-done((bf16[1024,512]{1,0:T(8,128)(2,1)}, bf16[1024,512]{1,0:T(8,128)(2,1)}, u32[]{:S(2)}, u32[]{:S(2)}) %collective-permute-start.1) | collective-permute-done | bytes 1048608 | tf_op jit(solution)/shard_map/ppermute | solution.py:20
  106.5 3.8 %bitcast_dynamic-update-slice_fusion.2 = bf16[40,16,64,128]{3,2,1,0:T(8,128)(2,1)} fusion(bf16[40,16,64,128]{3,2,1,0:T(8,128)(2,1)} %bitcast_dynamic-update-slice_fusion.3, bf16[8,128,512,1]{2,1,3,0:T(8,128)(2,1)} %bitcast.16, bf16[16,64,512,1]{2,1,0,3:T(8,128)(2,1)S(1)} %bitcast.65), kind=kOutput, calls=%fused_computation.4 | convolution fusion | flops 1074790400 | bytes 4194304 | tf_op jit(solution)/shard_map/hdc,btc->bhdt/dot_general | solution.py:144
  110.4 3.8 %bitcast_dynamic-update-slice_fusion.1 = bf16[40,16,64,128]{3,2,1,0:T(8,128)(2,1)} fusion(bf16[40,16,64,128]{3,2,1,0:T(8,128)(2,1)} %bitcast_dynamic-update-slice_fusion.2, bf16[8,128,512,1]{2,1,3,0:T(8,128)(2,1)} %bitcast.20, bf16[16,64,512,1]{2,1,0,3:T(8,128)(2,1)S(1)} %bitcast.66), kind=kOutput, calls=%fused_computation.3 | convolution fusion | flops 1074790400 | bytes 4194304 | tf_op jit(solution)/shard_map/hdc,btc->bhdt/dot_general | solution.py:144
  114.2 3.9 %bitcast_dynamic-update-slice_fusion.kvt_ref = bf16[40,16,64,128]{3,2,1,0:T(8,128)(2,1)} fusion(bf16[40,16,64,128]{3,2,1,0:T(8,128)(2,1)} %bitcast_dynamic-update-slice_fusion.1, bf16[8,128,512,1]{2,1,3,0:T(8,128)(2,1)} %bitcast.24, bf16[16,64,512,1]{2,1,0,3:T(8,128)(2,1)S(1)} %bitcast.67), kind=kOutput, calls=%fused_computation.2 | convolution fusion | flops 1074790400 | bytes 4194304 | tf_op jit(solution)/shard_map/hdc,btc->bhdt/dot_general | solution.py:144
  118.1 1.9 %fusion.bkvt_ref = bf16[16,64,512]{2,1,0:T(8,128)(2,1)} fusion(bf16[16,64,512]{2,1,0:T(8,128)(2,1)S(1)} %bitcast.68, bf16[512,512]{1,0:T(8,128)(2,1)S(1)} %collective-permute-done.12, bf16[512,512]{1,0:T(8,128)(2,1)S(1)} %broadcast_select_fusion, pred[512]{0:T(512)(128)(4,1)S(1)} %get-tuple-element.65), kind=kOutput, calls=%fused_computation.10 | convolution fusion | flops 537657344 | bytes 3146240 | tf_op jit(solution)/shard_map/hdc,nc->hdn/dot_general | solution.py:152
  120.0 35.5 %shard_map.73 = bf16[8,128,512]{2,1,0:T(8,128)(2,1)} custom-call(s32[96]{0:T(128)} %reshape.211.rel_ref, s32[8]{0:T(128)} %cnt_ref.1, bf16[8,8,128,64]{3,2,1,0:T(8,128)(2,1)} %bitcast.62, bf16[40,16,64,128]{3,2,1,0:T(8,128)(2,1)} %bitcast_dynamic-update-slice_fusion.kvt_ref, bf16[16,64,512]{2,1,0:T(8,128)(2,1)} %fusion.bkvt_ref, bf16[512,512]{1,0:T(8,128)(2,1)} %w_ref.1), custom_call_target="tpu_custom_call" | custom-call | tf_op jit(solution)/shard_map/pallas_call | solution.py:120
  (44 shorter events, 14.6 us)
Async XLA Ops:
  0.0 57.8 %copy-start = (bf16[512,512]{1,0:T(8,128)(2,1)S(1)}, bf16[512,512]{1,0:T(8,128)(2,1)}, u32[]{:S(2)}) copy-start(bf16[512,512]{1,0:T(8,128)(2,1)} %param.18) | copy-start | bytes 1572868
  6.5 16.6 %collective-permute-start.4 = (bf16[128,512]{1,0:T(8,128)(2,1)S(1)}, bf16[128,512]{1,0:T(8,128)(2,1)S(1)}, u32[]{:S(2)}, u32[]{:S(2)}) collective-permute-start(bf16[128,512]{1,0:T(8,128)(2,1)S(1)} %get-tuple-element.72), channel_id=1, source_target_pairs={{0,1},{1,2},{2,3},{3,4},{4,5},{5,6},{6,7},{7,0},{8,9},{9,10},{10,1... | collective-permute-start | bytes 393224 | tf_op jit(solution)/shard_map/ppermute | solution.py:49
  8.4 17.4 %collective-permute-start.5 = (bf16[128,512]{1,0:T(8,128)(2,1)S(1)}, bf16[128,512]{1,0:T(8,128)(2,1)S(1)}, u32[]{:S(2)}, u32[]{:S(2)}) collective-permute-start(bf16[128,512]{1,0:T(8,128)(2,1)S(1)} %get-tuple-element.72), channel_id=1, source_target_pairs={{0,2},{1,3},{2,4},{3,5},{4,6},{5,7},{6,0},{7,1},{8,10},{9,11},{10,... | collective-permute-start | bytes 393224 | tf_op jit(solution)/shard_map/ppermute | solution.py:49
  11.7 21.8 %collective-permute-start.6 = (bf16[128,512]{1,0:T(8,128)(2,1)S(1)}, bf16[128,512]{1,0:T(8,128)(2,1)S(1)}, u32[]{:S(2)}, u32[]{:S(2)}) collective-permute-start(bf16[128,512]{1,0:T(8,128)(2,1)S(1)} %get-tuple-element.72), channel_id=1, source_target_pairs={{0,3},{1,4},{2,5},{3,6},{4,7},{5,0},{6,1},{7,2},{8,11},{9,12},{10,... | collective-permute-start | bytes 393224 | tf_op jit(solution)/shard_map/ppermute | solution.py:49
  15.8 19.7 %collective-permute-start.7 = (bf16[128,512]{1,0:T(8,128)(2,1)S(1)}, bf16[128,512]{1,0:T(8,128)(2,1)S(1)}, u32[]{:S(2)}, u32[]{:S(2)}) collective-permute-start(bf16[128,512]{1,0:T(8,128)(2,1)S(1)} %get-tuple-element.72), channel_id=1, source_target_pairs={{0,4},{1,5},{2,6},{3,7},{4,0},{5,1},{6,2},{7,3},{8,12},{9,13},{10,... | collective-permute-start | bytes 393224 | tf_op jit(solution)/shard_map/ppermute | solution.py:49
  16.3 24.4 %collective-permute-start.8 = (bf16[128,512]{1,0:T(8,128)(2,1)S(1)}, bf16[128,512]{1,0:T(8,128)(2,1)S(1)}, u32[]{:S(2)}, u32[]{:S(2)}) collective-permute-start(bf16[128,512]{1,0:T(8,128)(2,1)S(1)} %get-tuple-element.72), channel_id=1, source_target_pairs={{0,5},{1,6},{2,7},{3,0},{4,1},{5,2},{6,3},{7,4},{8,13},{9,14},{10,... | collective-permute-start | bytes 393224 | tf_op jit(solution)/shard_map/ppermute | solution.py:49
  23.1 34.7 %copy-start.1 = (bf16[512,1024]{0,1:T(8,128)(2,1)}, bf16[512,1024]{0,1:T(8,128)(2,1)S(1)}, u32[]{:S(2)}) copy-start(bf16[512,1024]{0,1:T(8,128)(2,1)S(1)} %copy.14) | copy-start | bytes 3145732
  23.1 23.1 %collective-permute-start.9 = (bf16[128,512]{1,0:T(8,128)(2,1)S(1)}, bf16[128,512]{1,0:T(8,128)(2,1)S(1)}, u32[]{:S(2)}, u32[]{:S(2)}) collective-permute-start(bf16[128,512]{1,0:T(8,128)(2,1)S(1)} %get-tuple-element.72), channel_id=1, source_target_pairs={{0,6},{1,7},{2,0},{3,1},{4,2},{5,3},{6,4},{7,5},{8,14},{9,15},{10,... | collective-permute-start | bytes 393224 | tf_op jit(solution)/shard_map/ppermute | solution.py:49
  25.9 23.8 %collective-permute-start.10 = (bf16[128,512]{1,0:T(8,128)(2,1)S(1)}, bf16[128,512]{1,0:T(8,128)(2,1)S(1)}, u32[]{:S(2)}, u32[]{:S(2)}) collective-permute-start(bf16[128,512]{1,0:T(8,128)(2,1)S(1)} %get-tuple-element.72), channel_id=1, source_target_pairs={{0,7},{1,0},{2,1},{3,2},{4,3},{5,4},{6,5},{7,6},{8,15},{9,8},{10,9... | collective-permute-start | bytes 393224 | tf_op jit(solution)/shard_map/ppermute | solution.py:49
  33.5 50.0 %collective-permute-start = (bf16[1024,512]{1,0:T(8,128)(2,1)}, bf16[1024,512]{1,0:T(8,128)(2,1)}, u32[]{:S(2)}, u32[]{:S(2)}) collective-permute-start(bf16[1024,512]{1,0:T(8,128)(2,1)} %param.17), channel_id=1, source_target_pairs={{0,2},{1,3},{2,4},{3,5},{4,6},{5,7},{6,8},{7,9},{8,10},{9,11},{10,... | collective-permute-start | bytes 3145736 | tf_op jit(solution)/shard_map/ppermute | solution.py:20
  35.5 71.1 %collective-permute-start.1 = (bf16[1024,512]{1,0:T(8,128)(2,1)}, bf16[1024,512]{1,0:T(8,128)(2,1)}, u32[]{:S(2)}, u32[]{:S(2)}) collective-permute-start(bf16[1024,512]{1,0:T(8,128)(2,1)} %param.17), channel_id=1, source_target_pairs={{0,1},{1,2},{2,3},{3,4},{4,5},{5,6},{6,7},{7,8},{8,9},{9,10},{10,1... | collective-permute-start | bytes 3145736 | tf_op jit(solution)/shard_map/ppermute | solution.py:20
  40.7 69.7 %collective-permute-start.2 = (bf16[1024,512]{1,0:T(8,128)(2,1)}, bf16[1024,512]{1,0:T(8,128)(2,1)}, u32[]{:S(2)}, u32[]{:S(2)}) collective-permute-start(bf16[1024,512]{1,0:T(8,128)(2,1)} %param.17), channel_id=1, source_target_pairs={{1,0},{2,1},{3,2},{4,3},{5,4},{6,5},{7,6},{8,7},{9,8},{10,9},{11,1... | collective-permute-start | bytes 3145736 | tf_op jit(solution)/shard_map/ppermute | solution.py:20
  46.2 68.0 %collective-permute-start.3 = (bf16[1024,512]{1,0:T(8,128)(2,1)}, bf16[1024,512]{1,0:T(8,128)(2,1)}, u32[]{:S(2)}, u32[]{:S(2)}) collective-permute-start(bf16[1024,512]{1,0:T(8,128)(2,1)} %param.17), channel_id=1, source_target_pairs={{2,0},{3,1},{4,2},{5,3},{6,4},{7,5},{8,6},{9,7},{10,8},{11,9},{12,... | collective-permute-start | bytes 3145736 | tf_op jit(solution)/shard_map/ppermute | solution.py:20
  52.6 21.7 %collective-permute-start.11 = (bf16[512,512]{1,0:T(8,128)(2,1)}, bf16[512,512]{1,0:T(8,128)(2,1)}, u32[]{:S(2)}, u32[]{:S(2)}) collective-permute-start(bf16[512,512]{1,0:T(8,128)(2,1)} %select_select_fusion), channel_id=1, source_target_pairs={{0,8},{1,9},{2,10},{3,11},{4,12},{5,13},{6,14},{7,15},{8,0},{9,1},... | collective-permute-start | bytes 1572872 | tf_op jit(solution)/shard_map/ppermute | solution.py:27
  53.9 6.8 %copy-start.3 = (s32[8,12]{1,0:T(8,128)S(1)}, s32[8,12]{1,0:T(8,128)}, u32[]{:S(2)}) copy-start(s32[8,12]{1,0:T(8,128)} %param.21) | copy-start | bytes 1156
  66.1 17.4 %copy-start.2 = (bf16[512,1024]{0,1:T(8,128)(2,1)S(1)}, bf16[512,1024]{0,1:T(8,128)(2,1)}, u32[]{:S(2)}) copy-start(bf16[512,1024]{0,1:T(8,128)(2,1)} %copy-done.1) | copy-start | bytes 3145732
  75.7 42.4 %collective-permute-start.12 = (bf16[512,512]{1,0:T(8,128)(2,1)S(1)}, bf16[512,512]{1,0:T(8,128)(2,1)S(1)}, u32[]{:S(2)}, u32[]{:S(2)}) collective-permute-start(bf16[512,512]{1,0:T(8,128)(2,1)S(1)} %broadcast_select_fusion), channel_id=1, source_target_pairs={{0,16},{1,17},{2,18},{3,19},{4,20},{5,21},{6,22},{7,23},{8,24},{9,... | collective-permute-start | bytes 1572872 | tf_op jit(solution)/shard_map/ppermute | solution.py:27

commit v11 on v10

--- a/solution.py
+++ b/solution.py
@@ -39,7 +39,9 @@
     my_start = jnp.sum((owner < member).astype(jnp.int32))
     padded_ids = jnp.concatenate([bnd_ids, jnp.zeros((BCAP,), jnp.int32)])
     my_ids = lax.dynamic_slice_in_dim(padded_ids, my_start, BCAP)
-    compact = jnp.take(tokens, jnp.clip(my_ids - member * tok_dev, 0, tok_dev - 1), axis=0)
+    local = jnp.clip(my_ids - member * tok_dev, 0, tok_dev - 1)
+    select = (local[:, None] == jnp.arange(tok_dev, dtype=jnp.int32)[None, :]).astype(tokens.dtype)
+    compact = jnp.dot(select, tokens, preferred_element_type=jnp.float32).astype(tokens.dtype)
     pieces = [compact]
     for step in range(1, group):
         pairs = [

time: 159 us -> 157 us (0.987)
  local copies, waits for them, and re-layouts: 19.5 us -> 17.2 us
    gather x1 -> x0, local copies, waits for them, and re-layouts: 2.24 us -> none  [boundary_rows(): jnp.take(tokens, jnp.clip(my_ids - member * tok_dev, 0, tok_dev - 1), axi...]
where the time goes in v11:
time: 157 us; the launch traced here: 155 us
  starting transfers between devices  38.7 us (25%)
  Pallas kernels  35.5 us (23%)
  waiting for transfers between devices  30.6 us (19%)
  matrix products  25.6 us (16%)
  local copies, waits for them, and re-layouts  17.2 us (11%)
  other arithmetic  4.77 us (3%)
  between operations  2.18 us (1%)
    pallas_call x1, Pallas kernels, attention(): pl.pallas_call(attention_kernel, grid_spec=grid_spec, out_shape=jax.Shape...  35.5 us
    ppermute x4, waiting for transfers between devices, from_behind(): lax.ppermute(value, axis, [(source, source + steps) for source in range(f...  25.2 us
    ppermute x7, starting transfers between devices, boundary_rows(): pieces.append(lax.ppermute(compact, 'curve', pairs))  19.8 us
    dot_general x5, matrix products, on_device(): jnp.einsum('hdc,btc->bhdt', kv_w, piece.reshape(nblocks, BLOCK, width), p...  19.3 us
    ppermute x4, starting transfers between devices, from_behind(): lax.ppermute(value, axis, [(source, source + steps) for source in range(f...  16 us
    scatter x1, local copies, waits for them, and re-layouts, on_device(): kvt = kvt.at[index * nblocks:(index + 1) * nblocks].set(part)  8.31 us
    ppermute x7, waiting for transfers between devices, boundary_rows(): pieces.append(lax.ppermute(compact, 'curve', pairs))  5.41 us
    reshape x2, local copies, waits for them, and re-layouts, on_device(): queries.reshape(nblocks, BLOCK, HEADS, head_dim).transpose(0, 2, 1, 3)  4.69 us
  transfers between devices with their start and end apart: 13, of which 3 were waited for; matrix products, arithmetic and copies ran while one was open for 27% of the time, Pallas kernels for 0%

profile of v11, /device:TPU:18, one launch (start us, length us, event | category | flops | bytes accessed | tf_op | source)
XLA Modules:
  0.0 154.7 jit_solution(12258609992652293940)
XLA Ops:
  5.7 2.0 %collective-permute-start.4 = (bf16[128,512]{1,0:T(8,128)(2,1)S(1)}, bf16[128,512]{1,0:T(8,128)(2,1)S(1)}, u32[]{:S(2)}, u32[]{:S(2)}) collective-permute-start(bf16[128,512]{1,0:T(8,128)(2,1)S(1)} %get-tuple-element.74), channel_id=1, source_target_pairs={{0,1},{1,2},{2,3},{3,4},{4,5},{5,6},{6,7},{7,0},{8,9},{9,10},{10,1... | collective-permute-start | bytes 393224 | tf_op jit(solution)/shard_map/ppermute | solution.py:51
  7.7 3.3 %collective-permute-start.5 = (bf16[128,512]{1,0:T(8,128)(2,1)S(1)}, bf16[128,512]{1,0:T(8,128)(2,1)S(1)}, u32[]{:S(2)}, u32[]{:S(2)}) collective-permute-start(bf16[128,512]{1,0:T(8,128)(2,1)S(1)} %get-tuple-element.74), channel_id=1, source_target_pairs={{0,2},{1,3},{2,4},{3,5},{4,6},{5,7},{6,0},{7,1},{8,10},{9,11},{10,... | collective-permute-start | bytes 393224 | tf_op jit(solution)/shard_map/ppermute | solution.py:51
  11.0 4.0 %collective-permute-start.6 = (bf16[128,512]{1,0:T(8,128)(2,1)S(1)}, bf16[128,512]{1,0:T(8,128)(2,1)S(1)}, u32[]{:S(2)}, u32[]{:S(2)}) collective-permute-start(bf16[128,512]{1,0:T(8,128)(2,1)S(1)} %get-tuple-element.74), channel_id=1, source_target_pairs={{0,3},{1,4},{2,5},{3,6},{4,7},{5,0},{6,1},{7,2},{8,11},{9,12},{10,... | collective-permute-start | bytes 393224 | tf_op jit(solution)/shard_map/ppermute | solution.py:51
  15.5 4.9 %collective-permute-start.8 = (bf16[128,512]{1,0:T(8,128)(2,1)S(1)}, bf16[128,512]{1,0:T(8,128)(2,1)S(1)}, u32[]{:S(2)}, u32[]{:S(2)}) collective-permute-start(bf16[128,512]{1,0:T(8,128)(2,1)S(1)} %get-tuple-element.74), channel_id=1, source_target_pairs={{0,5},{1,6},{2,7},{3,0},{4,1},{5,2},{6,3},{7,4},{8,13},{9,14},{10,... | collective-permute-start | bytes 393224 | tf_op jit(solution)/shard_map/ppermute | solution.py:51
  22.3 2.7 %collective-permute-start.9 = (bf16[128,512]{1,0:T(8,128)(2,1)S(1)}, bf16[128,512]{1,0:T(8,128)(2,1)S(1)}, u32[]{:S(2)}, u32[]{:S(2)}) collective-permute-start(bf16[128,512]{1,0:T(8,128)(2,1)S(1)} %get-tuple-element.74), channel_id=1, source_target_pairs={{0,6},{1,7},{2,0},{3,1},{4,2},{5,3},{6,4},{7,5},{8,14},{9,15},{10,... | collective-permute-start | bytes 393224 | tf_op jit(solution)/shard_map/ppermute | solution.py:51
  25.1 2.2 %collective-permute-start.10 = (bf16[128,512]{1,0:T(8,128)(2,1)S(1)}, bf16[128,512]{1,0:T(8,128)(2,1)S(1)}, u32[]{:S(2)}, u32[]{:S(2)}) collective-permute-start(bf16[128,512]{1,0:T(8,128)(2,1)S(1)} %get-tuple-element.74), channel_id=1, source_target_pairs={{0,7},{1,0},{2,1},{3,2},{4,3},{5,4},{6,5},{7,6},{8,15},{9,8},{10,9... | collective-permute-start | bytes 393224 | tf_op jit(solution)/shard_map/ppermute | solution.py:51
  27.4 5.4 %collective-permute-done.6 = bf16[128,512]{1,0:T(8,128)(2,1)S(1)} collective-permute-done((bf16[128,512]{1,0:T(8,128)(2,1)S(1)}, bf16[128,512]{1,0:T(8,128)(2,1)S(1)}, u32[]{:S(2)}, u32[]{:S(2)}) %collective-permute-start.6) | collective-permute-done | bytes 131104 | tf_op jit(solution)/shard_map/ppermute | solution.py:51
  32.8 1.9 %collective-permute-start = (bf16[1024,512]{1,0:T(8,128)(2,1)}, bf16[1024,512]{1,0:T(8,128)(2,1)}, u32[]{:S(2)}, u32[]{:S(2)}) collective-permute-start(bf16[1024,512]{1,0:T(8,128)(2,1)} %param.17), channel_id=1, source_target_pairs={{0,2},{1,3},{2,4},{3,5},{4,6},{5,7},{6,8},{7,9},{8,10},{9,11},{10,... | collective-permute-start | bytes 3145736 | tf_op jit(solution)/shard_map/ppermute | solution.py:20
  34.7 5.2 %collective-permute-start.1 = (bf16[1024,512]{1,0:T(8,128)(2,1)}, bf16[1024,512]{1,0:T(8,128)(2,1)}, u32[]{:S(2)}, u32[]{:S(2)}) collective-permute-start(bf16[1024,512]{1,0:T(8,128)(2,1)} %param.17), channel_id=1, source_target_pairs={{0,1},{1,2},{2,3},{3,4},{4,5},{5,6},{6,7},{7,8},{8,9},{9,10},{10,1... | collective-permute-start | bytes 3145736 | tf_op jit(solution)/shard_map/ppermute | solution.py:20
  39.9 5.5 %collective-permute-start.2 = (bf16[1024,512]{1,0:T(8,128)(2,1)}, bf16[1024,512]{1,0:T(8,128)(2,1)}, u32[]{:S(2)}, u32[]{:S(2)}) collective-permute-start(bf16[1024,512]{1,0:T(8,128)(2,1)} %param.17), channel_id=1, source_target_pairs={{1,0},{2,1},{3,2},{4,3},{5,4},{6,5},{7,6},{8,7},{9,8},{10,9},{11,1... | collective-permute-start | bytes 3145736 | tf_op jit(solution)/shard_map/ppermute | solution.py:20
  45.5 3.4 %collective-permute-start.3 = (bf16[1024,512]{1,0:T(8,128)(2,1)}, bf16[1024,512]{1,0:T(8,128)(2,1)}, u32[]{:S(2)}, u32[]{:S(2)}) collective-permute-start(bf16[1024,512]{1,0:T(8,128)(2,1)} %param.17), channel_id=1, source_target_pairs={{2,0},{3,1},{4,2},{5,3},{6,4},{7,5},{8,6},{9,7},{10,8},{11,9},{12,... | collective-permute-start | bytes 3145736 | tf_op jit(solution)/shard_map/ppermute | solution.py:20
  48.9 2.0 %gather_fusion = bf16[512,512]{1,0:T(8,128)(2,1)S(1)} fusion(bf16[1024,512]{1,0:T(8,128)(2,1)S(1)} %constant_dynamic-update-slice_fusion, s32[1024]{0:T(1024)S(1)} %pad_clamp_fusion), kind=kCustom, calls=%fused_computation | custom fusion | bytes 1050624 | tf_op jit(solution)/shard_map/jit(_take)/gather | solution.py:57
  53.2 3.8 %convert_bitcast_fusion = bf16[8,16,64,128]{3,2,1,0:T(8,128)(2,1)} fusion(bf16[8,128,512,1]{2,1,3,0:T(8,128)(2,1)} %bitcast.3, bf16[16,64,512,1]{2,1,0,3:T(8,128)(2,1)S(1)} %bitcast.64), kind=kOutput, calls=%fused_computation.6 | convolution fusion | flops 1074790400 | bytes 4194304 | tf_op jit(solution)/shard_map/hdc,btc->bhdt/dot_general | solution.py:146
  57.0 2.9 %convolution_convert_fusion.1 = bf16[1024,512]{1,0:T(8,128)(2,1)} fusion(bf16[1024,512]{1,0:T(8,128)(2,1)} %param.17, bf16[512,512]{1,0:T(8,128)(2,1)S(1)} %copy-done), kind=kOutput, calls=%fused_computation.8 | convolution fusion | flops 537395200 | bytes 2621440 | tf_op jit(solution)/shard_map/dot_general | solution.py:134
  60.6 2.8 %reshape.232 = bf16[8,128,8,64]{3,2,1,0:T(8,128)(2,1)S(1)} reshape(bf16[1024,512]{1,0:T(8,128)(2,1)} %convolution_convert_fusion.1) | data formatting | bytes 2097152 | tf_op jit(solution)/shard_map/reshape | solution.py:135
  65.3 8.3 %scatter.16 = bf16[40,16,64,128]{3,2,1,0:T(8,128)(2,1)} pad(bf16[8,16,64,128]{3,2,1,0:T(8,128)(2,1)} %convert_bitcast_fusion, bf16[]{:T(256)} %constant.236.clone.1), padding=16_16x0_0x0_0x0_0 | pad | bytes 12582914 | tf_op jit(solution)/shard_map/scatter | solution.py:152
  76.6 6.1 %collective-permute-done = bf16[1024,512]{1,0:T(8,128)(2,1)} collective-permute-done((bf16[1024,512]{1,0:T(8,128)(2,1)}, bf16[1024,512]{1,0:T(8,128)(2,1)}, u32[]{:S(2)}, u32[]{:S(2)}) %collective-permute-start) | collective-permute-done | bytes 1048608 | tf_op jit(solution)/shard_map/ppermute | solution.py:20
  82.7 3.8 %bitcast_dynamic-update-slice_fusion.3 = bf16[40,16,64,128]{3,2,1,0:T(8,128)(2,1)} fusion(bf16[40,16,64,128]{3,2,1,0:T(8,128)(2,1)} %scatter.16, bf16[8,128,512,1]{2,1,3,0:T(8,128)(2,1)} %bitcast.10, bf16[16,64,512,1]{2,1,0,3:T(8,128)(2,1)S(1)} %bitcast.65), kind=kOutput, calls=%fused_computation.4 | convolution fusion | flops 1074790400 | bytes 4194304 | tf_op jit(solution)/shard_map/hdc,btc->bhdt/dot_general | solution.py:146
  86.5 19.1 %collective-permute-done.1 = bf16[1024,512]{1,0:T(8,128)(2,1)} collective-permute-done((bf16[1024,512]{1,0:T(8,128)(2,1)}, bf16[1024,512]{1,0:T(8,128)(2,1)}, u32[]{:S(2)}, u32[]{:S(2)}) %collective-permute-start.1) | collective-permute-done | bytes 1048608 | tf_op jit(solution)/shard_map/ppermute | solution.py:20
  105.6 3.8 %bitcast_dynamic-update-slice_fusion.2 = bf16[40,16,64,128]{3,2,1,0:T(8,128)(2,1)} fusion(bf16[40,16,64,128]{3,2,1,0:T(8,128)(2,1)} %bitcast_dynamic-update-slice_fusion.3, bf16[8,128,512,1]{2,1,3,0:T(8,128)(2,1)} %bitcast.16, bf16[16,64,512,1]{2,1,0,3:T(8,128)(2,1)S(1)} %bitcast.66), kind=kOutput, calls=%fused_computation.3 | convolution fusion | flops 1074790400 | bytes 4194304 | tf_op jit(solution)/shard_map/hdc,btc->bhdt/dot_general | solution.py:146
  109.5 3.8 %bitcast_dynamic-update-slice_fusion.1 = bf16[40,16,64,128]{3,2,1,0:T(8,128)(2,1)} fusion(bf16[40,16,64,128]{3,2,1,0:T(8,128)(2,1)} %bitcast_dynamic-update-slice_fusion.2, bf16[8,128,512,1]{2,1,3,0:T(8,128)(2,1)} %bitcast.20, bf16[16,64,512,1]{2,1,0,3:T(8,128)(2,1)S(1)} %bitcast.67), kind=kOutput, calls=%fused_computation.2 | convolution fusion | flops 1074790400 | bytes 4194304 | tf_op jit(solution)/shard_map/hdc,btc->bhdt/dot_general | solution.py:146
  113.3 3.9 %bitcast_dynamic-update-slice_fusion.kvt_ref = bf16[40,16,64,128]{3,2,1,0:T(8,128)(2,1)} fusion(bf16[40,16,64,128]{3,2,1,0:T(8,128)(2,1)} %bitcast_dynamic-update-slice_fusion.1, bf16[8,128,512,1]{2,1,3,0:T(8,128)(2,1)} %bitcast.24, bf16[16,64,512,1]{2,1,0,3:T(8,128)(2,1)S(1)} %bitcast.68), kind=kOutput, calls=%fused_computation.1 | convolution fusion | flops 1074790400 | bytes 4194304 | tf_op jit(solution)/shard_map/hdc,btc->bhdt/dot_general | solution.py:146
  117.2 1.9 %fusion.bkvt_ref = bf16[16,64,512]{2,1,0:T(8,128)(2,1)} fusion(bf16[16,64,512]{2,1,0:T(8,128)(2,1)S(1)} %bitcast.69, bf16[512,512]{1,0:T(8,128)(2,1)S(1)} %collective-permute-done.12, bf16[512,512]{1,0:T(8,128)(2,1)S(1)} %broadcast_select_fusion, pred[512]{0:T(512)(128)(4,1)S(1)} %get-tuple-element.65), kind=kOutput, calls=%fused_computation.9 | convolution fusion | flops 537657344 | bytes 3146240 | tf_op jit(solution)/shard_map/hdc,nc->hdn/dot_general | solution.py:154
  119.1 35.5 %shard_map.73 = bf16[8,128,512]{2,1,0:T(8,128)(2,1)} custom-call(s32[96]{0:T(128)} %reshape.207.rel_ref, s32[8]{0:T(128)} %cnt_ref.1, bf16[8,8,128,64]{3,2,1,0:T(8,128)(2,1)} %bitcast.63, bf16[40,16,64,128]{3,2,1,0:T(8,128)(2,1)} %bitcast_dynamic-update-slice_fusion.kvt_ref, bf16[16,64,512]{2,1,0:T(8,128)(2,1)} %fusion.bkvt_ref, bf16[512,512]{1,0:T(8,128)(2,1)} %w_ref.1), custom_call_target="tpu_custom_call" | custom-call | tf_op jit(solution)/shard_map/pallas_call | solution.py:122
  (42 shorter events, 14.0 us)
Async XLA Ops:
  0.0 57.0 %copy-start = (bf16[512,512]{1,0:T(8,128)(2,1)S(1)}, bf16[512,512]{1,0:T(8,128)(2,1)}, u32[]{:S(2)}) copy-start(bf16[512,512]{1,0:T(8,128)(2,1)} %param.18) | copy-start | bytes 1572868
  5.7 16.6 %collective-permute-start.4 = (bf16[128,512]{1,0:T(8,128)(2,1)S(1)}, bf16[128,512]{1,0:T(8,128)(2,1)S(1)}, u32[]{:S(2)}, u32[]{:S(2)}) collective-permute-start(bf16[128,512]{1,0:T(8,128)(2,1)S(1)} %get-tuple-element.74), channel_id=1, source_target_pairs={{0,1},{1,2},{2,3},{3,4},{4,5},{5,6},{6,7},{7,0},{8,9},{9,10},{10,1... | collective-permute-start | bytes 393224 | tf_op jit(solution)/shard_map/ppermute | solution.py:51
  7.7 17.4 %collective-permute-start.5 = (bf16[128,512]{1,0:T(8,128)(2,1)S(1)}, bf16[128,512]{1,0:T(8,128)(2,1)S(1)}, u32[]{:S(2)}, u32[]{:S(2)}) collective-permute-start(bf16[128,512]{1,0:T(8,128)(2,1)S(1)} %get-tuple-element.74), channel_id=1, source_target_pairs={{0,2},{1,3},{2,4},{3,5},{4,6},{5,7},{6,0},{7,1},{8,10},{9,11},{10,... | collective-permute-start | bytes 393224 | tf_op jit(solution)/shard_map/ppermute | solution.py:51
  11.0 21.8 %collective-permute-start.6 = (bf16[128,512]{1,0:T(8,128)(2,1)S(1)}, bf16[128,512]{1,0:T(8,128)(2,1)S(1)}, u32[]{:S(2)}, u32[]{:S(2)}) collective-permute-start(bf16[128,512]{1,0:T(8,128)(2,1)S(1)} %get-tuple-element.74), channel_id=1, source_target_pairs={{0,3},{1,4},{2,5},{3,6},{4,7},{5,0},{6,1},{7,2},{8,11},{9,12},{10,... | collective-permute-start | bytes 393224 | tf_op jit(solution)/shard_map/ppermute | solution.py:51
  15.0 19.7 %collective-permute-start.7 = (bf16[128,512]{1,0:T(8,128)(2,1)S(1)}, bf16[128,512]{1,0:T(8,128)(2,1)S(1)}, u32[]{:S(2)}, u32[]{:S(2)}) collective-permute-start(bf16[128,512]{1,0:T(8,128)(2,1)S(1)} %get-tuple-element.74), channel_id=1, source_target_pairs={{0,4},{1,5},{2,6},{3,7},{4,0},{5,1},{6,2},{7,3},{8,12},{9,13},{10,... | collective-permute-start | bytes 393224 | tf_op jit(solution)/shard_map/ppermute | solution.py:51
  15.5 24.4 %collective-permute-start.8 = (bf16[128,512]{1,0:T(8,128)(2,1)S(1)}, bf16[128,512]{1,0:T(8,128)(2,1)S(1)}, u32[]{:S(2)}, u32[]{:S(2)}) collective-permute-start(bf16[128,512]{1,0:T(8,128)(2,1)S(1)} %get-tuple-element.74), channel_id=1, source_target_pairs={{0,5},{1,6},{2,7},{3,0},{4,1},{5,2},{6,3},{7,4},{8,13},{9,14},{10,... | collective-permute-start | bytes 393224 | tf_op jit(solution)/shard_map/ppermute | solution.py:51
  22.3 34.7 %copy-start.1 = (bf16[512,1024]{0,1:T(8,128)(2,1)}, bf16[512,1024]{0,1:T(8,128)(2,1)S(1)}, u32[]{:S(2)}) copy-start(bf16[512,1024]{0,1:T(8,128)(2,1)S(1)} %copy.14) | copy-start | bytes 3145732
  22.3 23.1 %collective-permute-start.9 = (bf16[128,512]{1,0:T(8,128)(2,1)S(1)}, bf16[128,512]{1,0:T(8,128)(2,1)S(1)}, u32[]{:S(2)}, u32[]{:S(2)}) collective-permute-start(bf16[128,512]{1,0:T(8,128)(2,1)S(1)} %get-tuple-element.74), channel_id=1, source_target_pairs={{0,6},{1,7},{2,0},{3,1},{4,2},{5,3},{6,4},{7,5},{8,14},{9,15},{10,... | collective-permute-start | bytes 393224 | tf_op jit(solution)/shard_map/ppermute | solution.py:51
  25.1 23.8 %collective-permute-start.10 = (bf16[128,512]{1,0:T(8,128)(2,1)S(1)}, bf16[128,512]{1,0:T(8,128)(2,1)S(1)}, u32[]{:S(2)}, u32[]{:S(2)}) collective-permute-start(bf16[128,512]{1,0:T(8,128)(2,1)S(1)} %get-tuple-element.74), channel_id=1, source_target_pairs={{0,7},{1,0},{2,1},{3,2},{4,3},{5,4},{6,5},{7,6},{8,15},{9,8},{10,9... | collective-permute-start | bytes 393224 | tf_op jit(solution)/shard_map/ppermute | solution.py:51
  32.8 49.9 %collective-permute-start = (bf16[1024,512]{1,0:T(8,128)(2,1)}, bf16[1024,512]{1,0:T(8,128)(2,1)}, u32[]{:S(2)}, u32[]{:S(2)}) collective-permute-start(bf16[1024,512]{1,0:T(8,128)(2,1)} %param.17), channel_id=1, source_target_pairs={{0,2},{1,3},{2,4},{3,5},{4,6},{5,7},{6,8},{7,9},{8,10},{9,11},{10,... | collective-permute-start | bytes 3145736 | tf_op jit(solution)/shard_map/ppermute | solution.py:20
  34.7 70.9 %collective-permute-start.1 = (bf16[1024,512]{1,0:T(8,128)(2,1)}, bf16[1024,512]{1,0:T(8,128)(2,1)}, u32[]{:S(2)}, u32[]{:S(2)}) collective-permute-start(bf16[1024,512]{1,0:T(8,128)(2,1)} %param.17), channel_id=1, source_target_pairs={{0,1},{1,2},{2,3},{3,4},{4,5},{5,6},{6,7},{7,8},{8,9},{9,10},{10,1... | collective-permute-start | bytes 3145736 | tf_op jit(solution)/shard_map/ppermute | solution.py:20
  39.9 69.5 %collective-permute-start.2 = (bf16[1024,512]{1,0:T(8,128)(2,1)}, bf16[1024,512]{1,0:T(8,128)(2,1)}, u32[]{:S(2)}, u32[]{:S(2)}) collective-permute-start(bf16[1024,512]{1,0:T(8,128)(2,1)} %param.17), channel_id=1, source_target_pairs={{1,0},{2,1},{3,2},{4,3},{5,4},{6,5},{7,6},{8,7},{9,8},{10,9},{11,1... | collective-permute-start | bytes 3145736 | tf_op jit(solution)/shard_map/ppermute | solution.py:20
  45.5 67.9 %collective-permute-start.3 = (bf16[1024,512]{1,0:T(8,128)(2,1)}, bf16[1024,512]{1,0:T(8,128)(2,1)}, u32[]{:S(2)}, u32[]{:S(2)}) collective-permute-start(bf16[1024,512]{1,0:T(8,128)(2,1)} %param.17), channel_id=1, source_target_pairs={{2,0},{3,1},{4,2},{5,3},{6,4},{7,5},{8,6},{9,7},{10,8},{11,9},{12,... | collective-permute-start | bytes 3145736 | tf_op jit(solution)/shard_map/ppermute | solution.py:20
  51.9 21.7 %collective-permute-start.11 = (bf16[512,512]{1,0:T(8,128)(2,1)}, bf16[512,512]{1,0:T(8,128)(2,1)}, u32[]{:S(2)}, u32[]{:S(2)}) collective-permute-start(bf16[512,512]{1,0:T(8,128)(2,1)} %select_select_fusion), channel_id=1, source_target_pairs={{0,8},{1,9},{2,10},{3,11},{4,12},{5,13},{6,14},{7,15},{8,0},{9,1},... | collective-permute-start | bytes 1572872 | tf_op jit(solution)/shard_map/ppermute | solution.py:27
  53.2 6.7 %copy-start.3 = (s32[8,12]{1,0:T(8,128)S(1)}, s32[8,12]{1,0:T(8,128)}, u32[]{:S(2)}) copy-start(s32[8,12]{1,0:T(8,128)} %param.21) | copy-start | bytes 1156
  65.3 17.4 %copy-start.2 = (bf16[512,1024]{0,1:T(8,128)(2,1)S(1)}, bf16[512,1024]{0,1:T(8,128)(2,1)}, u32[]{:S(2)}) copy-start(bf16[512,1024]{0,1:T(8,128)(2,1)} %copy-done.1) | copy-start | bytes 3145732
  74.9 42.3 %collective-permute-start.12 = (bf16[512,512]{1,0:T(8,128)(2,1)S(1)}, bf16[512,512]{1,0:T(8,128)(2,1)S(1)}, u32[]{:S(2)}, u32[]{:S(2)}) collective-permute-start(bf16[512,512]{1,0:T(8,128)(2,1)S(1)} %broadcast_select_fusion), channel_id=1, source_target_pairs={{0,16},{1,17},{2,18},{3,19},{4,20},{5,21},{6,22},{7,23},{8,24},{9,... | collective-permute-start | bytes 1572872 | tf_op jit(solution)/shard_map/ppermute | solution.py:27

commit v12 on v11

--- a/solution.py
+++ b/solution.py
@@ -140,6 +140,11 @@
         else:
             pieces.append(from_behind(tokens, "curve", -offset))
     kv_w = w_keyval.reshape(width, 2 * HEADS, head_dim).transpose(1, 2, 0)
+    gathered = boundary_rows(tokens, bnd_ids, member)
+    bkvt = jnp.einsum(
+        "hdc,nc->hdn", kv_w, gathered, preferred_element_type=jnp.float32
+    ).astype(jnp.bfloat16)
+    bkvt, pieces[0] = lax.optimization_barrier((bkvt, pieces[0]))
     kvt = jnp.zeros((5 * nblocks, 2 * HEADS, head_dim, BLOCK), jnp.bfloat16)
     for index in (2, 0, 1, 3, 4):
         piece = pieces[index]
@@ -150,10 +155,6 @@
             preferred_element_type=jnp.float32,
         ).astype(jnp.bfloat16)
         kvt = kvt.at[index * nblocks : (index + 1) * nblocks].set(part)
-    gathered = boundary_rows(tokens, bnd_ids, member)
-    bkvt = jnp.einsum(
-        "hdc,nc->hdn", kv_w, gathered, preferred_element_type=jnp.float32
-    ).astype(jnp.bfloat16)
     first_block = (member - 2) * nblocks
     rel = jnp.clip(block_list - first_block, 0, 5 * nblocks - 1).reshape(-1).astype(jnp.int32)
     mixed = attention(rel, block_count.astype(jnp.int32), queries, kvt, bkvt, w_out)

time: 157 us -> 171 us (1.089)
  waiting for transfers between devices: 30.6 us -> 43.1 us
  Pallas kernels: 35.5 us -> 37.6 us
    ppermute x2, waiting for transfers between devices: 0.01 us -> 16.4 us  [share_rows(): other = lax.ppermute(rows, 'curve', pairs)]
    ppermute x4, waiting for transfers between devices: 25.2 us -> 13.1 us  [from_behind(): lax.ppermute(value, axis, [(source, source + steps) for source in range(f...]
    ppermute x7, waiting for transfers between devices: 5.41 us -> 13.6 us  [boundary_rows(): pieces.append(lax.ppermute(compact, 'curve', pairs))]
    pallas_call x1, Pallas kernels: 35.5 us -> 37.6 us  [attention(): pl.pallas_call(attention_kernel, grid_spec=grid_spec, out_shape=jax.Shape...]
  transfers between devices with their start and end apart: 13 -> 13, of which waited for: 3 -> 7; matrix products, arithmetic and copies ran while one was open for 27% -> 22% of each run, Pallas kernels for 0% -> 0%
where the time goes in v12:
time: 171 us; the launch traced here: 169 us
  waiting for transfers between devices  43.1 us (25%)
  starting transfers between devices  38.4 us (22%)
  Pallas kernels  37.6 us (22%)
  matrix products  26.8 us (16%)
  local copies, waits for them, and re-layouts  16.2 us (9%)
  other arithmetic  4.76 us (3%)
  between operations  2.14 us (1%)
    pallas_call x1, Pallas kernels, attention(): pl.pallas_call(attention_kernel, grid_spec=grid_spec, out_shape=jax.Shape...  37.6 us
    ppermute x7, starting transfers between devices, boundary_rows(): pieces.append(lax.ppermute(compact, 'curve', pairs))  20.3 us
    dot_general x5, matrix products, on_device(): jnp.einsum('hdc,btc->bhdt', kv_w, piece.reshape(nblocks, BLOCK, width), p...  19.3 us
    ppermute x2, waiting for transfers between devices, share_rows(): other = lax.ppermute(rows, 'curve', pairs)  16.4 us
    ppermute x4, starting transfers between devices, from_behind(): lax.ppermute(value, axis, [(source, source + steps) for source in range(f...  15.7 us
    ppermute x7, waiting for transfers between devices, boundary_rows(): pieces.append(lax.ppermute(compact, 'curve', pairs))  13.6 us
    ppermute x4, waiting for transfers between devices, from_behind(): lax.ppermute(value, axis, [(source, source + steps) for source in range(f...  13.1 us
    scatter x1, local copies, waits for them, and re-layouts, on_device(): kvt = kvt.at[index * nblocks:(index + 1) * nblocks].set(part)  8.3 us
  transfers between devices with their start and end apart: 13, of which 7 were waited for; matrix products, arithmetic and copies ran while one was open for 22% of the time, Pallas kernels for 0%

profile of v12, /device:TPU:18, one launch (start us, length us, event | category | flops | bytes accessed | tf_op | source)
XLA Modules:
  0.0 169.0 jit_solution(9660287304520352432)
XLA Ops:
  7.8 3.3 %collective-permute-start.1 = (bf16[128,512]{1,0:T(8,128)(2,1)S(1)}, bf16[128,512]{1,0:T(8,128)(2,1)S(1)}, u32[]{:S(2)}, u32[]{:S(2)}) collective-permute-start(bf16[128,512]{1,0:T(8,128)(2,1)S(1)} %get-tuple-element.78), channel_id=1, source_target_pairs={{0,2},{1,3},{2,4},{3,5},{4,6},{5,7},{6,0},{7,1},{8,10},{9,11},{10,... | collective-permute-start | bytes 393224 | tf_op jit(solution)/shard_map/ppermute | solution.py:51
  11.0 4.0 %collective-permute-start.2 = (bf16[128,512]{1,0:T(8,128)(2,1)S(1)}, bf16[128,512]{1,0:T(8,128)(2,1)S(1)}, u32[]{:S(2)}, u32[]{:S(2)}) collective-permute-start(bf16[128,512]{1,0:T(8,128)(2,1)S(1)} %get-tuple-element.78), channel_id=1, source_target_pairs={{0,3},{1,4},{2,5},{3,6},{4,7},{5,0},{6,1},{7,2},{8,11},{9,12},{10,... | collective-permute-start | bytes 393224 | tf_op jit(solution)/shard_map/ppermute | solution.py:51
  15.6 4.9 %collective-permute-start.4 = (bf16[128,512]{1,0:T(8,128)(2,1)S(1)}, bf16[128,512]{1,0:T(8,128)(2,1)S(1)}, u32[]{:S(2)}, u32[]{:S(2)}) collective-permute-start(bf16[128,512]{1,0:T(8,128)(2,1)S(1)} %get-tuple-element.78), channel_id=1, source_target_pairs={{0,5},{1,6},{2,7},{3,0},{4,1},{5,2},{6,3},{7,4},{8,13},{9,14},{10,... | collective-permute-start | bytes 393224 | tf_op jit(solution)/shard_map/ppermute | solution.py:51
  20.9 2.7 %collective-permute-start.5 = (bf16[128,512]{1,0:T(8,128)(2,1)S(1)}, bf16[128,512]{1,0:T(8,128)(2,1)S(1)}, u32[]{:S(2)}, u32[]{:S(2)}) collective-permute-start(bf16[128,512]{1,0:T(8,128)(2,1)S(1)} %get-tuple-element.78), channel_id=1, source_target_pairs={{0,6},{1,7},{2,0},{3,1},{4,2},{5,3},{6,4},{7,5},{8,14},{9,15},{10,... | collective-permute-start | bytes 393224 | tf_op jit(solution)/shard_map/ppermute | solution.py:51
  24.6 2.8 %collective-permute-start.6 = (bf16[128,512]{1,0:T(8,128)(2,1)S(1)}, bf16[128,512]{1,0:T(8,128)(2,1)S(1)}, u32[]{:S(2)}, u32[]{:S(2)}) collective-permute-start(bf16[128,512]{1,0:T(8,128)(2,1)S(1)} %get-tuple-element.78), channel_id=1, source_target_pairs={{0,7},{1,0},{2,1},{3,2},{4,3},{5,4},{6,5},{7,6},{8,15},{9,8},{10,9... | collective-permute-start | bytes 393224 | tf_op jit(solution)/shard_map/ppermute | solution.py:51
  27.5 5.4 %collective-permute-done.2 = bf16[128,512]{1,0:T(8,128)(2,1)S(1)} collective-permute-done((bf16[128,512]{1,0:T(8,128)(2,1)S(1)}, bf16[128,512]{1,0:T(8,128)(2,1)S(1)}, u32[]{:S(2)}, u32[]{:S(2)}) %collective-permute-start.2) | collective-permute-done | bytes 131104 | tf_op jit(solution)/shard_map/ppermute | solution.py:51
  32.9 3.7 %collective-permute-done.4 = bf16[128,512]{1,0:T(8,128)(2,1)S(1)} collective-permute-done((bf16[128,512]{1,0:T(8,128)(2,1)S(1)}, bf16[128,512]{1,0:T(8,128)(2,1)S(1)}, u32[]{:S(2)}, u32[]{:S(2)}) %collective-permute-start.4) | collective-permute-done | bytes 131104 | tf_op jit(solution)/shard_map/ppermute | solution.py:51
  36.6 2.3 %collective-permute-done.5 = bf16[128,512]{1,0:T(8,128)(2,1)S(1)} collective-permute-done((bf16[128,512]{1,0:T(8,128)(2,1)S(1)}, bf16[128,512]{1,0:T(8,128)(2,1)S(1)}, u32[]{:S(2)}, u32[]{:S(2)}) %collective-permute-start.5) | collective-permute-done | bytes 131104 | tf_op jit(solution)/shard_map/ppermute | solution.py:51
  44.4 4.9 %collective-permute-start.9 = (bf16[1024,512]{1,0:T(8,128)(2,1)}, bf16[1024,512]{1,0:T(8,128)(2,1)}, u32[]{:S(2)}, u32[]{:S(2)}) collective-permute-start(bf16[1024,512]{1,0:T(8,128)(2,1)} %param.17), channel_id=1, source_target_pairs={{0,2},{1,3},{2,4},{3,5},{4,6},{5,7},{6,8},{7,9},{8,10},{9,11},{10,... | collective-permute-start | bytes 3145736 | tf_op jit(solution)/shard_map/ppermute | solution.py:20
  49.3 3.1 %collective-permute-start.10 = (bf16[1024,512]{1,0:T(8,128)(2,1)}, bf16[1024,512]{1,0:T(8,128)(2,1)}, u32[]{:S(2)}, u32[]{:S(2)}) collective-permute-start(bf16[1024,512]{1,0:T(8,128)(2,1)} %param.17), channel_id=1, source_target_pairs={{0,1},{1,2},{2,3},{3,4},{4,5},{5,6},{6,7},{7,8},{8,9},{9,10},{10,1... | collective-permute-start | bytes 3145736 | tf_op jit(solution)/shard_map/ppermute | solution.py:20
  52.4 4.9 %collective-permute-start.11 = (bf16[1024,512]{1,0:T(8,128)(2,1)}, bf16[1024,512]{1,0:T(8,128)(2,1)}, u32[]{:S(2)}, u32[]{:S(2)}) collective-permute-start(bf16[1024,512]{1,0:T(8,128)(2,1)} %param.17), channel_id=1, source_target_pairs={{1,0},{2,1},{3,2},{4,3},{5,4},{6,5},{7,6},{8,7},{9,8},{10,9},{11,1... | collective-permute-start | bytes 3145736 | tf_op jit(solution)/shard_map/ppermute | solution.py:20
  57.3 2.9 %collective-permute-start.12 = (bf16[1024,512]{1,0:T(8,128)(2,1)}, bf16[1024,512]{1,0:T(8,128)(2,1)}, u32[]{:S(2)}, u32[]{:S(2)}) collective-permute-start(bf16[1024,512]{1,0:T(8,128)(2,1)} %param.17), channel_id=1, source_target_pairs={{2,0},{3,1},{4,2},{5,3},{6,4},{7,5},{8,6},{9,7},{10,8},{11,9},{12,... | collective-permute-start | bytes 3145736 | tf_op jit(solution)/shard_map/ppermute | solution.py:20
  60.8 16.4 %collective-permute-done.7 = bf16[512,512]{1,0:T(8,128)(2,1)} collective-permute-done((bf16[512,512]{1,0:T(8,128)(2,1)}, bf16[512,512]{1,0:T(8,128)(2,1)}, u32[]{:S(2)}, u32[]{:S(2)}) %collective-permute-start.7) | collective-permute-done | bytes 524320 | tf_op jit(solution)/shard_map/ppermute | solution.py:27
  79.5 3.9 %convert_bitcast_fusion = bf16[8,16,64,128]{3,2,1,0:T(8,128)(2,1)} fusion(bf16[8,128,512,1]{2,1,3,0:T(8,128)(2,1)} %bitcast.3, bf16[16,64,512,1]{2,1,0,3:T(8,128)(2,1)S(1)} %bitcast.64), kind=kOutput, calls=%fused_computation.6 | convolution fusion | flops 1074790400 | bytes 4194304 | tf_op jit(solution)/shard_map/hdc,btc->bhdt/dot_general | solution.py:151
  83.4 2.9 %convolution_convert_fusion.1 = bf16[1024,512]{1,0:T(8,128)(2,1)} fusion(bf16[1024,512]{1,0:T(8,128)(2,1)} %param.17, bf16[512,512]{1,0:T(8,128)(2,1)S(1)} %copy-done), kind=kOutput, calls=%fused_computation.8 | convolution fusion | flops 537395200 | bytes 2621440 | tf_op jit(solution)/shard_map/dot_general | solution.py:134
  86.9 2.8 %reshape.232 = bf16[8,128,8,64]{3,2,1,0:T(8,128)(2,1)S(1)} reshape(bf16[1024,512]{1,0:T(8,128)(2,1)} %convolution_convert_fusion.1) | data formatting | bytes 2097152 | tf_op jit(solution)/shard_map/reshape | solution.py:135
  91.6 8.3 %scatter.16 = bf16[40,16,64,128]{3,2,1,0:T(8,128)(2,1)} pad(bf16[8,16,64,128]{3,2,1,0:T(8,128)(2,1)} %convert_bitcast_fusion, bf16[]{:T(256)} %constant.236.clone.1), padding=16_16x0_0x0_0x0_0 | pad | bytes 12582914 | tf_op jit(solution)/shard_map/scatter | solution.py:157
  99.9 3.0 %fusion.bkvt_ref = bf16[16,64,512]{2,1,0:T(8,128)(2,1)} fusion(bf16[16,64,512]{2,1,0:T(8,128)(2,1)S(1)} %bitcast.65, bf16[512,512]{1,0:T(8,128)(2,1)} %collective-permute-done.8, bf16[512,512]{1,0:T(8,128)(2,1)S(1)} %broadcast_select_fusion, pred[512]{0:T(512)(128)(4,1)S(1)} %get-tuple-element.69), kind=kOutput, calls=%fused_computation.9 | convolution fusion | flops 537657344 | bytes 3146240 | tf_op jit(solution)/shard_map/hdc,nc->hdn/dot_general | solution.py:144
  102.9 3.8 %bitcast_dynamic-update-slice_fusion.3 = bf16[40,16,64,128]{3,2,1,0:T(8,128)(2,1)} fusion(bf16[40,16,64,128]{3,2,1,0:T(8,128)(2,1)} %scatter.16, bf16[8,128,512,1]{2,1,3,0:T(8,128)(2,1)} %bitcast.13, bf16[16,64,512,1]{2,1,0,3:T(8,128)(2,1)S(1)} %bitcast.66), kind=kOutput, calls=%fused_computation.4 | convolution fusion | flops 1074790400 | bytes 4194304 | tf_op jit(solution)/shard_map/hdc,btc->bhdt/dot_general | solution.py:151
  106.7 13.1 %collective-permute-done.10 = bf16[1024,512]{1,0:T(8,128)(2,1)} collective-permute-done((bf16[1024,512]{1,0:T(8,128)(2,1)}, bf16[1024,512]{1,0:T(8,128)(2,1)}, u32[]{:S(2)}, u32[]{:S(2)}) %collective-permute-start.10) | collective-permute-done | bytes 1048608 | tf_op jit(solution)/shard_map/ppermute | solution.py:20
  119.8 3.8 %bitcast_dynamic-update-slice_fusion.2 = bf16[40,16,64,128]{3,2,1,0:T(8,128)(2,1)} fusion(bf16[40,16,64,128]{3,2,1,0:T(8,128)(2,1)} %bitcast_dynamic-update-slice_fusion.3, bf16[8,128,512,1]{2,1,3,0:T(8,128)(2,1)} %bitcast.18, bf16[16,64,512,1]{2,1,0,3:T(8,128)(2,1)S(1)} %bitcast.67), kind=kOutput, calls=%fused_computation.3 | convolution fusion | flops 1074790400 | bytes 4194304 | tf_op jit(solution)/shard_map/hdc,btc->bhdt/dot_general | solution.py:151
  123.6 3.8 %bitcast_dynamic-update-slice_fusion.1 = bf16[40,16,64,128]{3,2,1,0:T(8,128)(2,1)} fusion(bf16[40,16,64,128]{3,2,1,0:T(8,128)(2,1)} %bitcast_dynamic-update-slice_fusion.2, bf16[8,128,512,1]{2,1,3,0:T(8,128)(2,1)} %bitcast.22, bf16[16,64,512,1]{2,1,0,3:T(8,128)(2,1)S(1)} %bitcast.68), kind=kOutput, calls=%fused_computation.2 | convolution fusion | flops 1074790400 | bytes 4194304 | tf_op jit(solution)/shard_map/hdc,btc->bhdt/dot_general | solution.py:151
  127.5 3.9 %bitcast_dynamic-update-slice_fusion.kvt_ref = bf16[40,16,64,128]{3,2,1,0:T(8,128)(2,1)} fusion(bf16[40,16,64,128]{3,2,1,0:T(8,128)(2,1)} %bitcast_dynamic-update-slice_fusion.1, bf16[8,128,512,1]{2,1,3,0:T(8,128)(2,1)} %bitcast.26, bf16[16,64,512,1]{2,1,0,3:T(8,128)(2,1)S(1)} %bitcast.69), kind=kOutput, calls=%fused_computation.1 | convolution fusion | flops 1074790400 | bytes 4194304 | tf_op jit(solution)/shard_map/hdc,btc->bhdt/dot_general | solution.py:151
  131.4 37.6 %shard_map.73 = bf16[8,128,512]{2,1,0:T(8,128)(2,1)} custom-call(s32[96]{0:T(128)} %reshape.207.rel_ref, s32[8]{0:T(128)} %cnt_ref.1, bf16[8,8,128,64]{3,2,1,0:T(8,128)(2,1)} %bitcast.63, bf16[40,16,64,128]{3,2,1,0:T(8,128)(2,1)} %bitcast_dynamic-update-slice_fusion.kvt_ref, bf16[16,64,512]{2,1,0:T(8,128)(2,1)} %fusion.bkvt_ref, bf16[512,512]{1,0:T(8,128)(2,1)} %w_ref.1), custom_call_target="tpu_custom_call" | custom-call | tf_op jit(solution)/shard_map/pallas_call | solution.py:122
  (44 shorter events, 18.6 us)
Async XLA Ops:
  0.0 83.4 %copy-start = (bf16[512,512]{1,0:T(8,128)(2,1)S(1)}, bf16[512,512]{1,0:T(8,128)(2,1)}, u32[]{:S(2)}) copy-start(bf16[512,512]{1,0:T(8,128)(2,1)} %param.18) | copy-start | bytes 1572868
  4.1 56.1 %copy-start.1 = (bf16[512,1024]{1,0:T(8,128)(2,1)S(1)}, bf16[512,1024]{1,0:T(8,128)(2,1)}, u32[]{:S(2)}) copy-start(bf16[512,1024]{1,0:T(8,128)(2,1)} %param.19) | copy-start | bytes 3145732
  5.8 15.1 %collective-permute-start = (bf16[128,512]{1,0:T(8,128)(2,1)S(1)}, bf16[128,512]{1,0:T(8,128)(2,1)S(1)}, u32[]{:S(2)}, u32[]{:S(2)}) collective-permute-start(bf16[128,512]{1,0:T(8,128)(2,1)S(1)} %get-tuple-element.78), channel_id=1, source_target_pairs={{0,1},{1,2},{2,3},{3,4},{4,5},{5,6},{6,7},{7,0},{8,9},{9,10},{10,1... | collective-permute-start | bytes 393224 | tf_op jit(solution)/shard_map/ppermute | solution.py:51
  7.8 16.9 %collective-permute-start.1 = (bf16[128,512]{1,0:T(8,128)(2,1)S(1)}, bf16[128,512]{1,0:T(8,128)(2,1)S(1)}, u32[]{:S(2)}, u32[]{:S(2)}) collective-permute-start(bf16[128,512]{1,0:T(8,128)(2,1)S(1)} %get-tuple-element.78), channel_id=1, source_target_pairs={{0,2},{1,3},{2,4},{3,5},{4,6},{5,7},{6,0},{7,1},{8,10},{9,11},{10,... | collective-permute-start | bytes 393224 | tf_op jit(solution)/shard_map/ppermute | solution.py:51
  11.0 21.8 %collective-permute-start.2 = (bf16[128,512]{1,0:T(8,128)(2,1)S(1)}, bf16[128,512]{1,0:T(8,128)(2,1)S(1)}, u32[]{:S(2)}, u32[]{:S(2)}) collective-permute-start(bf16[128,512]{1,0:T(8,128)(2,1)S(1)} %get-tuple-element.78), channel_id=1, source_target_pairs={{0,3},{1,4},{2,5},{3,6},{4,7},{5,0},{6,1},{7,2},{8,11},{9,12},{10,... | collective-permute-start | bytes 393224 | tf_op jit(solution)/shard_map/ppermute | solution.py:51
  15.1 17.8 %collective-permute-start.3 = (bf16[128,512]{1,0:T(8,128)(2,1)S(1)}, bf16[128,512]{1,0:T(8,128)(2,1)S(1)}, u32[]{:S(2)}, u32[]{:S(2)}) collective-permute-start(bf16[128,512]{1,0:T(8,128)(2,1)S(1)} %get-tuple-element.78), channel_id=1, source_target_pairs={{0,4},{1,5},{2,6},{3,7},{4,0},{5,1},{6,2},{7,3},{8,12},{9,13},{10,... | collective-permute-start | bytes 393224 | tf_op jit(solution)/shard_map/ppermute | solution.py:51
  15.6 21.0 %collective-permute-start.4 = (bf16[128,512]{1,0:T(8,128)(2,1)S(1)}, bf16[128,512]{1,0:T(8,128)(2,1)S(1)}, u32[]{:S(2)}, u32[]{:S(2)}) collective-permute-start(bf16[128,512]{1,0:T(8,128)(2,1)S(1)} %get-tuple-element.78), channel_id=1, source_target_pairs={{0,5},{1,6},{2,7},{3,0},{4,1},{5,2},{6,3},{7,4},{8,13},{9,14},{10,... | collective-permute-start | bytes 393224 | tf_op jit(solution)/shard_map/ppermute | solution.py:51
  20.9 18.0 %collective-permute-start.5 = (bf16[128,512]{1,0:T(8,128)(2,1)S(1)}, bf16[128,512]{1,0:T(8,128)(2,1)S(1)}, u32[]{:S(2)}, u32[]{:S(2)}) collective-permute-start(bf16[128,512]{1,0:T(8,128)(2,1)S(1)} %get-tuple-element.78), channel_id=1, source_target_pairs={{0,6},{1,7},{2,0},{3,1},{4,2},{5,3},{6,4},{7,5},{8,14},{9,15},{10,... | collective-permute-start | bytes 393224 | tf_op jit(solution)/shard_map/ppermute | solution.py:51
  24.6 15.5 %collective-permute-start.6 = (bf16[128,512]{1,0:T(8,128)(2,1)S(1)}, bf16[128,512]{1,0:T(8,128)(2,1)S(1)}, u32[]{:S(2)}, u32[]{:S(2)}) collective-permute-start(bf16[128,512]{1,0:T(8,128)(2,1)S(1)} %get-tuple-element.78), channel_id=1, source_target_pairs={{0,7},{1,0},{2,1},{3,2},{4,3},{5,4},{6,5},{7,6},{8,15},{9,8},{10,9... | collective-permute-start | bytes 393224 | tf_op jit(solution)/shard_map/ppermute | solution.py:51
  43.1 34.0 %collective-permute-start.7 = (bf16[512,512]{1,0:T(8,128)(2,1)}, bf16[512,512]{1,0:T(8,128)(2,1)}, u32[]{:S(2)}, u32[]{:S(2)}) collective-permute-start(bf16[512,512]{1,0:T(8,128)(2,1)} %select_select_fusion), channel_id=1, source_target_pairs={{0,8},{1,9},{2,10},{3,11},{4,12},{5,13},{6,14},{7,15},{8,0},{9,1},... | collective-permute-start | bytes 1572872 | tf_op jit(solution)/shard_map/ppermute | solution.py:27
  44.4 58.5 %collective-permute-start.9 = (bf16[1024,512]{1,0:T(8,128)(2,1)}, bf16[1024,512]{1,0:T(8,128)(2,1)}, u32[]{:S(2)}, u32[]{:S(2)}) collective-permute-start(bf16[1024,512]{1,0:T(8,128)(2,1)} %param.17), channel_id=1, source_target_pairs={{0,2},{1,3},{2,4},{3,5},{4,6},{5,7},{6,8},{7,9},{8,10},{9,11},{10,... | collective-permute-start | bytes 3145736 | tf_op jit(solution)/shard_map/ppermute | solution.py:20
  49.3 70.5 %collective-permute-start.10 = (bf16[1024,512]{1,0:T(8,128)(2,1)}, bf16[1024,512]{1,0:T(8,128)(2,1)}, u32[]{:S(2)}, u32[]{:S(2)}) collective-permute-start(bf16[1024,512]{1,0:T(8,128)(2,1)} %param.17), channel_id=1, source_target_pairs={{0,1},{1,2},{2,3},{3,4},{4,5},{5,6},{6,7},{7,8},{8,9},{9,10},{10,1... | collective-permute-start | bytes 3145736 | tf_op jit(solution)/shard_map/ppermute | solution.py:20
  52.4 71.2 %collective-permute-start.11 = (bf16[1024,512]{1,0:T(8,128)(2,1)}, bf16[1024,512]{1,0:T(8,128)(2,1)}, u32[]{:S(2)}, u32[]{:S(2)}) collective-permute-start(bf16[1024,512]{1,0:T(8,128)(2,1)} %param.17), channel_id=1, source_target_pairs={{1,0},{2,1},{3,2},{4,3},{5,4},{6,5},{7,6},{8,7},{9,8},{10,9},{11,1... | collective-permute-start | bytes 3145736 | tf_op jit(solution)/shard_map/ppermute | solution.py:20
  57.3 70.2 %collective-permute-start.12 = (bf16[1024,512]{1,0:T(8,128)(2,1)}, bf16[1024,512]{1,0:T(8,128)(2,1)}, u32[]{:S(2)}, u32[]{:S(2)}) collective-permute-start(bf16[1024,512]{1,0:T(8,128)(2,1)} %param.17), channel_id=1, source_target_pairs={{2,0},{3,1},{4,2},{5,3},{6,4},{7,5},{8,6},{9,7},{10,8},{11,9},{12,... | collective-permute-start | bytes 3145736 | tf_op jit(solution)/shard_map/ppermute | solution.py:20
  60.7 25.5 %copy-start.2 = (bf16[512,1024]{0,1:T(8,128)(2,1)}, bf16[512,1024]{0,1:T(8,128)(2,1)S(1)}, u32[]{:S(2)}) copy-start(bf16[512,1024]{0,1:T(8,128)(2,1)S(1)} %copy.14) | copy-start | bytes 3145732
  78.5 21.4 %collective-permute-start.8 = (bf16[512,512]{1,0:T(8,128)(2,1)S(1)}, bf16[512,512]{1,0:T(8,128)(2,1)}, u32[]{:S(2)}, u32[]{:S(2)}) collective-permute-start(bf16[512,512]{1,0:T(8,128)(2,1)S(1)} %broadcast_select_fusion), channel_id=1, source_target_pairs={{0,16},{1,17},{2,18},{3,19},{4,20},{5,21},{6,22},{7,23},{8,24},{9,... | collective-permute-start | bytes 1572872 | tf_op jit(solution)/shard_map/ppermute | solution.py:27
  79.5 6.8 %copy-start.4 = (s32[8,12]{1,0:T(8,128)S(1)}, s32[8,12]{1,0:T(8,128)}, u32[]{:S(2)}) copy-start(s32[8,12]{1,0:T(8,128)} %param.21) | copy-start | bytes 1156
  91.6 8.3 %copy-start.3 = (bf16[512,1024]{0,1:T(8,128)(2,1)S(1)}, bf16[512,1024]{0,1:T(8,128)(2,1)}, u32[]{:S(2)}) copy-start(bf16[512,1024]{0,1:T(8,128)(2,1)} %copy-done.2) | copy-start | bytes 3145732

commit v13 on v12

--- a/solution.py
+++ b/solution.py
@@ -144,7 +144,7 @@
     bkvt = jnp.einsum(
         "hdc,nc->hdn", kv_w, gathered, preferred_element_type=jnp.float32
     ).astype(jnp.bfloat16)
-    bkvt, pieces[0] = lax.optimization_barrier((bkvt, pieces[0]))
+    bkvt, pieces[3] = lax.optimization_barrier((bkvt, pieces[3]))
     kvt = jnp.zeros((5 * nblocks, 2 * HEADS, head_dim, BLOCK), jnp.bfloat16)
     for index in (2, 0, 1, 3, 4):
         piece = pieces[index]

time: 171 us -> 164 us (0.959)
  waiting for transfers between devices: 43.1 us -> 39.7 us
  matrix products: 26.8 us -> 24.6 us
  starting transfers between devices: 38.4 us -> 36.4 us
    ppermute x4, waiting for transfers between devices: 13.1 us -> 33.4 us  [from_behind(): lax.ppermute(value, axis, [(source, source + steps) for source in range(f...]
    ppermute x2, waiting for transfers between devices: 16.4 us -> 2.32 us  [share_rows(): other = lax.ppermute(rows, 'curve', pairs)]
    ppermute x7, waiting for transfers between devices: 13.6 us -> 3.91 us  [boundary_rows(): pieces.append(lax.ppermute(compact, 'curve', pairs))]
    ppermute x7, starting transfers between devices: 20.3 us -> 18.5 us  [boundary_rows(): pieces.append(lax.ppermute(compact, 'curve', pairs))]
  transfers between devices with their start and end apart: 13 -> 13, of which waited for: 7 -> 4; matrix products, arithmetic and copies ran while one was open for 22% -> 23% of each run, Pallas kernels for 0% -> 0%
where the time goes in v13:
time: 164 us; the launch traced here: 161 us
  waiting for transfers between devices  39.7 us (24%)
  Pallas kernels  37.6 us (23%)
  starting transfers between devices  36.4 us (22%)
  matrix products  24.6 us (15%)
  local copies, waits for them, and re-layouts  15.6 us (10%)
  other arithmetic  4.94 us (3%)
  between operations  2.18 us (1%)
    pallas_call x1, Pallas kernels, attention(): pl.pallas_call(attention_kernel, grid_spec=grid_spec, out_shape=jax.Shape...  37.6 us
    ppermute x4, waiting for transfers between devices, from_behind(): lax.ppermute(value, axis, [(source, source + steps) for source in range(f...  33.4 us
    ppermute x7, starting transfers between devices, boundary_rows(): pieces.append(lax.ppermute(compact, 'curve', pairs))  18.5 us
    dot_general x5, matrix products, on_device(): jnp.einsum('hdc,btc->bhdt', kv_w, piece.reshape(nblocks, BLOCK, width), p...  18.2 us
    ppermute x4, starting transfers between devices, from_behind(): lax.ppermute(value, axis, [(source, source + steps) for source in range(f...  15.9 us
    scatter x1, local copies, waits for them, and re-layouts, on_device(): kvt = kvt.at[index * nblocks:(index + 1) * nblocks].set(part)  6.85 us
    reshape x2, local copies, waits for them, and re-layouts, on_device(): queries.reshape(nblocks, BLOCK, HEADS, head_dim).transpose(0, 2, 1, 3)  4.69 us
    ppermute x7, waiting for transfers between devices, boundary_rows(): pieces.append(lax.ppermute(compact, 'curve', pairs))  3.91 us
  transfers between devices with their start and end apart: 13, of which 4 were waited for; matrix products, arithmetic and copies ran while one was open for 23% of the time, Pallas kernels for 0%

profile of v13, /device:TPU:18, one launch (start us, length us, event | category | flops | bytes accessed | tf_op | source)
XLA Modules:
  0.0 161.0 jit_solution(3379818232224752111)
XLA Ops:
  5.7 2.0 %collective-permute-start.2 = (bf16[128,512]{1,0:T(8,128)(2,1)S(1)}, bf16[128,512]{1,0:T(8,128)(2,1)S(1)}, u32[]{:S(2)}, u32[]{:S(2)}) collective-permute-start(bf16[128,512]{1,0:T(8,128)(2,1)S(1)} %get-tuple-element.78), channel_id=1, source_target_pairs={{0,1},{1,2},{2,3},{3,4},{4,5},{5,6},{6,7},{7,0},{8,9},{9,10},{10,1... | collective-permute-start | bytes 393224 | tf_op jit(solution)/shard_map/ppermute | solution.py:51
  7.7 3.3 %collective-permute-start.3 = (bf16[128,512]{1,0:T(8,128)(2,1)S(1)}, bf16[128,512]{1,0:T(8,128)(2,1)S(1)}, u32[]{:S(2)}, u32[]{:S(2)}) collective-permute-start(bf16[128,512]{1,0:T(8,128)(2,1)S(1)} %get-tuple-element.78), channel_id=1, source_target_pairs={{0,2},{1,3},{2,4},{3,5},{4,6},{5,7},{6,0},{7,1},{8,10},{9,11},{10,... | collective-permute-start | bytes 393224 | tf_op jit(solution)/shard_map/ppermute | solution.py:51
  11.0 4.0 %collective-permute-start.4 = (bf16[128,512]{1,0:T(8,128)(2,1)S(1)}, bf16[128,512]{1,0:T(8,128)(2,1)S(1)}, u32[]{:S(2)}, u32[]{:S(2)}) collective-permute-start(bf16[128,512]{1,0:T(8,128)(2,1)S(1)} %get-tuple-element.78), channel_id=1, source_target_pairs={{0,3},{1,4},{2,5},{3,6},{4,7},{5,0},{6,1},{7,2},{8,11},{9,12},{10,... | collective-permute-start | bytes 393224 | tf_op jit(solution)/shard_map/ppermute | solution.py:51
  15.6 4.9 %collective-permute-start.6 = (bf16[128,512]{1,0:T(8,128)(2,1)S(1)}, bf16[128,512]{1,0:T(8,128)(2,1)S(1)}, u32[]{:S(2)}, u32[]{:S(2)}) collective-permute-start(bf16[128,512]{1,0:T(8,128)(2,1)S(1)} %get-tuple-element.78), channel_id=1, source_target_pairs={{0,5},{1,6},{2,7},{3,0},{4,1},{5,2},{6,3},{7,4},{8,13},{9,14},{10,... | collective-permute-start | bytes 393224 | tf_op jit(solution)/shard_map/ppermute | solution.py:51
  20.8 2.9 %convolution_convert_fusion.1 = bf16[1024,512]{1,0:T(8,128)(2,1)} fusion(bf16[1024,512]{1,0:T(8,128)(2,1)} %param.17, bf16[512,512]{1,0:T(8,128)(2,1)S(1)} %copy-done), kind=kOutput, calls=%fused_computation.8 | convolution fusion | flops 537395200 | bytes 2621440 | tf_op jit(solution)/shard_map/dot_general | solution.py:134
  25.1 2.7 %collective-permute-start.7 = (bf16[128,512]{1,0:T(8,128)(2,1)S(1)}, bf16[128,512]{1,0:T(8,128)(2,1)S(1)}, u32[]{:S(2)}, u32[]{:S(2)}) collective-permute-start(bf16[128,512]{1,0:T(8,128)(2,1)S(1)} %get-tuple-element.78), channel_id=1, source_target_pairs={{0,6},{1,7},{2,0},{3,1},{4,2},{5,3},{6,4},{7,5},{8,14},{9,15},{10,... | collective-permute-start | bytes 393224 | tf_op jit(solution)/shard_map/ppermute | solution.py:51
  28.9 3.9 %collective-permute-done.4 = bf16[128,512]{1,0:T(8,128)(2,1)S(1)} collective-permute-done((bf16[128,512]{1,0:T(8,128)(2,1)S(1)}, bf16[128,512]{1,0:T(8,128)(2,1)S(1)}, u32[]{:S(2)}, u32[]{:S(2)}) %collective-permute-start.4) | collective-permute-done | bytes 131104 | tf_op jit(solution)/shard_map/ppermute | solution.py:51
  32.8 1.9 %collective-permute-start.11 = (bf16[1024,512]{1,0:T(8,128)(2,1)}, bf16[1024,512]{1,0:T(8,128)(2,1)}, u32[]{:S(2)}, u32[]{:S(2)}) collective-permute-start(bf16[1024,512]{1,0:T(8,128)(2,1)} %param.17), channel_id=1, source_target_pairs={{1,0},{2,1},{3,2},{4,3},{5,4},{6,5},{7,6},{8,7},{9,8},{10,9},{11,1... | collective-permute-start | bytes 3145736 | tf_op jit(solution)/shard_map/ppermute | solution.py:20
  34.8 6.4 %collective-permute-start = (bf16[1024,512]{1,0:T(8,128)(2,1)}, bf16[1024,512]{1,0:T(8,128)(2,1)}, u32[]{:S(2)}, u32[]{:S(2)}) collective-permute-start(bf16[1024,512]{1,0:T(8,128)(2,1)} %param.17), channel_id=1, source_target_pairs={{0,2},{1,3},{2,4},{3,5},{4,6},{5,7},{6,8},{7,9},{8,10},{9,11},{10,... | collective-permute-start | bytes 3145736 | tf_op jit(solution)/shard_map/ppermute | solution.py:20
  41.2 1.9 %collective-permute-start.1 = (bf16[1024,512]{1,0:T(8,128)(2,1)}, bf16[1024,512]{1,0:T(8,128)(2,1)}, u32[]{:S(2)}, u32[]{:S(2)}) collective-permute-start(bf16[1024,512]{1,0:T(8,128)(2,1)} %param.17), channel_id=1, source_target_pairs={{0,1},{1,2},{2,3},{3,4},{4,5},{5,6},{6,7},{7,8},{8,9},{9,10},{10,1... | collective-permute-start | bytes 3145736 | tf_op jit(solution)/shard_map/ppermute | solution.py:20
  43.1 5.7 %collective-permute-start.12 = (bf16[1024,512]{1,0:T(8,128)(2,1)}, bf16[1024,512]{1,0:T(8,128)(2,1)}, u32[]{:S(2)}, u32[]{:S(2)}) collective-permute-start(bf16[1024,512]{1,0:T(8,128)(2,1)} %param.17), channel_id=1, source_target_pairs={{2,0},{3,1},{4,2},{5,3},{6,4},{7,5},{8,6},{9,7},{10,8},{11,9},{12,... | collective-permute-start | bytes 3145736 | tf_op jit(solution)/shard_map/ppermute | solution.py:20
  48.9 2.0 %gather_fusion = bf16[512,512]{1,0:T(8,128)(2,1)S(1)} fusion(bf16[1024,512]{1,0:T(8,128)(2,1)S(1)} %constant_dynamic-update-slice_fusion, s32[1024]{0:T(1024)S(1)} %pad_clamp_fusion), kind=kCustom, calls=%fused_computation | custom fusion | bytes 1050624 | tf_op jit(solution)/shard_map/jit(_take)/gather | solution.py:57
  54.1 2.8 %reshape.232 = bf16[8,128,8,64]{3,2,1,0:T(8,128)(2,1)S(1)} reshape(bf16[1024,512]{1,0:T(8,128)(2,1)} %convolution_convert_fusion.1) | data formatting | bytes 2097152 | tf_op jit(solution)/shard_map/reshape | solution.py:135
  56.9 1.9 %copy.23 = bf16[8,128,8,64]{3,1,2,0:T(8,128)(2,1)} copy(bf16[8,128,8,64]{3,2,1,0:T(8,128)(2,1)S(1)} %reshape.232) | data formatting | bytes 2097152 | tf_op jit(solution)/shard_map/reshape | solution.py:135
  58.8 2.5 %convert_bitcast_fusion = bf16[8,16,64,128]{3,2,1,0:T(8,128)(2,1)S(1)} fusion(bf16[8,128,512,1]{2,1,3,0:T(8,128)(2,1)} %bitcast.3, bf16[16,64,512,1]{2,1,0,3:T(8,128)(2,1)S(1)} %bitcast.65), kind=kOutput, calls=%fused_computation.6 | convolution fusion | flops 1074790400 | bytes 4194304 | tf_op jit(solution)/shard_map/hdc,btc->bhdt/dot_general | solution.py:151
  61.3 6.8 %scatter.16 = bf16[40,16,64,128]{3,2,1,0:T(8,128)(2,1)} pad(bf16[8,16,64,128]{3,2,1,0:T(8,128)(2,1)S(1)} %convert_bitcast_fusion, bf16[]{:T(256)} %constant.236.clone.1), padding=16_16x0_0x0_0x0_0 | pad | bytes 12582914 | tf_op jit(solution)/shard_map/scatter | solution.py:157
  70.0 13.3 %collective-permute-done = bf16[1024,512]{1,0:T(8,128)(2,1)} collective-permute-done((bf16[1024,512]{1,0:T(8,128)(2,1)}, bf16[1024,512]{1,0:T(8,128)(2,1)}, u32[]{:S(2)}, u32[]{:S(2)}) %collective-permute-start) | collective-permute-done | bytes 1048608 | tf_op jit(solution)/shard_map/ppermute | solution.py:20
  83.2 4.2 %bitcast_dynamic-update-slice_fusion.3 = bf16[40,16,64,128]{3,2,1,0:T(8,128)(2,1)} fusion(bf16[40,16,64,128]{3,2,1,0:T(8,128)(2,1)} %scatter.16, bf16[8,128,512,1]{2,1,3,0:T(8,128)(2,1)} %bitcast.10, bf16[16,64,512,1]{2,1,0,3:T(8,128)(2,1)} %bitcast.64), kind=kOutput, calls=%fused_computation.4 | convolution fusion | flops 1074790400 | bytes 4194304 | tf_op jit(solution)/shard_map/hdc,btc->bhdt/dot_general | solution.py:151
  87.4 20.2 %collective-permute-done.1 = bf16[1024,512]{1,0:T(8,128)(2,1)} collective-permute-done((bf16[1024,512]{1,0:T(8,128)(2,1)}, bf16[1024,512]{1,0:T(8,128)(2,1)}, u32[]{:S(2)}, u32[]{:S(2)}) %collective-permute-start.1) | collective-permute-done | bytes 1048608 | tf_op jit(solution)/shard_map/ppermute | solution.py:20
  107.6 3.8 %bitcast_dynamic-update-slice_fusion.2 = bf16[40,16,64,128]{3,2,1,0:T(8,128)(2,1)} fusion(bf16[40,16,64,128]{3,2,1,0:T(8,128)(2,1)} %bitcast_dynamic-update-slice_fusion.3, bf16[8,128,512,1]{2,1,3,0:T(8,128)(2,1)} %bitcast.16, bf16[16,64,512,1]{2,1,0,3:T(8,128)(2,1)S(1)} %bitcast.66), kind=kOutput, calls=%fused_computation.3 | convolution fusion | flops 1074790400 | bytes 4194304 | tf_op jit(solution)/shard_map/hdc,btc->bhdt/dot_general | solution.py:151
  111.4 2.3 %collective-permute-done.10 = bf16[512,512]{1,0:T(8,128)(2,1)S(1)} collective-permute-done((bf16[512,512]{1,0:T(8,128)(2,1)S(1)}, bf16[512,512]{1,0:T(8,128)(2,1)S(1)}, u32[]{:S(2)}, u32[]{:S(2)}) %collective-permute-start.10) | collective-permute-done | bytes 524320 | tf_op jit(solution)/shard_map/ppermute | solution.py:27
  115.6 3.9 %bitcast_dynamic-update-slice_fusion.1 = bf16[40,16,64,128]{3,2,1,0:T(8,128)(2,1)} fusion(bf16[40,16,64,128]{3,2,1,0:T(8,128)(2,1)} %bitcast_dynamic-update-slice_fusion.2, bf16[8,128,512,1]{2,1,3,0:T(8,128)(2,1)} %bitcast.22, bf16[16,64,512,1]{2,1,0,3:T(8,128)(2,1)S(1)} %bitcast.68), kind=kOutput, calls=%fused_computation.2 | convolution fusion | flops 1074790400 | bytes 4194304 | tf_op jit(solution)/shard_map/hdc,btc->bhdt/dot_general | solution.py:151
  119.5 3.9 %bitcast_dynamic-update-slice_fusion.kvt_ref = bf16[40,16,64,128]{3,2,1,0:T(8,128)(2,1)} fusion(bf16[40,16,64,128]{3,2,1,0:T(8,128)(2,1)} %bitcast_dynamic-update-slice_fusion.1, bf16[8,128,512,1]{2,1,3,0:T(8,128)(2,1)} %bitcast.26, bf16[16,64,512,1]{2,1,0,3:T(8,128)(2,1)S(1)} %bitcast.69), kind=kOutput, calls=%fused_computation.1 | convolution fusion | flops 1074790400 | bytes 4194304 | tf_op jit(solution)/shard_map/hdc,btc->bhdt/dot_general | solution.py:151
  123.3 37.6 %shard_map.73 = bf16[8,128,512]{2,1,0:T(8,128)(2,1)} custom-call(s32[96]{0:T(128)} %reshape.207.rel_ref, s32[8]{0:T(128)} %cnt_ref.1, bf16[8,8,128,64]{3,2,1,0:T(8,128)(2,1)} %bitcast.63, bf16[40,16,64,128]{3,2,1,0:T(8,128)(2,1)} %bitcast_dynamic-update-slice_fusion.kvt_ref, bf16[16,64,512]{2,1,0:T(8,128)(2,1)} %fusion.bkvt_ref, bf16[512,512]{1,0:T(8,128)(2,1)} %w_ref.1), custom_call_target="tpu_custom_call" | custom-call | tf_op jit(solution)/shard_map/pallas_call | solution.py:122
  (44 shorter events, 14.1 us)
Async XLA Ops:
  0.0 20.8 %copy-start = (bf16[512,512]{1,0:T(8,128)(2,1)S(1)}, bf16[512,512]{1,0:T(8,128)(2,1)}, u32[]{:S(2)}) copy-start(bf16[512,512]{1,0:T(8,128)(2,1)} %param.18) | copy-start | bytes 1572868
  0.0 23.8 %copy-start.1 = (bf16[512,1024]{1,0:T(8,128)(2,1)S(1)}, bf16[512,1024]{1,0:T(8,128)(2,1)}, u32[]{:S(2)}) copy-start(bf16[512,1024]{1,0:T(8,128)(2,1)} %param.19) | copy-start | bytes 3145732
  5.7 19.4 %collective-permute-start.2 = (bf16[128,512]{1,0:T(8,128)(2,1)S(1)}, bf16[128,512]{1,0:T(8,128)(2,1)S(1)}, u32[]{:S(2)}, u32[]{:S(2)}) collective-permute-start(bf16[128,512]{1,0:T(8,128)(2,1)S(1)} %get-tuple-element.78), channel_id=1, source_target_pairs={{0,1},{1,2},{2,3},{3,4},{4,5},{5,6},{6,7},{7,0},{8,9},{9,10},{10,1... | collective-permute-start | bytes 393224 | tf_op jit(solution)/shard_map/ppermute | solution.py:51
  7.7 20.1 %collective-permute-start.3 = (bf16[128,512]{1,0:T(8,128)(2,1)S(1)}, bf16[128,512]{1,0:T(8,128)(2,1)S(1)}, u32[]{:S(2)}, u32[]{:S(2)}) collective-permute-start(bf16[128,512]{1,0:T(8,128)(2,1)S(1)} %get-tuple-element.78), channel_id=1, source_target_pairs={{0,2},{1,3},{2,4},{3,5},{4,6},{5,7},{6,0},{7,1},{8,10},{9,11},{10,... | collective-permute-start | bytes 393224 | tf_op jit(solution)/shard_map/ppermute | solution.py:51
  11.0 21.8 %collective-permute-start.4 = (bf16[128,512]{1,0:T(8,128)(2,1)S(1)}, bf16[128,512]{1,0:T(8,128)(2,1)S(1)}, u32[]{:S(2)}, u32[]{:S(2)}) collective-permute-start(bf16[128,512]{1,0:T(8,128)(2,1)S(1)} %get-tuple-element.78), channel_id=1, source_target_pairs={{0,3},{1,4},{2,5},{3,6},{4,7},{5,0},{6,1},{7,2},{8,11},{9,12},{10,... | collective-permute-start | bytes 393224 | tf_op jit(solution)/shard_map/ppermute | solution.py:51
  15.1 19.7 %collective-permute-start.5 = (bf16[128,512]{1,0:T(8,128)(2,1)S(1)}, bf16[128,512]{1,0:T(8,128)(2,1)S(1)}, u32[]{:S(2)}, u32[]{:S(2)}) collective-permute-start(bf16[128,512]{1,0:T(8,128)(2,1)S(1)} %get-tuple-element.78), channel_id=1, source_target_pairs={{0,4},{1,5},{2,6},{3,7},{4,0},{5,1},{6,2},{7,3},{8,12},{9,13},{10,... | collective-permute-start | bytes 393224 | tf_op jit(solution)/shard_map/ppermute | solution.py:51
  15.6 25.6 %collective-permute-start.6 = (bf16[128,512]{1,0:T(8,128)(2,1)S(1)}, bf16[128,512]{1,0:T(8,128)(2,1)S(1)}, u32[]{:S(2)}, u32[]{:S(2)}) collective-permute-start(bf16[128,512]{1,0:T(8,128)(2,1)S(1)} %get-tuple-element.78), channel_id=1, source_target_pairs={{0,5},{1,6},{2,7},{3,0},{4,1},{5,2},{6,3},{7,4},{8,13},{9,14},{10,... | collective-permute-start | bytes 393224 | tf_op jit(solution)/shard_map/ppermute | solution.py:51
  25.1 28.3 %copy-start.4 = (s32[8,12]{1,0:T(8,128)S(1)}, s32[8,12]{1,0:T(8,128)}, u32[]{:S(2)}) copy-start(s32[8,12]{1,0:T(8,128)} %param.21) | copy-start | bytes 1156
  25.1 18.0 %collective-permute-start.7 = (bf16[128,512]{1,0:T(8,128)(2,1)S(1)}, bf16[128,512]{1,0:T(8,128)(2,1)S(1)}, u32[]{:S(2)}, u32[]{:S(2)}) collective-permute-start(bf16[128,512]{1,0:T(8,128)(2,1)S(1)} %get-tuple-element.78), channel_id=1, source_target_pairs={{0,6},{1,7},{2,0},{3,1},{4,2},{5,3},{6,4},{7,5},{8,14},{9,15},{10,... | collective-permute-start | bytes 393224 | tf_op jit(solution)/shard_map/ppermute | solution.py:51
  27.8 21.0 %collective-permute-start.8 = (bf16[128,512]{1,0:T(8,128)(2,1)S(1)}, bf16[128,512]{1,0:T(8,128)(2,1)S(1)}, u32[]{:S(2)}, u32[]{:S(2)}) collective-permute-start(bf16[128,512]{1,0:T(8,128)(2,1)S(1)} %get-tuple-element.78), channel_id=1, source_target_pairs={{0,7},{1,0},{2,1},{3,2},{4,3},{5,4},{6,5},{7,6},{8,15},{9,8},{10,9... | collective-permute-start | bytes 393224 | tf_op jit(solution)/shard_map/ppermute | solution.py:51
  32.8 82.8 %collective-permute-start.11 = (bf16[1024,512]{1,0:T(8,128)(2,1)}, bf16[1024,512]{1,0:T(8,128)(2,1)}, u32[]{:S(2)}, u32[]{:S(2)}) collective-permute-start(bf16[1024,512]{1,0:T(8,128)(2,1)} %param.17), channel_id=1, source_target_pairs={{1,0},{2,1},{3,2},{4,3},{5,4},{6,5},{7,6},{8,7},{9,8},{10,9},{11,1... | collective-permute-start | bytes 3145736 | tf_op jit(solution)/shard_map/ppermute | solution.py:20
  34.8 48.5 %collective-permute-start = (bf16[1024,512]{1,0:T(8,128)(2,1)}, bf16[1024,512]{1,0:T(8,128)(2,1)}, u32[]{:S(2)}, u32[]{:S(2)}) collective-permute-start(bf16[1024,512]{1,0:T(8,128)(2,1)} %param.17), channel_id=1, source_target_pairs={{0,2},{1,3},{2,4},{3,5},{4,6},{5,7},{6,8},{7,9},{8,10},{9,11},{10,... | collective-permute-start | bytes 3145736 | tf_op jit(solution)/shard_map/ppermute | solution.py:20
  41.2 66.4 %collective-permute-start.1 = (bf16[1024,512]{1,0:T(8,128)(2,1)}, bf16[1024,512]{1,0:T(8,128)(2,1)}, u32[]{:S(2)}, u32[]{:S(2)}) collective-permute-start(bf16[1024,512]{1,0:T(8,128)(2,1)} %param.17), channel_id=1, source_target_pairs={{0,1},{1,2},{2,3},{3,4},{4,5},{5,6},{6,7},{7,8},{8,9},{9,10},{10,1... | collective-permute-start | bytes 3145736 | tf_op jit(solution)/shard_map/ppermute | solution.py:20
  43.1 76.3 %collective-permute-start.12 = (bf16[1024,512]{1,0:T(8,128)(2,1)}, bf16[1024,512]{1,0:T(8,128)(2,1)}, u32[]{:S(2)}, u32[]{:S(2)}) collective-permute-start(bf16[1024,512]{1,0:T(8,128)(2,1)} %param.17), channel_id=1, source_target_pairs={{2,0},{3,1},{4,2},{5,3},{6,4},{7,5},{8,6},{9,7},{10,8},{11,9},{12,... | collective-permute-start | bytes 3145736 | tf_op jit(solution)/shard_map/ppermute | solution.py:20
  51.9 16.3 %collective-permute-start.9 = (bf16[512,512]{1,0:T(8,128)(2,1)}, bf16[512,512]{1,0:T(8,128)(2,1)}, u32[]{:S(2)}, u32[]{:S(2)}) collective-permute-start(bf16[512,512]{1,0:T(8,128)(2,1)} %select_select_fusion), channel_id=1, source_target_pairs={{0,8},{1,9},{2,10},{3,11},{4,12},{5,13},{6,14},{7,15},{8,0},{9,1},... | collective-permute-start | bytes 1572872 | tf_op jit(solution)/shard_map/ppermute | solution.py:27
  56.9 1.9 %copy-start.2 = (bf16[512,1024]{0,1:T(8,128)(2,1)S(1)}, bf16[512,1024]{0,1:T(8,128)(2,1)}, u32[]{:S(2)}) copy-start(bf16[512,1024]{0,1:T(8,128)(2,1)} %copy.14) | copy-start | bytes 3145732
  68.1 39.4 %copy-start.3 = (bf16[512,1024]{0,1:T(8,128)(2,1)S(1)}, bf16[512,1024]{0,1:T(8,128)(2,1)}, u32[]{:S(2)}) copy-start(bf16[512,1024]{0,1:T(8,128)(2,1)} %copy.14) | copy-start | bytes 3145732
  69.5 44.2 %collective-permute-start.10 = (bf16[512,512]{1,0:T(8,128)(2,1)S(1)}, bf16[512,512]{1,0:T(8,128)(2,1)S(1)}, u32[]{:S(2)}, u32[]{:S(2)}) collective-permute-start(bf16[512,512]{1,0:T(8,128)(2,1)S(1)} %broadcast_select_fusion), channel_id=1, source_target_pairs={{0,16},{1,17},{2,18},{3,19},{4,20},{5,21},{6,22},{7,23},{8,24},{9,... | collective-permute-start | bytes 1572872 | tf_op jit(solution)/shard_map/ppermute | solution.py:27

commit v14 on v11

--- a/solution.py
+++ b/solution.py
@@ -10,7 +10,7 @@
 NB = 12
 BCAP = 128
 ROW = 8
-CLASSES = (4, 8, NB)
+CLASSES = (4, 8, 10, NB)
 LOG2E = 1.4426950408889634
 
 

time: 157 us -> 163 us (1.038)
  Pallas kernels: 35.5 us -> 42 us
    pallas_call x1, Pallas kernels: 35.5 us -> 42 us  [attention(): pl.pallas_call(attention_kernel, grid_spec=grid_spec, out_shape=jax.Shape...]
  transfers between devices with their start and end apart: 13 -> 13, of which waited for: 3 -> 3; matrix products, arithmetic and copies ran while one was open for 27% -> 26% of each run, Pallas kernels for 0% -> 0%
where the time goes in v14:
time: 163 us; the launch traced here: 161 us
  Pallas kernels  42 us (26%)
  starting transfers between devices  38.7 us (24%)
  waiting for transfers between devices  30.6 us (19%)
  matrix products  25.6 us (16%)
  local copies, waits for them, and re-layouts  17.2 us (11%)
  other arithmetic  4.77 us (3%)
  between operations  2.18 us (1%)
    pallas_call x1, Pallas kernels, attention(): pl.pallas_call(attention_kernel, grid_spec=grid_spec, out_shape=jax.Shape...  42 us
    ppermute x4, waiting for transfers between devices, from_behind(): lax.ppermute(value, axis, [(source, source + steps) for source in range(f...  25.2 us
    ppermute x7, starting transfers between devices, boundary_rows(): pieces.append(lax.ppermute(compact, 'curve', pairs))  19.8 us
    dot_general x5, matrix products, on_device(): jnp.einsum('hdc,btc->bhdt', kv_w, piece.reshape(nblocks, BLOCK, width), p...  19.3 us
    ppermute x4, starting transfers between devices, from_behind(): lax.ppermute(value, axis, [(source, source + steps) for source in range(f...  16 us
    scatter x1, local copies, waits for them, and re-layouts, on_device(): kvt = kvt.at[index * nblocks:(index + 1) * nblocks].set(part)  8.31 us
    ppermute x7, waiting for transfers between devices, boundary_rows(): pieces.append(lax.ppermute(compact, 'curve', pairs))  5.41 us
    reshape x2, local copies, waits for them, and re-layouts, on_device(): queries.reshape(nblocks, BLOCK, HEADS, head_dim).transpose(0, 2, 1, 3)  4.69 us
  transfers between devices with their start and end apart: 13, of which 3 were waited for; matrix products, arithmetic and copies ran while one was open for 26% of the time, Pallas kernels for 0%

profile of v14, /device:TPU:18, one launch (start us, length us, event | category | flops | bytes accessed | tf_op | source)
XLA Modules:
  0.0 161.1 jit_solution(18342922409785509947)
XLA Ops:
  5.7 2.0 %collective-permute-start.4 = (bf16[128,512]{1,0:T(8,128)(2,1)S(1)}, bf16[128,512]{1,0:T(8,128)(2,1)S(1)}, u32[]{:S(2)}, u32[]{:S(2)}) collective-permute-start(bf16[128,512]{1,0:T(8,128)(2,1)S(1)} %get-tuple-element.74), channel_id=1, source_target_pairs={{0,1},{1,2},{2,3},{3,4},{4,5},{5,6},{6,7},{7,0},{8,9},{9,10},{10,1... | collective-permute-start | bytes 393224 | tf_op jit(solution)/shard_map/ppermute | solution.py:51
  7.7 3.3 %collective-permute-start.5 = (bf16[128,512]{1,0:T(8,128)(2,1)S(1)}, bf16[128,512]{1,0:T(8,128)(2,1)S(1)}, u32[]{:S(2)}, u32[]{:S(2)}) collective-permute-start(bf16[128,512]{1,0:T(8,128)(2,1)S(1)} %get-tuple-element.74), channel_id=1, source_target_pairs={{0,2},{1,3},{2,4},{3,5},{4,6},{5,7},{6,0},{7,1},{8,10},{9,11},{10,... | collective-permute-start | bytes 393224 | tf_op jit(solution)/shard_map/ppermute | solution.py:51
  11.0 4.0 %collective-permute-start.6 = (bf16[128,512]{1,0:T(8,128)(2,1)S(1)}, bf16[128,512]{1,0:T(8,128)(2,1)S(1)}, u32[]{:S(2)}, u32[]{:S(2)}) collective-permute-start(bf16[128,512]{1,0:T(8,128)(2,1)S(1)} %get-tuple-element.74), channel_id=1, source_target_pairs={{0,3},{1,4},{2,5},{3,6},{4,7},{5,0},{6,1},{7,2},{8,11},{9,12},{10,... | collective-permute-start | bytes 393224 | tf_op jit(solution)/shard_map/ppermute | solution.py:51
  15.5 4.9 %collective-permute-start.8 = (bf16[128,512]{1,0:T(8,128)(2,1)S(1)}, bf16[128,512]{1,0:T(8,128)(2,1)S(1)}, u32[]{:S(2)}, u32[]{:S(2)}) collective-permute-start(bf16[128,512]{1,0:T(8,128)(2,1)S(1)} %get-tuple-element.74), channel_id=1, source_target_pairs={{0,5},{1,6},{2,7},{3,0},{4,1},{5,2},{6,3},{7,4},{8,13},{9,14},{10,... | collective-permute-start | bytes 393224 | tf_op jit(solution)/shard_map/ppermute | solution.py:51
  22.3 2.7 %collective-permute-start.9 = (bf16[128,512]{1,0:T(8,128)(2,1)S(1)}, bf16[128,512]{1,0:T(8,128)(2,1)S(1)}, u32[]{:S(2)}, u32[]{:S(2)}) collective-permute-start(bf16[128,512]{1,0:T(8,128)(2,1)S(1)} %get-tuple-element.74), channel_id=1, source_target_pairs={{0,6},{1,7},{2,0},{3,1},{4,2},{5,3},{6,4},{7,5},{8,14},{9,15},{10,... | collective-permute-start | bytes 393224 | tf_op jit(solution)/shard_map/ppermute | solution.py:51
  25.1 2.2 %collective-permute-start.10 = (bf16[128,512]{1,0:T(8,128)(2,1)S(1)}, bf16[128,512]{1,0:T(8,128)(2,1)S(1)}, u32[]{:S(2)}, u32[]{:S(2)}) collective-permute-start(bf16[128,512]{1,0:T(8,128)(2,1)S(1)} %get-tuple-element.74), channel_id=1, source_target_pairs={{0,7},{1,0},{2,1},{3,2},{4,3},{5,4},{6,5},{7,6},{8,15},{9,8},{10,9... | collective-permute-start | bytes 393224 | tf_op jit(solution)/shard_map/ppermute | solution.py:51
  27.4 5.4 %collective-permute-done.6 = bf16[128,512]{1,0:T(8,128)(2,1)S(1)} collective-permute-done((bf16[128,512]{1,0:T(8,128)(2,1)S(1)}, bf16[128,512]{1,0:T(8,128)(2,1)S(1)}, u32[]{:S(2)}, u32[]{:S(2)}) %collective-permute-start.6) | collective-permute-done | bytes 131104 | tf_op jit(solution)/shard_map/ppermute | solution.py:51
  32.8 1.9 %collective-permute-start = (bf16[1024,512]{1,0:T(8,128)(2,1)}, bf16[1024,512]{1,0:T(8,128)(2,1)}, u32[]{:S(2)}, u32[]{:S(2)}) collective-permute-start(bf16[1024,512]{1,0:T(8,128)(2,1)} %param.17), channel_id=1, source_target_pairs={{0,2},{1,3},{2,4},{3,5},{4,6},{5,7},{6,8},{7,9},{8,10},{9,11},{10,... | collective-permute-start | bytes 3145736 | tf_op jit(solution)/shard_map/ppermute | solution.py:20
  34.7 5.2 %collective-permute-start.1 = (bf16[1024,512]{1,0:T(8,128)(2,1)}, bf16[1024,512]{1,0:T(8,128)(2,1)}, u32[]{:S(2)}, u32[]{:S(2)}) collective-permute-start(bf16[1024,512]{1,0:T(8,128)(2,1)} %param.17), channel_id=1, source_target_pairs={{0,1},{1,2},{2,3},{3,4},{4,5},{5,6},{6,7},{7,8},{8,9},{9,10},{10,1... | collective-permute-start | bytes 3145736 | tf_op jit(solution)/shard_map/ppermute | solution.py:20
  39.9 5.5 %collective-permute-start.2 = (bf16[1024,512]{1,0:T(8,128)(2,1)}, bf16[1024,512]{1,0:T(8,128)(2,1)}, u32[]{:S(2)}, u32[]{:S(2)}) collective-permute-start(bf16[1024,512]{1,0:T(8,128)(2,1)} %param.17), channel_id=1, source_target_pairs={{1,0},{2,1},{3,2},{4,3},{5,4},{6,5},{7,6},{8,7},{9,8},{10,9},{11,1... | collective-permute-start | bytes 3145736 | tf_op jit(solution)/shard_map/ppermute | solution.py:20
  45.5 3.4 %collective-permute-start.3 = (bf16[1024,512]{1,0:T(8,128)(2,1)}, bf16[1024,512]{1,0:T(8,128)(2,1)}, u32[]{:S(2)}, u32[]{:S(2)}) collective-permute-start(bf16[1024,512]{1,0:T(8,128)(2,1)} %param.17), channel_id=1, source_target_pairs={{2,0},{3,1},{4,2},{5,3},{6,4},{7,5},{8,6},{9,7},{10,8},{11,9},{12,... | collective-permute-start | bytes 3145736 | tf_op jit(solution)/shard_map/ppermute | solution.py:20
  48.9 2.0 %gather_fusion = bf16[512,512]{1,0:T(8,128)(2,1)S(1)} fusion(bf16[1024,512]{1,0:T(8,128)(2,1)S(1)} %constant_dynamic-update-slice_fusion, s32[1024]{0:T(1024)S(1)} %pad_clamp_fusion), kind=kCustom, calls=%fused_computation | custom fusion | bytes 1050624 | tf_op jit(solution)/shard_map/jit(_take)/gather | solution.py:57
  53.2 3.8 %convert_bitcast_fusion = bf16[8,16,64,128]{3,2,1,0:T(8,128)(2,1)} fusion(bf16[8,128,512,1]{2,1,3,0:T(8,128)(2,1)} %bitcast.3, bf16[16,64,512,1]{2,1,0,3:T(8,128)(2,1)S(1)} %bitcast.64), kind=kOutput, calls=%fused_computation.6 | convolution fusion | flops 1074790400 | bytes 4194304 | tf_op jit(solution)/shard_map/hdc,btc->bhdt/dot_general | solution.py:146
  57.0 2.9 %convolution_convert_fusion.1 = bf16[1024,512]{1,0:T(8,128)(2,1)} fusion(bf16[1024,512]{1,0:T(8,128)(2,1)} %param.17, bf16[512,512]{1,0:T(8,128)(2,1)S(1)} %copy-done), kind=kOutput, calls=%fused_computation.8 | convolution fusion | flops 537395200 | bytes 2621440 | tf_op jit(solution)/shard_map/dot_general | solution.py:134
  60.6 2.8 %reshape.232 = bf16[8,128,8,64]{3,2,1,0:T(8,128)(2,1)S(1)} reshape(bf16[1024,512]{1,0:T(8,128)(2,1)} %convolution_convert_fusion.1) | data formatting | bytes 2097152 | tf_op jit(solution)/shard_map/reshape | solution.py:135
  65.3 8.3 %scatter.16 = bf16[40,16,64,128]{3,2,1,0:T(8,128)(2,1)} pad(bf16[8,16,64,128]{3,2,1,0:T(8,128)(2,1)} %convert_bitcast_fusion, bf16[]{:T(256)} %constant.236.clone.1), padding=16_16x0_0x0_0x0_0 | pad | bytes 12582914 | tf_op jit(solution)/shard_map/scatter | solution.py:152
  76.6 6.1 %collective-permute-done = bf16[1024,512]{1,0:T(8,128)(2,1)} collective-permute-done((bf16[1024,512]{1,0:T(8,128)(2,1)}, bf16[1024,512]{1,0:T(8,128)(2,1)}, u32[]{:S(2)}, u32[]{:S(2)}) %collective-permute-start) | collective-permute-done | bytes 1048608 | tf_op jit(solution)/shard_map/ppermute | solution.py:20
  82.7 3.8 %bitcast_dynamic-update-slice_fusion.3 = bf16[40,16,64,128]{3,2,1,0:T(8,128)(2,1)} fusion(bf16[40,16,64,128]{3,2,1,0:T(8,128)(2,1)} %scatter.16, bf16[8,128,512,1]{2,1,3,0:T(8,128)(2,1)} %bitcast.10, bf16[16,64,512,1]{2,1,0,3:T(8,128)(2,1)S(1)} %bitcast.65), kind=kOutput, calls=%fused_computation.4 | convolution fusion | flops 1074790400 | bytes 4194304 | tf_op jit(solution)/shard_map/hdc,btc->bhdt/dot_general | solution.py:146
  86.5 19.1 %collective-permute-done.1 = bf16[1024,512]{1,0:T(8,128)(2,1)} collective-permute-done((bf16[1024,512]{1,0:T(8,128)(2,1)}, bf16[1024,512]{1,0:T(8,128)(2,1)}, u32[]{:S(2)}, u32[]{:S(2)}) %collective-permute-start.1) | collective-permute-done | bytes 1048608 | tf_op jit(solution)/shard_map/ppermute | solution.py:20
  105.6 3.8 %bitcast_dynamic-update-slice_fusion.2 = bf16[40,16,64,128]{3,2,1,0:T(8,128)(2,1)} fusion(bf16[40,16,64,128]{3,2,1,0:T(8,128)(2,1)} %bitcast_dynamic-update-slice_fusion.3, bf16[8,128,512,1]{2,1,3,0:T(8,128)(2,1)} %bitcast.16, bf16[16,64,512,1]{2,1,0,3:T(8,128)(2,1)S(1)} %bitcast.66), kind=kOutput, calls=%fused_computation.3 | convolution fusion | flops 1074790400 | bytes 4194304 | tf_op jit(solution)/shard_map/hdc,btc->bhdt/dot_general | solution.py:146
  109.5 3.8 %bitcast_dynamic-update-slice_fusion.1 = bf16[40,16,64,128]{3,2,1,0:T(8,128)(2,1)} fusion(bf16[40,16,64,128]{3,2,1,0:T(8,128)(2,1)} %bitcast_dynamic-update-slice_fusion.2, bf16[8,128,512,1]{2,1,3,0:T(8,128)(2,1)} %bitcast.20, bf16[16,64,512,1]{2,1,0,3:T(8,128)(2,1)S(1)} %bitcast.67), kind=kOutput, calls=%fused_computation.2 | convolution fusion | flops 1074790400 | bytes 4194304 | tf_op jit(solution)/shard_map/hdc,btc->bhdt/dot_general | solution.py:146
  113.3 3.9 %bitcast_dynamic-update-slice_fusion.kvt_ref = bf16[40,16,64,128]{3,2,1,0:T(8,128)(2,1)} fusion(bf16[40,16,64,128]{3,2,1,0:T(8,128)(2,1)} %bitcast_dynamic-update-slice_fusion.1, bf16[8,128,512,1]{2,1,3,0:T(8,128)(2,1)} %bitcast.24, bf16[16,64,512,1]{2,1,0,3:T(8,128)(2,1)S(1)} %bitcast.68), kind=kOutput, calls=%fused_computation.1 | convolution fusion | flops 1074790400 | bytes 4194304 | tf_op jit(solution)/shard_map/hdc,btc->bhdt/dot_general | solution.py:146
  117.2 1.9 %fusion.bkvt_ref = bf16[16,64,512]{2,1,0:T(8,128)(2,1)} fusion(bf16[16,64,512]{2,1,0:T(8,128)(2,1)S(1)} %bitcast.69, bf16[512,512]{1,0:T(8,128)(2,1)S(1)} %collective-permute-done.12, bf16[512,512]{1,0:T(8,128)(2,1)S(1)} %broadcast_select_fusion, pred[512]{0:T(512)(128)(4,1)S(1)} %get-tuple-element.65), kind=kOutput, calls=%fused_computation.9 | convolution fusion | flops 537657344 | bytes 3146240 | tf_op jit(solution)/shard_map/hdc,nc->hdn/dot_general | solution.py:154
  119.1 42.0 %shard_map.73 = bf16[8,128,512]{2,1,0:T(8,128)(2,1)} custom-call(s32[96]{0:T(128)} %reshape.207.rel_ref, s32[8]{0:T(128)} %cnt_ref.1, bf16[8,8,128,64]{3,2,1,0:T(8,128)(2,1)} %bitcast.63, bf16[40,16,64,128]{3,2,1,0:T(8,128)(2,1)} %bitcast_dynamic-update-slice_fusion.kvt_ref, bf16[16,64,512]{2,1,0:T(8,128)(2,1)} %fusion.bkvt_ref, bf16[512,512]{1,0:T(8,128)(2,1)} %w_ref.1), custom_call_target="tpu_custom_call" | custom-call | tf_op jit(solution)/shard_map/pallas_call | solution.py:122
  (42 shorter events, 14.0 us)
Async XLA Ops:
  0.0 57.0 %copy-start = (bf16[512,512]{1,0:T(8,128)(2,1)S(1)}, bf16[512,512]{1,0:T(8,128)(2,1)}, u32[]{:S(2)}) copy-start(bf16[512,512]{1,0:T(8,128)(2,1)} %param.18) | copy-start | bytes 1572868
  5.7 16.6 %collective-permute-start.4 = (bf16[128,512]{1,0:T(8,128)(2,1)S(1)}, bf16[128,512]{1,0:T(8,128)(2,1)S(1)}, u32[]{:S(2)}, u32[]{:S(2)}) collective-permute-start(bf16[128,512]{1,0:T(8,128)(2,1)S(1)} %get-tuple-element.74), channel_id=1, source_target_pairs={{0,1},{1,2},{2,3},{3,4},{4,5},{5,6},{6,7},{7,0},{8,9},{9,10},{10,1... | collective-permute-start | bytes 393224 | tf_op jit(solution)/shard_map/ppermute | solution.py:51
  7.7 17.4 %collective-permute-start.5 = (bf16[128,512]{1,0:T(8,128)(2,1)S(1)}, bf16[128,512]{1,0:T(8,128)(2,1)S(1)}, u32[]{:S(2)}, u32[]{:S(2)}) collective-permute-start(bf16[128,512]{1,0:T(8,128)(2,1)S(1)} %get-tuple-element.74), channel_id=1, source_target_pairs={{0,2},{1,3},{2,4},{3,5},{4,6},{5,7},{6,0},{7,1},{8,10},{9,11},{10,... | collective-permute-start | bytes 393224 | tf_op jit(solution)/shard_map/ppermute | solution.py:51
  11.0 21.8 %collective-permute-start.6 = (bf16[128,512]{1,0:T(8,128)(2,1)S(1)}, bf16[128,512]{1,0:T(8,128)(2,1)S(1)}, u32[]{:S(2)}, u32[]{:S(2)}) collective-permute-start(bf16[128,512]{1,0:T(8,128)(2,1)S(1)} %get-tuple-element.74), channel_id=1, source_target_pairs={{0,3},{1,4},{2,5},{3,6},{4,7},{5,0},{6,1},{7,2},{8,11},{9,12},{10,... | collective-permute-start | bytes 393224 | tf_op jit(solution)/shard_map/ppermute | solution.py:51
  15.0 19.7 %collective-permute-start.7 = (bf16[128,512]{1,0:T(8,128)(2,1)S(1)}, bf16[128,512]{1,0:T(8,128)(2,1)S(1)}, u32[]{:S(2)}, u32[]{:S(2)}) collective-permute-start(bf16[128,512]{1,0:T(8,128)(2,1)S(1)} %get-tuple-element.74), channel_id=1, source_target_pairs={{0,4},{1,5},{2,6},{3,7},{4,0},{5,1},{6,2},{7,3},{8,12},{9,13},{10,... | collective-permute-start | bytes 393224 | tf_op jit(solution)/shard_map/ppermute | solution.py:51
  15.5 24.4 %collective-permute-start.8 = (bf16[128,512]{1,0:T(8,128)(2,1)S(1)}, bf16[128,512]{1,0:T(8,128)(2,1)S(1)}, u32[]{:S(2)}, u32[]{:S(2)}) collective-permute-start(bf16[128,512]{1,0:T(8,128)(2,1)S(1)} %get-tuple-element.74), channel_id=1, source_target_pairs={{0,5},{1,6},{2,7},{3,0},{4,1},{5,2},{6,3},{7,4},{8,13},{9,14},{10,... | collective-permute-start | bytes 393224 | tf_op jit(solution)/shard_map/ppermute | solution.py:51
  22.3 34.7 %copy-start.1 = (bf16[512,1024]{0,1:T(8,128)(2,1)}, bf16[512,1024]{0,1:T(8,128)(2,1)S(1)}, u32[]{:S(2)}) copy-start(bf16[512,1024]{0,1:T(8,128)(2,1)S(1)} %copy.14) | copy-start | bytes 3145732
  22.3 23.1 %collective-permute-start.9 = (bf16[128,512]{1,0:T(8,128)(2,1)S(1)}, bf16[128,512]{1,0:T(8,128)(2,1)S(1)}, u32[]{:S(2)}, u32[]{:S(2)}) collective-permute-start(bf16[128,512]{1,0:T(8,128)(2,1)S(1)} %get-tuple-element.74), channel_id=1, source_target_pairs={{0,6},{1,7},{2,0},{3,1},{4,2},{5,3},{6,4},{7,5},{8,14},{9,15},{10,... | collective-permute-start | bytes 393224 | tf_op jit(solution)/shard_map/ppermute | solution.py:51
  25.1 23.8 %collective-permute-start.10 = (bf16[128,512]{1,0:T(8,128)(2,1)S(1)}, bf16[128,512]{1,0:T(8,128)(2,1)S(1)}, u32[]{:S(2)}, u32[]{:S(2)}) collective-permute-start(bf16[128,512]{1,0:T(8,128)(2,1)S(1)} %get-tuple-element.74), channel_id=1, source_target_pairs={{0,7},{1,0},{2,1},{3,2},{4,3},{5,4},{6,5},{7,6},{8,15},{9,8},{10,9... | collective-permute-start | bytes 393224 | tf_op jit(solution)/shard_map/ppermute | solution.py:51
  32.8 49.9 %collective-permute-start = (bf16[1024,512]{1,0:T(8,128)(2,1)}, bf16[1024,512]{1,0:T(8,128)(2,1)}, u32[]{:S(2)}, u32[]{:S(2)}) collective-permute-start(bf16[1024,512]{1,0:T(8,128)(2,1)} %param.17), channel_id=1, source_target_pairs={{0,2},{1,3},{2,4},{3,5},{4,6},{5,7},{6,8},{7,9},{8,10},{9,11},{10,... | collective-permute-start | bytes 3145736 | tf_op jit(solution)/shard_map/ppermute | solution.py:20
  34.7 70.9 %collective-permute-start.1 = (bf16[1024,512]{1,0:T(8,128)(2,1)}, bf16[1024,512]{1,0:T(8,128)(2,1)}, u32[]{:S(2)}, u32[]{:S(2)}) collective-permute-start(bf16[1024,512]{1,0:T(8,128)(2,1)} %param.17), channel_id=1, source_target_pairs={{0,1},{1,2},{2,3},{3,4},{4,5},{5,6},{6,7},{7,8},{8,9},{9,10},{10,1... | collective-permute-start | bytes 3145736 | tf_op jit(solution)/shard_map/ppermute | solution.py:20
  39.9 69.5 %collective-permute-start.2 = (bf16[1024,512]{1,0:T(8,128)(2,1)}, bf16[1024,512]{1,0:T(8,128)(2,1)}, u32[]{:S(2)}, u32[]{:S(2)}) collective-permute-start(bf16[1024,512]{1,0:T(8,128)(2,1)} %param.17), channel_id=1, source_target_pairs={{1,0},{2,1},{3,2},{4,3},{5,4},{6,5},{7,6},{8,7},{9,8},{10,9},{11,1... | collective-permute-start | bytes 3145736 | tf_op jit(solution)/shard_map/ppermute | solution.py:20
  45.5 67.9 %collective-permute-start.3 = (bf16[1024,512]{1,0:T(8,128)(2,1)}, bf16[1024,512]{1,0:T(8,128)(2,1)}, u32[]{:S(2)}, u32[]{:S(2)}) collective-permute-start(bf16[1024,512]{1,0:T(8,128)(2,1)} %param.17), channel_id=1, source_target_pairs={{2,0},{3,1},{4,2},{5,3},{6,4},{7,5},{8,6},{9,7},{10,8},{11,9},{12,... | collective-permute-start | bytes 3145736 | tf_op jit(solution)/shard_map/ppermute | solution.py:20
  51.9 21.7 %collective-permute-start.11 = (bf16[512,512]{1,0:T(8,128)(2,1)}, bf16[512,512]{1,0:T(8,128)(2,1)}, u32[]{:S(2)}, u32[]{:S(2)}) collective-permute-start(bf16[512,512]{1,0:T(8,128)(2,1)} %select_select_fusion), channel_id=1, source_target_pairs={{0,8},{1,9},{2,10},{3,11},{4,12},{5,13},{6,14},{7,15},{8,0},{9,1},... | collective-permute-start | bytes 1572872 | tf_op jit(solution)/shard_map/ppermute | solution.py:27
  53.2 6.7 %copy-start.3 = (s32[8,12]{1,0:T(8,128)S(1)}, s32[8,12]{1,0:T(8,128)}, u32[]{:S(2)}) copy-start(s32[8,12]{1,0:T(8,128)} %param.21) | copy-start | bytes 1156
  65.3 17.4 %copy-start.2 = (bf16[512,1024]{0,1:T(8,128)(2,1)S(1)}, bf16[512,1024]{0,1:T(8,128)(2,1)}, u32[]{:S(2)}) copy-start(bf16[512,1024]{0,1:T(8,128)(2,1)} %copy-done.1) | copy-start | bytes 3145732
  74.9 42.3 %collective-permute-start.12 = (bf16[512,512]{1,0:T(8,128)(2,1)S(1)}, bf16[512,512]{1,0:T(8,128)(2,1)S(1)}, u32[]{:S(2)}, u32[]{:S(2)}) collective-permute-start(bf16[512,512]{1,0:T(8,128)(2,1)S(1)} %broadcast_select_fusion), channel_id=1, source_target_pairs={{0,16},{1,17},{2,18},{3,19},{4,20},{5,21},{6,22},{7,23},{8,24},{9,... | collective-permute-start | bytes 1572872 | tf_op jit(solution)/shard_map/ppermute | solution.py:27
